TPU v7x, 32 devices: a whole 2x2x4 slice. The times are simulated.
32 devices in a mesh: cuts: 8 (over y, x, core), row: 4 (over z).
Axes of the slice: x: 2, y: 2, z: 4, core: 2. Of those that a mesh axis runs over, the one named last changes fastest.
Arguments:
- vectors: bfloat16 [8, 128, 98304], P('cuts', None, 'row'), may hold values from -100 to 100
- counts: int32 [8], P('cuts'), may hold values from 64 to 128, as said below
- offsets: int32 [8, 2], P('cuts'), may hold values from 0 to 96, as said below
- margin_blocks: bfloat16 [1024, 96, 288], P('row'), may hold values from -0.5 to 1.5
- energy_blocks: bfloat16 [1024, 96, 288], P('row'), may hold values from -1 to 6
- block_columns: int32 [1024, 3], P('row'), may hold values from 0 to 1023, as said below
Outputs:
- ritz_residual: bfloat16 [8, 128, 98304], P('cuts', None, 'row')
- margin_pencil: float32 [8, 128, 128], P('cuts')
- energy_pencil: float32 [8, 128, 128], P('cuts')
Inputs may be any that keep to these rules, and one draw needn't show every extreme that they name: `counts`: some slice has all 128 vectors valid and another exactly 64. offsets[s, 0] is at most 8; offsets[s, 1] + 32 lies between counts[s] - 8 and counts[s]; so both windows lie among the valid vectors. block_columns[i, 0] = i, block_columns[i, 1] lies in i - 2 to i and block_columns[i, 2] in i to i + 2.
All inputs are finite; a program needn't handle non-finite values.
Results may differ from a plain program's by a relative error of at most 0.00225.
The roundings to bfloat16 on the way count: a program that leaves them out, or rounds other values in their place, can miss the bound.
Values may be sent and summed in bfloat16 or wider, within the bound.
No kernel may reach another device: no remote copies, remote signals or barrier semaphores. Data moves between devices by JAX's collectives and lax.ppermute only.
A program may use at most 256 MiB of HBM per device.

v0:
```python
import jax
import jax.numpy as jnp
from jax import lax
from jax.sharding import PartitionSpec as P

NMAT = 98304
WIN = 32


def from_behind(block, axis, distance):
    devices = range(lax.axis_size(axis))
    route = [(i - distance, i) for i in devices if i - distance in devices]
    return lax.ppermute(block, axis, route)


def padded_2(cells, sides, width):
    for axis, dim in sides:
        count = lax.axis_size(axis)
        ends = count - 1
        head = lax.slice_in_dim(cells, 0, width, axis=dim)
        tail = lax.slice_in_dim(cells, cells.shape[dim] - width, cells.shape[dim], axis=dim)
        cells = jnp.concatenate(
            [
                lax.ppermute(tail, axis, [(i, (i + 1) % count) for i in range(ends)]),
                cells,
                lax.ppermute(head, axis, [((i + 1) % count, i) for i in range(ends)]),
            ],
            axis=dim,
        )
    return cells


def block_product(matrices, shifts, padded):
    width = padded.shape[0]
    block_rows = shifts.shape[0]
    size_block = matrices[0].shape[1]
    grid = padded.reshape(width, block_rows + 4, size_block)
    centre = grid[:, 2 : 2 + block_rows]
    choices_of = ((0,), (-2, -1, 0), (0, 1, 2))
    picked_all = []
    for column_slot in range(len(choices_of)):
        picked = centre
        for distance in choices_of[column_slot]:
            if distance != 0:
                view = grid[:, 2 + distance : 2 + distance + block_rows]
                hit = (shifts[:, column_slot] == distance)[None, :, None]
                picked = jnp.where(hit, view, picked)
        picked_all.append(picked)
    results = []
    for blocks in matrices:
        total = None
        for column_slot in range(len(choices_of)):
            part_blocks = blocks[:, :, column_slot * size_block : (column_slot + 1) * size_block]
            term = jnp.einsum(
                "cnb,nab->cna",
                picked_all[column_slot],
                part_blocks,
                preferred_element_type=jnp.float32,
            )
            total = term if total is None else total + term
        results.append(total.reshape(width, block_rows * size_block).astype(jnp.bfloat16))
    return results


def shards(vectors, counts, offsets, margin_blocks, energy_blocks, block_columns):
    own_vectors = vectors[0]
    vector_count = own_vectors.shape[0]
    block_rows = margin_blocks.shape[0]
    size_block = margin_blocks.shape[1]
    rim_width = 2 * size_block
    valid_mask = jnp.arange(vector_count, dtype=jnp.int32) < counts[0]
    masked = jnp.where(valid_mask[:, None], own_vectors, jnp.zeros((), own_vectors.dtype))
    lower_window = lax.dynamic_slice_in_dim(masked, offsets[0, 0], WIN, 0)
    upper_window = lax.dynamic_slice_in_dim(masked, offsets[0, 1], WIN, 0)
    own_blocks = lax.axis_index("row") * block_rows + jnp.arange(block_rows, dtype=jnp.int32)
    shifts = block_columns - own_blocks[:, None]
    from_below = [from_behind(upper_window, "cuts", distance) for distance in (2, 1)]
    from_above = [from_behind(lower_window, "cuts", -distance) for distance in (1, 2)]
    windows = jnp.concatenate(from_below + from_above, axis=0)
    padded_windows = padded_2(windows, (("row", 1),), rim_width)
    margin_windows = block_product((margin_blocks,), shifts, padded_windows)[0]
    partial_margin = jnp.dot(margin_windows, masked.T, preferred_element_type=jnp.float32)
    margin = lax.psum(partial_margin, "row") / NMAT
    removed = jnp.dot(margin.astype(jnp.bfloat16).T, windows, preferred_element_type=jnp.float32)
    cleaned = (masked.astype(jnp.float32) - removed).astype(jnp.bfloat16)
    padded_cleaned = padded_2(cleaned, (("row", 1),), rim_width)
    margin_cleaned, energy_cleaned = block_product(
        (margin_blocks, energy_blocks), shifts, padded_cleaned
    )
    margin_part = jnp.dot(cleaned, margin_cleaned.T, preferred_element_type=jnp.float32)
    energy_part = jnp.dot(cleaned, energy_cleaned.T, preferred_element_type=jnp.float32)
    margin_total, energy_total = lax.psum((margin_part, energy_part), "row")
    margin_pencil = margin_total / NMAT
    energy_pencil = energy_total / NMAT
    margin_diag = jnp.diagonal(margin_pencil)
    energy_diag = jnp.diagonal(energy_pencil)
    theta = jnp.where(
        valid_mask,
        energy_diag / jnp.where(valid_mask, margin_diag, jnp.float32(1.0)),
        jnp.float32(0.0),
    )
    residual = (
        energy_cleaned.astype(jnp.float32) - theta[:, None] * margin_cleaned.astype(jnp.float32)
    ).astype(jnp.bfloat16)
    return (residual[None], margin_pencil[None], energy_pencil[None])


def solution(mesh):
    placed = (
        P("cuts", None, "row"),
        P("cuts"),
        P("cuts", None),
        P("row", None, None),
        P("row", None, None),
        P("row", None),
    )
    return jax.shard_map(
        shards,
        mesh=mesh,
        in_specs=placed,
        out_specs=(P("cuts", None, "row"), P("cuts", None, None), P("cuts", None, None)),
        check_vma=False,
    )
```

profile of v0, /device:TPU:12, one launch (start us, length us, event | category | flops | bytes accessed | tf_op | source)
XLA Modules:
  0.0 496.6 jit_solution(1936045789571381187)
XLA Ops:
  33.8 10.8 %fusion.36 = (bf16[256,96,96]{0,2,1:T(8,128)(2,1)}, bf16[256,96,96]{0,2,1:T(8,128)(2,1)}, bf16[256,96,96]{0,2,1:T(8,128)(2,1)}) fusion(bf16[256,96,288]{0,2,1:T(8,128)(2,1)} %param.9), kind=kLoop, calls=%fused_computation.64 | loop fusion | bytes 28311552 | tf_op jit(solution)/shard_map/slice | solution.py:53
  44.6 17.2 %collective-permute-done = bf16[32,24576]{1,0:T(8,128)(2,1)} collective-permute-done((bf16[32,24576]{1,0:T(8,128)(2,1)}, bf16[32,24576]{1,0:T(8,128)(2,1)}, u32[]{:S(2)}, u32[]{:S(2)}) %collective-permute-start) | collective-permute-done | bytes 1572896 | tf_op jit(solution)/shard_map/ppermute | solution.py:13
  63.3 29.9 %collective-permute-done.1 = bf16[32,24576]{1,0:T(8,128)(2,1)} collective-permute-done((bf16[32,24576]{1,0:T(8,128)(2,1)}, bf16[32,24576]{1,0:T(8,128)(2,1)}, u32[]{:S(2)}, u32[]{:S(2)}) %collective-permute-start.1) | collective-permute-done | bytes 1572896 | tf_op jit(solution)/shard_map/ppermute | solution.py:13
  94.9 31.3 %collective-permute-done.3 = bf16[32,24576]{1,0:T(8,128)(2,1)S(1)} collective-permute-done((bf16[32,24576]{1,0:T(8,128)(2,1)}, bf16[32,24576]{1,0:T(8,128)(2,1)S(1)}, u32[]{:S(2)}, u32[]{:S(2)}) %collective-permute-start.3) | collective-permute-done | bytes 1572896 | tf_op jit(solution)/shard_map/ppermute | solution.py:13
  135.0 8.4 %copy.31 = bf16[256,96,96]{2,1,0:T(8,128)(2,1)} copy(bf16[256,96,96]{0,2,1:T(8,128)(2,1)} %get-tuple-element.13) | data formatting | bytes 9437184
  143.4 8.4 %copy.30 = bf16[256,96,96]{2,1,0:T(8,128)(2,1)} copy(bf16[256,96,96]{0,2,1:T(8,128)(2,1)} %get-tuple-element.14) | data formatting | bytes 9437184
  151.8 8.5 %copy.32 = bf16[256,96,96]{2,1,0:T(8,128)(2,1)} copy(bf16[256,96,96]{0,2,1:T(8,128)(2,1)} %get-tuple-element.12) | data formatting | bytes 9437184
  160.3 13.5 %concatenate.15 = bf16[128,24960]{1,0:T(8,128)(2,1)} concatenate(bf16[128,192]{1,0:T(8,128)(2,1)S(1)} %collective-permute-done.4, bf16[128,24576]{1,0:T(8,128)(2,1)} %copy-done.4, bf16[128,192]{1,0:T(8,128)(2,1)S(1)} %collective-permute-done.5), dimensions={1} | concatenate | bytes 12779520 | tf_op jit(solution)/shard_map/concatenate | solution.py:22
  173.8 9.2 %copy.19 = bf16[128,24960]{0,1:T(8,128)(2,1)} copy(bf16[128,24960]{1,0:T(8,128)(2,1)} %concatenate.15) | data formatting | bytes 12779520 | tf_op jit(solution)/shard_map/concatenate | solution.py:22
  183.0 11.1 %fusion.21 = f32[256,128,96]{1,2,0:T(8,128)} fusion(bf16[256,96,96]{2,1,0:T(8,128)(2,1)} %copy.30, bf16[128,260,96]{0,2,1:T(8,128)(2,1)} %bitcast.69), kind=kOutput, calls=%fused_computation.33 | convolution fusion | flops 603979776 | bytes 25165824 | tf_op jit(solution)/shard_map/cnb,nab->cna/dot_general | solution.py:54
  194.1 14.7 %fusion.8 = f32[256,128,96]{1,2,0:T(8,128)} fusion(bf16[256,96,96]{2,1,0:T(8,128)(2,1)} %copy.31, bf16[128,260,96]{0,2,1:T(8,128)(2,1)} %bitcast.70, pred[256]{0:T(512)(128)(4,1)S(1)} %get-tuple-element.4, pred[256]{0:T(512)(128)(4,1)S(1)} %get-tuple-element.6), kind=kOutput, calls=%fused_computation.18 | convolution fusion | flops 610271232 | bytes 37749248 | tf_op jit(solution)/shard_map/cnb,nab->cna/dot_general | solution.py:54
  208.8 18.4 %add_convert_fusion.2 = bf16[256,128,96]{1,2,0:T(8,128)(2,1)} fusion(f32[256,128,96]{1,2,0:T(8,128)} %fusion.21, f32[256,128,96]{1,2,0:T(8,128)} %fusion.8, bf16[256,96,96]{2,1,0:T(8,128)(2,1)S(1)} %bitcast.68, bf16[128,260,96]{0,2,1:T(8,128)(2,1)} %bitcast.71, pred[256]{0:T(512)(128)(4,1)S(1)} %get-tuple-element.5, pred[256]{0:T(512)(128)(4,1)S(1)} %get-tuple-element.3), kind=kOutput, calls=%fused_computation.7 | convolution fusion | flops 619708416 | bytes 55050752 | tf_op jit(solution)/shard_map/cnb,nab->cna/dot_general | solution.py:54
  234.7 10.8 %fusion.35 = (bf16[256,96,96]{0,2,1:T(8,128)(2,1)}, bf16[256,96,96]{0,2,1:T(8,128)(2,1)}, bf16[256,96,96]{0,2,1:T(8,128)(2,1)}) fusion(bf16[256,96,288]{0,2,1:T(8,128)(2,1)} %param.10), kind=kLoop, calls=%fused_computation.63 | loop fusion | bytes 28311552 | tf_op jit(solution)/shard_map/slice | solution.py:53
  245.5 25.1 %all-reduce.4.cloned.1.call-done = f32[128,128]{1,0:T(8,128)} async-done(((f32[128,128]{1,0:T(8,128)}), f32[128,128]{1,0:T(8,128)}) %all-reduce.4.cloned.1.call-update) | async-done | bytes 65552 | tf_op jit(solution)/shard_map/psum | solution.py:83
  285.6 8.4 %copy.33 = bf16[256,96,96]{2,1,0:T(8,128)(2,1)} copy(bf16[256,96,96]{0,2,1:T(8,128)(2,1)} %get-tuple-element.10) | data formatting | bytes 9437184
  294.0 8.3 %copy.29 = bf16[256,96,96]{2,1,0:T(8,128)(2,1)} copy(bf16[256,96,96]{0,2,1:T(8,128)(2,1)} %get-tuple-element.11) | data formatting | bytes 9437184
  302.3 8.5 %copy.34 = bf16[256,96,96]{2,1,0:T(8,128)(2,1)} copy(bf16[256,96,96]{0,2,1:T(8,128)(2,1)} %get-tuple-element.9) | data formatting | bytes 9437184
  310.7 13.5 %concatenate.16 = bf16[128,24960]{1,0:T(8,128)(2,1)} concatenate(bf16[128,192]{1,0:T(8,128)(2,1)S(1)} %collective-permute-done.6, bf16[128,24576]{1,0:T(8,128)(2,1)} %copy-done.1, bf16[128,192]{1,0:T(8,128)(2,1)S(1)} %collective-permute-done.7), dimensions={1} | concatenate | bytes 12779520 | tf_op jit(solution)/shard_map/concatenate | solution.py:22
  324.2 9.2 %copy.23 = bf16[128,24960]{0,1:T(8,128)(2,1)} copy(bf16[128,24960]{1,0:T(8,128)(2,1)} %concatenate.16) | data formatting | bytes 12779520 | tf_op jit(solution)/shard_map/concatenate | solution.py:22
  333.4 13.8 %fusion.1 = (bf16[128,256,96]{0,2,1:T(8,128)(2,1)}, bf16[128,256,96]{0,2,1:T(8,128)(2,1)S(1)}) fusion(bf16[128,260,96]{0,2,1:T(8,128)(2,1)} %bitcast.56, pred[256]{0:T(512)(128)(4,1)S(1)} %get-tuple-element.5, pred[256]{0:T(512)(128)(4,1)S(1)} %get-tuple-element.3, pred[256]{0:T(512)(128)(4,1)S(1)} %get-tuple-element.4, pred[256]{0:T(512)(128)(4,1)S(1)} %get-tuple-element.6), kind=kLoop, calls=%fused_computation.9 | loop fusion | flops 12582912 | bytes 44041216 | tf_op jit(solution)/shard_map/jit(_where)/select_n | solution.py:47
  347.3 11.4 %fusion.25 = f32[256,128,96]{1,2,0:T(8,128)} fusion(bf16[256,96,96]{2,1,0:T(8,128)(2,1)} %copy.30, bf16[128,260,96]{0,2,1:T(8,128)(2,1)S(1)} %bitcast.57), kind=kOutput, calls=%fused_computation.37 | convolution fusion | flops 603979776 | bytes 23592960 | tf_op jit(solution)/shard_map/cnb,nab->cna/dot_general | solution.py:54
  358.7 9.1 %fusion.43 = f32[256,128,96]{1,2,0:T(8,128)} fusion(bf16[256,96,96]{2,1,0:T(8,128)(2,1)} %copy.31, bf16[128,256,96]{0,2,1:T(8,128)(2,1)S(1)} %get-tuple-element.16), kind=kOutput, calls=%fused_computation.71 | convolution fusion | flops 603979776 | bytes 23592960 | tf_op jit(solution)/shard_map/cnb,nab->cna/dot_general | solution.py:54
  367.8 15.8 %add_convert_fusion = bf16[256,128,96]{1,2,0:T(8,128)(2,1)} fusion(f32[256,128,96]{1,2,0:T(8,128)} %fusion.25, f32[256,128,96]{1,2,0:T(8,128)} %fusion.43, bf16[256,96,96]{2,1,0:T(8,128)(2,1)} %copy.32, bf16[128,256,96]{0,2,1:T(8,128)(2,1)} %get-tuple-element.15), kind=kOutput, calls=%fused_computation.5 | convolution fusion | flops 613416960 | bytes 42467328 | tf_op jit(solution)/shard_map/cnb,nab->cna/dot_general | solution.py:54
  383.7 7.2 %fusion.41 = f32[128,128]{1,0:T(8,128)} fusion(bf16[128,24576]{1,0:T(8,128)(2,1)} %copy-done.1, bf16[128,24576]{0,1:T(8,128)(2,1)} %bitcast.63), kind=kOutput, calls=%fused_computation.69 | convolution fusion | flops 805306368 | bytes 12648448 | tf_op jit(solution)/shard_map/dot_general | solution.py:90
  390.9 9.3 %fusion.42 = f32[256,128,96]{1,2,0:T(8,128)} fusion(bf16[256,96,96]{2,1,0:T(8,128)(2,1)} %copy.33, bf16[128,256,96]{0,2,1:T(8,128)(2,1)S(1)} %bitcast.62), kind=kOutput, calls=%fused_computation.70 | convolution fusion | flops 603979776 | bytes 23592960 | tf_op jit(solution)/shard_map/cnb,nab->cna/dot_general | solution.py:54
  400.2 9.1 %fusion.23 = f32[256,128,96]{1,2,0:T(8,128)} fusion(bf16[256,96,96]{2,1,0:T(8,128)(2,1)} %copy.29, bf16[128,260,96]{0,2,1:T(8,128)(2,1)S(1)} %bitcast.60), kind=kOutput, calls=%fused_computation.35 | convolution fusion | flops 603979776 | bytes 23592960 | tf_op jit(solution)/shard_map/cnb,nab->cna/dot_general | solution.py:54
  409.3 15.8 %add_convert_fusion.1 = bf16[256,128,96]{1,2,0:T(8,128)(2,1)} fusion(f32[256,128,96]{1,2,0:T(8,128)} %fusion.23, f32[256,128,96]{1,2,0:T(8,128)} %fusion.42, bf16[256,96,96]{2,1,0:T(8,128)(2,1)} %copy.34, bf16[128,256,96]{0,2,1:T(8,128)(2,1)} %get-tuple-element.15), kind=kOutput, calls=%fused_computation.6 | convolution fusion | flops 613416960 | bytes 42467328 | tf_op jit(solution)/shard_map/cnb,nab->cna/dot_general | solution.py:54
  432.1 7.4 %bitcast_convert_fusion = f32[1,128,24576]{1,2,0:T(8,128)} fusion(bf16[1,128,24576]{1,2,0:T(8,128)(2,1)} %bitcast.64), kind=kLoop, calls=%fused_computation.20 | loop fusion | flops 3145728 | bytes 18874368 | tf_op jit(solution)/shard_map/convert_element_type | solution.py:103
  439.5 7.5 %bitcast_convert_fusion.1 = f32[1,128,24576]{1,2,0:T(8,128)} fusion(bf16[1,128,24576]{1,2,0:T(8,128)(2,1)} %bitcast.66), kind=kLoop, calls=%fused_computation.21 | loop fusion | flops 3145728 | bytes 18874368 | tf_op jit(solution)/shard_map/convert_element_type | solution.py:103
  447.0 12.6 %copy.27 = f32[1,128,24576]{2,1,0:T(8,128)} copy(f32[1,128,24576]{1,2,0:T(8,128)} %bitcast_convert_fusion) | data formatting | bytes 25165824 | tf_op jit(solution)/shard_map/convert_element_type | solution.py:103
  459.6 12.6 %copy.28 = f32[1,128,24576]{2,1,0:T(8,128)} copy(f32[1,128,24576]{1,2,0:T(8,128)} %bitcast_convert_fusion.1) | data formatting | bytes 25165824 | tf_op jit(solution)/shard_map/convert_element_type | solution.py:103
  478.0 11.8 %subtract_convert_fusion = bf16[1,128,24576]{2,1,0:T(8,128)(2,1)} fusion(f32[1,128,24576]{2,1,0:T(8,128)} %copy.28, f32[1,128,24576]{2,1,0:T(8,128)} %copy.27, f32[128]{0:T(128)S(1)} %divide_select_fusion), kind=kLoop, calls=%fused_computation.4 | loop fusion | flops 9437184 | bytes 31457792 | tf_op jit(solution)/shard_map/convert_element_type | solution.py:104
  (66 shorter events, 69.1 us)
Async XLA Ops:
  7.2 263.4 %all-reduce.4.cloned.1.call-start = ((), (), s32[]{:S(2)}) async-start(), calls=%async_computation | async-start | bytes 131072 | tf_op jit(solution)/shard_map/psum | solution.py:83
  16.3 2.6 copy-start.3
  18.9 14.8 %copy-start.5 = (s32[256,3]{0,1:T(4,128)S(1)}, s32[256,3]{0,1:T(4,128)}, u32[]{:S(2)}) copy-start(s32[256,3]{0,1:T(4,128)} %param.11) | copy-start | bytes 9220
  21.4 40.4 %collective-permute-start = (bf16[32,24576]{1,0:T(8,128)(2,1)}, bf16[32,24576]{1,0:T(8,128)(2,1)}, u32[]{:S(2)}, u32[]{:S(2)}) collective-permute-start(bf16[32,24576]{1,0:T(8,128)(2,1)} %get-tuple-element.22), channel_id=1, source_target_pairs={{0,8},{4,12},{8,16},{12,20},{16,24},{20,28},{1,9},{5,13},{9,17},{1... | collective-permute-start | bytes 4718600 | tf_op jit(solution)/shard_map/ppermute | solution.py:13
  24.8 68.4 %collective-permute-start.1 = (bf16[32,24576]{1,0:T(8,128)(2,1)}, bf16[32,24576]{1,0:T(8,128)(2,1)}, u32[]{:S(2)}, u32[]{:S(2)}) collective-permute-start(bf16[32,24576]{1,0:T(8,128)(2,1)} %get-tuple-element.22), channel_id=1, source_target_pairs={{0,4},{4,8},{8,12},{12,16},{16,20},{20,24},{24,28},{1,5},{5,9},{9,... | collective-permute-start | bytes 4718600 | tf_op jit(solution)/shard_map/ppermute | solution.py:13
  26.8 68.0 %collective-permute-start.2 = (bf16[32,24576]{1,0:T(8,128)(2,1)}, bf16[32,24576]{1,0:T(8,128)(2,1)S(1)}, u32[]{:S(2)}, u32[]{:S(2)}) collective-permute-start(bf16[32,24576]{1,0:T(8,128)(2,1)} %get-tuple-element.21), channel_id=1, source_target_pairs={{4,0},{8,4},{12,8},{16,12},{20,16},{24,20},{28,24},{5,1},{9,5},{13... | collective-permute-start | bytes 4718600 | tf_op jit(solution)/shard_map/ppermute | solution.py:13
  31.3 94.9 %collective-permute-start.3 = (bf16[32,24576]{1,0:T(8,128)(2,1)}, bf16[32,24576]{1,0:T(8,128)(2,1)S(1)}, u32[]{:S(2)}, u32[]{:S(2)}) collective-permute-start(bf16[32,24576]{1,0:T(8,128)(2,1)} %get-tuple-element.21), channel_id=1, source_target_pairs={{8,0},{12,4},{16,8},{20,12},{24,16},{28,20},{9,1},{13,5},{17,9},{2... | collective-permute-start | bytes 4718600 | tf_op jit(solution)/shard_map/ppermute | solution.py:13
  126.3 2.7 copy-start.4
  129.1 31.2 %collective-permute-start.4 = (bf16[128,192]{1,0:T(8,128)(2,1)S(1)}, bf16[128,192]{1,0:T(8,128)(2,1)S(1)}, u32[]{:S(2)}, u32[]{:S(2)}) collective-permute-start(bf16[128,192]{1,0:T(8,128)(2,1)S(1)} %get-tuple-element.20), channel_id=1, source_target_pairs={{0,1},{1,2},{2,3},{4,5},{5,6},{6,7},{8,9},{9,10},{10,11},{12,13},{... | collective-permute-start | bytes 147464 | tf_op jit(solution)/shard_map/ppermute | solution.py:24
  132.6 27.7 %collective-permute-start.5 = (bf16[128,192]{1,0:T(8,128)(2,1)S(1)}, bf16[128,192]{1,0:T(8,128)(2,1)S(1)}, u32[]{:S(2)}, u32[]{:S(2)}) collective-permute-start(bf16[128,192]{1,0:T(8,128)(2,1)S(1)} %get-tuple-element.19), channel_id=1, source_target_pairs={{1,0},{2,1},{3,2},{5,4},{6,5},{7,6},{9,8},{10,9},{11,10},{13,12},{... | collective-permute-start | bytes 147464 | tf_op jit(solution)/shard_map/ppermute | solution.py:26
  183.0 25.8 %slice-start.4 = ((s8[6291456]{0:T(1024)(128)(4,1)}), s8[4194304]{0:T(1024)(128)(4,1)S(1)}, s32[]{:S(2)}) async-start(s8[6291456]{0:T(1024)(128)(4,1)} %bitcast.67), calls=%async_computation.6 | async-start | bytes 8388608
  194.1 14.8 %slice-start.5 = ((s8[6291456]{0:T(1024)(128)(4,1)}), s8[2097152]{0:T(1024)(128)(4,1)S(1)}, s32[]{:S(2)}) async-start(s8[6291456]{0:T(1024)(128)(4,1)} %bitcast.67), calls=%async_computation.7 | async-start | bytes 4194304
  234.5 239.5 %all-reduce.6.cloned.1.call-start = ((), (), s32[]{:S(2)}) async-start(), calls=%async_computation.1 | async-start | bytes 262144 | tf_op jit(solution)/shard_map/psum | solution.py:92
  277.0 2.6 copy-start.1
  279.7 31.1 %collective-permute-start.6 = (bf16[128,192]{1,0:T(8,128)(2,1)S(1)}, bf16[128,192]{1,0:T(8,128)(2,1)S(1)}, u32[]{:S(2)}, u32[]{:S(2)}) collective-permute-start(bf16[128,192]{1,0:T(8,128)(2,1)S(1)} %get-tuple-element.18), channel_id=1, source_target_pairs={{0,1},{1,2},{2,3},{4,5},{5,6},{6,7},{8,9},{9,10},{10,11},{12,13},{... | collective-permute-start | bytes 147464 | tf_op jit(solution)/shard_map/ppermute | solution.py:24
  282.9 27.9 %collective-permute-start.7 = (bf16[128,192]{1,0:T(8,128)(2,1)S(1)}, bf16[128,192]{1,0:T(8,128)(2,1)S(1)}, u32[]{:S(2)}, u32[]{:S(2)}) collective-permute-start(bf16[128,192]{1,0:T(8,128)(2,1)S(1)} %get-tuple-element.17), channel_id=1, source_target_pairs={{1,0},{2,1},{3,2},{5,4},{6,5},{7,6},{9,8},{10,9},{11,10},{13,12},{... | collective-permute-start | bytes 147464 | tf_op jit(solution)/shard_map/ppermute | solution.py:26
  333.4 13.8 %copy-start = (bf16[128,24960]{0,1:T(8,128)(2,1)S(1)}, bf16[128,24960]{0,1:T(8,128)(2,1)}, u32[]{:S(2)}) copy-start(bf16[128,24960]{0,1:T(8,128)(2,1)} %copy.23) | copy-start | bytes 19169284
  347.3 11.4 %copy-start.2 = (bf16[128,256,96]{0,2,1:T(8,128)(2,1)}, bf16[128,256,96]{0,2,1:T(8,128)(2,1)S(1)}, u32[]{:S(2)}) copy-start(bf16[128,256,96]{0,2,1:T(8,128)(2,1)S(1)} %get-tuple-element.16) | copy-start | bytes 18874372
  383.7 7.2 %slice-start.2 = ((s8[6291456]{0:T(1024)(128)(4,1)}), s8[4194304]{0:T(1024)(128)(4,1)S(1)}, s32[]{:S(2)}) async-start(s8[6291456]{0:T(1024)(128)(4,1)} %bitcast.61), calls=%async_computation.4 | async-start | bytes 8388608
  383.7 7.2 %slice-start.3 = ((s8[6291456]{0:T(1024)(128)(4,1)}), s8[2097152]{0:T(1024)(128)(4,1)S(1)}, s32[]{:S(2)}) async-start(s8[6291456]{0:T(1024)(128)(4,1)} %bitcast.61), calls=%async_computation.5 | async-start | bytes 4194304
  383.7 16.5 %slice-start = ((s8[6389760]{0:T(1024)(128)(4,1)}), s8[4194304]{0:T(1024)(128)(4,1)S(1)}, s32[]{:S(2)}) async-start(s8[6389760]{0:T(1024)(128)(4,1)} %bitcast.58), calls=%async_computation.2 | async-start | bytes 8388608
  390.9 9.3 %slice-start.1 = ((s8[6389760]{0:T(1024)(128)(4,1)}), s8[2195456]{0:T(1024)(128)(4,1)S(1)}, s32[]{:S(2)}) async-start(s8[6389760]{0:T(1024)(128)(4,1)} %bitcast.58), calls=%async_computation.3 | async-start | bytes 4390912
Sparse Core Ops, SparseCore 0:
  234.6 35.9 all-reduce.3
  439.6 34.2 all-reduce.5
where the time goes:
time: 501 us; the launch traced here: 497 us
  local copies, waits for them, and re-layouts  160 us (32%)
  matrix products  143 us (29%)
  waiting for transfers between devices  105 us (21%)
  other arithmetic  45.3 us (9%)
  starting transfers between devices  24.2 us (5%)
  between operations  18.8 us (4%)
    dot_general x9, matrix products, block_product(): jnp.einsum('cnb,nab->cna', picked_all[column_slot], part_blocks, preferre...  115 us
    ppermute x4, waiting for transfers between devices, from_behind(): return lax.ppermute(block, axis, route)  78.4 us
    unnamed x33, local copies, waits for them, and re-layouts  61.5 us
    concatenate x4, local copies, waits for them, and re-layouts, padded_2(): jnp.concatenate([lax.ppermute(tail, axis, [(i, (i + 1) % count) for i in...  45.4 us
    psum x1, waiting for transfers between devices, shards(): margin = lax.psum(partial_margin, 'row') / NMAT  25.1 us
    slice x2, local copies, waits for them, and re-layouts, block_product(): blocks[:, :, column_slot * size_block:(column_slot + 1) * size_block]  21.6 us
    select_n x1, other arithmetic, block_product(): picked = jnp.where(hit, view, picked)  13.8 us
    convert_element_type x1, local copies, waits for them, and re-layouts, shards(): energy_cleaned.astype(jnp.float32)  12.6 us
  transfers between devices with their start and end apart: 10, of which 5 were waited for; matrix products, arithmetic and copies ran while one was open for 22% of the time, Pallas kernels for 0%

commit v1 on v0

v1 whole, which is shorter than its diff:
```python
import functools

import jax
import jax.numpy as jnp
from jax import lax
from jax.experimental import pallas as pl
from jax.experimental.pallas import tpu as pltpu
from jax.sharding import PartitionSpec as P

WIN = 32
NNZ = 3
HALO = 2


def from_behind(block, axis, distance):
    devices = range(lax.axis_size(axis))
    route = [(i - distance, i) for i in devices if i - distance in devices]
    return lax.ppermute(block, axis, route)


def row_halos(cells, width):
    count = lax.axis_size("row")
    ends = count - 1
    head = cells[:width]
    tail = cells[cells.shape[0] - width :]
    lower = lax.ppermute(tail, "row", [(i, i + 1) for i in range(ends)])
    upper = lax.ppermute(head, "row", [(i + 1, i) for i in range(ends)])
    return lower, upper


def apply_kernel(shift_ref, x_hbm, lo_ref, hi_ref, *refs, group, blk, nmat):
    mats = refs[:nmat]
    outs = refs[nmat : 2 * nmat]
    xpad, sem = refs[2 * nmat], refs[2 * nmat + 1]
    g = pl.program_id(0)
    entries = x_hbm.shape[0]
    halo = HALO * blk

    @pl.when(g == 0)
    def _():
        copy = pltpu.make_async_copy(x_hbm, xpad.at[pl.ds(halo, entries)], sem.at[0])
        copy.start()
        xpad[pl.ds(0, halo), :] = lo_ref[...]
        xpad[pl.ds(halo + entries, halo), :] = hi_ref[...]
        copy.wait()

    def body(j, carry):
        row = g * group + j
        parts = []
        for k in range(NNZ):
            src = row + shift_ref[row * NNZ + k] + HALO
            start = pl.multiple_of(src * blk, 16)
            parts.append(xpad[pl.ds(start, blk), :])
        xs = jnp.concatenate(parts, axis=0)
        for m in range(nmat):
            r = jnp.dot(mats[m][j], xs, preferred_element_type=jnp.float32)
            outs[m][pl.ds(pl.multiple_of(j * blk, 16), blk), :] = r.astype(outs[m].dtype)
        return carry

    lax.fori_loop(0, group, body, 0)


def block_apply(matrices, shifts_flat, cells):
    entries, slots = cells.shape
    block_rows, blk, width = matrices[0].shape
    lower, upper = row_halos(cells, HALO * blk)
    group = 32 if block_rows % 32 == 0 else block_rows
    nmat = len(matrices)
    kernel = functools.partial(apply_kernel, group=group, blk=blk, nmat=nmat)
    mat_spec = pl.BlockSpec((group, blk, width), lambda g, s: (g, 0, 0))
    out_spec = pl.BlockSpec((group * blk, slots), lambda g, s: (g, 0))
    halo_spec = pl.BlockSpec((HALO * blk, slots), lambda g, s: (0, 0))
    grid_spec = pltpu.PrefetchScalarGridSpec(
        num_scalar_prefetch=1,
        grid=(block_rows // group,),
        in_specs=[pl.BlockSpec(memory_space=pl.ANY), halo_spec, halo_spec] + [mat_spec] * nmat,
        out_specs=[out_spec] * nmat,
        scratch_shapes=[
            pltpu.VMEM((entries + 2 * HALO * blk, slots), cells.dtype),
            pltpu.SemaphoreType.DMA((1,)),
        ],
    )
    return pl.pallas_call(
        kernel,
        grid_spec=grid_spec,
        out_shape=[jax.ShapeDtypeStruct((entries, slots), jnp.bfloat16)] * nmat,
        compiler_params=pltpu.CompilerParams(dimension_semantics=("arbitrary",)),
    )(shifts_flat, cells, lower, upper, *matrices)


def tn_dot(a, b):
    return lax.dot_general(a, b, (((0,), (0,)), ((), ())), preferred_element_type=jnp.float32)


def shards(vectors, counts, offsets, margin_blocks, energy_blocks, block_columns):
    own_vectors = vectors[0]
    vector_count, entries = own_vectors.shape
    nmat_total = entries * lax.axis_size("row")
    block_rows = margin_blocks.shape[0]
    valid_mask = jnp.arange(vector_count, dtype=jnp.int32) < counts[0]
    masked = jnp.where(valid_mask[:, None], own_vectors, jnp.zeros((), own_vectors.dtype))
    lower_window = lax.dynamic_slice_in_dim(masked, offsets[0, 0], WIN, 0)
    upper_window = lax.dynamic_slice_in_dim(masked, offsets[0, 1], WIN, 0)
    own_blocks = lax.axis_index("row") * block_rows + jnp.arange(block_rows, dtype=jnp.int32)
    shifts_flat = (block_columns - own_blocks[:, None]).reshape(-1)
    from_below = [from_behind(upper_window, "cuts", distance) for distance in (2, 1)]
    from_above = [from_behind(lower_window, "cuts", -distance) for distance in (1, 2)]
    masked_t = masked.T
    windows_t = jnp.concatenate(from_below + from_above, axis=0).T
    (margin_windows_t,) = block_apply((margin_blocks,), shifts_flat, windows_t)
    partial_margin = tn_dot(margin_windows_t, masked_t)
    margin = lax.psum(partial_margin, "row") / nmat_total
    removed_t = jnp.dot(windows_t, margin.astype(jnp.bfloat16), preferred_element_type=jnp.float32)
    cleaned_t = (masked_t.astype(jnp.float32) - removed_t).astype(jnp.bfloat16)
    margin_cleaned_t, energy_cleaned_t = block_apply(
        (margin_blocks, energy_blocks), shifts_flat, cleaned_t
    )
    margin_part = tn_dot(cleaned_t, margin_cleaned_t)
    energy_part = tn_dot(cleaned_t, energy_cleaned_t)
    margin_total, energy_total = lax.psum((margin_part, energy_part), "row")
    margin_pencil = margin_total / nmat_total
    energy_pencil = energy_total / nmat_total
    margin_diag = jnp.diagonal(margin_pencil)
    energy_diag = jnp.diagonal(energy_pencil)
    theta = jnp.where(
        valid_mask,
        energy_diag / jnp.where(valid_mask, margin_diag, jnp.float32(1.0)),
        jnp.float32(0.0),
    )
    residual_t = (
        energy_cleaned_t.astype(jnp.float32) - theta[None, :] * margin_cleaned_t.astype(jnp.float32)
    ).astype(jnp.bfloat16)
    residual = residual_t.T
    return (residual[None], margin_pencil[None], energy_pencil[None])


def solution(mesh):
    placed = (
        P("cuts", None, "row"),
        P("cuts"),
        P("cuts", None),
        P("row", None, None),
        P("row", None, None),
        P("row", None),
    )
    return jax.shard_map(
        shards,
        mesh=mesh,
        in_specs=placed,
        out_specs=(P("cuts", None, "row"), P("cuts", None, None), P("cuts", None, None)),
        check_vma=False,
    )
```

time: 501 us -> 469 us (0.936)
  matrix products: 143 us -> 33.5 us
  Pallas kernels: 0 us -> 104 us
  local copies, waits for them, and re-layouts: 160 us -> 120 us
  waiting for transfers between devices: 105 us -> 139 us
  other arithmetic: 45.3 us -> 26.3 us
    dot_general x13 -> x4, matrix products: 143 us -> 33.5 us  [the longest x3 16.8 us: tn_dot(): lax.dot_general(a, b, (((0,), (0,)), ((), ())), preferred_element_type=jn...]
    pallas_call x0 -> x2, Pallas kernels: none -> 104 us  [block_apply(): pl.pallas_call(kernel, grid_spec=grid_spec, out_shape=[jax.ShapeDtypeStru...]
    concatenate x5 -> x0, local copies, waits for them, and re-layouts: 45.5 us -> none  [the longest x4 45.4 us: padded_2(): jnp.concatenate([lax.ppermute(tail, axis, [(i, (i + 1) % count) for i in...]
    psum x1, waiting for transfers between devices: 1.73 us -> 34.3 us  [shards(): margin_total, energy_total = lax.psum((margin_part, energy_part), 'row')]
    convert_element_type x3 -> x0, other arithmetic: 26.6 us -> none  [the longest x1 11.8 us: shards(): residual = (energy_cleaned.astype(jnp.float32) - theta[:, None] * margin_...]
    convert_element_type x2 -> x0, local copies, waits for them, and re-layouts: 25.2 us -> none  [the longest x1 12.6 us: shards(): energy_cleaned.astype(jnp.float32)]
    ppermute x0 -> x4, local copies, waits for them, and re-layouts: none -> 25.1 us  [from_behind(): return lax.ppermute(block, axis, route)]
    slice x5 -> x3, local copies, waits for them, and re-layouts: 23.1 us -> 1.33 us  [the longest x1 1.31 us: shards(): upper_window = lax.dynamic_slice_in_dim(masked, offsets[0, 1], WIN, 0)]
  transfers between devices with their start and end apart: 10 -> 10, of which waited for: 5 -> 5; matrix products, arithmetic and copies ran while one was open for 22% -> 15% of each run, Pallas kernels for 0% -> 0%
where the time goes in v1:
time: 469 us; the launch traced here: 465 us
  waiting for transfers between devices  139 us (30%)
  local copies, waits for them, and re-layouts  120 us (26%)
  Pallas kernels  104 us (22%)
  matrix products  33.5 us (7%)
  other arithmetic  26.3 us (6%)
  starting transfers between devices  24.2 us (5%)
  between operations  18.8 us (4%)
    pallas_call x2, Pallas kernels, block_apply(): pl.pallas_call(kernel, grid_spec=grid_spec, out_shape=[jax.ShapeDtypeStru...  104 us
    unnamed x24, local copies, waits for them, and re-layouts  72.7 us
    ppermute x4, waiting for transfers between devices, from_behind(): return lax.ppermute(block, axis, route)  68.1 us
    psum x1, waiting for transfers between devices, shards(): margin = lax.psum(partial_margin, 'row') / nmat_total  36 us
    psum x1, waiting for transfers between devices, shards(): margin_total, energy_total = lax.psum((margin_part, energy_part), 'row')  34.3 us
    ppermute x4, local copies, waits for them, and re-layouts, from_behind(): return lax.ppermute(block, axis, route)  25.1 us
    dot_general x3, matrix products, tn_dot(): lax.dot_general(a, b, (((0,), (0,)), ((), ())), preferred_element_type=jn...  16.8 us
    dot_general x1, matrix products, shards(): jnp.dot(windows_t, margin.astype(jnp.bfloat16), preferred_element_type=jn...  16.7 us
  transfers between devices with their start and end apart: 10, of which 5 were waited for; matrix products, arithmetic and copies ran while one was open for 15% of the time, Pallas kernels for 0%

profile of v1, /device:TPU:12, one launch (start us, length us, event | category | flops | bytes accessed | tf_op | source)
XLA Modules:
  0.0 464.8 jit_solution(5022340625650466484)
XLA Ops:
  11.8 8.6 %copy.21 = bf16[1,128,24576]{1,2,0:T(8,128)(2,1)} copy(bf16[1,128,24576]{2,1,0:T(8,128)(2,1)} %param.6) | data formatting | bytes 12582912 | tf_op args[0]
  21.7 3.6 bitcast_select_fusion
  25.3 6.8 %constant_dynamic-slice_fusion.1 = (bf16[32,24576]{0,1:T(8,128)(2,1)}, bf16[32,24576]{0,1:T(8,128)(2,1)}) fusion(bf16[128,24576]{0,1:T(8,128)(2,1)S(1)} %bitcast_select_fusion, s32[]{:T(128)S(6)} %select_n.32, s32[]{:T(128)S(6)} %select_n.33), kind=kLoop, calls=%fused_computation.17 | loop fusion | bytes 6291464 | tf_op jit(solution)/shard_map/dynamic_slice | solution.py:103
  32.2 5.1 %copy.22 = bf16[32,24576]{1,0:T(8,128)(2,1)S(1)} copy(bf16[32,24576]{0,1:T(8,128)(2,1)} %get-tuple-element.22) | data formatting | bytes 3145728 | tf_op jit(solution)/shard_map/dynamic_slice | solution.py:103
  37.3 3.4 collective-permute-start
  42.6 5.1 %copy.24 = bf16[32,24576]{1,0:T(8,128)(2,1)S(1)} copy(bf16[32,24576]{0,1:T(8,128)(2,1)} %get-tuple-element.23) | data formatting | bytes 3145728 | tf_op jit(solution)/shard_map/dynamic_slice | solution.py:102
  47.7 4.5 collective-permute-start.2
  54.7 22.7 %collective-permute-done = bf16[32,24576]{1,0:T(8,128)(2,1)} collective-permute-done((bf16[32,24576]{1,0:T(8,128)(2,1)S(1)}, bf16[32,24576]{1,0:T(8,128)(2,1)}, u32[]{:S(2)}, u32[]{:S(2)}) %collective-permute-start) | collective-permute-done | bytes 1572896 | tf_op jit(solution)/shard_map/ppermute | solution.py:18
  77.5 6.4 %copy.26 = bf16[32,24576]{0,1:T(8,128)(2,1)} copy(bf16[32,24576]{1,0:T(8,128)(2,1)} %collective-permute-done) | data formatting | bytes 3145728 | tf_op jit(solution)/shard_map/ppermute | solution.py:18
  83.8 25.1 %collective-permute-done.1 = bf16[32,24576]{1,0:T(8,128)(2,1)} collective-permute-done((bf16[32,24576]{1,0:T(8,128)(2,1)S(1)}, bf16[32,24576]{1,0:T(8,128)(2,1)}, u32[]{:S(2)}, u32[]{:S(2)}) %collective-permute-start.1) | collective-permute-done | bytes 1572896 | tf_op jit(solution)/shard_map/ppermute | solution.py:18
  108.9 6.2 %copy.27 = bf16[32,24576]{0,1:T(8,128)(2,1)} copy(bf16[32,24576]{1,0:T(8,128)(2,1)} %collective-permute-done.1) | data formatting | bytes 3145728 | tf_op jit(solution)/shard_map/ppermute | solution.py:18
  115.1 6.3 %copy.28 = bf16[32,24576]{0,1:T(8,128)(2,1)} copy(bf16[32,24576]{1,0:T(8,128)(2,1)} %collective-permute-done.2) | data formatting | bytes 3145728 | tf_op jit(solution)/shard_map/ppermute | solution.py:18
  121.4 20.3 %collective-permute-done.3 = bf16[32,24576]{1,0:T(8,128)(2,1)} collective-permute-done((bf16[32,24576]{1,0:T(8,128)(2,1)S(1)}, bf16[32,24576]{1,0:T(8,128)(2,1)}, u32[]{:S(2)}, u32[]{:S(2)}) %collective-permute-start.3) | collective-permute-done | bytes 1572896 | tf_op jit(solution)/shard_map/ppermute | solution.py:18
  141.7 6.3 %copy.29 = bf16[32,24576]{0,1:T(8,128)(2,1)} copy(bf16[32,24576]{1,0:T(8,128)(2,1)} %collective-permute-done.3) | data formatting | bytes 3145728 | tf_op jit(solution)/shard_map/ppermute | solution.py:18
  148.0 12.3 %fusion.19.x_hbm = bf16[24576,128]{1,0:T(8,128)(2,1)S(1)} fusion(bf16[32,24576]{0,1:T(8,128)(2,1)} %copy.29, bf16[32,24576]{0,1:T(8,128)(2,1)} %copy.28, bf16[32,24576]{0,1:T(8,128)(2,1)} %copy.27, bf16[32,24576]{0,1:T(8,128)(2,1)} %copy.26), kind=kLoop, calls=%fused_computation.28 | loop fusion | flops 25165824 | bytes 12582912 | tf_op jit(solution)/shard_map/transpose | solution.py:109
  160.3 2.6 copy-done.4
  162.9 3.5 collective-permute-start.4
  168.7 23.4 %copy.30.refs_0_ = bf16[256,96,288]{2,1,0:T(8,128)(2,1)} copy(bf16[256,96,288]{0,2,1:T(8,128)(2,1)} %param.9) | data formatting | bytes 28311552 | tf_op args[3]
  194.3 49.5 %shard_map.85 = bf16[24576,128]{1,0:T(8,128)(2,1)} custom-call(s32[768]{0:T(1024)} %reshape.28.shift_ref, bf16[24576,128]{1,0:T(8,128)(2,1)} %copy-done.4, bf16[192,128]{1,0:T(8,128)(2,1)} %copy-done.5, bf16[192,128]{1,0:T(8,128)(2,1)} %copy-done.7, bf16[256,96,288]{2,1,0:T(8,128)(2,1)} %copy.30.refs_0_), custom_call_target="tpu_custom_call" | custom-call | tf_op jit(solution)/shard_map/pallas_call | solution.py:83
  243.8 7.1 %fusion.9 = f32[128,128]{1,0:T(8,128)} fusion(bf16[24576,128]{1,0:T(8,128)(2,1)} %shard_map.85, bf16[128,24576]{0,1:T(8,128)(2,1)} %copy-done), kind=kOutput, calls=%fused_computation.25 | convolution fusion | flops 805306368 | bytes 12648448 | tf_op jit(solution)/shard_map/dot_general | solution.py:92
  251.1 36.0 %all-reduce.4.cloned.1.call-done = f32[128,128]{1,0:T(8,128)} async-done(((f32[128,128]{1,0:T(8,128)}), f32[128,128]{1,0:T(8,128)}) %all-reduce.4.cloned.1.call-update) | async-done | bytes 65552 | tf_op jit(solution)/shard_map/psum | solution.py:112
  287.2 16.7 %fusion.x_hbm = bf16[24576,128]{1,0:T(8,128)(2,1)S(1)} fusion(bf16[128,24576]{0,1:T(8,128)(2,1)} %copy-done, f32[128,128]{1,0:T(8,128)} %all-reduce.4.cloned.1.call-done, bf16[32,24576]{0,1:T(8,128)(2,1)} %copy.29, bf16[32,24576]{0,1:T(8,128)(2,1)} %copy.28, bf16[32,24576]{0,1:T(8,128)(2,1)} %copy.27, bf16[32,24576]{0,1:T(8,128)(2,1)} %copy.26), kind=kOutput, calls=%fused_computation.3 | convolution fusion | flops 839942144 | bytes 18939904 | tf_op jit(solution)/shard_map/dot_general | solution.py:113
  303.9 2.7 copy-done.1
  306.6 3.2 collective-permute-start.6
  309.8 2.7 collective-permute-start.7
  312.4 23.4 %copy.32.refs_1_ = bf16[256,96,288]{2,1,0:T(8,128)(2,1)} copy(bf16[256,96,288]{0,2,1:T(8,128)(2,1)} %param.10) | data formatting | bytes 28311552 | tf_op args[4]
  337.1 54.3 %shard_map.86 = (bf16[24576,128]{1,0:T(8,128)(2,1)}, bf16[24576,128]{1,0:T(8,128)(2,1)}) custom-call(s32[768]{0:T(1024)} %reshape.28.shift_ref, bf16[24576,128]{1,0:T(8,128)(2,1)} %copy-done.1, bf16[192,128]{1,0:T(8,128)(2,1)} %copy-done.6, bf16[192,128]{1,0:T(8,128)(2,1)} %copy-done.8, bf16[256,96,288]{2,1,0:T(8,128)(2,1)} %copy.30.refs_0_, ...), custom_call_target="tpu_custom_call" | custom-call | tf_op jit(solution)/shard_map/pallas_call | solution.py:83
  391.5 7.2 %fusion.11 = f32[128,128]{1,0:T(8,128)} fusion(bf16[24576,128]{1,0:T(8,128)(2,1)} %copy-done.1, bf16[24576,128]{1,0:T(8,128)(2,1)} %get-tuple-element.6), kind=kOutput, calls=%fused_computation.27 | convolution fusion | flops 805306368 | bytes 12648448 | tf_op jit(solution)/shard_map/dot_general | solution.py:92
  399.7 2.5 fusion.10
  402.2 34.3 %all-reduce.6.cloned.1.call-done = (f32[128,128]{1,0:T(8,128)}, f32[128,128]{1,0:T(8,128)}) async-done(((f32[128,128]{1,0:T(8,128)}, f32[128,128]{1,0:T(8,128)}), (f32[128,128]{1,0:T(8,128)}, f32[128,128]{1,0:T(8,128)})) %all-reduce.6.cloned.1.call-update) | async-done | bytes 131088 | tf_op jit(solution)/shard_map/psum | solution.py:120
  440.6 8.8 %fusion.1 = bf16[1,128,24576]{1,2,0:T(8,128)(2,1)} fusion(bf16[24576,128]{1,0:T(8,128)(2,1)} %get-tuple-element.6, bf16[24576,128]{1,0:T(8,128)(2,1)} %get-tuple-element.5, f32[128]{0:T(128)S(1)} %divide_select_fusion), kind=kLoop, calls=%fused_computation.5 | loop fusion | flops 15728640 | bytes 18874880 | tf_op jit(solution)/shard_map/broadcast_in_dim | solution.py:134
  449.4 8.6 %copy.33 = bf16[1,128,24576]{2,1,0:T(8,128)(2,1)} copy(bf16[1,128,24576]{1,2,0:T(8,128)(2,1)} %fusion.1) | data formatting | bytes 12582912
  (43 shorter events, 16.8 us)
Async XLA Ops:
  7.2 280.0 %all-reduce.4.cloned.1.call-start = ((), (), s32[]{:S(2)}) async-start(), calls=%async_computation | async-start | bytes 131072 | tf_op jit(solution)/shard_map/psum | solution.py:112
  25.3 6.9 %copy-start = (bf16[128,24576]{0,1:T(8,128)(2,1)}, bf16[128,24576]{0,1:T(8,128)(2,1)S(1)}, u32[]{:S(2)}) copy-start(bf16[128,24576]{0,1:T(8,128)(2,1)S(1)} %bitcast_select_fusion) | copy-start | bytes 18874372
  37.3 40.2 %collective-permute-start = (bf16[32,24576]{1,0:T(8,128)(2,1)S(1)}, bf16[32,24576]{1,0:T(8,128)(2,1)}, u32[]{:S(2)}, u32[]{:S(2)}) collective-permute-start(bf16[32,24576]{1,0:T(8,128)(2,1)S(1)} %copy.22), channel_id=1, source_target_pairs={{0,8},{4,12},{8,16},{12,20},{16,24},{20,28},{1,9},{5,13},{9,17},{1... | collective-permute-start | bytes 4718600 | tf_op jit(solution)/shard_map/ppermute | solution.py:18
  40.7 68.2 %collective-permute-start.1 = (bf16[32,24576]{1,0:T(8,128)(2,1)S(1)}, bf16[32,24576]{1,0:T(8,128)(2,1)}, u32[]{:S(2)}, u32[]{:S(2)}) collective-permute-start(bf16[32,24576]{1,0:T(8,128)(2,1)S(1)} %copy.22), channel_id=1, source_target_pairs={{0,4},{4,8},{8,12},{12,16},{16,20},{20,24},{24,28},{1,5},{5,9},{9,... | collective-permute-start | bytes 4718600 | tf_op jit(solution)/shard_map/ppermute | solution.py:18
  47.7 67.4 %collective-permute-start.2 = (bf16[32,24576]{1,0:T(8,128)(2,1)S(1)}, bf16[32,24576]{1,0:T(8,128)(2,1)}, u32[]{:S(2)}, u32[]{:S(2)}) collective-permute-start(bf16[32,24576]{1,0:T(8,128)(2,1)S(1)} %copy.24), channel_id=1, source_target_pairs={{4,0},{8,4},{12,8},{16,12},{20,16},{24,20},{28,24},{5,1},{9,5},{13... | collective-permute-start | bytes 4718600 | tf_op jit(solution)/shard_map/ppermute | solution.py:18
  52.3 89.5 %collective-permute-start.3 = (bf16[32,24576]{1,0:T(8,128)(2,1)S(1)}, bf16[32,24576]{1,0:T(8,128)(2,1)}, u32[]{:S(2)}, u32[]{:S(2)}) collective-permute-start(bf16[32,24576]{1,0:T(8,128)(2,1)S(1)} %copy.24), channel_id=1, source_target_pairs={{8,0},{12,4},{16,8},{20,12},{24,16},{28,20},{9,1},{13,5},{17,9},{2... | collective-permute-start | bytes 4718600 | tf_op jit(solution)/shard_map/ppermute | solution.py:18
  148.0 20.7 %copy-start.9 = (s32[256,3]{0,1:T(4,128)S(1)}, s32[256,3]{0,1:T(4,128)}, u32[]{:S(2)}) copy-start(s32[256,3]{0,1:T(4,128)} %param.11) | copy-start | bytes 9220
  160.3 2.6 copy-start.4
  162.9 30.2 %collective-permute-start.4 = (bf16[192,128]{1,0:T(8,128)(2,1)S(1)}, bf16[192,128]{1,0:T(8,128)(2,1)S(1)}, u32[]{:S(2)}, u32[]{:S(2)}) collective-permute-start(bf16[192,128]{1,0:T(8,128)(2,1)S(1)} %get-tuple-element.21), channel_id=1, source_target_pairs={{0,1},{1,2},{2,3},{4,5},{5,6},{6,7},{8,9},{9,10},{10,11},{12,13},{... | collective-permute-start | bytes 147464 | tf_op jit(solution)/shard_map/ppermute | solution.py:26
  166.4 26.7 %collective-permute-start.5 = (bf16[192,128]{1,0:T(8,128)(2,1)S(1)}, bf16[192,128]{1,0:T(8,128)(2,1)S(1)}, u32[]{:S(2)}, u32[]{:S(2)}) collective-permute-start(bf16[192,128]{1,0:T(8,128)(2,1)S(1)} %get-tuple-element.20), channel_id=1, source_target_pairs={{1,0},{2,1},{3,2},{5,4},{6,5},{7,6},{9,8},{10,9},{11,10},{13,12},{... | collective-permute-start | bytes 147464 | tf_op jit(solution)/shard_map/ppermute | solution.py:27
  193.0 0.6 copy-start.5
  193.7 0.6 copy-start.7
  250.9 185.6 %all-reduce.6.cloned.1.call-start = ((), (), s32[]{:S(2)}) async-start(), calls=%async_computation.1 | async-start | bytes 262144 | tf_op jit(solution)/shard_map/psum | solution.py:120
  303.9 2.7 copy-start.1
  306.6 29.3 %collective-permute-start.6 = (bf16[192,128]{1,0:T(8,128)(2,1)S(1)}, bf16[192,128]{1,0:T(8,128)(2,1)S(1)}, u32[]{:S(2)}, u32[]{:S(2)}) collective-permute-start(bf16[192,128]{1,0:T(8,128)(2,1)S(1)} %get-tuple-element.19), channel_id=1, source_target_pairs={{0,1},{1,2},{2,3},{4,5},{5,6},{6,7},{8,9},{9,10},{10,11},{12,13},{... | collective-permute-start | bytes 147464 | tf_op jit(solution)/shard_map/ppermute | solution.py:26
  309.8 26.1 %collective-permute-start.7 = (bf16[192,128]{1,0:T(8,128)(2,1)S(1)}, bf16[192,128]{1,0:T(8,128)(2,1)S(1)}, u32[]{:S(2)}, u32[]{:S(2)}) collective-permute-start(bf16[192,128]{1,0:T(8,128)(2,1)S(1)} %get-tuple-element.18), channel_id=1, source_target_pairs={{1,0},{2,1},{3,2},{5,4},{6,5},{7,6},{9,8},{10,9},{11,10},{13,12},{... | collective-permute-start | bytes 147464 | tf_op jit(solution)/shard_map/ppermute | solution.py:27
  335.8 0.6 copy-start.6
  336.5 0.6 copy-start.8
  391.4 7.2 %copy-start.2 = (bf16[24576,128]{1,0:T(8,128)(2,1)S(1)}, bf16[24576,128]{1,0:T(8,128)(2,1)}, u32[]{:S(2)}) copy-start(bf16[24576,128]{1,0:T(8,128)(2,1)} %copy-done.1) | copy-start | bytes 18874372
  391.4 8.2 %copy-start.3 = (bf16[24576,128]{1,0:T(8,128)(2,1)S(1)}, bf16[24576,128]{1,0:T(8,128)(2,1)}, u32[]{:S(2)}) copy-start(bf16[24576,128]{1,0:T(8,128)(2,1)} %get-tuple-element.5) | copy-start | bytes 18874372
Sparse Core Ops, SparseCore 0:
  251.0 36.1 all-reduce.3
  402.3 34.1 all-reduce.5

commit v2 on v1

--- a/solution.py
+++ b/solution.py
@@ -5,6 +5,7 @@
 from jax import lax
 from jax.experimental import pallas as pl
 from jax.experimental.pallas import tpu as pltpu
+from jax.experimental.layout import Layout, with_layout_constraint
 from jax.sharding import PartitionSpec as P
 
 WIN = 32
@@ -52,12 +53,14 @@
             start = pl.multiple_of(src * blk, 16)
             parts.append(xpad[pl.ds(start, blk), :])
         xs = jnp.concatenate(parts, axis=0)
+        lhs = jnp.concatenate([m[j] for m in mats], axis=0) if nmat > 1 else mats[0][j]
+        r = jnp.dot(lhs, xs, preferred_element_type=jnp.float32)
         for m in range(nmat):
-            r = jnp.dot(mats[m][j], xs, preferred_element_type=jnp.float32)
-            outs[m][pl.ds(pl.multiple_of(j * blk, 16), blk), :] = r.astype(outs[m].dtype)
+            part = r[m * blk : (m + 1) * blk]
+            outs[m][pl.ds(pl.multiple_of(j * blk, 16), blk), :] = part.astype(outs[m].dtype)
         return carry
 
-    lax.fori_loop(0, group, body, 0)
+    lax.fori_loop(0, group, body, 0, unroll=8)
 
 
 def block_apply(matrices, shifts_flat, cells):
@@ -88,6 +91,22 @@
     )(shifts_flat, cells, lower, upper, *matrices)
 
 
+def row_sum(part):
+    count = lax.axis_size("row")
+    here = lax.axis_index("row")
+    got = [part] + [
+        lax.ppermute(part, "row", [(i, (i + step) % count) for i in range(count)])
+        for step in range(1, count)
+    ]
+    stacked = jnp.stack(got)
+    order = (here - jnp.arange(count, dtype=jnp.int32)) % count
+    by_source = jnp.take(stacked, order, axis=0)
+    total = by_source[0]
+    for r in range(1, count):
+        total = total + by_source[r]
+    return total
+
+
 def tn_dot(a, b):
     return lax.dot_general(a, b, (((0,), (0,)), ((), ())), preferred_element_type=jnp.float32)
 
@@ -98,18 +117,32 @@
     nmat_total = entries * lax.axis_size("row")
     block_rows = margin_blocks.shape[0]
     valid_mask = jnp.arange(vector_count, dtype=jnp.int32) < counts[0]
-    masked = jnp.where(valid_mask[:, None], own_vectors, jnp.zeros((), own_vectors.dtype))
-    lower_window = lax.dynamic_slice_in_dim(masked, offsets[0, 0], WIN, 0)
-    upper_window = lax.dynamic_slice_in_dim(masked, offsets[0, 1], WIN, 0)
+    window_rows = jnp.arange(WIN, dtype=jnp.int32)[:, None]
+    lower_window = jnp.where(
+        window_rows + offsets[0, 0] < counts[0],
+        lax.dynamic_slice_in_dim(own_vectors, offsets[0, 0], WIN, 0),
+        jnp.zeros((), own_vectors.dtype),
+    )
+    upper_window = jnp.where(
+        window_rows + offsets[0, 1] < counts[0],
+        lax.dynamic_slice_in_dim(own_vectors, offsets[0, 1], WIN, 0),
+        jnp.zeros((), own_vectors.dtype),
+    )
     own_blocks = lax.axis_index("row") * block_rows + jnp.arange(block_rows, dtype=jnp.int32)
     shifts_flat = (block_columns - own_blocks[:, None]).reshape(-1)
     from_below = [from_behind(upper_window, "cuts", distance) for distance in (2, 1)]
     from_above = [from_behind(lower_window, "cuts", -distance) for distance in (1, 2)]
-    masked_t = masked.T
-    windows_t = jnp.concatenate(from_below + from_above, axis=0).T
+    masked_t = jnp.where(valid_mask[None, :], own_vectors.T, jnp.zeros((), own_vectors.dtype))
+    row_major = Layout(major_to_minor=(0, 1, 2))
+    margin_blocks = with_layout_constraint(margin_blocks, row_major)
+    energy_blocks = with_layout_constraint(energy_blocks, row_major)
+    received, masked_t, margin_blocks, energy_blocks = lax.optimization_barrier(
+        (from_below + from_above, masked_t, margin_blocks, energy_blocks)
+    )
+    windows_t = jnp.concatenate(received, axis=0).T
     (margin_windows_t,) = block_apply((margin_blocks,), shifts_flat, windows_t)
     partial_margin = tn_dot(margin_windows_t, masked_t)
-    margin = lax.psum(partial_margin, "row") / nmat_total
+    margin = row_sum(partial_margin) / nmat_total
     removed_t = jnp.dot(windows_t, margin.astype(jnp.bfloat16), preferred_element_type=jnp.float32)
     cleaned_t = (masked_t.astype(jnp.float32) - removed_t).astype(jnp.bfloat16)
     margin_cleaned_t, energy_cleaned_t = block_apply(
@@ -117,7 +150,7 @@
     )
     margin_part = tn_dot(cleaned_t, margin_cleaned_t)
     energy_part = tn_dot(cleaned_t, energy_cleaned_t)
-    margin_total, energy_total = lax.psum((margin_part, energy_part), "row")
+    margin_total, energy_total = row_sum(jnp.stack([margin_part, energy_part]))
     margin_pencil = margin_total / nmat_total
     energy_pencil = energy_total / nmat_total
     margin_diag = jnp.diagonal(margin_pencil)

time: 469 us -> 301 us (0.64)
  waiting for transfers between devices: 139 us -> 48.5 us
  Pallas kernels: 104 us -> 45.6 us
  local copies, waits for them, and re-layouts: 120 us -> 103 us
  between operations: 18.8 us -> 5.5 us
  other arithmetic: 26.3 us -> 32.8 us
  starting transfers between devices: 24.2 us -> 30.3 us
    psum x2 -> x0, waiting for transfers between devices: 70.4 us -> none  [the longest x1 36 us: shards(): margin = lax.psum(partial_margin, 'row') / nmat_total]
    pallas_call x2, Pallas kernels: 104 us -> 45.6 us  [block_apply(): pl.pallas_call(kernel, grid_spec=grid_spec, out_shape=[jax.ShapeDtypeStru...]
    ppermute x4, waiting for transfers between devices: 68.1 us -> 30.4 us  [from_behind(): return lax.ppermute(block, axis, route)]
    ppermute x4 -> x0, local copies, waits for them, and re-layouts: 25.1 us -> none  [from_behind(): return lax.ppermute(block, axis, route)]
    optimization_barrier x0 -> x4, local copies, waits for them, and re-layouts: none -> 24.9 us  [shards(): lax.optimization_barrier((from_below + from_above, masked_t, margin_block...]
    dynamic_slice x3 -> x0, local copies, waits for them, and re-layouts: 17 us -> none  [the longest x2 11.9 us: shards(): upper_window = lax.dynamic_slice_in_dim(masked, offsets[0, 1], WIN, 0)]
    ppermute x0 -> x6, waiting for transfers between devices: none -> 11.4 us  [row_sum(): lax.ppermute(part, 'row', [(i, (i + step) % count) for i in range(count)])]
    select_n x1 -> x5, other arithmetic: 3.61 us -> 9.62 us  [the longest x1 6.42 us: shards(): jnp.where(valid_mask[None, :], own_vectors.T, jnp.zeros((), own_vectors.d...]
  transfers between devices with their start and end apart: 10 -> 14, of which waited for: 5 -> 9; matrix products, arithmetic and copies ran while one was open for 15% -> 21% of each run, Pallas kernels for 0% -> 0%
where the time goes in v2:
time: 301 us; the launch traced here: 295 us
  local copies, waits for them, and re-layouts  103 us (34%)
  waiting for transfers between devices  48.5 us (16%)
  Pallas kernels  45.6 us (15%)
  other arithmetic  32.8 us (11%)
  starting transfers between devices  30.3 us (10%)
  matrix products  29.6 us (10%)
  between operations  5.5 us (2%)
    unnamed x22, local copies, waits for them, and re-layouts  72.2 us
    pallas_call x2, Pallas kernels, block_apply(): pl.pallas_call(kernel, grid_spec=grid_spec, out_shape=[jax.ShapeDtypeStru...  45.6 us
    ppermute x4, waiting for transfers between devices, from_behind(): return lax.ppermute(block, axis, route)  30.4 us
    optimization_barrier x4, local copies, waits for them, and re-layouts, shards(): lax.optimization_barrier((from_below + from_above, masked_t, margin_block...  24.9 us
    dot_general x3, matrix products, tn_dot(): lax.dot_general(a, b, (((0,), (0,)), ((), ())), preferred_element_type=jn...  14.9 us
    dot_general x1, matrix products, shards(): jnp.dot(windows_t, margin.astype(jnp.bfloat16), preferred_element_type=jn...  14.7 us
    ppermute x4, starting transfers between devices, from_behind(): return lax.ppermute(block, axis, route)  12.3 us
    transpose x1, other arithmetic, shards(): windows_t = jnp.concatenate(received, axis=0).T  12.3 us
  transfers between devices with their start and end apart: 14, of which 9 were waited for; matrix products, arithmetic and copies ran while one was open for 21% of the time, Pallas kernels for 0%

profile of v2, /device:TPU:12, one launch (start us, length us, event | category | flops | bytes accessed | tf_op | source)
XLA Modules:
  0.0 295.2 jit_solution(15206611939152405300)
XLA Ops:
  7.8 3.0 %bitcast_select_fusion.1 = (bf16[32,24576]{1,0:T(8,128)(2,1)S(1)}, bf16[32,24576]{1,0:T(8,128)(2,1)S(1)}) fusion(bf16[1,128,24576]{2,1,0:T(8,128)(2,1)} %param.6, s32[]{:T(128)S(6)} %select_n.89, pred[32]{0:T(512)(128)(4,1)S(1)} %get-tuple-element.44, s32[]{:T(128)S(6)} %select_n.87, pred[32]{0:T(512)(128)(4,1)S(1)} %get-tuple-element.45), kind=kLoop, calls=%fused_computation.10 | loop fusion | flops 1572864 | bytes 6291528 | tf_op jit(solution)/shard_map/jit(_where)/select_n | solution.py:121
  10.8 3.5 %collective-permute-start = (bf16[32,24576]{1,0:T(8,128)(2,1)S(1)}, bf16[32,24576]{1,0:T(8,128)(2,1)}, u32[]{:S(2)}, u32[]{:S(2)}) collective-permute-start(bf16[32,24576]{1,0:T(8,128)(2,1)S(1)} %get-tuple-element.35), channel_id=1, source_target_pairs={{0,8},{4,12},{8,16},{12,20},{16,24},{20,28},{1,9},{5,13},{9,17},{1... | collective-permute-start | bytes 4718600 | tf_op jit(solution)/shard_map/ppermute | solution.py:19
  16.3 4.5 %collective-permute-start.2 = (bf16[32,24576]{1,0:T(8,128)(2,1)S(1)}, bf16[32,24576]{1,0:T(8,128)(2,1)}, u32[]{:S(2)}, u32[]{:S(2)}) collective-permute-start(bf16[32,24576]{1,0:T(8,128)(2,1)S(1)} %get-tuple-element.34), channel_id=1, source_target_pairs={{4,0},{8,4},{12,8},{16,12},{20,16},{24,20},{28,24},{5,1},{9,5},{13... | collective-permute-start | bytes 4718600 | tf_op jit(solution)/shard_map/ppermute | solution.py:19
  20.8 2.3 collective-permute-start.3
  23.1 8.6 %copy.23 = bf16[1,128,24576]{1,2,0:T(8,128)(2,1)} copy(bf16[1,128,24576]{2,1,0:T(8,128)(2,1)} %param.6) | data formatting | bytes 12582912 | tf_op args[0]
  31.7 6.4 %fusion.1 = bf16[24576,128]{1,0:T(8,128)(2,1)} fusion(bf16[1,128,24576]{1,2,0:T(8,128)(2,1)} %copy.23, pred[128]{0:T(512)(128)(4,1)S(1)} %iota_compare_fusion), kind=kLoop, calls=%fused_computation.9 | loop fusion | flops 3145728 | bytes 12583040 | tf_op jit(solution)/shard_map/jit(_where)/select_n | solution.py:135
  38.2 23.4 %copy.24.refs_0_ = bf16[256,96,288]{2,1,0:T(8,128)(2,1)} copy(bf16[256,96,288]{0,2,1:T(8,128)(2,1)} %param.9) | data formatting | bytes 28311552 | tf_op args[3]
  61.6 23.3 %copy.25.refs_1_ = bf16[256,96,288]{2,1,0:T(8,128)(2,1)} copy(bf16[256,96,288]{0,2,1:T(8,128)(2,1)} %param.10) | data formatting | bytes 28311552 | tf_op args[4]
  85.0 30.3 %collective-permute-done.3 = bf16[32,24576]{1,0:T(8,128)(2,1)} collective-permute-done((bf16[32,24576]{1,0:T(8,128)(2,1)S(1)}, bf16[32,24576]{1,0:T(8,128)(2,1)}, u32[]{:S(2)}, u32[]{:S(2)}) %collective-permute-start.3) | collective-permute-done | bytes 1572896 | tf_op jit(solution)/shard_map/ppermute | solution.py:19
  115.4 6.2 %copy.26 = bf16[32,24576]{0,1:T(8,128)(2,1)} copy(bf16[32,24576]{1,0:T(8,128)(2,1)} %collective-permute-done) | data formatting | bytes 3145728 | tf_op jit(solution)/shard_map/optimization_barrier | solution.py:139
  121.6 6.2 %copy.27 = bf16[32,24576]{0,1:T(8,128)(2,1)} copy(bf16[32,24576]{1,0:T(8,128)(2,1)} %collective-permute-done.1) | data formatting | bytes 3145728 | tf_op jit(solution)/shard_map/optimization_barrier | solution.py:139
  127.8 6.2 %copy.28 = bf16[32,24576]{0,1:T(8,128)(2,1)} copy(bf16[32,24576]{1,0:T(8,128)(2,1)} %collective-permute-done.2) | data formatting | bytes 3145728 | tf_op jit(solution)/shard_map/optimization_barrier | solution.py:139
  134.1 6.2 %copy.29 = bf16[32,24576]{0,1:T(8,128)(2,1)} copy(bf16[32,24576]{1,0:T(8,128)(2,1)} %collective-permute-done.3) | data formatting | bytes 3145728 | tf_op jit(solution)/shard_map/optimization_barrier | solution.py:139
  140.3 12.3 %fusion.30.x_hbm = bf16[24576,128]{1,0:T(8,128)(2,1)S(1)} fusion(bf16[32,24576]{0,1:T(8,128)(2,1)} %copy.29, bf16[32,24576]{0,1:T(8,128)(2,1)} %copy.28, bf16[32,24576]{0,1:T(8,128)(2,1)} %copy.27, bf16[32,24576]{0,1:T(8,128)(2,1)} %copy.26), kind=kLoop, calls=%fused_computation.62 | loop fusion | flops 25165824 | bytes 12582912 | tf_op jit(solution)/shard_map/transpose | solution.py:142
  152.5 2.6 copy-done.3
  155.2 3.5 %collective-permute-start.4 = (bf16[192,128]{1,0:T(8,128)(2,1)S(1)}, bf16[192,128]{1,0:T(8,128)(2,1)S(1)}, u32[]{:S(2)}, u32[]{:S(2)}) collective-permute-start(bf16[192,128]{1,0:T(8,128)(2,1)S(1)} %get-tuple-element.33), channel_id=1, source_target_pairs={{0,1},{1,2},{2,3},{4,5},{5,6},{6,7},{8,9},{9,10},{10,11},{12,13},{... | collective-permute-start | bytes 147464 | tf_op jit(solution)/shard_map/ppermute | solution.py:27
  158.6 2.4 collective-permute-start.5
  162.0 2.7 collective-permute-done.5.hi_ref
  165.2 18.9 %shard_map.85 = bf16[24576,128]{1,0:T(8,128)(2,1)} custom-call(s32[768]{0:T(1024)} %reshape.121.shift_ref, bf16[24576,128]{1,0:T(8,128)(2,1)} %copy-done.3, bf16[192,128]{1,0:T(8,128)(2,1)} %copy-done.4, bf16[192,128]{1,0:T(8,128)(2,1)} %copy-done.6, bf16[256,96,288]{2,1,0:T(8,128)(2,1)} %copy.24.refs_0_), custom_call_target="tpu_custom_call" | custom-call | tf_op jit(solution)/shard_map/pallas_call | solution.py:86
  184.1 6.4 %fusion.22 = f32[128,128]{1,0:T(8,128)S(1)} fusion(bf16[24576,128]{1,0:T(8,128)(2,1)} %shard_map.85, bf16[24576,128]{1,0:T(8,128)(2,1)} %fusion.1), kind=kOutput, calls=%fused_computation.61 | convolution fusion | flops 805306368 | bytes 12648448 | tf_op jit(solution)/shard_map/dot_general | solution.py:111
  191.4 2.3 collective-permute-start.8
  193.7 2.7 collective-permute-done.7
  198.7 14.7 %subtract_convert_fusion.1.x_hbm = bf16[24576,128]{1,0:T(8,128)(2,1)S(1)} fusion(bf16[24576,128]{1,0:T(8,128)(2,1)} %fusion.1, f32[4,128,128]{2,1,0:T(8,128)S(1)} %broadcast_select_fusion.1, bf16[32,24576]{0,1:T(8,128)(2,1)} %copy.29, bf16[32,24576]{0,1:T(8,128)(2,1)} %copy.28, bf16[32,24576]{0,1:T(8,128)(2,1)} %copy.27, bf16[32,24576]{0,1:T(8,128)(2,1)} %copy.26), kind=kOutput, calls=%fused_computation.5 | convolution fusion | flops 839991296 | bytes 19136512 | tf_op jit(solution)/shard_map/dot_general | solution.py:146
  213.4 2.7 copy-done
  216.1 5.0 %collective-permute-start.10 = (bf16[192,128]{1,0:T(8,128)(2,1)S(1)}, bf16[192,128]{1,0:T(8,128)(2,1)S(1)}, u32[]{:S(2)}, u32[]{:S(2)}) collective-permute-start(bf16[192,128]{1,0:T(8,128)(2,1)S(1)} %get-tuple-element.30), channel_id=1, source_target_pairs={{1,0},{2,1},{3,2},{5,4},{6,5},{7,6},{9,8},{10,9},{11,10},{13,12},{... | collective-permute-start | bytes 147464 | tf_op jit(solution)/shard_map/ppermute | solution.py:28
  223.1 4.0 %collective-permute-done.9.lo_ref = bf16[192,128]{1,0:T(8,128)(2,1)S(1)} collective-permute-done((bf16[192,128]{1,0:T(8,128)(2,1)S(1)}, bf16[192,128]{1,0:T(8,128)(2,1)S(1)}, u32[]{:S(2)}, u32[]{:S(2)}) %collective-permute-start.9) | collective-permute-done | bytes 49184 | tf_op jit(solution)/shard_map/ppermute | solution.py:27
  227.7 26.7 %shard_map.86 = (bf16[24576,128]{1,0:T(8,128)(2,1)}, bf16[24576,128]{1,0:T(8,128)(2,1)}) custom-call(s32[768]{0:T(1024)} %reshape.121.shift_ref, bf16[24576,128]{1,0:T(8,128)(2,1)} %copy-done, bf16[192,128]{1,0:T(8,128)(2,1)} %copy-done.7, bf16[192,128]{1,0:T(8,128)(2,1)} %copy-done.5, bf16[256,96,288]{2,1,0:T(8,128)(2,1)} %copy.24.refs_0_, ...), custom_call_target="tpu_custom_call" | custom-call | tf_op jit(solution)/shard_map/pallas_call | solution.py:86
  254.5 6.6 %convolution_bitcast_fusion.1 = f32[1,128,128]{2,1,0:T(8,128)S(1)} fusion(bf16[24576,128]{1,0:T(8,128)(2,1)} %copy-done, bf16[24576,128]{1,0:T(8,128)(2,1)} %get-tuple-element.20), kind=kOutput, calls=%fused_computation.13 | convolution fusion | flops 805306368 | bytes 12648448 | tf_op jit(solution)/shard_map/dot_general | solution.py:111
  266.7 2.9 collective-permute-done.11
  269.6 2.4 collective-permute-done.12
  277.8 8.8 %fusion = bf16[1,128,24576]{1,2,0:T(8,128)(2,1)} fusion(bf16[24576,128]{1,0:T(8,128)(2,1)} %get-tuple-element.20, bf16[24576,128]{1,0:T(8,128)(2,1)} %get-tuple-element.19, f32[128]{0:T(128)S(1)} %divide_select_fusion), kind=kLoop, calls=%fused_computation.6 | loop fusion | flops 15728640 | bytes 18874880 | tf_op jit(solution)/shard_map/broadcast_in_dim | solution.py:167
  286.6 8.6 %copy.30 = bf16[1,128,24576]{2,1,0:T(8,128)(2,1)} copy(bf16[1,128,24576]{1,2,0:T(8,128)(2,1)} %fusion) | data formatting | bytes 12582912
  (57 shorter events, 23.0 us)
Async XLA Ops:
  10.8 74.2 %collective-permute-start = (bf16[32,24576]{1,0:T(8,128)(2,1)S(1)}, bf16[32,24576]{1,0:T(8,128)(2,1)}, u32[]{:S(2)}, u32[]{:S(2)}) collective-permute-start(bf16[32,24576]{1,0:T(8,128)(2,1)S(1)} %get-tuple-element.35), channel_id=1, source_target_pairs={{0,8},{4,12},{8,16},{12,20},{16,24},{20,28},{1,9},{5,13},{9,17},{1... | collective-permute-start | bytes 4718600 | tf_op jit(solution)/shard_map/ppermute | solution.py:19
  14.3 70.7 %collective-permute-start.1 = (bf16[32,24576]{1,0:T(8,128)(2,1)S(1)}, bf16[32,24576]{1,0:T(8,128)(2,1)}, u32[]{:S(2)}, u32[]{:S(2)}) collective-permute-start(bf16[32,24576]{1,0:T(8,128)(2,1)S(1)} %get-tuple-element.35), channel_id=1, source_target_pairs={{0,4},{4,8},{8,12},{12,16},{16,20},{20,24},{24,28},{1,5},{5,9},{9,... | collective-permute-start | bytes 4718600 | tf_op jit(solution)/shard_map/ppermute | solution.py:19
  16.3 68.8 %collective-permute-start.2 = (bf16[32,24576]{1,0:T(8,128)(2,1)S(1)}, bf16[32,24576]{1,0:T(8,128)(2,1)}, u32[]{:S(2)}, u32[]{:S(2)}) collective-permute-start(bf16[32,24576]{1,0:T(8,128)(2,1)S(1)} %get-tuple-element.34), channel_id=1, source_target_pairs={{4,0},{8,4},{12,8},{16,12},{20,16},{24,20},{28,24},{5,1},{9,5},{13... | collective-permute-start | bytes 4718600 | tf_op jit(solution)/shard_map/ppermute | solution.py:19
  20.8 94.6 %collective-permute-start.3 = (bf16[32,24576]{1,0:T(8,128)(2,1)S(1)}, bf16[32,24576]{1,0:T(8,128)(2,1)}, u32[]{:S(2)}, u32[]{:S(2)}) collective-permute-start(bf16[32,24576]{1,0:T(8,128)(2,1)S(1)} %get-tuple-element.34), channel_id=1, source_target_pairs={{8,0},{12,4},{16,8},{20,12},{24,16},{28,20},{9,1},{13,5},{17,9},{2... | collective-permute-start | bytes 4718600 | tf_op jit(solution)/shard_map/ppermute | solution.py:19
  61.6 23.4 %copy-start.8 = (s32[256,3]{0,1:T(4,128)S(1)}, s32[256,3]{0,1:T(4,128)}, u32[]{:S(2)}) copy-start(s32[256,3]{0,1:T(4,128)} %param.11) | copy-start | bytes 9220
  152.5 2.6 copy-start.3
  155.2 6.8 %collective-permute-start.4 = (bf16[192,128]{1,0:T(8,128)(2,1)S(1)}, bf16[192,128]{1,0:T(8,128)(2,1)S(1)}, u32[]{:S(2)}, u32[]{:S(2)}) collective-permute-start(bf16[192,128]{1,0:T(8,128)(2,1)S(1)} %get-tuple-element.33), channel_id=1, source_target_pairs={{0,1},{1,2},{2,3},{4,5},{5,6},{6,7},{8,9},{9,10},{10,11},{12,13},{... | collective-permute-start | bytes 147464 | tf_op jit(solution)/shard_map/ppermute | solution.py:27
  158.6 6.0 %collective-permute-start.5 = (bf16[192,128]{1,0:T(8,128)(2,1)S(1)}, bf16[192,128]{1,0:T(8,128)(2,1)S(1)}, u32[]{:S(2)}, u32[]{:S(2)}) collective-permute-start(bf16[192,128]{1,0:T(8,128)(2,1)S(1)} %get-tuple-element.32), channel_id=1, source_target_pairs={{1,0},{2,1},{3,2},{5,4},{6,5},{7,6},{9,8},{10,9},{11,10},{13,12},{... | collective-permute-start | bytes 147464 | tf_op jit(solution)/shard_map/ppermute | solution.py:28
  162.0 2.7 copy-start.4
  164.6 0.6 copy-start.6
  190.6 5.9 %collective-permute-start.7 = (f32[128,128]{1,0:T(8,128)S(1)}, f32[128,128]{1,0:T(8,128)S(1)}, u32[]{:S(2)}, u32[]{:S(2)}) collective-permute-start(f32[128,128]{1,0:T(8,128)S(1)} %fusion.22), channel_id=1, source_target_pairs={{0,2},{1,3},{2,0},{3,1},{4,6},{5,7},{6,4},{7,5},{8,10},{9,11},{10,... | collective-permute-start | bytes 196616 | tf_op jit(solution)/shard_map/ppermute | solution.py:98
  191.4 5.7 %collective-permute-start.8 = (f32[128,128]{1,0:T(8,128)S(1)}, f32[128,128]{1,0:T(8,128)S(1)}, u32[]{:S(2)}, u32[]{:S(2)}) collective-permute-start(f32[128,128]{1,0:T(8,128)S(1)} %fusion.22), channel_id=1, source_target_pairs={{0,3},{1,0},{2,1},{3,2},{4,7},{5,4},{6,5},{7,6},{8,11},{9,8},{10,9... | collective-permute-start | bytes 196616 | tf_op jit(solution)/shard_map/ppermute | solution.py:98
  193.7 4.3 %collective-permute-start.6 = (f32[128,128]{1,0:T(8,128)S(1)}, f32[128,128]{1,0:T(8,128)S(1)}, u32[]{:S(2)}, u32[]{:S(2)}) collective-permute-start(f32[128,128]{1,0:T(8,128)S(1)} %fusion.22), channel_id=1, source_target_pairs={{0,1},{1,2},{2,3},{3,0},{4,5},{5,6},{6,7},{7,4},{8,9},{9,10},{10,1... | collective-permute-start | bytes 196616 | tf_op jit(solution)/shard_map/ppermute | solution.py:98
  213.4 2.7 copy-start
  216.1 7.0 %collective-permute-start.10 = (bf16[192,128]{1,0:T(8,128)(2,1)S(1)}, bf16[192,128]{1,0:T(8,128)(2,1)S(1)}, u32[]{:S(2)}, u32[]{:S(2)}) collective-permute-start(bf16[192,128]{1,0:T(8,128)(2,1)S(1)} %get-tuple-element.30), channel_id=1, source_target_pairs={{1,0},{2,1},{3,2},{5,4},{6,5},{7,6},{9,8},{10,9},{11,10},{13,12},{... | collective-permute-start | bytes 147464 | tf_op jit(solution)/shard_map/ppermute | solution.py:28
  221.1 6.0 %collective-permute-start.9 = (bf16[192,128]{1,0:T(8,128)(2,1)S(1)}, bf16[192,128]{1,0:T(8,128)(2,1)S(1)}, u32[]{:S(2)}, u32[]{:S(2)}) collective-permute-start(bf16[192,128]{1,0:T(8,128)(2,1)S(1)} %get-tuple-element.31), channel_id=1, source_target_pairs={{0,1},{1,2},{2,3},{4,5},{5,6},{6,7},{8,9},{9,10},{10,11},{12,13},{... | collective-permute-start | bytes 147464 | tf_op jit(solution)/shard_map/ppermute | solution.py:27
  223.1 4.0 %copy-start.5 = (bf16[192,128]{1,0:T(8,128)(2,1)}, bf16[192,128]{1,0:T(8,128)(2,1)S(1)}, u32[]{:S(2)}) copy-start(bf16[192,128]{1,0:T(8,128)(2,1)S(1)} %collective-permute-done.10.hi_ref) | copy-start | bytes 147460
  227.1 0.6 copy-start.7
  254.4 6.6 %copy-start.1 = (bf16[24576,128]{1,0:T(8,128)(2,1)S(1)}, bf16[24576,128]{1,0:T(8,128)(2,1)}, u32[]{:S(2)}) copy-start(bf16[24576,128]{1,0:T(8,128)(2,1)} %copy-done) | copy-start | bytes 18874372
  254.5 8.2 %copy-start.2 = (bf16[24576,128]{1,0:T(8,128)(2,1)S(1)}, bf16[24576,128]{1,0:T(8,128)(2,1)}, u32[]{:S(2)}) copy-start(bf16[24576,128]{1,0:T(8,128)(2,1)} %get-tuple-element.19) | copy-start | bytes 18874372
  264.5 5.0 %collective-permute-start.11 = (f32[2,128,128]{2,1,0:T(8,128)S(1)}, f32[2,128,128]{2,1,0:T(8,128)S(1)}, u32[]{:S(2)}, u32[]{:S(2)}) collective-permute-start(f32[2,128,128]{2,1,0:T(8,128)S(1)} %get-tuple-element.41), channel_id=1, source_target_pairs={{0,1},{1,2},{2,3},{3,0},{4,5},{5,6},{6,7},{7,4},{8,9},{9,10},{10,1... | collective-permute-start | bytes 393224 | tf_op jit(solution)/shard_map/ppermute | solution.py:98
  264.6 7.4 %collective-permute-start.12 = (f32[2,128,128]{2,1,0:T(8,128)S(1)}, f32[2,128,128]{2,1,0:T(8,128)S(1)}, u32[]{:S(2)}, u32[]{:S(2)}) collective-permute-start(f32[2,128,128]{2,1,0:T(8,128)S(1)} %get-tuple-element.41), channel_id=1, source_target_pairs={{0,2},{1,3},{2,0},{3,1},{4,6},{5,7},{6,4},{7,5},{8,10},{9,11},{10,... | collective-permute-start | bytes 393224 | tf_op jit(solution)/shard_map/ppermute | solution.py:98
  266.7 7.2 %collective-permute-start.13 = (f32[2,128,128]{2,1,0:T(8,128)S(1)}, f32[2,128,128]{2,1,0:T(8,128)S(1)}, u32[]{:S(2)}, u32[]{:S(2)}) collective-permute-start(f32[2,128,128]{2,1,0:T(8,128)S(1)} %get-tuple-element.41), channel_id=1, source_target_pairs={{0,3},{1,0},{2,1},{3,2},{4,7},{5,4},{6,5},{7,6},{8,11},{9,8},{10,9... | collective-permute-start | bytes 393224 | tf_op jit(solution)/shard_map/ppermute | solution.py:98

commit v3 on v2

--- a/solution.py
+++ b/solution.py
@@ -22,28 +22,41 @@
 def row_halos(cells, width):
     count = lax.axis_size("row")
     ends = count - 1
-    head = cells[:width]
-    tail = cells[cells.shape[0] - width :]
+    head = cells[:, :width]
+    tail = cells[:, cells.shape[1] - width :]
     lower = lax.ppermute(tail, "row", [(i, i + 1) for i in range(ends)])
     upper = lax.ppermute(head, "row", [(i + 1, i) for i in range(ends)])
     return lower, upper
 
 
-def apply_kernel(shift_ref, x_hbm, lo_ref, hi_ref, *refs, group, blk, nmat):
+def flip(tile):
+    return tile.astype(jnp.float32).T.astype(jnp.bfloat16)
+
+
+def apply_kernel(shift_ref, x_hbm, lo_ref, hi_ref, *refs, group, blk, nmat, chunk):
     mats = refs[:nmat]
     outs = refs[nmat : 2 * nmat]
-    xpad, sem = refs[2 * nmat], refs[2 * nmat + 1]
+    accs = refs[2 * nmat : 3 * nmat]
+    xbuf, xpad, sem = refs[3 * nmat :]
     g = pl.program_id(0)
-    entries = x_hbm.shape[0]
+    entries = x_hbm.shape[1]
     halo = HALO * blk
+    rim = lo_ref.shape[1]
 
     @pl.when(g == 0)
     def _():
-        copy = pltpu.make_async_copy(x_hbm, xpad.at[pl.ds(halo, entries)], sem.at[0])
+        copy = pltpu.make_async_copy(x_hbm, xbuf, sem.at[0])
         copy.start()
-        xpad[pl.ds(0, halo), :] = lo_ref[...]
-        xpad[pl.ds(halo + entries, halo), :] = hi_ref[...]
+        xpad[pl.ds(0, halo), :] = flip(lo_ref[...])[rim - halo :]
+        xpad[pl.ds(halo + entries, halo), :] = flip(hi_ref[...])[:halo]
         copy.wait()
+
+        def turn(c, carry):
+            col = pl.multiple_of(c * chunk, chunk)
+            xpad[pl.ds(halo + col, chunk), :] = flip(xbuf[:, pl.ds(col, chunk)])
+            return carry
+
+        lax.fori_loop(0, entries // chunk, turn, 0)
 
     def body(j, carry):
         row = g * group + j
@@ -57,28 +70,35 @@
         r = jnp.dot(lhs, xs, preferred_element_type=jnp.float32)
         for m in range(nmat):
             part = r[m * blk : (m + 1) * blk]
-            outs[m][pl.ds(pl.multiple_of(j * blk, 16), blk), :] = part.astype(outs[m].dtype)
+            accs[m][pl.ds(pl.multiple_of(j * blk, 16), blk), :] = part.astype(accs[m].dtype)
         return carry
 
     lax.fori_loop(0, group, body, 0, unroll=8)
+    for m in range(nmat):
+        for c in range(group * blk // chunk):
+            outs[m][:, pl.ds(c * chunk, chunk)] = flip(accs[m][pl.ds(c * chunk, chunk), :])
 
 
 def block_apply(matrices, shifts_flat, cells):
-    entries, slots = cells.shape
+    slots, entries = cells.shape
     block_rows, blk, width = matrices[0].shape
-    lower, upper = row_halos(cells, HALO * blk)
+    rim = 256
+    lower, upper = row_halos(cells, rim)
     group = 32 if block_rows % 32 == 0 else block_rows
+    chunk = 512
     nmat = len(matrices)
-    kernel = functools.partial(apply_kernel, group=group, blk=blk, nmat=nmat)
+    kernel = functools.partial(apply_kernel, group=group, blk=blk, nmat=nmat, chunk=chunk)
     mat_spec = pl.BlockSpec((group, blk, width), lambda g, s: (g, 0, 0))
-    out_spec = pl.BlockSpec((group * blk, slots), lambda g, s: (g, 0))
-    halo_spec = pl.BlockSpec((HALO * blk, slots), lambda g, s: (0, 0))
+    out_spec = pl.BlockSpec((slots, group * blk), lambda g, s: (0, g))
+    halo_spec = pl.BlockSpec((slots, rim), lambda g, s: (0, 0))
     grid_spec = pltpu.PrefetchScalarGridSpec(
         num_scalar_prefetch=1,
         grid=(block_rows // group,),
         in_specs=[pl.BlockSpec(memory_space=pl.ANY), halo_spec, halo_spec] + [mat_spec] * nmat,
         out_specs=[out_spec] * nmat,
-        scratch_shapes=[
+        scratch_shapes=[pltpu.VMEM((group * blk, slots), jnp.bfloat16)] * nmat
+        + [
+            pltpu.VMEM((slots, entries), cells.dtype),
             pltpu.VMEM((entries + 2 * HALO * blk, slots), cells.dtype),
             pltpu.SemaphoreType.DMA((1,)),
         ],
@@ -86,8 +106,10 @@
     return pl.pallas_call(
         kernel,
         grid_spec=grid_spec,
-        out_shape=[jax.ShapeDtypeStruct((entries, slots), jnp.bfloat16)] * nmat,
-        compiler_params=pltpu.CompilerParams(dimension_semantics=("arbitrary",)),
+        out_shape=[jax.ShapeDtypeStruct((slots, entries), jnp.bfloat16)] * nmat,
+        compiler_params=pltpu.CompilerParams(
+            dimension_semantics=("arbitrary",), vmem_limit_bytes=56 * 1024 * 1024
+        ),
     )(shifts_flat, cells, lower, upper, *matrices)
 
 
@@ -107,8 +129,8 @@
     return total
 
 
-def tn_dot(a, b):
-    return lax.dot_general(a, b, (((0,), (0,)), ((), ())), preferred_element_type=jnp.float32)
+def nt_dot(a, b):
+    return lax.dot_general(a, b, (((1,), (1,)), ((), ())), preferred_element_type=jnp.float32)
 
 
 def shards(vectors, counts, offsets, margin_blocks, energy_blocks, block_columns):
@@ -132,24 +154,24 @@
     shifts_flat = (block_columns - own_blocks[:, None]).reshape(-1)
     from_below = [from_behind(upper_window, "cuts", distance) for distance in (2, 1)]
     from_above = [from_behind(lower_window, "cuts", -distance) for distance in (1, 2)]
-    masked_t = jnp.where(valid_mask[None, :], own_vectors.T, jnp.zeros((), own_vectors.dtype))
     row_major = Layout(major_to_minor=(0, 1, 2))
     margin_blocks = with_layout_constraint(margin_blocks, row_major)
     energy_blocks = with_layout_constraint(energy_blocks, row_major)
-    received, masked_t, margin_blocks, energy_blocks = lax.optimization_barrier(
-        (from_below + from_above, masked_t, margin_blocks, energy_blocks)
-    )
-    windows_t = jnp.concatenate(received, axis=0).T
-    (margin_windows_t,) = block_apply((margin_blocks,), shifts_flat, windows_t)
-    partial_margin = tn_dot(margin_windows_t, masked_t)
+    received, margin_blocks, energy_blocks = lax.optimization_barrier(
+        (from_below + from_above, margin_blocks, energy_blocks)
+    )
+    masked = jnp.where(valid_mask[:, None], own_vectors, jnp.zeros((), own_vectors.dtype))
+    windows = jnp.concatenate(received, axis=0)
+    (margin_windows,) = block_apply((margin_blocks,), shifts_flat, windows)
+    partial_margin = nt_dot(margin_windows, masked)
     margin = row_sum(partial_margin) / nmat_total
-    removed_t = jnp.dot(windows_t, margin.astype(jnp.bfloat16), preferred_element_type=jnp.float32)
-    cleaned_t = (masked_t.astype(jnp.float32) - removed_t).astype(jnp.bfloat16)
-    margin_cleaned_t, energy_cleaned_t = block_apply(
-        (margin_blocks, energy_blocks), shifts_flat, cleaned_t
-    )
-    margin_part = tn_dot(cleaned_t, margin_cleaned_t)
-    energy_part = tn_dot(cleaned_t, energy_cleaned_t)
+    removed = lax.dot_general(
+        margin.astype(jnp.bfloat16), windows, (((0,), (0,)), ((), ())), preferred_element_type=jnp.float32
+    )
+    cleaned = (masked.astype(jnp.float32) - removed).astype(jnp.bfloat16)
+    margin_cleaned, energy_cleaned = block_apply((margin_blocks, energy_blocks), shifts_flat, cleaned)
+    margin_part = nt_dot(cleaned, margin_cleaned)
+    energy_part = nt_dot(cleaned, energy_cleaned)
     margin_total, energy_total = row_sum(jnp.stack([margin_part, energy_part]))
     margin_pencil = margin_total / nmat_total
     energy_pencil = energy_total / nmat_total
@@ -160,10 +182,9 @@
         energy_diag / jnp.where(valid_mask, margin_diag, jnp.float32(1.0)),
         jnp.float32(0.0),
     )
-    residual_t = (
-        energy_cleaned_t.astype(jnp.float32) - theta[None, :] * margin_cleaned_t.astype(jnp.float32)
+    residual = (
+        energy_cleaned.astype(jnp.float32) - theta[:, None] * margin_cleaned.astype(jnp.float32)
     ).astype(jnp.bfloat16)
-    residual = residual_t.T
     return (residual[None], margin_pencil[None], energy_pencil[None])
 
 

time: 301 us -> 258 us (0.86)
  local copies, waits for them, and re-layouts: 103 us -> 60.3 us
  other arithmetic: 32.8 us -> 16.6 us
  waiting for transfers between devices: 48.5 us -> 60.6 us
  Pallas kernels: 45.6 us -> 57.5 us
  matrix products: 29.6 us -> 21.3 us
    optimization_barrier x4 -> x0, local copies, waits for them, and re-layouts: 24.9 us -> none  [shards(): lax.optimization_barrier((from_below + from_above, masked_t, margin_block...]
    unnamed x22 -> x23, local copies, waits for them, and re-layouts: 72.2 us -> 52.9 us
    ppermute x4, waiting for transfers between devices: 30.4 us -> 44.6 us  [from_behind(): return lax.ppermute(block, axis, route)]
    transpose x1 -> x0, other arithmetic: 12.3 us -> none  [shards(): windows_t = jnp.concatenate(received, axis=0).T]
    pallas_call x2, Pallas kernels: 45.6 us -> 57.5 us  [block_apply(): pl.pallas_call(kernel, grid_spec=grid_spec, out_shape=[jax.ShapeDtypeStru...]
    dot_general x4, matrix products: 29.6 us -> 21.3 us  [the longest x3 14.8 us: nt_dot(): lax.dot_general(a, b, (((1,), (1,)), ((), ())), preferred_element_type=jn...]
    select_n x1 -> x0, other arithmetic: 6.42 us -> none  [shards(): jnp.where(valid_mask[None, :], own_vectors.T, jnp.zeros((), own_vectors.d...]
  transfers between devices with their start and end apart: 14 -> 14, of which waited for: 9 -> 13; matrix products, arithmetic and copies ran while one was open for 21% -> 19% of each run, Pallas kernels for 0% -> 0%
where the time goes in v3:
time: 258 us; the launch traced here: 253 us
  waiting for transfers between devices  60.6 us (23%)
  local copies, waits for them, and re-layouts  60.3 us (23%)
  Pallas kernels  57.5 us (22%)
  starting transfers between devices  31.4 us (12%)
  matrix products  21.3 us (8%)
  other arithmetic  16.6 us (6%)
  between operations  5.47 us (2%)
    pallas_call x2, Pallas kernels, block_apply(): pl.pallas_call(kernel, grid_spec=grid_spec, out_shape=[jax.ShapeDtypeStru...  57.5 us
    unnamed x23, local copies, waits for them, and re-layouts  52.9 us
    ppermute x4, waiting for transfers between devices, from_behind(): return lax.ppermute(block, axis, route)  44.6 us
    dot_general x3, matrix products, nt_dot(): lax.dot_general(a, b, (((1,), (1,)), ((), ())), preferred_element_type=jn...  14.8 us
    ppermute x4, starting transfers between devices, from_behind(): return lax.ppermute(block, axis, route)  12.3 us
    ppermute x6, waiting for transfers between devices, row_sum(): lax.ppermute(part, 'row', [(i, (i + step) % count) for i in range(count)])  9.69 us
    broadcast_in_dim x1, other arithmetic, shards(): return (residual[None], margin_pencil[None], energy_pencil[None])  9.47 us
    ppermute x6, starting transfers between devices, row_sum(): lax.ppermute(part, 'row', [(i, (i + step) % count) for i in range(count)])  7.28 us
  transfers between devices with their start and end apart: 14, of which 13 were waited for; matrix products, arithmetic and copies ran while one was open for 19% of the time, Pallas kernels for 0%

profile of v3, /device:TPU:12, one launch (start us, length us, event | category | flops | bytes accessed | tf_op | source)
XLA Modules:
  0.0 253.2 jit_solution(16950229961507793021)
XLA Ops:
  7.8 4.8 %bitcast_select_fusion.2 = (bf16[32,24576]{1,0:T(8,128)(2,1)}, bf16[32,24576]{1,0:T(8,128)(2,1)}) fusion(bf16[1,128,24576]{2,1,0:T(8,128)(2,1)} %param.6, s32[]{:T(128)S(6)} %select_n.89, pred[32]{0:T(512)(128)(4,1)S(1)} %get-tuple-element.33, s32[]{:T(128)S(6)} %select_n.87, pred[32]{0:T(512)(128)(4,1)S(1)} %get-tuple-element.34), kind=kLoop, calls=%fused_computation.10 | loop fusion | flops 1572864 | bytes 6291528 | tf_op jit(solution)/shard_map/jit(_where)/select_n | solution.py:143
  12.6 3.4 %collective-permute-start = (bf16[32,24576]{1,0:T(8,128)(2,1)}, bf16[32,24576]{1,0:T(8,128)(2,1)S(1)}, u32[]{:S(2)}, u32[]{:S(2)}) collective-permute-start(bf16[32,24576]{1,0:T(8,128)(2,1)} %get-tuple-element.24), channel_id=1, source_target_pairs={{0,8},{4,12},{8,16},{12,20},{16,24},{20,28},{1,9},{5,13},{9,17},{1... | collective-permute-start | bytes 4718600 | tf_op jit(solution)/shard_map/ppermute | solution.py:19
  16.0 1.9 collective-permute-start.1
  17.9 4.5 %collective-permute-start.2 = (bf16[32,24576]{1,0:T(8,128)(2,1)}, bf16[32,24576]{1,0:T(8,128)(2,1)}, u32[]{:S(2)}, u32[]{:S(2)}) collective-permute-start(bf16[32,24576]{1,0:T(8,128)(2,1)} %get-tuple-element.23), channel_id=1, source_target_pairs={{4,0},{8,4},{12,8},{16,12},{20,16},{24,20},{28,24},{5,1},{9,5},{13... | collective-permute-start | bytes 4718600 | tf_op jit(solution)/shard_map/ppermute | solution.py:19
  22.5 2.4 collective-permute-start.3
  24.9 23.4 %copy.12.refs_0_ = bf16[256,96,288]{2,1,0:T(8,128)(2,1)} copy(bf16[256,96,288]{0,2,1:T(8,128)(2,1)} %param.9) | data formatting | bytes 28311552 | tf_op args[3]
  48.4 23.3 %copy.13.refs_1_ = bf16[256,96,288]{2,1,0:T(8,128)(2,1)} copy(bf16[256,96,288]{0,2,1:T(8,128)(2,1)} %param.10) | data formatting | bytes 28311552 | tf_op args[4]
  72.7 11.4 %collective-permute-done.1 = bf16[32,24576]{1,0:T(8,128)(2,1)} collective-permute-done((bf16[32,24576]{1,0:T(8,128)(2,1)}, bf16[32,24576]{1,0:T(8,128)(2,1)}, u32[]{:S(2)}, u32[]{:S(2)}) %collective-permute-start.1) | collective-permute-done | bytes 1572896 | tf_op jit(solution)/shard_map/ppermute | solution.py:19
  84.8 32.6 %collective-permute-done.3 = bf16[32,24576]{1,0:T(8,128)(2,1)} collective-permute-done((bf16[32,24576]{1,0:T(8,128)(2,1)}, bf16[32,24576]{1,0:T(8,128)(2,1)}, u32[]{:S(2)}, u32[]{:S(2)}) %collective-permute-start.3) | collective-permute-done | bytes 1572896 | tf_op jit(solution)/shard_map/ppermute | solution.py:19
  117.4 1.5 constant_dynamic-update-slice_fusion.2
  119.0 1.5 constant_dynamic-update-slice_fusion.1
  120.5 1.5 constant_dynamic-update-slice_fusion.x_hbm
  122.0 3.5 %collective-permute-start.4 = (bf16[128,256]{1,0:T(8,128)(2,1)S(1)}, bf16[128,256]{1,0:T(8,128)(2,1)S(1)}, u32[]{:S(2)}, u32[]{:S(2)}) collective-permute-start(bf16[128,256]{1,0:T(8,128)(2,1)S(1)} %get-tuple-element.22), channel_id=1, source_target_pairs={{0,1},{1,2},{2,3},{4,5},{5,6},{6,7},{8,9},{9,10},{10,11},{12,13},{... | collective-permute-start | bytes 196616 | tf_op jit(solution)/shard_map/ppermute | solution.py:27
  125.5 2.4 collective-permute-start.5
  128.2 3.5 %collective-permute-done.5.hi_ref = bf16[128,256]{1,0:T(8,128)(2,1)S(1)} collective-permute-done((bf16[128,256]{1,0:T(8,128)(2,1)S(1)}, bf16[128,256]{1,0:T(8,128)(2,1)S(1)}, u32[]{:S(2)}, u32[]{:S(2)}) %collective-permute-start.5) | collective-permute-done | bytes 65568 | tf_op jit(solution)/shard_map/ppermute | solution.py:28
  132.3 25.1 %shard_map.85 = bf16[128,24576]{1,0:T(8,128)(2,1)} custom-call(s32[768]{0:T(1024)} %reshape.121.shift_ref, bf16[128,24576]{1,0:T(8,128)(2,1)} %copy-done.2, bf16[128,256]{1,0:T(8,128)(2,1)} %copy-done.5, bf16[128,256]{1,0:T(8,128)(2,1)} %copy-done.7, bf16[256,96,288]{2,1,0:T(8,128)(2,1)} %copy.12.refs_0_), custom_call_target="tpu_custom_call" | custom-call | tf_op jit(solution)/shard_map/pallas_call | solution.py:106
  157.4 6.5 %fusion.2 = f32[128,128]{1,0:T(8,128)S(1)} fusion(bf16[128,24576]{1,0:T(8,128)(2,1)} %shard_map.85, bf16[1,128,24576]{2,1,0:T(8,128)(2,1)} %param.6, pred[128]{0:T(512)(128)(4,1)S(1)} %iota_compare_fusion), kind=kOutput, calls=%fused_computation.9 | convolution fusion | flops 808452096 | bytes 12648576 | tf_op jit(solution)/shard_map/dot_general | solution.py:133
  163.9 1.6 collective-permute-start.6
  167.1 1.8 collective-permute-done.6
  168.9 1.9 collective-permute-done.7
  172.1 6.5 %fusion.x_hbm = bf16[128,24576]{1,0:T(8,128)(2,1)S(1)} fusion(bf16[128,24576]{1,0:T(8,128)(2,1)} %copy-done.2, bf16[1,128,24576]{2,1,0:T(8,128)(2,1)} %param.6, pred[128]{0:T(512)(128)(4,1)S(1)} %iota_compare_fusion, f32[4,128,128]{2,1,0:T(8,128)S(1)} %broadcast_select_fusion.1), kind=kOutput, calls=%fused_computation.5 | convolution fusion | flops 817971200 | bytes 19136640 | tf_op jit(solution)/shard_map/dot_general | solution.py:168
  178.6 2.4 collective-permute-start.10
  181.0 3.6 %collective-permute-start.9 = (bf16[128,256]{1,0:T(8,128)(2,1)S(1)}, bf16[128,256]{1,0:T(8,128)(2,1)S(1)}, u32[]{:S(2)}, u32[]{:S(2)}) collective-permute-start(bf16[128,256]{1,0:T(8,128)(2,1)S(1)} %get-tuple-element.20), channel_id=1, source_target_pairs={{0,1},{1,2},{2,3},{4,5},{5,6},{6,7},{8,9},{9,10},{10,11},{12,13},{... | collective-permute-start | bytes 196616 | tf_op jit(solution)/shard_map/ppermute | solution.py:27
  184.8 2.4 collective-permute-done.9.lo_ref
  187.8 32.4 %shard_map.86 = (bf16[128,24576]{1,0:T(8,128)(2,1)}, bf16[128,24576]{1,0:T(8,128)(2,1)}) custom-call(s32[768]{0:T(1024)} %reshape.121.shift_ref, bf16[128,24576]{1,0:T(8,128)(2,1)} %copy-done, bf16[128,256]{1,0:T(8,128)(2,1)} %copy-done.6, bf16[128,256]{1,0:T(8,128)(2,1)} %copy-done.4, bf16[256,96,288]{2,1,0:T(8,128)(2,1)} %copy.12.refs_0_, ...), custom_call_target="tpu_custom_call" | custom-call | tf_op jit(solution)/shard_map/pallas_call | solution.py:106
  220.3 6.5 %convolution_bitcast_fusion.1 = f32[1,128,128]{2,1,0:T(8,128)S(1)} fusion(bf16[128,24576]{1,0:T(8,128)(2,1)} %copy-done, bf16[128,24576]{1,0:T(8,128)(2,1)} %get-tuple-element.18), kind=kOutput, calls=%fused_computation.13 | convolution fusion | flops 805306368 | bytes 12648448 | tf_op jit(solution)/shard_map/dot_general | solution.py:133
  226.8 1.6 copy-done.3
  228.4 1.8 convolution_bitcast_fusion
  230.3 1.6 collective-permute-start.11
  232.4 1.9 collective-permute-start.13
  235.3 3.3 %collective-permute-done.12 = f32[2,128,128]{2,1,0:T(8,128)S(1)} collective-permute-done((f32[2,128,128]{2,1,0:T(8,128)S(1)}, f32[2,128,128]{2,1,0:T(8,128)S(1)}, u32[]{:S(2)}, u32[]{:S(2)}) %collective-permute-start.12) | collective-permute-done | bytes 131104 | tf_op jit(solution)/shard_map/ppermute | solution.py:120
  243.8 9.5 %fusion.1 = bf16[1,128,24576]{2,1,0:T(8,128)(2,1)} fusion(bf16[128,24576]{1,0:T(8,128)(2,1)} %get-tuple-element.18, bf16[128,24576]{1,0:T(8,128)(2,1)} %get-tuple-element.17, f32[128]{0:T(128)S(1)} %divide_select_fusion), kind=kLoop, calls=%fused_computation.7 | loop fusion | flops 15728640 | bytes 18874880 | tf_op jit(solution)/shard_map/broadcast_in_dim | solution.py:188
  (53 shorter events, 15.6 us)
Async XLA Ops:
  12.6 60.1 %collective-permute-start = (bf16[32,24576]{1,0:T(8,128)(2,1)}, bf16[32,24576]{1,0:T(8,128)(2,1)S(1)}, u32[]{:S(2)}, u32[]{:S(2)}) collective-permute-start(bf16[32,24576]{1,0:T(8,128)(2,1)} %get-tuple-element.24), channel_id=1, source_target_pairs={{0,8},{4,12},{8,16},{12,20},{16,24},{20,28},{1,9},{5,13},{9,17},{1... | collective-permute-start | bytes 4718600 | tf_op jit(solution)/shard_map/ppermute | solution.py:19
  16.0 68.1 %collective-permute-start.1 = (bf16[32,24576]{1,0:T(8,128)(2,1)}, bf16[32,24576]{1,0:T(8,128)(2,1)}, u32[]{:S(2)}, u32[]{:S(2)}) collective-permute-start(bf16[32,24576]{1,0:T(8,128)(2,1)} %get-tuple-element.24), channel_id=1, source_target_pairs={{0,4},{4,8},{8,12},{12,16},{16,20},{20,24},{24,28},{1,5},{5,9},{9,... | collective-permute-start | bytes 4718600 | tf_op jit(solution)/shard_map/ppermute | solution.py:19
  17.9 66.9 %collective-permute-start.2 = (bf16[32,24576]{1,0:T(8,128)(2,1)}, bf16[32,24576]{1,0:T(8,128)(2,1)}, u32[]{:S(2)}, u32[]{:S(2)}) collective-permute-start(bf16[32,24576]{1,0:T(8,128)(2,1)} %get-tuple-element.23), channel_id=1, source_target_pairs={{4,0},{8,4},{12,8},{16,12},{20,16},{24,20},{28,24},{5,1},{9,5},{13... | collective-permute-start | bytes 4718600 | tf_op jit(solution)/shard_map/ppermute | solution.py:19
  22.5 94.9 %collective-permute-start.3 = (bf16[32,24576]{1,0:T(8,128)(2,1)}, bf16[32,24576]{1,0:T(8,128)(2,1)}, u32[]{:S(2)}, u32[]{:S(2)}) collective-permute-start(bf16[32,24576]{1,0:T(8,128)(2,1)} %get-tuple-element.23), channel_id=1, source_target_pairs={{8,0},{12,4},{16,8},{20,12},{24,16},{28,20},{9,1},{13,5},{17,9},{2... | collective-permute-start | bytes 4718600 | tf_op jit(solution)/shard_map/ppermute | solution.py:19
  48.4 23.4 %copy-start.8 = (s32[256,3]{0,1:T(4,128)S(1)}, s32[256,3]{0,1:T(4,128)}, u32[]{:S(2)}) copy-start(s32[256,3]{0,1:T(4,128)} %param.11) | copy-start | bytes 9220
  122.0 9.7 %copy-start.2 = (bf16[128,24576]{1,0:T(8,128)(2,1)}, bf16[128,24576]{1,0:T(8,128)(2,1)S(1)}, u32[]{:S(2)}) copy-start(bf16[128,24576]{1,0:T(8,128)(2,1)S(1)} %constant_dynamic-update-slice_fusion.x_hbm) | copy-start | bytes 18874372
  122.0 6.2 %collective-permute-start.4 = (bf16[128,256]{1,0:T(8,128)(2,1)S(1)}, bf16[128,256]{1,0:T(8,128)(2,1)S(1)}, u32[]{:S(2)}, u32[]{:S(2)}) collective-permute-start(bf16[128,256]{1,0:T(8,128)(2,1)S(1)} %get-tuple-element.22), channel_id=1, source_target_pairs={{0,1},{1,2},{2,3},{4,5},{5,6},{6,7},{8,9},{9,10},{10,11},{12,13},{... | collective-permute-start | bytes 196616 | tf_op jit(solution)/shard_map/ppermute | solution.py:27
  125.5 6.2 %collective-permute-start.5 = (bf16[128,256]{1,0:T(8,128)(2,1)S(1)}, bf16[128,256]{1,0:T(8,128)(2,1)S(1)}, u32[]{:S(2)}, u32[]{:S(2)}) collective-permute-start(bf16[128,256]{1,0:T(8,128)(2,1)S(1)} %get-tuple-element.21), channel_id=1, source_target_pairs={{1,0},{2,1},{3,2},{5,4},{6,5},{7,6},{9,8},{10,9},{11,10},{13,12},{... | collective-permute-start | bytes 196616 | tf_op jit(solution)/shard_map/ppermute | solution.py:28
  128.2 3.5 %copy-start.5 = (bf16[128,256]{1,0:T(8,128)(2,1)}, bf16[128,256]{1,0:T(8,128)(2,1)S(1)}, u32[]{:S(2)}) copy-start(bf16[128,256]{1,0:T(8,128)(2,1)S(1)} %collective-permute-done.4.lo_ref) | copy-start | bytes 196612
  131.7 0.6 copy-start.7
  163.9 5.0 %collective-permute-start.6 = (f32[128,128]{1,0:T(8,128)S(1)}, f32[128,128]{1,0:T(8,128)S(1)}, u32[]{:S(2)}, u32[]{:S(2)}) collective-permute-start(f32[128,128]{1,0:T(8,128)S(1)} %fusion.2), channel_id=1, source_target_pairs={{0,1},{1,2},{2,3},{3,0},{4,5},{5,6},{6,7},{7,4},{8,9},{9,10},{10,1... | collective-permute-start | bytes 196616 | tf_op jit(solution)/shard_map/ppermute | solution.py:120
  165.5 5.2 %collective-permute-start.7 = (f32[128,128]{1,0:T(8,128)S(1)}, f32[128,128]{1,0:T(8,128)S(1)}, u32[]{:S(2)}, u32[]{:S(2)}) collective-permute-start(f32[128,128]{1,0:T(8,128)S(1)} %fusion.2), channel_id=1, source_target_pairs={{0,2},{1,3},{2,0},{3,1},{4,6},{5,7},{6,4},{7,5},{8,10},{9,11},{10,... | collective-permute-start | bytes 196616 | tf_op jit(solution)/shard_map/ppermute | solution.py:120
  166.8 4.6 %collective-permute-start.8 = (f32[128,128]{1,0:T(8,128)S(1)}, f32[128,128]{1,0:T(8,128)S(1)}, u32[]{:S(2)}, u32[]{:S(2)}) collective-permute-start(f32[128,128]{1,0:T(8,128)S(1)} %fusion.2), channel_id=1, source_target_pairs={{0,3},{1,0},{2,1},{3,2},{4,7},{5,4},{6,5},{7,6},{8,11},{9,8},{10,9... | collective-permute-start | bytes 196616 | tf_op jit(solution)/shard_map/ppermute | solution.py:120
  178.6 8.6 %copy-start = (bf16[128,24576]{1,0:T(8,128)(2,1)}, bf16[128,24576]{1,0:T(8,128)(2,1)S(1)}, u32[]{:S(2)}) copy-start(bf16[128,24576]{1,0:T(8,128)(2,1)S(1)} %fusion.x_hbm) | copy-start | bytes 18874372
  178.6 6.2 %collective-permute-start.10 = (bf16[128,256]{1,0:T(8,128)(2,1)S(1)}, bf16[128,256]{1,0:T(8,128)(2,1)S(1)}, u32[]{:S(2)}, u32[]{:S(2)}) collective-permute-start(bf16[128,256]{1,0:T(8,128)(2,1)S(1)} %get-tuple-element.19), channel_id=1, source_target_pairs={{1,0},{2,1},{3,2},{5,4},{6,5},{7,6},{9,8},{10,9},{11,10},{13,12},{... | collective-permute-start | bytes 196616 | tf_op jit(solution)/shard_map/ppermute | solution.py:28
  181.0 6.2 %collective-permute-start.9 = (bf16[128,256]{1,0:T(8,128)(2,1)S(1)}, bf16[128,256]{1,0:T(8,128)(2,1)S(1)}, u32[]{:S(2)}, u32[]{:S(2)}) collective-permute-start(bf16[128,256]{1,0:T(8,128)(2,1)S(1)} %get-tuple-element.20), channel_id=1, source_target_pairs={{0,1},{1,2},{2,3},{4,5},{5,6},{6,7},{8,9},{9,10},{10,11},{12,13},{... | collective-permute-start | bytes 196616 | tf_op jit(solution)/shard_map/ppermute | solution.py:27
  184.8 2.4 copy-start.4
  187.2 0.6 copy-start.6
  220.2 6.6 %copy-start.1 = (bf16[128,24576]{1,0:T(8,128)(2,1)S(1)}, bf16[128,24576]{1,0:T(8,128)(2,1)}, u32[]{:S(2)}) copy-start(bf16[128,24576]{1,0:T(8,128)(2,1)} %copy-done) | copy-start | bytes 18874372
  220.2 8.2 %copy-start.3 = (bf16[128,24576]{1,0:T(8,128)(2,1)S(1)}, bf16[128,24576]{1,0:T(8,128)(2,1)}, u32[]{:S(2)}) copy-start(bf16[128,24576]{1,0:T(8,128)(2,1)} %get-tuple-element.17) | copy-start | bytes 18874372
  230.3 5.0 %collective-permute-start.11 = (f32[2,128,128]{2,1,0:T(8,128)S(1)}, f32[2,128,128]{2,1,0:T(8,128)S(1)}, u32[]{:S(2)}, u32[]{:S(2)}) collective-permute-start(f32[2,128,128]{2,1,0:T(8,128)S(1)} %get-tuple-element.30), channel_id=1, source_target_pairs={{0,1},{1,2},{2,3},{3,0},{4,5},{5,6},{6,7},{7,4},{8,9},{9,10},{10,1... | collective-permute-start | bytes 393224 | tf_op jit(solution)/shard_map/ppermute | solution.py:120
  231.9 6.7 %collective-permute-start.12 = (f32[2,128,128]{2,1,0:T(8,128)S(1)}, f32[2,128,128]{2,1,0:T(8,128)S(1)}, u32[]{:S(2)}, u32[]{:S(2)}) collective-permute-start(f32[2,128,128]{2,1,0:T(8,128)S(1)} %get-tuple-element.30), channel_id=1, source_target_pairs={{0,2},{1,3},{2,0},{3,1},{4,6},{5,7},{6,4},{7,5},{8,10},{9,11},{10,... | collective-permute-start | bytes 393224 | tf_op jit(solution)/shard_map/ppermute | solution.py:120
  232.4 7.3 %collective-permute-start.13 = (f32[2,128,128]{2,1,0:T(8,128)S(1)}, f32[2,128,128]{2,1,0:T(8,128)S(1)}, u32[]{:S(2)}, u32[]{:S(2)}) collective-permute-start(f32[2,128,128]{2,1,0:T(8,128)S(1)} %get-tuple-element.30), channel_id=1, source_target_pairs={{0,3},{1,0},{2,1},{3,2},{4,7},{5,4},{6,5},{7,6},{8,11},{9,8},{10,9... | collective-permute-start | bytes 393224 | tf_op jit(solution)/shard_map/ppermute | solution.py:120

commit v4 on v3

--- a/solution.py
+++ b/solution.py
@@ -152,14 +152,25 @@
     )
     own_blocks = lax.axis_index("row") * block_rows + jnp.arange(block_rows, dtype=jnp.int32)
     shifts_flat = (block_columns - own_blocks[:, None]).reshape(-1)
-    from_below = [from_behind(upper_window, "cuts", distance) for distance in (2, 1)]
-    from_above = [from_behind(lower_window, "cuts", -distance) for distance in (1, 2)]
+    cuts_count = lax.axis_size("cuts")
+    odd = lax.axis_index("cuts") % 2 == 1
+    evens = range(0, cuts_count, 2)
+    odds = range(1, cuts_count, 2)
+    upper_1 = from_behind(upper_window, "cuts", 1)
+    lower_1 = from_behind(lower_window, "cuts", -1)
+    upper_direct = lax.ppermute(upper_window, "cuts", [(i, i + 2) for i in evens if i + 2 < cuts_count])
+    lower_direct = lax.ppermute(lower_window, "cuts", [(i, i - 2) for i in odds if i - 2 >= 0])
     row_major = Layout(major_to_minor=(0, 1, 2))
     margin_blocks = with_layout_constraint(margin_blocks, row_major)
     energy_blocks = with_layout_constraint(energy_blocks, row_major)
-    received, margin_blocks, energy_blocks = lax.optimization_barrier(
-        (from_below + from_above, margin_blocks, energy_blocks)
-    )
+    upper_1, lower_1, upper_direct, lower_direct, margin_blocks, energy_blocks = lax.optimization_barrier(
+        (upper_1, lower_1, upper_direct, lower_direct, margin_blocks, energy_blocks)
+    )
+    upper_2 = jnp.where(
+        odd, lax.ppermute(upper_1, "cuts", [(i, i + 1) for i in evens if i + 1 < cuts_count]), upper_direct
+    )
+    lower_2 = jnp.where(odd, lower_direct, lax.ppermute(lower_1, "cuts", [(i, i - 1) for i in odds]))
+    received = [upper_2, upper_1, lower_1, lower_2]
     masked = jnp.where(valid_mask[:, None], own_vectors, jnp.zeros((), own_vectors.dtype))
     windows = jnp.concatenate(received, axis=0)
     (margin_windows,) = block_apply((margin_blocks,), shifts_flat, windows)

time: 258 us -> 236 us (0.915); the launches traced: 253 us -> 234 us
  waiting for transfers between devices: 60.6 us -> 41.7 us
  other arithmetic: 16.6 us -> 21.4 us
  local copies, waits for them, and re-layouts: 60.3 us -> 55.6 us
    ppermute x4 -> x2, waiting for transfers between devices: 44.6 us -> 0.01 us  [from_behind(): return lax.ppermute(block, axis, route)]
    ppermute x0 -> x4, waiting for transfers between devices: none -> 19.4 us  [the longest x1 16.9 us: shards(): lax.ppermute(upper_window, 'cuts', [(i, i + 2) for i in evens if i + 2 <...]
    ppermute x0 -> x4, starting transfers between devices: none -> 6.98 us  [the longest x1 2.5 us: shards(): lax.ppermute(upper_window, 'cuts', [(i, i + 2) for i in evens if i + 2 <...]
    ppermute x6, waiting for transfers between devices: 9.69 us -> 15.5 us  [row_sum(): lax.ppermute(part, 'row', [(i, (i + step) % count) for i in range(count)])]
    ppermute x4 -> x2, starting transfers between devices: 12.3 us -> 6.45 us  [from_behind(): return lax.ppermute(block, axis, route)]
    unnamed x23 -> x28, local copies, waits for them, and re-layouts: 52.9 us -> 49.7 us
    concatenate x0 -> x1, other arithmetic: none -> 2.95 us  [shards(): windows = jnp.concatenate(received, axis=0)]
  transfers between devices with their start and end apart: 14 -> 16, of which waited for: 13 -> 12; matrix products, arithmetic and copies ran while one was open for 19% -> 21% of each run, Pallas kernels for 0% -> 0%
where the time goes in v4:
time: 236 us; the launch traced here: 234 us
  Pallas kernels  57.5 us (24%)
  local copies, waits for them, and re-layouts  55.6 us (24%)
  waiting for transfers between devices  41.7 us (18%)
  starting transfers between devices  32.5 us (14%)
  other arithmetic  21.4 us (9%)
  matrix products  20.1 us (9%)
  between operations  5.53 us (2%)
    pallas_call x2, Pallas kernels, block_apply(): pl.pallas_call(kernel, grid_spec=grid_spec, out_shape=[jax.ShapeDtypeStru...  57.5 us
    unnamed x28, local copies, waits for them, and re-layouts  49.7 us
    ppermute x1, waiting for transfers between devices, shards(): lax.ppermute(upper_window, 'cuts', [(i, i + 2) for i in evens if i + 2 <...  16.9 us
    ppermute x6, waiting for transfers between devices, row_sum(): lax.ppermute(part, 'row', [(i, (i + step) % count) for i in range(count)])  15.5 us
    dot_general x3, matrix products, nt_dot(): lax.dot_general(a, b, (((1,), (1,)), ((), ())), preferred_element_type=jn...  14.8 us
    broadcast_in_dim x1, other arithmetic, shards(): return (residual[None], margin_pencil[None], energy_pencil[None])  9.47 us
    ppermute x6, starting transfers between devices, row_sum(): lax.ppermute(part, 'row', [(i, (i + step) % count) for i in range(count)])  7.37 us
    ppermute x2, starting transfers between devices, from_behind(): return lax.ppermute(block, axis, route)  6.45 us
  transfers between devices with their start and end apart: 16, of which 12 were waited for; matrix products, arithmetic and copies ran while one was open for 21% of the time, Pallas kernels for 0%

profile of v4, /device:TPU:12, one launch (start us, length us, event | category | flops | bytes accessed | tf_op | source)
XLA Modules:
  0.0 234.5 jit_solution(2576102955580188879)
XLA Ops:
  7.8 4.8 %bitcast_select_fusion.2 = (bf16[32,24576]{1,0:T(8,128)(2,1)}, bf16[32,24576]{1,0:T(8,128)(2,1)}) fusion(bf16[1,128,24576]{2,1,0:T(8,128)(2,1)} %param.6, s32[]{:T(128)S(6)} %select_n.109, pred[32]{0:T(512)(128)(4,1)S(1)} %get-tuple-element.33, s32[]{:T(128)S(6)} %select_n.107, pred[32]{0:T(512)(128)(4,1)S(1)} %get-tuple-element.34), kind=kLoop, calls=%fused_computation.11 | loop fusion | flops 1572864 | bytes 6291528 | tf_op jit(solution)/shard_map/jit(_where)/select_n | solution.py:143
  12.6 1.9 collective-permute-start
  14.5 4.5 %collective-permute-start.1 = (bf16[32,24576]{1,0:T(8,128)(2,1)}, bf16[32,24576]{1,0:T(8,128)(2,1)}, u32[]{:S(2)}, u32[]{:S(2)}) collective-permute-start(bf16[32,24576]{1,0:T(8,128)(2,1)} %get-tuple-element.23), channel_id=1, source_target_pairs={{4,0},{8,4},{12,8},{16,12},{20,16},{24,20},{28,24},{5,1},{9,5},{13... | collective-permute-start | bytes 4718600 | tf_op jit(solution)/shard_map/ppermute | solution.py:19
  19.0 2.5 %collective-permute-start.2 = (bf16[32,24576]{1,0:T(8,128)(2,1)}, bf16[32,24576]{1,0:T(8,128)(2,1)}, u32[]{:S(2)}, u32[]{:S(2)}) collective-permute-start(bf16[32,24576]{1,0:T(8,128)(2,1)} %get-tuple-element.24), channel_id=1, source_target_pairs={{0,8},{8,16},{16,24},{1,9},{9,17},{17,25},{2,10},{10,18},{18,26},{... | collective-permute-start | bytes 4718600 | tf_op jit(solution)/shard_map/ppermute | solution.py:161
  22.3 23.4 %copy.12.refs_0_ = bf16[256,96,288]{2,1,0:T(8,128)(2,1)} copy(bf16[256,96,288]{0,2,1:T(8,128)(2,1)} %param.9) | data formatting | bytes 28311552 | tf_op args[3]
  45.8 23.3 %copy.13.refs_1_ = bf16[256,96,288]{2,1,0:T(8,128)(2,1)} copy(bf16[256,96,288]{0,2,1:T(8,128)(2,1)} %param.10) | data formatting | bytes 28311552 | tf_op args[4]
  69.1 16.9 %collective-permute-done.2 = bf16[32,24576]{1,0:T(8,128)(2,1)} collective-permute-done((bf16[32,24576]{1,0:T(8,128)(2,1)}, bf16[32,24576]{1,0:T(8,128)(2,1)}, u32[]{:S(2)}, u32[]{:S(2)}) %collective-permute-start.2) | collective-permute-done | bytes 1572896 | tf_op jit(solution)/shard_map/ppermute | solution.py:161
  86.1 2.4 %collective-permute-start.4 = (bf16[32,24576]{1,0:T(8,128)(2,1)S(1)}, bf16[32,24576]{1,0:T(8,128)(2,1)}, u32[]{:S(2)}, u32[]{:S(2)}) collective-permute-start(bf16[32,24576]{1,0:T(8,128)(2,1)S(1)} %collective-permute-done), channel_id=1, source_target_pairs={{0,4},{8,12},{16,20},{24,28},{1,5},{9,13},{17,21},{25,29},{2,6},{1... | collective-permute-start | bytes 4718600 | tf_op jit(solution)/shard_map/ppermute | solution.py:170
  90.8 1.7 broadcast_select_fusion.1
  92.5 2.5 %collective-permute-done.5 = bf16[32,24576]{1,0:T(8,128)(2,1)S(1)} collective-permute-done((bf16[32,24576]{1,0:T(8,128)(2,1)}, bf16[32,24576]{1,0:T(8,128)(2,1)S(1)}, u32[]{:S(2)}, u32[]{:S(2)}) %collective-permute-start.5) | collective-permute-done | bytes 1572896 | tf_op jit(solution)/shard_map/ppermute | solution.py:172
  95.2 3.0 %pad_maximum_fusion.x_hbm = bf16[128,24576]{1,0:T(8,128)(2,1)S(1)} fusion(bf16[32,24576]{1,0:T(8,128)(2,1)S(1)} %broadcast_select_fusion, bf16[32,24576]{1,0:T(8,128)(2,1)} %collective-permute-done.1, bf16[32,24576]{1,0:T(8,128)(2,1)S(1)} %copy-done.6, bf16[32,24576]{1,0:T(8,128)(2,1)S(1)} %broadcast_select_fusion.1), kind=kLoop, calls=%fused_computation.8 | loop fusion | flops 25165824 | bytes 12582912 | tf_op jit(solution)/shard_map/concatenate | solution.py:175
  98.2 3.5 %collective-permute-start.6 = (bf16[128,256]{1,0:T(8,128)(2,1)S(1)}, bf16[128,256]{1,0:T(8,128)(2,1)S(1)}, u32[]{:S(2)}, u32[]{:S(2)}) collective-permute-start(bf16[128,256]{1,0:T(8,128)(2,1)S(1)} %get-tuple-element.22), channel_id=1, source_target_pairs={{0,1},{1,2},{2,3},{4,5},{5,6},{6,7},{8,9},{9,10},{10,11},{12,13},{... | collective-permute-start | bytes 196616 | tf_op jit(solution)/shard_map/ppermute | solution.py:27
  101.7 2.4 %collective-permute-start.7 = (bf16[128,256]{1,0:T(8,128)(2,1)S(1)}, bf16[128,256]{1,0:T(8,128)(2,1)S(1)}, u32[]{:S(2)}, u32[]{:S(2)}) collective-permute-start(bf16[128,256]{1,0:T(8,128)(2,1)S(1)} %get-tuple-element.21), channel_id=1, source_target_pairs={{1,0},{2,1},{3,2},{5,4},{6,5},{7,6},{9,8},{10,9},{11,10},{13,12},{... | collective-permute-start | bytes 196616 | tf_op jit(solution)/shard_map/ppermute | solution.py:28
  104.6 3.7 %collective-permute-done.7.hi_ref = bf16[128,256]{1,0:T(8,128)(2,1)S(1)} collective-permute-done((bf16[128,256]{1,0:T(8,128)(2,1)S(1)}, bf16[128,256]{1,0:T(8,128)(2,1)S(1)}, u32[]{:S(2)}, u32[]{:S(2)}) %collective-permute-start.7) | collective-permute-done | bytes 65568 | tf_op jit(solution)/shard_map/ppermute | solution.py:28
  108.9 25.1 %shard_map.85 = bf16[128,24576]{1,0:T(8,128)(2,1)} custom-call(s32[768]{0:T(1024)} %reshape.121.shift_ref, bf16[128,24576]{1,0:T(8,128)(2,1)} %copy-done.2, bf16[128,256]{1,0:T(8,128)(2,1)} %copy-done.9, bf16[128,256]{1,0:T(8,128)(2,1)} %copy-done.11, bf16[256,96,288]{2,1,0:T(8,128)(2,1)} %copy.12.refs_0_), custom_call_target="tpu_custom_call" | custom-call | tf_op jit(solution)/shard_map/pallas_call | solution.py:106
  134.1 6.5 %fusion.2 = f32[128,128]{1,0:T(8,128)S(1)} fusion(bf16[128,24576]{1,0:T(8,128)(2,1)} %shard_map.85, bf16[1,128,24576]{2,1,0:T(8,128)(2,1)} %param.6, pred[128]{0:T(512)(128)(4,1)S(1)} %iota_compare_fusion), kind=kOutput, calls=%fused_computation.10 | convolution fusion | flops 808452096 | bytes 12648576 | tf_op jit(solution)/shard_map/dot_general | solution.py:133
  140.6 1.6 collective-permute-start.8
  143.7 2.1 collective-permute-done.8
  145.8 2.4 %collective-permute-done.9 = f32[128,128]{1,0:T(8,128)S(1)} collective-permute-done((f32[128,128]{1,0:T(8,128)S(1)}, f32[128,128]{1,0:T(8,128)S(1)}, u32[]{:S(2)}, u32[]{:S(2)}) %collective-permute-start.9) | collective-permute-done | bytes 65568 | tf_op jit(solution)/shard_map/ppermute | solution.py:120
  150.4 5.3 %fusion.x_hbm = bf16[128,24576]{1,0:T(8,128)(2,1)S(1)} fusion(bf16[1,128,24576]{2,1,0:T(8,128)(2,1)} %param.6, pred[128]{0:T(512)(128)(4,1)S(1)} %iota_compare_fusion, f32[4,128,128]{2,1,0:T(8,128)S(1)} %broadcast_select_fusion.3, bf16[32,24576]{1,0:T(8,128)(2,1)} %copy-done.4, bf16[32,24576]{1,0:T(8,128)(2,1)} %collective-permute-done.1, ...), kind=kOutput, calls=%fused_computation.5 | convolution fusion | flops 843137024 | bytes 19136640 | tf_op jit(solution)/shard_map/dot_general | solution.py:179
  155.7 1.9 collective-permute-start.11
  157.7 3.9 %collective-permute-start.12 = (bf16[128,256]{1,0:T(8,128)(2,1)S(1)}, bf16[128,256]{1,0:T(8,128)(2,1)S(1)}, u32[]{:S(2)}, u32[]{:S(2)}) collective-permute-start(bf16[128,256]{1,0:T(8,128)(2,1)S(1)} %get-tuple-element.19), channel_id=1, source_target_pairs={{1,0},{2,1},{3,2},{5,4},{6,5},{7,6},{9,8},{10,9},{11,10},{13,12},{... | collective-permute-start | bytes 196616 | tf_op jit(solution)/shard_map/ppermute | solution.py:28
  161.9 2.3 collective-permute-done.12.hi_ref
  164.8 32.4 %shard_map.86 = (bf16[128,24576]{1,0:T(8,128)(2,1)}, bf16[128,24576]{1,0:T(8,128)(2,1)}) custom-call(s32[768]{0:T(1024)} %reshape.121.shift_ref, bf16[128,24576]{1,0:T(8,128)(2,1)} %copy-done, bf16[128,256]{1,0:T(8,128)(2,1)} %copy-done.8, bf16[128,256]{1,0:T(8,128)(2,1)} %copy-done.10, bf16[256,96,288]{2,1,0:T(8,128)(2,1)} %copy.12.refs_0_, ...), custom_call_target="tpu_custom_call" | custom-call | tf_op jit(solution)/shard_map/pallas_call | solution.py:106
  197.2 6.5 %convolution_bitcast_fusion.1 = f32[1,128,128]{2,1,0:T(8,128)S(1)} fusion(bf16[128,24576]{1,0:T(8,128)(2,1)} %copy-done, bf16[128,24576]{1,0:T(8,128)(2,1)} %get-tuple-element.18), kind=kOutput, calls=%fused_computation.16 | convolution fusion | flops 805306368 | bytes 12648448 | tf_op jit(solution)/shard_map/dot_general | solution.py:133
  203.8 1.6 copy-done.3
  205.4 1.8 convolution_bitcast_fusion
  207.3 2.2 collective-permute-start.13
  209.5 2.0 collective-permute-start.14
  211.5 5.8 %collective-permute-done.13 = f32[2,128,128]{2,1,0:T(8,128)S(1)} collective-permute-done((f32[2,128,128]{2,1,0:T(8,128)S(1)}, f32[2,128,128]{2,1,0:T(8,128)S(1)}, u32[]{:S(2)}, u32[]{:S(2)}) %collective-permute-start.13) | collective-permute-done | bytes 131104 | tf_op jit(solution)/shard_map/ppermute | solution.py:120
  218.8 2.3 collective-permute-done.15
  225.0 9.5 %fusion.1 = bf16[1,128,24576]{2,1,0:T(8,128)(2,1)} fusion(bf16[128,24576]{1,0:T(8,128)(2,1)} %get-tuple-element.18, bf16[128,24576]{1,0:T(8,128)(2,1)} %get-tuple-element.17, f32[128]{0:T(128)S(1)} %divide_select_fusion), kind=kLoop, calls=%fused_computation.7 | loop fusion | flops 15728640 | bytes 18874880 | tf_op jit(solution)/shard_map/broadcast_in_dim | solution.py:199
  (64 shorter events, 17.1 us)
Async XLA Ops:
  12.6 56.5 %collective-permute-start = (bf16[32,24576]{1,0:T(8,128)(2,1)}, bf16[32,24576]{1,0:T(8,128)(2,1)S(1)}, u32[]{:S(2)}, u32[]{:S(2)}) collective-permute-start(bf16[32,24576]{1,0:T(8,128)(2,1)} %get-tuple-element.24), channel_id=1, source_target_pairs={{0,4},{4,8},{8,12},{12,16},{16,20},{20,24},{24,28},{1,5},{5,9},{9,... | collective-permute-start | bytes 4718600 | tf_op jit(solution)/shard_map/ppermute | solution.py:19
  14.5 54.6 %collective-permute-start.1 = (bf16[32,24576]{1,0:T(8,128)(2,1)}, bf16[32,24576]{1,0:T(8,128)(2,1)}, u32[]{:S(2)}, u32[]{:S(2)}) collective-permute-start(bf16[32,24576]{1,0:T(8,128)(2,1)} %get-tuple-element.23), channel_id=1, source_target_pairs={{4,0},{8,4},{12,8},{16,12},{20,16},{24,20},{28,24},{5,1},{9,5},{13... | collective-permute-start | bytes 4718600 | tf_op jit(solution)/shard_map/ppermute | solution.py:19
  19.0 67.0 %collective-permute-start.2 = (bf16[32,24576]{1,0:T(8,128)(2,1)}, bf16[32,24576]{1,0:T(8,128)(2,1)}, u32[]{:S(2)}, u32[]{:S(2)}) collective-permute-start(bf16[32,24576]{1,0:T(8,128)(2,1)} %get-tuple-element.24), channel_id=1, source_target_pairs={{0,8},{8,16},{16,24},{1,9},{9,17},{17,25},{2,10},{10,18},{18,26},{... | collective-permute-start | bytes 4718600 | tf_op jit(solution)/shard_map/ppermute | solution.py:161
  21.5 64.5 %collective-permute-start.3 = (bf16[32,24576]{1,0:T(8,128)(2,1)}, bf16[32,24576]{1,0:T(8,128)(2,1)S(1)}, u32[]{:S(2)}, u32[]{:S(2)}) collective-permute-start(bf16[32,24576]{1,0:T(8,128)(2,1)} %get-tuple-element.23), channel_id=1, source_target_pairs={{12,4},{20,12},{28,20},{13,5},{21,13},{29,21},{14,6},{22,14},{30,2... | collective-permute-start | bytes 4718600 | tf_op jit(solution)/shard_map/ppermute | solution.py:162
  45.8 42.7 %copy-start.12 = (s32[256,3]{0,1:T(4,128)S(1)}, s32[256,3]{0,1:T(4,128)}, u32[]{:S(2)}) copy-start(s32[256,3]{0,1:T(4,128)} %param.11) | copy-start | bytes 9220
  69.1 21.7 %copy-start.5 = (bf16[32,24576]{1,0:T(8,128)(2,1)}, bf16[32,24576]{1,0:T(8,128)(2,1)S(1)}, u32[]{:S(2)}) copy-start(bf16[32,24576]{1,0:T(8,128)(2,1)S(1)} %collective-permute-done) | copy-start | bytes 4718596
  86.1 4.7 %copy-start.7 = (bf16[32,24576]{1,0:T(8,128)(2,1)}, bf16[32,24576]{1,0:T(8,128)(2,1)S(1)}, u32[]{:S(2)}) copy-start(bf16[32,24576]{1,0:T(8,128)(2,1)S(1)} %collective-permute-done.3) | copy-start | bytes 4718596
  86.1 4.7 %collective-permute-start.4 = (bf16[32,24576]{1,0:T(8,128)(2,1)S(1)}, bf16[32,24576]{1,0:T(8,128)(2,1)}, u32[]{:S(2)}, u32[]{:S(2)}) collective-permute-start(bf16[32,24576]{1,0:T(8,128)(2,1)S(1)} %collective-permute-done), channel_id=1, source_target_pairs={{0,4},{8,12},{16,20},{24,28},{1,5},{9,13},{17,21},{25,29},{2,6},{1... | collective-permute-start | bytes 4718600 | tf_op jit(solution)/shard_map/ppermute | solution.py:170
  89.5 5.5 %collective-permute-start.5 = (bf16[32,24576]{1,0:T(8,128)(2,1)}, bf16[32,24576]{1,0:T(8,128)(2,1)S(1)}, u32[]{:S(2)}, u32[]{:S(2)}) collective-permute-start(bf16[32,24576]{1,0:T(8,128)(2,1)} %collective-permute-done.1), channel_id=1, source_target_pairs={{4,0},{12,8},{20,16},{28,24},{5,1},{13,9},{21,17},{29,25},{6,2},{1... | collective-permute-start | bytes 4718600 | tf_op jit(solution)/shard_map/ppermute | solution.py:172
  90.8 4.4 %copy-start.6 = (bf16[32,24576]{1,0:T(8,128)(2,1)S(1)}, bf16[32,24576]{1,0:T(8,128)(2,1)}, u32[]{:S(2)}) copy-start(bf16[32,24576]{1,0:T(8,128)(2,1)} %copy-done.5) | copy-start | bytes 4718596
  95.2 3.0 %copy-start.4 = (bf16[32,24576]{1,0:T(8,128)(2,1)}, bf16[32,24576]{1,0:T(8,128)(2,1)S(1)}, u32[]{:S(2)}) copy-start(bf16[32,24576]{1,0:T(8,128)(2,1)S(1)} %broadcast_select_fusion) | copy-start | bytes 4718596
  98.2 10.1 %copy-start.2 = (bf16[128,24576]{1,0:T(8,128)(2,1)}, bf16[128,24576]{1,0:T(8,128)(2,1)S(1)}, u32[]{:S(2)}) copy-start(bf16[128,24576]{1,0:T(8,128)(2,1)S(1)} %pad_maximum_fusion.x_hbm) | copy-start | bytes 18874372
  98.2 6.3 %collective-permute-start.6 = (bf16[128,256]{1,0:T(8,128)(2,1)S(1)}, bf16[128,256]{1,0:T(8,128)(2,1)S(1)}, u32[]{:S(2)}, u32[]{:S(2)}) collective-permute-start(bf16[128,256]{1,0:T(8,128)(2,1)S(1)} %get-tuple-element.22), channel_id=1, source_target_pairs={{0,1},{1,2},{2,3},{4,5},{5,6},{6,7},{8,9},{9,10},{10,11},{12,13},{... | collective-permute-start | bytes 196616 | tf_op jit(solution)/shard_map/ppermute | solution.py:27
  101.7 6.6 %collective-permute-start.7 = (bf16[128,256]{1,0:T(8,128)(2,1)S(1)}, bf16[128,256]{1,0:T(8,128)(2,1)S(1)}, u32[]{:S(2)}, u32[]{:S(2)}) collective-permute-start(bf16[128,256]{1,0:T(8,128)(2,1)S(1)} %get-tuple-element.21), channel_id=1, source_target_pairs={{1,0},{2,1},{3,2},{5,4},{6,5},{7,6},{9,8},{10,9},{11,10},{13,12},{... | collective-permute-start | bytes 196616 | tf_op jit(solution)/shard_map/ppermute | solution.py:28
  104.6 3.7 %copy-start.9 = (bf16[128,256]{1,0:T(8,128)(2,1)}, bf16[128,256]{1,0:T(8,128)(2,1)S(1)}, u32[]{:S(2)}) copy-start(bf16[128,256]{1,0:T(8,128)(2,1)S(1)} %collective-permute-done.6.lo_ref) | copy-start | bytes 196612
  108.3 0.6 copy-start.11
  140.6 5.2 %collective-permute-start.8 = (f32[128,128]{1,0:T(8,128)S(1)}, f32[128,128]{1,0:T(8,128)S(1)}, u32[]{:S(2)}, u32[]{:S(2)}) collective-permute-start(f32[128,128]{1,0:T(8,128)S(1)} %fusion.2), channel_id=1, source_target_pairs={{0,1},{1,2},{2,3},{3,0},{4,5},{5,6},{6,7},{7,4},{8,9},{9,10},{10,1... | collective-permute-start | bytes 196616 | tf_op jit(solution)/shard_map/ppermute | solution.py:120
  142.1 6.0 %collective-permute-start.9 = (f32[128,128]{1,0:T(8,128)S(1)}, f32[128,128]{1,0:T(8,128)S(1)}, u32[]{:S(2)}, u32[]{:S(2)}) collective-permute-start(f32[128,128]{1,0:T(8,128)S(1)} %fusion.2), channel_id=1, source_target_pairs={{0,2},{1,3},{2,0},{3,1},{4,6},{5,7},{6,4},{7,5},{8,10},{9,11},{10,... | collective-permute-start | bytes 196616 | tf_op jit(solution)/shard_map/ppermute | solution.py:120
  143.4 6.3 %collective-permute-start.10 = (f32[128,128]{1,0:T(8,128)S(1)}, f32[128,128]{1,0:T(8,128)S(1)}, u32[]{:S(2)}, u32[]{:S(2)}) collective-permute-start(f32[128,128]{1,0:T(8,128)S(1)} %fusion.2), channel_id=1, source_target_pairs={{0,3},{1,0},{2,1},{3,2},{4,7},{5,4},{6,5},{7,6},{8,11},{9,8},{10,9... | collective-permute-start | bytes 196616 | tf_op jit(solution)/shard_map/ppermute | solution.py:120
  155.7 8.5 %copy-start = (bf16[128,24576]{1,0:T(8,128)(2,1)}, bf16[128,24576]{1,0:T(8,128)(2,1)S(1)}, u32[]{:S(2)}) copy-start(bf16[128,24576]{1,0:T(8,128)(2,1)S(1)} %fusion.x_hbm) | copy-start | bytes 18874372
  155.7 6.2 %collective-permute-start.11 = (bf16[128,256]{1,0:T(8,128)(2,1)S(1)}, bf16[128,256]{1,0:T(8,128)(2,1)S(1)}, u32[]{:S(2)}, u32[]{:S(2)}) collective-permute-start(bf16[128,256]{1,0:T(8,128)(2,1)S(1)} %get-tuple-element.20), channel_id=1, source_target_pairs={{0,1},{1,2},{2,3},{4,5},{5,6},{6,7},{8,9},{9,10},{10,11},{12,13},{... | collective-permute-start | bytes 196616 | tf_op jit(solution)/shard_map/ppermute | solution.py:27
  157.7 6.5 %collective-permute-start.12 = (bf16[128,256]{1,0:T(8,128)(2,1)S(1)}, bf16[128,256]{1,0:T(8,128)(2,1)S(1)}, u32[]{:S(2)}, u32[]{:S(2)}) collective-permute-start(bf16[128,256]{1,0:T(8,128)(2,1)S(1)} %get-tuple-element.19), channel_id=1, source_target_pairs={{1,0},{2,1},{3,2},{5,4},{6,5},{7,6},{9,8},{10,9},{11,10},{13,12},{... | collective-permute-start | bytes 196616 | tf_op jit(solution)/shard_map/ppermute | solution.py:28
  161.9 2.3 copy-start.8
  164.2 0.6 copy-start.10
  197.2 6.6 %copy-start.1 = (bf16[128,24576]{1,0:T(8,128)(2,1)S(1)}, bf16[128,24576]{1,0:T(8,128)(2,1)}, u32[]{:S(2)}) copy-start(bf16[128,24576]{1,0:T(8,128)(2,1)} %copy-done) | copy-start | bytes 18874372
  197.2 8.2 %copy-start.3 = (bf16[128,24576]{1,0:T(8,128)(2,1)S(1)}, bf16[128,24576]{1,0:T(8,128)(2,1)}, u32[]{:S(2)}) copy-start(bf16[128,24576]{1,0:T(8,128)(2,1)} %get-tuple-element.17) | copy-start | bytes 18874372
  207.3 10.1 %collective-permute-start.13 = (f32[2,128,128]{2,1,0:T(8,128)S(1)}, f32[2,128,128]{2,1,0:T(8,128)S(1)}, u32[]{:S(2)}, u32[]{:S(2)}) collective-permute-start(f32[2,128,128]{2,1,0:T(8,128)S(1)} %get-tuple-element.30), channel_id=1, source_target_pairs={{0,1},{1,2},{2,3},{3,0},{4,5},{5,6},{6,7},{7,4},{8,9},{9,10},{10,1... | collective-permute-start | bytes 393224 | tf_op jit(solution)/shard_map/ppermute | solution.py:120
  209.5 9.2 %collective-permute-start.14 = (f32[2,128,128]{2,1,0:T(8,128)S(1)}, f32[2,128,128]{2,1,0:T(8,128)S(1)}, u32[]{:S(2)}, u32[]{:S(2)}) collective-permute-start(f32[2,128,128]{2,1,0:T(8,128)S(1)} %get-tuple-element.30), channel_id=1, source_target_pairs={{0,2},{1,3},{2,0},{3,1},{4,6},{5,7},{6,4},{7,5},{8,10},{9,11},{10,... | collective-permute-start | bytes 393224 | tf_op jit(solution)/shard_map/ppermute | solution.py:120
  211.5 9.6 %collective-permute-start.15 = (f32[2,128,128]{2,1,0:T(8,128)S(1)}, f32[2,128,128]{2,1,0:T(8,128)S(1)}, u32[]{:S(2)}, u32[]{:S(2)}) collective-permute-start(f32[2,128,128]{2,1,0:T(8,128)S(1)} %get-tuple-element.30), channel_id=1, source_target_pairs={{0,3},{1,0},{2,1},{3,2},{4,7},{5,4},{6,5},{7,6},{8,11},{9,8},{10,9... | collective-permute-start | bytes 393224 | tf_op jit(solution)/shard_map/ppermute | solution.py:120

commit v5 on v4

--- a/solution.py
+++ b/solution.py
@@ -30,18 +30,30 @@
 
 
 def flip(tile):
-    return tile.astype(jnp.float32).T.astype(jnp.bfloat16)
-
-
-def apply_kernel(shift_ref, x_hbm, lo_ref, hi_ref, *refs, group, blk, nmat, chunk):
+    return tile.T
+
+
+def nt(a, b):
+    return lax.dot_general(a, b, (((1,), (1,)), ((), ())), preferred_element_type=jnp.float32)
+
+
+def apply_kernel(shift_ref, count_ref, x_hbm, lo_ref, hi_ref, *refs, group, blk, nmat, chunk, keep, given):
     mats = refs[:nmat]
-    outs = refs[nmat : 2 * nmat]
-    accs = refs[2 * nmat : 3 * nmat]
-    xbuf, xpad, sem = refs[3 * nmat :]
+    at = nmat
+    pair_ref = None
+    if given:
+        pair_ref = refs[at]
+        at += 1
+    outs = refs[at : at + nmat] if keep else ()
+    at += nmat if keep else 0
+    dots_ref = refs[at]
+    accs = refs[at + 1 : at + 1 + nmat]
+    xbuf, xpad, sem = refs[at + 1 + nmat :]
     g = pl.program_id(0)
-    entries = x_hbm.shape[1]
+    slots, entries = x_hbm.shape
     halo = HALO * blk
     rim = lo_ref.shape[1]
+    span = group * blk
 
     @pl.when(g == 0)
     def _():
@@ -49,6 +61,7 @@
         copy.start()
         xpad[pl.ds(0, halo), :] = flip(lo_ref[...])[rim - halo :]
         xpad[pl.ds(halo + entries, halo), :] = flip(hi_ref[...])[:halo]
+        dots_ref[...] = jnp.zeros(dots_ref.shape, dots_ref.dtype)
         copy.wait()
 
         def turn(c, carry):
@@ -73,29 +86,54 @@
             accs[m][pl.ds(pl.multiple_of(j * blk, 16), blk), :] = part.astype(accs[m].dtype)
         return carry
 
-    lax.fori_loop(0, group, body, 0, unroll=8)
-    for m in range(nmat):
-        for c in range(group * blk // chunk):
-            outs[m][:, pl.ds(c * chunk, chunk)] = flip(accs[m][pl.ds(c * chunk, chunk), :])
-
-
-def block_apply(matrices, shifts_flat, cells):
+    lax.fori_loop(0, group, body, 0, unroll=16)
+    live = lax.broadcasted_iota(jnp.int32, (slots, chunk), 0) < count_ref[0]
+    for c in range(span // chunk):
+        if given:
+            other = jnp.where(live, pair_ref[:, pl.ds(c * chunk, chunk)], jnp.zeros((), pair_ref.dtype))
+        else:
+            other = xbuf[:, pl.ds(pl.multiple_of(g * span + c * chunk, chunk), chunk)]
+        for m in range(nmat):
+            native = flip(accs[m][pl.ds(c * chunk, chunk), :])
+            if keep:
+                outs[m][:, pl.ds(c * chunk, chunk)] = native
+            if given:
+                dots_ref[m] += nt(native, other)
+            else:
+                dots_ref[m] += nt(other, native)
+
+
+def block_apply(matrices, shifts_flat, count, cells, pair=None):
     slots, entries = cells.shape
     block_rows, blk, width = matrices[0].shape
     rim = 256
     lower, upper = row_halos(cells, rim)
-    group = 32 if block_rows % 32 == 0 else block_rows
+    group = 64 if block_rows % 64 == 0 else block_rows
     chunk = 512
     nmat = len(matrices)
-    kernel = functools.partial(apply_kernel, group=group, blk=blk, nmat=nmat, chunk=chunk)
-    mat_spec = pl.BlockSpec((group, blk, width), lambda g, s: (g, 0, 0))
-    out_spec = pl.BlockSpec((slots, group * blk), lambda g, s: (0, g))
-    halo_spec = pl.BlockSpec((slots, rim), lambda g, s: (0, 0))
+    given = pair is not None
+    keep = not given
+    kernel = functools.partial(
+        apply_kernel, group=group, blk=blk, nmat=nmat, chunk=chunk, keep=keep, given=given
+    )
+    mat_spec = pl.BlockSpec((group, blk, width), lambda g, s, n: (g, 0, 0))
+    out_spec = pl.BlockSpec((slots, group * blk), lambda g, s, n: (0, g))
+    halo_spec = pl.BlockSpec((slots, rim), lambda g, s, n: (0, 0))
+    dots_spec = pl.BlockSpec((nmat, slots, slots), lambda g, s, n: (0, 0, 0))
+    in_specs = [pl.BlockSpec(memory_space=pl.ANY), halo_spec, halo_spec] + [mat_spec] * nmat
+    operands = [shifts_flat, count, cells, lower, upper, *matrices]
+    if given:
+        in_specs.append(out_spec)
+        operands.append(pair)
+    out_specs = ([out_spec] * nmat if keep else []) + [dots_spec]
+    out_shape = ([jax.ShapeDtypeStruct((slots, entries), jnp.bfloat16)] * nmat if keep else []) + [
+        jax.ShapeDtypeStruct((nmat, slots, slots), jnp.float32)
+    ]
     grid_spec = pltpu.PrefetchScalarGridSpec(
-        num_scalar_prefetch=1,
+        num_scalar_prefetch=2,
         grid=(block_rows // group,),
-        in_specs=[pl.BlockSpec(memory_space=pl.ANY), halo_spec, halo_spec] + [mat_spec] * nmat,
-        out_specs=[out_spec] * nmat,
+        in_specs=in_specs,
+        out_specs=out_specs,
         scratch_shapes=[pltpu.VMEM((group * blk, slots), jnp.bfloat16)] * nmat
         + [
             pltpu.VMEM((slots, entries), cells.dtype),
@@ -106,31 +144,31 @@
     return pl.pallas_call(
         kernel,
         grid_spec=grid_spec,
-        out_shape=[jax.ShapeDtypeStruct((slots, entries), jnp.bfloat16)] * nmat,
+        out_shape=out_shape,
         compiler_params=pltpu.CompilerParams(
             dimension_semantics=("arbitrary",), vmem_limit_bytes=56 * 1024 * 1024
         ),
-    )(shifts_flat, cells, lower, upper, *matrices)
+    )(*operands)
 
 
 def row_sum(part):
     count = lax.axis_size("row")
-    here = lax.axis_index("row")
-    got = [part] + [
-        lax.ppermute(part, "row", [(i, (i + step) % count) for i in range(count)])
-        for step in range(1, count)
-    ]
-    stacked = jnp.stack(got)
-    order = (here - jnp.arange(count, dtype=jnp.int32)) % count
-    by_source = jnp.take(stacked, order, axis=0)
-    total = by_source[0]
-    for r in range(1, count):
-        total = total + by_source[r]
-    return total
-
-
-def nt_dot(a, b):
-    return lax.dot_general(a, b, (((1,), (1,)), ((), ())), preferred_element_type=jnp.float32)
+    if count & (count - 1):
+        here = lax.axis_index("row")
+        got = [part] + [
+            lax.ppermute(part, "row", [(i, (i + step) % count) for i in range(count)])
+            for step in range(1, count)
+        ]
+        by_source = jnp.take(jnp.stack(got), (here - jnp.arange(count, dtype=jnp.int32)) % count, axis=0)
+        total = by_source[0]
+        for r in range(1, count):
+            total = total + by_source[r]
+        return total
+    step = 1
+    while step < count:
+        part = part + lax.ppermute(part, "row", [(i, i ^ step) for i in range(count)])
+        step *= 2
+    return part
 
 
 def shards(vectors, counts, offsets, margin_blocks, energy_blocks, block_columns):
@@ -171,21 +209,21 @@
     )
     lower_2 = jnp.where(odd, lower_direct, lax.ppermute(lower_1, "cuts", [(i, i - 1) for i in odds]))
     received = [upper_2, upper_1, lower_1, lower_2]
-    masked = jnp.where(valid_mask[:, None], own_vectors, jnp.zeros((), own_vectors.dtype))
     windows = jnp.concatenate(received, axis=0)
-    (margin_windows,) = block_apply((margin_blocks,), shifts_flat, windows)
-    partial_margin = nt_dot(margin_windows, masked)
-    margin = row_sum(partial_margin) / nmat_total
+    count = counts[:1]
+    (margin_dots,) = block_apply((margin_blocks,), shifts_flat, count, windows, pair=own_vectors)
+    margin = row_sum(margin_dots[0]) / nmat_total
     removed = lax.dot_general(
         margin.astype(jnp.bfloat16), windows, (((0,), (0,)), ((), ())), preferred_element_type=jnp.float32
     )
+    masked = jnp.where(valid_mask[:, None], own_vectors, jnp.zeros((), own_vectors.dtype))
     cleaned = (masked.astype(jnp.float32) - removed).astype(jnp.bfloat16)
-    margin_cleaned, energy_cleaned = block_apply((margin_blocks, energy_blocks), shifts_flat, cleaned)
-    margin_part = nt_dot(cleaned, margin_cleaned)
-    energy_part = nt_dot(cleaned, energy_cleaned)
-    margin_total, energy_total = row_sum(jnp.stack([margin_part, energy_part]))
-    margin_pencil = margin_total / nmat_total
-    energy_pencil = energy_total / nmat_total
+    margin_cleaned, energy_cleaned, pencil_dots = block_apply(
+        (margin_blocks, energy_blocks), shifts_flat, count, cleaned
+    )
+    pencils = row_sum(pencil_dots) / nmat_total
+    margin_pencil = pencils[0]
+    energy_pencil = pencils[1]
     margin_diag = jnp.diagonal(margin_pencil)
     energy_diag = jnp.diagonal(energy_pencil)
     theta = jnp.where(

time: 236 us -> 223 us (0.945)
  matrix products: 20.1 us -> 3.98 us
  starting transfers between devices: 32.5 us -> 28.5 us
  waiting for transfers between devices: 41.7 us -> 45.1 us
  local copies, waits for them, and re-layouts: 55.6 us -> 58.3 us
    dot_general x3 -> x0, matrix products: 14.8 us -> none  [nt_dot(): lax.dot_general(a, b, (((1,), (1,)), ((), ())), preferred_element_type=jn...]
    ppermute x6 -> x4, starting transfers between devices: 7.37 us -> 2.29 us  [row_sum(): lax.ppermute(part, 'row', [(i, i ^ step) for i in range(count)])]
    ppermute x6 -> x4, waiting for transfers between devices: 15.5 us -> 19.8 us  [row_sum(): lax.ppermute(part, 'row', [(i, i ^ step) for i in range(count)])]
    unnamed x28 -> x32, local copies, waits for them, and re-layouts: 49.7 us -> 53.5 us
  transfers between devices with their start and end apart: 16 -> 14, of which waited for: 12 -> 10; matrix products, arithmetic and copies ran while one was open for 21% -> 22% of each run, Pallas kernels for 0% -> 0%
where the time goes in v5:
time: 223 us; the launch traced here: 220 us
  local copies, waits for them, and re-layouts  58.3 us (26%)
  Pallas kernels  55.8 us (25%)
  waiting for transfers between devices  45.1 us (20%)
  starting transfers between devices  28.5 us (13%)
  other arithmetic  22.6 us (10%)
  between operations  5.46 us (2%)
  matrix products  3.98 us (2%)
    pallas_call x2, Pallas kernels, block_apply(): pl.pallas_call(kernel, grid_spec=grid_spec, out_shape=out_shape, compiler...  55.8 us
    unnamed x32, local copies, waits for them, and re-layouts  53.5 us
    ppermute x4, waiting for transfers between devices, row_sum(): lax.ppermute(part, 'row', [(i, i ^ step) for i in range(count)])  19.8 us
    ppermute x1, waiting for transfers between devices, shards(): lax.ppermute(upper_window, 'cuts', [(i, i + 2) for i in evens if i + 2 <...  15.9 us
    broadcast_in_dim x1, other arithmetic, shards(): return (residual[None], margin_pencil[None], energy_pencil[None])  9.47 us
    ppermute x2, starting transfers between devices, row_halos(): lower = lax.ppermute(tail, 'row', [(i, i + 1) for i in range(ends)])  6.96 us
    ppermute x2, waiting for transfers between devices, row_halos(): upper = lax.ppermute(head, 'row', [(i + 1, i) for i in range(ends)])  6.71 us
    ppermute x2, starting transfers between devices, from_behind(): return lax.ppermute(block, axis, route)  6.45 us
  transfers between devices with their start and end apart: 14, of which 10 were waited for; matrix products, arithmetic and copies ran while one was open for 22% of the time, Pallas kernels for 0%

profile of v5, /device:TPU:12, one launch (start us, length us, event | category | flops | bytes accessed | tf_op | source)
XLA Modules:
  0.0 219.7 jit_solution(15867841881192277028)
XLA Ops:
  0.6 1.3 fusion.7
  5.2 1.3 add_compare_fusion
  7.8 4.8 %bitcast_select_fusion = (bf16[32,24576]{1,0:T(8,128)(2,1)}, bf16[32,24576]{1,0:T(8,128)(2,1)}) fusion(bf16[1,128,24576]{2,1,0:T(8,128)(2,1)} %param.6, s32[]{:T(128)S(6)} %select_n.62, pred[32]{0:T(512)(128)(4,1)S(1)} %get-tuple-element.31, s32[]{:T(128)S(6)} %select_n.60, pred[32]{0:T(512)(128)(4,1)S(1)} %get-tuple-element.32), kind=kLoop, calls=%fused_computation.7 | loop fusion | flops 1572864 | bytes 6291528 | tf_op jit(solution)/shard_map/jit(_where)/select_n | solution.py:181
  12.6 1.9 collective-permute-start
  14.5 4.5 %collective-permute-start.1 = (bf16[32,24576]{1,0:T(8,128)(2,1)}, bf16[32,24576]{1,0:T(8,128)(2,1)S(1)}, u32[]{:S(2)}, u32[]{:S(2)}) collective-permute-start(bf16[32,24576]{1,0:T(8,128)(2,1)} %get-tuple-element.25), channel_id=1, source_target_pairs={{4,0},{8,4},{12,8},{16,12},{20,16},{24,20},{28,24},{5,1},{9,5},{13... | collective-permute-start | bytes 4718600 | tf_op jit(solution)/shard_map/ppermute | solution.py:19
  19.0 2.5 %collective-permute-start.2 = (bf16[32,24576]{1,0:T(8,128)(2,1)}, bf16[32,24576]{1,0:T(8,128)(2,1)}, u32[]{:S(2)}, u32[]{:S(2)}) collective-permute-start(bf16[32,24576]{1,0:T(8,128)(2,1)} %get-tuple-element.26), channel_id=1, source_target_pairs={{0,8},{8,16},{16,24},{1,9},{9,17},{17,25},{2,10},{10,18},{18,26},{... | collective-permute-start | bytes 4718600 | tf_op jit(solution)/shard_map/ppermute | solution.py:199
  21.5 1.8 collective-permute-start.3
  23.4 23.4 %copy.12.refs_0_ = bf16[256,96,288]{2,1,0:T(8,128)(2,1)} copy(bf16[256,96,288]{0,2,1:T(8,128)(2,1)} %param.9) | data formatting | bytes 28311552 | tf_op args[3]
  46.8 23.4 %copy.13.refs_1_ = bf16[256,96,288]{2,1,0:T(8,128)(2,1)} copy(bf16[256,96,288]{0,2,1:T(8,128)(2,1)} %param.10) | data formatting | bytes 28311552 | tf_op args[4]
  70.2 15.9 %collective-permute-done.2 = bf16[32,24576]{1,0:T(8,128)(2,1)} collective-permute-done((bf16[32,24576]{1,0:T(8,128)(2,1)}, bf16[32,24576]{1,0:T(8,128)(2,1)}, u32[]{:S(2)}, u32[]{:S(2)}) %collective-permute-start.2) | collective-permute-done | bytes 1572896 | tf_op jit(solution)/shard_map/ppermute | solution.py:199
  86.1 2.4 %collective-permute-start.4 = (bf16[32,24576]{1,0:T(8,128)(2,1)S(1)}, bf16[32,24576]{1,0:T(8,128)(2,1)}, u32[]{:S(2)}, u32[]{:S(2)}) collective-permute-start(bf16[32,24576]{1,0:T(8,128)(2,1)S(1)} %collective-permute-done), channel_id=1, source_target_pairs={{0,4},{8,12},{16,20},{24,28},{1,5},{9,13},{17,21},{25,29},{2,6},{1... | collective-permute-start | bytes 4718600 | tf_op jit(solution)/shard_map/ppermute | solution.py:208
  88.5 1.3 collective-permute-start.5
  90.5 1.6 broadcast_select_fusion.1
  92.1 1.7 collective-permute-done.5
  94.1 3.5 %pad_maximum_fusion.x_hbm = bf16[128,24576]{1,0:T(8,128)(2,1)S(1)} fusion(bf16[32,24576]{1,0:T(8,128)(2,1)S(1)} %broadcast_select_fusion, bf16[32,24576]{1,0:T(8,128)(2,1)} %copy-done.7, bf16[32,24576]{1,0:T(8,128)(2,1)} %copy-done.6, bf16[32,24576]{1,0:T(8,128)(2,1)S(1)} %broadcast_select_fusion.1), kind=kLoop, calls=%fused_computation.6 | loop fusion | flops 25165824 | bytes 12582912 | tf_op jit(solution)/shard_map/concatenate | solution.py:212
  97.6 2.7 %copy-done = bf16[128,24576]{1,0:T(8,128)(2,1)} copy-done((bf16[128,24576]{1,0:T(8,128)(2,1)}, bf16[128,24576]{1,0:T(8,128)(2,1)S(1)}, u32[]{:S(2)}) %copy-start) | copy-done | bytes 6291480
  100.3 3.5 %collective-permute-start.6 = (bf16[128,256]{1,0:T(8,128)(2,1)S(1)}, bf16[128,256]{1,0:T(8,128)(2,1)S(1)}, u32[]{:S(2)}, u32[]{:S(2)}) collective-permute-start(bf16[128,256]{1,0:T(8,128)(2,1)S(1)} %get-tuple-element.24), channel_id=1, source_target_pairs={{0,1},{1,2},{2,3},{4,5},{5,6},{6,7},{8,9},{9,10},{10,11},{12,13},{... | collective-permute-start | bytes 196616 | tf_op jit(solution)/shard_map/ppermute | solution.py:27
  103.8 2.4 %collective-permute-start.7 = (bf16[128,256]{1,0:T(8,128)(2,1)S(1)}, bf16[128,256]{1,0:T(8,128)(2,1)S(1)}, u32[]{:S(2)}, u32[]{:S(2)}) collective-permute-start(bf16[128,256]{1,0:T(8,128)(2,1)S(1)} %get-tuple-element.23), channel_id=1, source_target_pairs={{1,0},{2,1},{3,2},{5,4},{6,5},{7,6},{9,8},{10,9},{11,10},{13,12},{... | collective-permute-start | bytes 196616 | tf_op jit(solution)/shard_map/ppermute | solution.py:28
  107.1 3.2 %collective-permute-done.7.hi_ref = bf16[128,256]{1,0:T(8,128)(2,1)S(1)} collective-permute-done((bf16[128,256]{1,0:T(8,128)(2,1)S(1)}, bf16[128,256]{1,0:T(8,128)(2,1)S(1)}, u32[]{:S(2)}, u32[]{:S(2)}) %collective-permute-start.7) | collective-permute-done | bytes 65568 | tf_op jit(solution)/shard_map/ppermute | solution.py:28
  111.0 23.5 %shard_map.85 = f32[1,128,128]{2,1,0:T(8,128)} custom-call(s32[768]{0:T(1024)} %reshape.42.shift_ref, s32[1]{0:T(128)} %copy.14.count_ref, bf16[128,24576]{1,0:T(8,128)(2,1)} %copy-done, bf16[128,256]{1,0:T(8,128)(2,1)} %copy-done.8, bf16[128,256]{1,0:T(8,128)(2,1)} %copy-done.10, bf16[256,96,288]{2,1,0:T(8,128)(2,1)} %copy.12.refs_0_, ...), custom_call_target="tpu_custom_call" | custom-call | tf_op jit(solution)/shard_map/pallas_call | solution.py:144
  134.9 4.0 %collective-permute-done.8 = f32[128,128]{1,0:T(8,128)S(1)} collective-permute-done((f32[128,128]{1,0:T(8,128)}, f32[128,128]{1,0:T(8,128)S(1)}, u32[]{:S(2)}, u32[]{:S(2)}) %collective-permute-start.8) | collective-permute-done | bytes 65568 | tf_op jit(solution)/shard_map/ppermute | solution.py:169
  141.0 4.0 %collective-permute-done.9 = f32[128,128]{1,0:T(8,128)S(1)} collective-permute-done((f32[128,128]{1,0:T(8,128)S(1)}, f32[128,128]{1,0:T(8,128)S(1)}, u32[]{:S(2)}, u32[]{:S(2)}) %collective-permute-start.9) | collective-permute-done | bytes 65568 | tf_op jit(solution)/shard_map/ppermute | solution.py:169
  145.1 4.0 %fusion.x_hbm = bf16[128,24576]{1,0:T(8,128)(2,1)S(1)} fusion(pred[128]{0:T(512)(128)(4,1)S(1)} %iota_compare_fusion, f32[128,128]{1,0:T(8,128)S(1)} %bitcast_add_fusion, f32[128,128]{1,0:T(8,128)S(1)} %collective-permute-done.9, bf16[1,128,24576]{2,1,0:T(8,128)(2,1)S(1)} %bitcast.22, bf16[32,24576]{1,0:T(8,128)(2,1)} %copy-done.3, ...), kind=kOutput, calls=%fused_computation.3 | convolution fusion | flops 843104256 | bytes 19005568 | tf_op jit(solution)/shard_map/dot_general | solution.py:216
  149.1 2.7 %copy-done.1 = bf16[128,24576]{1,0:T(8,128)(2,1)} copy-done((bf16[128,24576]{1,0:T(8,128)(2,1)}, bf16[128,24576]{1,0:T(8,128)(2,1)S(1)}, u32[]{:S(2)}) %copy-start.1) | copy-done | bytes 6291480
  151.8 3.5 %collective-permute-start.10 = (bf16[128,256]{1,0:T(8,128)(2,1)S(1)}, bf16[128,256]{1,0:T(8,128)(2,1)S(1)}, u32[]{:S(2)}, u32[]{:S(2)}) collective-permute-start(bf16[128,256]{1,0:T(8,128)(2,1)S(1)} %get-tuple-element.22), channel_id=1, source_target_pairs={{0,1},{1,2},{2,3},{4,5},{5,6},{6,7},{8,9},{9,10},{10,11},{12,13},{... | collective-permute-start | bytes 196616 | tf_op jit(solution)/shard_map/ppermute | solution.py:27
  155.2 2.4 %collective-permute-start.11 = (bf16[128,256]{1,0:T(8,128)(2,1)S(1)}, bf16[128,256]{1,0:T(8,128)(2,1)S(1)}, u32[]{:S(2)}, u32[]{:S(2)}) collective-permute-start(bf16[128,256]{1,0:T(8,128)(2,1)S(1)} %get-tuple-element.21), channel_id=1, source_target_pairs={{1,0},{2,1},{3,2},{5,4},{6,5},{7,6},{9,8},{10,9},{11,10},{13,12},{... | collective-permute-start | bytes 196616 | tf_op jit(solution)/shard_map/ppermute | solution.py:28
  157.9 3.5 %collective-permute-done.11.hi_ref = bf16[128,256]{1,0:T(8,128)(2,1)S(1)} collective-permute-done((bf16[128,256]{1,0:T(8,128)(2,1)S(1)}, bf16[128,256]{1,0:T(8,128)(2,1)S(1)}, u32[]{:S(2)}, u32[]{:S(2)}) %collective-permute-start.11) | collective-permute-done | bytes 65568 | tf_op jit(solution)/shard_map/ppermute | solution.py:28
  162.0 32.4 %shard_map.86 = (bf16[128,24576]{1,0:T(8,128)(2,1)}, bf16[128,24576]{1,0:T(8,128)(2,1)}, f32[2,128,128]{2,1,0:T(8,128)}) custom-call(s32[768]{0:T(1024)} %reshape.42.shift_ref, s32[1]{0:T(128)} %copy.14.count_ref, bf16[128,24576]{1,0:T(8,128)(2,1)} %copy-done.1, bf16[128,256]{1,0:T(8,128)(2,1)} %copy-done.9, bf16[128,256]{1,0:T(8,128)(2,1)} %copy-done.11, ...), custom_call_target="tpu_custom_call" | custom-call | tf_op jit(solution)/shard_map/pallas_call | solution.py:144
  194.9 5.8 %collective-permute-done.12 = f32[2,128,128]{2,1,0:T(8,128)S(1)} collective-permute-done((f32[2,128,128]{2,1,0:T(8,128)}, f32[2,128,128]{2,1,0:T(8,128)S(1)}, u32[]{:S(2)}, u32[]{:S(2)}) %collective-permute-start.12) | collective-permute-done | bytes 131104 | tf_op jit(solution)/shard_map/ppermute | solution.py:169
  201.7 5.9 %collective-permute-done.13 = f32[2,128,128]{2,1,0:T(8,128)S(1)} collective-permute-done((f32[2,128,128]{2,1,0:T(8,128)S(1)}, f32[2,128,128]{2,1,0:T(8,128)S(1)}, u32[]{:S(2)}, u32[]{:S(2)}) %collective-permute-start.13) | collective-permute-done | bytes 131104 | tf_op jit(solution)/shard_map/ppermute | solution.py:169
  207.7 1.2 gather_fusion
  210.3 9.5 %fusion.1 = bf16[1,128,24576]{2,1,0:T(8,128)(2,1)} fusion(bf16[128,24576]{1,0:T(8,128)(2,1)} %get-tuple-element.20, bf16[128,24576]{1,0:T(8,128)(2,1)} %get-tuple-element.18, f32[128]{0:T(128)S(1)} %divide_select_fusion), kind=kLoop, calls=%fused_computation.5 | loop fusion | flops 15728640 | bytes 18874880 | tf_op jit(solution)/shard_map/broadcast_in_dim | solution.py:237
  (54 shorter events, 8.9 us)
Async XLA Ops:
  12.6 57.6 %collective-permute-start = (bf16[32,24576]{1,0:T(8,128)(2,1)}, bf16[32,24576]{1,0:T(8,128)(2,1)S(1)}, u32[]{:S(2)}, u32[]{:S(2)}) collective-permute-start(bf16[32,24576]{1,0:T(8,128)(2,1)} %get-tuple-element.26), channel_id=1, source_target_pairs={{0,4},{4,8},{8,12},{12,16},{16,20},{20,24},{24,28},{1,5},{5,9},{9,... | collective-permute-start | bytes 4718600 | tf_op jit(solution)/shard_map/ppermute | solution.py:19
  14.5 55.7 %collective-permute-start.1 = (bf16[32,24576]{1,0:T(8,128)(2,1)}, bf16[32,24576]{1,0:T(8,128)(2,1)S(1)}, u32[]{:S(2)}, u32[]{:S(2)}) collective-permute-start(bf16[32,24576]{1,0:T(8,128)(2,1)} %get-tuple-element.25), channel_id=1, source_target_pairs={{4,0},{8,4},{12,8},{16,12},{20,16},{24,20},{28,24},{5,1},{9,5},{13... | collective-permute-start | bytes 4718600 | tf_op jit(solution)/shard_map/ppermute | solution.py:19
  19.0 67.0 %collective-permute-start.2 = (bf16[32,24576]{1,0:T(8,128)(2,1)}, bf16[32,24576]{1,0:T(8,128)(2,1)}, u32[]{:S(2)}, u32[]{:S(2)}) collective-permute-start(bf16[32,24576]{1,0:T(8,128)(2,1)} %get-tuple-element.26), channel_id=1, source_target_pairs={{0,8},{8,16},{16,24},{1,9},{9,17},{17,25},{2,10},{10,18},{18,26},{... | collective-permute-start | bytes 4718600 | tf_op jit(solution)/shard_map/ppermute | solution.py:199
  21.5 64.5 %collective-permute-start.3 = (bf16[32,24576]{1,0:T(8,128)(2,1)}, bf16[32,24576]{1,0:T(8,128)(2,1)}, u32[]{:S(2)}, u32[]{:S(2)}) collective-permute-start(bf16[32,24576]{1,0:T(8,128)(2,1)} %get-tuple-element.25), channel_id=1, source_target_pairs={{12,4},{20,12},{28,20},{13,5},{21,13},{29,21},{14,6},{22,14},{30,2... | collective-permute-start | bytes 4718600 | tf_op jit(solution)/shard_map/ppermute | solution.py:200
  70.2 23.6 %copy-start.6 = (bf16[32,24576]{1,0:T(8,128)(2,1)}, bf16[32,24576]{1,0:T(8,128)(2,1)S(1)}, u32[]{:S(2)}) copy-start(bf16[32,24576]{1,0:T(8,128)(2,1)S(1)} %collective-permute-done) | copy-start | bytes 4718596
  70.2 23.6 %copy-start.7 = (bf16[32,24576]{1,0:T(8,128)(2,1)}, bf16[32,24576]{1,0:T(8,128)(2,1)S(1)}, u32[]{:S(2)}) copy-start(bf16[32,24576]{1,0:T(8,128)(2,1)S(1)} %collective-permute-done.1) | copy-start | bytes 4718596
  86.1 4.4 %collective-permute-start.4 = (bf16[32,24576]{1,0:T(8,128)(2,1)S(1)}, bf16[32,24576]{1,0:T(8,128)(2,1)}, u32[]{:S(2)}, u32[]{:S(2)}) collective-permute-start(bf16[32,24576]{1,0:T(8,128)(2,1)S(1)} %collective-permute-done), channel_id=1, source_target_pairs={{0,4},{8,12},{16,20},{24,28},{1,5},{9,13},{17,21},{25,29},{2,6},{1... | collective-permute-start | bytes 4718600 | tf_op jit(solution)/shard_map/ppermute | solution.py:208
  88.5 5.3 %collective-permute-start.5 = (bf16[32,24576]{1,0:T(8,128)(2,1)S(1)}, bf16[32,24576]{1,0:T(8,128)(2,1)S(1)}, u32[]{:S(2)}, u32[]{:S(2)}) collective-permute-start(bf16[32,24576]{1,0:T(8,128)(2,1)S(1)} %collective-permute-done.1), channel_id=1, source_target_pairs={{4,0},{12,8},{20,16},{28,24},{5,1},{13,9},{21,17},{29,25},{6,2},{1... | collective-permute-start | bytes 4718600 | tf_op jit(solution)/shard_map/ppermute | solution.py:210
  92.1 5.5 %copy-start.2 = (bf16[32,24576]{1,0:T(8,128)(2,1)}, bf16[32,24576]{1,0:T(8,128)(2,1)S(1)}, u32[]{:S(2)}) copy-start(bf16[32,24576]{1,0:T(8,128)(2,1)S(1)} %broadcast_select_fusion.1) | copy-start | bytes 4718596
  94.0 3.5 %copy-start.3 = (bf16[32,24576]{1,0:T(8,128)(2,1)}, bf16[32,24576]{1,0:T(8,128)(2,1)S(1)}, u32[]{:S(2)}) copy-start(bf16[32,24576]{1,0:T(8,128)(2,1)S(1)} %broadcast_select_fusion) | copy-start | bytes 4718596
  94.0 12.1 %copy-start.12 = (s32[256,3]{0,1:T(4,128)S(1)}, s32[256,3]{0,1:T(4,128)}, u32[]{:S(2)}) copy-start(s32[256,3]{0,1:T(4,128)} %param.11) | copy-start | bytes 9220
  94.0 51.0 %slice-start = ((s8[6291456]{0:T(1024)(128)(4,1)}), s8[2097152]{0:T(1024)(128)(4,1)S(1)}, s32[]{:S(2)}) async-start(s8[6291456]{0:T(1024)(128)(4,1)} %bitcast.21), calls=%async_computation | async-start | bytes 4194304
  97.6 2.7 %copy-start = (bf16[128,24576]{1,0:T(8,128)(2,1)}, bf16[128,24576]{1,0:T(8,128)(2,1)S(1)}, u32[]{:S(2)}) copy-start(bf16[128,24576]{1,0:T(8,128)(2,1)S(1)} %pad_maximum_fusion.x_hbm) | copy-start | bytes 18874372
  100.3 6.8 %collective-permute-start.6 = (bf16[128,256]{1,0:T(8,128)(2,1)S(1)}, bf16[128,256]{1,0:T(8,128)(2,1)S(1)}, u32[]{:S(2)}, u32[]{:S(2)}) collective-permute-start(bf16[128,256]{1,0:T(8,128)(2,1)S(1)} %get-tuple-element.24), channel_id=1, source_target_pairs={{0,1},{1,2},{2,3},{4,5},{5,6},{6,7},{8,9},{9,10},{10,11},{12,13},{... | collective-permute-start | bytes 196616 | tf_op jit(solution)/shard_map/ppermute | solution.py:27
  103.8 6.6 %collective-permute-start.7 = (bf16[128,256]{1,0:T(8,128)(2,1)S(1)}, bf16[128,256]{1,0:T(8,128)(2,1)S(1)}, u32[]{:S(2)}, u32[]{:S(2)}) collective-permute-start(bf16[128,256]{1,0:T(8,128)(2,1)S(1)} %get-tuple-element.23), channel_id=1, source_target_pairs={{1,0},{2,1},{3,2},{5,4},{6,5},{7,6},{9,8},{10,9},{11,10},{13,12},{... | collective-permute-start | bytes 196616 | tf_op jit(solution)/shard_map/ppermute | solution.py:28
  107.1 3.2 %copy-start.8 = (bf16[128,256]{1,0:T(8,128)(2,1)}, bf16[128,256]{1,0:T(8,128)(2,1)S(1)}, u32[]{:S(2)}) copy-start(bf16[128,256]{1,0:T(8,128)(2,1)S(1)} %collective-permute-done.6.lo_ref) | copy-start | bytes 196612
  110.3 0.6 copy-start.10
  111.0 34.1 %slice-start.1 = ((s8[6291456]{0:T(1024)(128)(4,1)}), s8[4194304]{0:T(1024)(128)(4,1)S(1)}, s32[]{:S(2)}) async-start(s8[6291456]{0:T(1024)(128)(4,1)} %bitcast.21), calls=%async_computation.1 | async-start | bytes 8388608
  134.4 4.5 %collective-permute-start.8 = (f32[128,128]{1,0:T(8,128)}, f32[128,128]{1,0:T(8,128)S(1)}, u32[]{:S(2)}, u32[]{:S(2)}) collective-permute-start(f32[128,128]{1,0:T(8,128)} %bitcast.25), channel_id=1, source_target_pairs={{0,1},{1,0},{2,3},{3,2},{4,5},{5,4},{6,7},{7,6},{8,9},{9,8},{10,11... | collective-permute-start | bytes 196616 | tf_op jit(solution)/shard_map/ppermute | solution.py:169
  139.8 5.2 %collective-permute-start.9 = (f32[128,128]{1,0:T(8,128)S(1)}, f32[128,128]{1,0:T(8,128)S(1)}, u32[]{:S(2)}, u32[]{:S(2)}) collective-permute-start(f32[128,128]{1,0:T(8,128)S(1)} %bitcast_add_fusion), channel_id=1, source_target_pairs={{0,2},{1,3},{2,0},{3,1},{4,6},{5,7},{6,4},{7,5},{8,10},{9,11},{10,... | collective-permute-start | bytes 196616 | tf_op jit(solution)/shard_map/ppermute | solution.py:169
  149.0 2.7 %copy-start.1 = (bf16[128,24576]{1,0:T(8,128)(2,1)}, bf16[128,24576]{1,0:T(8,128)(2,1)S(1)}, u32[]{:S(2)}) copy-start(bf16[128,24576]{1,0:T(8,128)(2,1)S(1)} %fusion.x_hbm) | copy-start | bytes 18874372
  151.8 6.2 %collective-permute-start.10 = (bf16[128,256]{1,0:T(8,128)(2,1)S(1)}, bf16[128,256]{1,0:T(8,128)(2,1)S(1)}, u32[]{:S(2)}, u32[]{:S(2)}) collective-permute-start(bf16[128,256]{1,0:T(8,128)(2,1)S(1)} %get-tuple-element.22), channel_id=1, source_target_pairs={{0,1},{1,2},{2,3},{4,5},{5,6},{6,7},{8,9},{9,10},{10,11},{12,13},{... | collective-permute-start | bytes 196616 | tf_op jit(solution)/shard_map/ppermute | solution.py:27
  155.2 6.2 %collective-permute-start.11 = (bf16[128,256]{1,0:T(8,128)(2,1)S(1)}, bf16[128,256]{1,0:T(8,128)(2,1)S(1)}, u32[]{:S(2)}, u32[]{:S(2)}) collective-permute-start(bf16[128,256]{1,0:T(8,128)(2,1)S(1)} %get-tuple-element.21), channel_id=1, source_target_pairs={{1,0},{2,1},{3,2},{5,4},{6,5},{7,6},{9,8},{10,9},{11,10},{13,12},{... | collective-permute-start | bytes 196616 | tf_op jit(solution)/shard_map/ppermute | solution.py:28
  157.9 3.5 %copy-start.9 = (bf16[128,256]{1,0:T(8,128)(2,1)}, bf16[128,256]{1,0:T(8,128)(2,1)S(1)}, u32[]{:S(2)}) copy-start(bf16[128,256]{1,0:T(8,128)(2,1)S(1)} %collective-permute-done.10.lo_ref) | copy-start | bytes 196612
  161.4 0.6 copy-start.11
  194.4 6.3 %collective-permute-start.12 = (f32[2,128,128]{2,1,0:T(8,128)}, f32[2,128,128]{2,1,0:T(8,128)S(1)}, u32[]{:S(2)}, u32[]{:S(2)}) collective-permute-start(f32[2,128,128]{2,1,0:T(8,128)} %get-tuple-element.19), channel_id=1, source_target_pairs={{0,1},{1,0},{2,3},{3,2},{4,5},{5,4},{6,7},{7,6},{8,9},{9,8},{10,11... | collective-permute-start | bytes 393224 | tf_op jit(solution)/shard_map/ppermute | solution.py:169
  201.6 6.0 %collective-permute-start.13 = (f32[2,128,128]{2,1,0:T(8,128)S(1)}, f32[2,128,128]{2,1,0:T(8,128)S(1)}, u32[]{:S(2)}, u32[]{:S(2)}) collective-permute-start(f32[2,128,128]{2,1,0:T(8,128)S(1)} %add.71), channel_id=1, source_target_pairs={{0,2},{1,3},{2,0},{3,1},{4,6},{5,7},{6,4},{7,5},{8,10},{9,11},{10,... | collective-permute-start | bytes 393224 | tf_op jit(solution)/shard_map/ppermute | solution.py:169
  207.7 12.0 %copy-start.4 = (f32[1,128,128]{2,1,0:T(8,128)}, f32[1,128,128]{2,1,0:T(8,128)S(1)}, u32[]{:S(2)}) copy-start(f32[1,128,128]{2,1,0:T(8,128)S(1)} %get-tuple-element.27) | copy-start | bytes 196612
  207.7 12.0 %copy-start.5 = (f32[1,128,128]{2,1,0:T(8,128)}, f32[1,128,128]{2,1,0:T(8,128)S(1)}, u32[]{:S(2)}) copy-start(f32[1,128,128]{2,1,0:T(8,128)S(1)} %get-tuple-element.28) | copy-start | bytes 196612

commit v6 on v5

--- a/solution.py
+++ b/solution.py
@@ -103,11 +103,10 @@
                 dots_ref[m] += nt(other, native)
 
 
-def block_apply(matrices, shifts_flat, count, cells, pair=None):
+def block_apply(matrices, shifts_flat, count, cells, lower, upper, pair=None):
     slots, entries = cells.shape
     block_rows, blk, width = matrices[0].shape
-    rim = 256
-    lower, upper = row_halos(cells, rim)
+    rim = lower.shape[1]
     group = 64 if block_rows % 64 == 0 else block_rows
     chunk = 512
     nmat = len(matrices)
@@ -194,32 +193,56 @@
     odd = lax.axis_index("cuts") % 2 == 1
     evens = range(0, cuts_count, 2)
     odds = range(1, cuts_count, 2)
-    upper_1 = from_behind(upper_window, "cuts", 1)
-    lower_1 = from_behind(lower_window, "cuts", -1)
-    upper_direct = lax.ppermute(upper_window, "cuts", [(i, i + 2) for i in evens if i + 2 < cuts_count])
-    lower_direct = lax.ppermute(lower_window, "cuts", [(i, i - 2) for i in odds if i - 2 >= 0])
+    rim = 256
+
+    def exchange(upper, lower):
+        return (
+            from_behind(upper, "cuts", 1),
+            from_behind(lower, "cuts", -1),
+            lax.ppermute(upper, "cuts", [(i, i + 2) for i in evens if i + 2 < cuts_count]),
+            lax.ppermute(lower, "cuts", [(i, i - 2) for i in odds if i - 2 >= 0]),
+        )
+
+    def finish(upper_1, lower_1, upper_direct, lower_direct):
+        upper_2 = jnp.where(
+            odd, lax.ppermute(upper_1, "cuts", [(i, i + 1) for i in evens if i + 1 < cuts_count]), upper_direct
+        )
+        lower_2 = jnp.where(odd, lower_direct, lax.ppermute(lower_1, "cuts", [(i, i - 1) for i in odds]))
+        return [upper_2, upper_1, lower_1, lower_2]
+
+    masked = jnp.where(valid_mask[:, None], own_vectors, jnp.zeros((), own_vectors.dtype))
+    below, above = row_halos(jnp.concatenate([upper_window, lower_window, masked], axis=0), rim)
+    masked_lower, masked_upper = below[2 * WIN :], above[2 * WIN :]
+    upper_ext = jnp.concatenate([upper_window, below[:WIN], above[:WIN]], axis=1)
+    lower_ext = jnp.concatenate([lower_window, below[WIN : 2 * WIN], above[WIN : 2 * WIN]], axis=1)
+    big = exchange(upper_ext, lower_ext)
     row_major = Layout(major_to_minor=(0, 1, 2))
     margin_blocks = with_layout_constraint(margin_blocks, row_major)
     energy_blocks = with_layout_constraint(energy_blocks, row_major)
-    upper_1, lower_1, upper_direct, lower_direct, margin_blocks, energy_blocks = lax.optimization_barrier(
-        (upper_1, lower_1, upper_direct, lower_direct, margin_blocks, energy_blocks)
-    )
-    upper_2 = jnp.where(
-        odd, lax.ppermute(upper_1, "cuts", [(i, i + 1) for i in evens if i + 1 < cuts_count]), upper_direct
-    )
-    lower_2 = jnp.where(odd, lower_direct, lax.ppermute(lower_1, "cuts", [(i, i - 1) for i in odds]))
-    received = [upper_2, upper_1, lower_1, lower_2]
-    windows = jnp.concatenate(received, axis=0)
+    big, margin_blocks, energy_blocks = lax.optimization_barrier((big, margin_blocks, energy_blocks))
+    received = jnp.concatenate(finish(*big), axis=0)
+    windows = received[:, :entries]
+    windows_lower = received[:, entries : entries + rim]
+    windows_upper = received[:, entries + rim :]
     count = counts[:1]
-    (margin_dots,) = block_apply((margin_blocks,), shifts_flat, count, windows, pair=own_vectors)
+    (margin_dots,) = block_apply(
+        (margin_blocks,), shifts_flat, count, windows, windows_lower, windows_upper, pair=own_vectors
+    )
     margin = row_sum(margin_dots[0]) / nmat_total
-    removed = lax.dot_general(
-        margin.astype(jnp.bfloat16), windows, (((0,), (0,)), ((), ())), preferred_element_type=jnp.float32
-    )
-    masked = jnp.where(valid_mask[:, None], own_vectors, jnp.zeros((), own_vectors.dtype))
-    cleaned = (masked.astype(jnp.float32) - removed).astype(jnp.bfloat16)
+    margin_b = margin.astype(jnp.bfloat16)
+
+    def clean(kept, wins):
+        removed = lax.dot_general(margin_b, wins, (((0,), (0,)), ((), ())), preferred_element_type=jnp.float32)
+        return (kept.astype(jnp.float32) - removed).astype(jnp.bfloat16)
+
+    cleaned = clean(masked, windows)
     margin_cleaned, energy_cleaned, pencil_dots = block_apply(
-        (margin_blocks, energy_blocks), shifts_flat, count, cleaned
+        (margin_blocks, energy_blocks),
+        shifts_flat,
+        count,
+        cleaned,
+        clean(masked_lower, windows_lower),
+        clean(masked_upper, windows_upper),
     )
     pencils = row_sum(pencil_dots) / nmat_total
     margin_pencil = pencils[0]

time: 223 us -> 219 us (0.982)
  waiting for transfers between devices: 45.1 us -> 37.2 us
  matrix products: 3.98 us -> 9 us
    ppermute x4, waiting for transfers between devices: 18.3 us -> 2.26 us  [the longest x1 2.25 us: finish(): lax.ppermute(lower_1, 'cuts', [(i, i - 1) for i in odds])]
    ppermute x2, waiting for transfers between devices: 0.01 us -> 14.8 us  [from_behind(): return lax.ppermute(block, axis, route)]
    dot_general x1 -> x3, matrix products: 3.98 us -> 9 us  [clean(): lax.dot_general(margin_b, wins, (((0,), (0,)), ((), ())), preferred_eleme...]
    unnamed x32 -> x22, local copies, waits for them, and re-layouts: 53.5 us -> 49.3 us
    ppermute x4, waiting for transfers between devices: 19.8 us -> 16 us  [row_sum(): lax.ppermute(part, 'row', [(i, i ^ step) for i in range(count)])]
    slice x3 -> x4, local copies, waits for them, and re-layouts: 1.33 us -> 5.06 us  [the longest x1 3.74 us: shards(): windows = received[:, :entries]]
    ppermute x4, starting transfers between devices: 2.29 us -> 5.8 us  [row_sum(): lax.ppermute(part, 'row', [(i, i ^ step) for i in range(count)])]
    ppermute x2 -> x1, starting transfers between devices: 6.96 us -> 3.48 us  [row_halos(): lower = lax.ppermute(tail, 'row', [(i, i + 1) for i in range(ends)])]
  transfers between devices with their start and end apart: 14 -> 12, of which waited for: 10 -> 8; matrix products, arithmetic and copies ran while one was open for 22% -> 24% of each run, Pallas kernels for 0% -> 0%
where the time goes in v6:
time: 219 us; the launch traced here: 215 us
  local copies, waits for them, and re-layouts  57.8 us (26%)
  Pallas kernels  56.5 us (26%)
  waiting for transfers between devices  37.2 us (17%)
  starting transfers between devices  26.6 us (12%)
  other arithmetic  22.6 us (10%)
  matrix products  9 us (4%)
  between operations  5.44 us (2%)
    pallas_call x2, Pallas kernels, block_apply(): pl.pallas_call(kernel, grid_spec=grid_spec, out_shape=out_shape, compiler...  56.5 us
    unnamed x22, local copies, waits for them, and re-layouts  49.3 us
    ppermute x4, waiting for transfers between devices, row_sum(): lax.ppermute(part, 'row', [(i, i ^ step) for i in range(count)])  16 us
    ppermute x2, waiting for transfers between devices, from_behind(): return lax.ppermute(block, axis, route)  14.8 us
    broadcast_in_dim x1, other arithmetic, shards(): return (residual[None], margin_pencil[None], energy_pencil[None])  9.47 us
    dot_general x3, matrix products, clean(): lax.dot_general(margin_b, wins, (((0,), (0,)), ((), ())), preferred_eleme...  9 us
    ppermute x4, starting transfers between devices, row_sum(): lax.ppermute(part, 'row', [(i, i ^ step) for i in range(count)])  5.8 us
    ppermute x2, starting transfers between devices, from_behind(): return lax.ppermute(block, axis, route)  5.53 us
  transfers between devices with their start and end apart: 12, of which 8 were waited for; matrix products, arithmetic and copies ran while one was open for 24% of the time, Pallas kernels for 0%

profile of v6, /device:TPU:12, one launch (start us, length us, event | category | flops | bytes accessed | tf_op | source)
XLA Modules:
  0.0 215.1 jit_solution(12888998514416561902)
XLA Ops:
  0.6 1.3 fusion.6
  5.2 1.3 add_compare_fusion
  7.8 3.4 %broadcast_select_fusion = bf16[128,24576]{1,0:T(8,128)(2,1)S(1)} fusion(pred[128]{0:T(512)(128)(4,1)S(1)} %iota_compare_fusion, bf16[1,128,24576]{2,1,0:T(8,128)(2,1)} %param.6), kind=kLoop, calls=%fused_computation.7 | loop fusion | flops 3145728 | bytes 12583040 | tf_op jit(solution)/shard_map/jit(_where)/select_n | solution.py:213
  11.2 1.6 copy-done.2
  13.9 3.5 %collective-permute-start = (bf16[192,256]{1,0:T(8,128)(2,1)S(1)}, bf16[192,256]{1,0:T(8,128)(2,1)S(1)}, u32[]{:S(2)}, u32[]{:S(2)}) collective-permute-start(bf16[192,256]{1,0:T(8,128)(2,1)S(1)} %get-tuple-element.21), channel_id=1, source_target_pairs={{0,1},{1,2},{2,3},{4,5},{5,6},{6,7},{8,9},{9,10},{10,11},{12,13},{... | collective-permute-start | bytes 294920 | tf_op jit(solution)/shard_map/ppermute | solution.py:27
  17.4 2.4 %collective-permute-start.1 = (bf16[192,256]{1,0:T(8,128)(2,1)S(1)}, bf16[192,256]{1,0:T(8,128)(2,1)S(1)}, u32[]{:S(2)}, u32[]{:S(2)}) collective-permute-start(bf16[192,256]{1,0:T(8,128)(2,1)S(1)} %get-tuple-element.22), channel_id=1, source_target_pairs={{1,0},{2,1},{3,2},{5,4},{6,5},{7,6},{9,8},{10,9},{11,10},{13,12},{... | collective-permute-start | bytes 294920 | tf_op jit(solution)/shard_map/ppermute | solution.py:28
  20.4 3.5 %collective-permute-done.1 = bf16[192,256]{1,0:T(8,128)(2,1)S(1)} collective-permute-done((bf16[192,256]{1,0:T(8,128)(2,1)S(1)}, bf16[192,256]{1,0:T(8,128)(2,1)S(1)}, u32[]{:S(2)}, u32[]{:S(2)}) %collective-permute-start.1) | collective-permute-done | bytes 98336 | tf_op jit(solution)/shard_map/ppermute | solution.py:28
  23.9 1.3 pad_maximum_fusion.2
  25.2 1.9 collective-permute-start.3
  27.1 1.8 collective-permute-start.5
  28.9 1.3 pad_maximum_fusion.1
  30.2 3.6 %collective-permute-start.2 = (bf16[32,25088]{1,0:T(8,128)(2,1)}, bf16[32,25088]{1,0:T(8,128)(2,1)S(1)}, u32[]{:S(2)}, u32[]{:S(2)}) collective-permute-start(bf16[32,25088]{1,0:T(8,128)(2,1)} %pad_maximum_fusion.1), channel_id=1, source_target_pairs={{0,4},{4,8},{8,12},{12,16},{16,20},{20,24},{24,28},{1,5},{5,9},{9,... | collective-permute-start | bytes 4816904 | tf_op jit(solution)/shard_map/ppermute | solution.py:19
  33.8 3.7 %collective-permute-start.4 = (bf16[32,25088]{1,0:T(8,128)(2,1)}, bf16[32,25088]{1,0:T(8,128)(2,1)}, u32[]{:S(2)}, u32[]{:S(2)}) collective-permute-start(bf16[32,25088]{1,0:T(8,128)(2,1)} %pad_maximum_fusion.1), channel_id=1, source_target_pairs={{0,8},{8,16},{16,24},{1,9},{9,17},{17,25},{2,10},{10,18},{18,26},{... | collective-permute-start | bytes 4816904 | tf_op jit(solution)/shard_map/ppermute | solution.py:202
  37.5 23.4 %copy.12.refs_0_ = bf16[256,96,288]{2,1,0:T(8,128)(2,1)} copy(bf16[256,96,288]{0,2,1:T(8,128)(2,1)} %param.9) | data formatting | bytes 28311552 | tf_op args[3]
  60.9 23.3 %copy.13.refs_1_ = bf16[256,96,288]{2,1,0:T(8,128)(2,1)} copy(bf16[256,96,288]{0,2,1:T(8,128)(2,1)} %param.10) | data formatting | bytes 28311552 | tf_op args[4]
  84.3 14.8 %collective-permute-done.2 = bf16[32,25088]{1,0:T(8,128)(2,1)S(1)} collective-permute-done((bf16[32,25088]{1,0:T(8,128)(2,1)}, bf16[32,25088]{1,0:T(8,128)(2,1)S(1)}, u32[]{:S(2)}, u32[]{:S(2)}) %collective-permute-start.2) | collective-permute-done | bytes 1605664 | tf_op jit(solution)/shard_map/ppermute | solution.py:19
  99.1 2.5 %collective-permute-start.6 = (bf16[32,25088]{1,0:T(8,128)(2,1)S(1)}, bf16[32,25088]{1,0:T(8,128)(2,1)}, u32[]{:S(2)}, u32[]{:S(2)}) collective-permute-start(bf16[32,25088]{1,0:T(8,128)(2,1)S(1)} %collective-permute-done.2), channel_id=1, source_target_pairs={{0,4},{8,12},{16,20},{24,28},{1,5},{9,13},{17,21},{25,29},{2,6},{1... | collective-permute-start | bytes 4816904 | tf_op jit(solution)/shard_map/ppermute | solution.py:208
  102.5 1.5 collective-permute-start.7
  103.9 1.6 broadcast_select_fusion.2
  105.6 2.3 %collective-permute-done.7 = bf16[32,25088]{1,0:T(8,128)(2,1)S(1)} collective-permute-done((bf16[32,25088]{1,0:T(8,128)(2,1)S(1)}, bf16[32,25088]{1,0:T(8,128)(2,1)S(1)}, u32[]{:S(2)}, u32[]{:S(2)}) %collective-permute-start.7) | collective-permute-done | bytes 1605664 | tf_op jit(solution)/shard_map/ppermute | solution.py:210
  109.3 3.7 %slice.70.x_hbm = bf16[128,24576]{1,0:T(8,128)(2,1)} slice(bf16[128,25088]{1,0:T(8,128)(2,1)S(1)} %pad_maximum_fusion), slice={[0:128], [0:24576]} | slice | bytes 12582912 | tf_op jit(solution)/shard_map/slice | solution.py:224
  114.0 24.0 %shard_map.85 = f32[1,128,128]{2,1,0:T(8,128)} custom-call(s32[768]{0:T(1024)} %reshape.42.shift_ref, s32[1]{0:T(128)} %copy.14.count_ref, bf16[128,24576]{1,0:T(8,128)(2,1)} %slice.70.x_hbm, bf16[128,256]{1,0:T(8,128)(2,1)} %get-tuple-element.24.lo_ref, bf16[128,256]{1,0:T(8,128)(2,1)} %get-tuple-element.23.hi_ref, bf16[256,96,288]{2,1,0:T(8,128)(2,1)} %copy.12.refs_0_, ...), custom_call_target="tpu_custom_call" | custom-call | tf_op jit(solution)/shard_map/pallas_call | solution.py:143
  138.5 4.2 %collective-permute-done.8 = f32[128,128]{1,0:T(8,128)S(1)} collective-permute-done((f32[128,128]{1,0:T(8,128)}, f32[128,128]{1,0:T(8,128)S(1)}, u32[]{:S(2)}, u32[]{:S(2)}) %collective-permute-start.8) | collective-permute-done | bytes 65568 | tf_op jit(solution)/shard_map/ppermute | solution.py:168
  144.5 4.5 %collective-permute-done.9 = f32[128,128]{1,0:T(8,128)S(1)} collective-permute-done((f32[128,128]{1,0:T(8,128)S(1)}, f32[128,128]{1,0:T(8,128)S(1)}, u32[]{:S(2)}, u32[]{:S(2)}) %collective-permute-start.9) | collective-permute-done | bytes 65568 | tf_op jit(solution)/shard_map/ppermute | solution.py:168
  149.0 7.3 %fusion.x_hbm = bf16[128,24576]{1,0:T(8,128)(2,1)} fusion(bf16[128,128]{1,0:T(8,128)(2,1)S(1)} %multiply_convert_fusion, bf16[128,24576]{1,0:T(8,128)(2,1)S(1)} %bitcast.26, bf16[128,25088]{1,0:T(8,128)(2,1)} %copy-done.1), kind=kOutput, calls=%fused_computation.3 | convolution fusion | flops 814743552 | bytes 18907136 | tf_op jit(solution)/shard_map/dot_general | solution.py:235
  158.1 32.4 %shard_map.86 = (bf16[128,24576]{1,0:T(8,128)(2,1)}, bf16[128,24576]{1,0:T(8,128)(2,1)}, f32[2,128,128]{2,1,0:T(8,128)}) custom-call(s32[768]{0:T(1024)} %reshape.42.shift_ref, s32[1]{0:T(128)} %copy.14.count_ref, bf16[128,24576]{1,0:T(8,128)(2,1)} %fusion.x_hbm, bf16[128,256]{1,0:T(8,128)(2,1)} %subtract_convert_fusion.2.lo_ref, ...), custom_call_target="tpu_custom_call" | custom-call | tf_op jit(solution)/shard_map/pallas_call | solution.py:143
  190.5 1.8 collective-permute-start.10
  192.3 3.4 %collective-permute-done.10 = f32[2,128,128]{2,1,0:T(8,128)S(1)} collective-permute-done((f32[2,128,128]{2,1,0:T(8,128)}, f32[2,128,128]{2,1,0:T(8,128)S(1)}, u32[]{:S(2)}, u32[]{:S(2)}) %collective-permute-start.10) | collective-permute-done | bytes 131104 | tf_op jit(solution)/shard_map/ppermute | solution.py:168
  196.6 2.5 %collective-permute-start.11 = (f32[2,128,128]{2,1,0:T(8,128)S(1)}, f32[2,128,128]{2,1,0:T(8,128)S(1)}, u32[]{:S(2)}, u32[]{:S(2)}) collective-permute-start(f32[2,128,128]{2,1,0:T(8,128)S(1)} %add.71), channel_id=1, source_target_pairs={{0,2},{1,3},{2,0},{3,1},{4,6},{5,7},{6,4},{7,5},{8,10},{9,11},{10,... | collective-permute-start | bytes 393224 | tf_op jit(solution)/shard_map/ppermute | solution.py:168
  199.2 3.9 %collective-permute-done.11 = f32[2,128,128]{2,1,0:T(8,128)S(1)} collective-permute-done((f32[2,128,128]{2,1,0:T(8,128)S(1)}, f32[2,128,128]{2,1,0:T(8,128)S(1)}, u32[]{:S(2)}, u32[]{:S(2)}) %collective-permute-start.11) | collective-permute-done | bytes 131104 | tf_op jit(solution)/shard_map/ppermute | solution.py:168
  203.1 1.2 gather_fusion
  205.7 9.5 %fusion.1 = bf16[1,128,24576]{2,1,0:T(8,128)(2,1)} fusion(bf16[128,24576]{1,0:T(8,128)(2,1)} %get-tuple-element.20, bf16[128,24576]{1,0:T(8,128)(2,1)} %get-tuple-element.18, f32[128]{0:T(128)S(1)} %divide_select_fusion), kind=kLoop, calls=%fused_computation.6 | loop fusion | flops 15728640 | bytes 18874880 | tf_op jit(solution)/shard_map/broadcast_in_dim | solution.py:260
  (49 shorter events, 11.2 us)
Async XLA Ops:
  7.8 5.1 %copy-start.2 = (bf16[1,128,24576]{2,1,0:T(8,128)(2,1)S(1)}, bf16[1,128,24576]{2,1,0:T(8,128)(2,1)}, u32[]{:S(2)}) copy-start(bf16[1,128,24576]{2,1,0:T(8,128)(2,1)} %param.6) | copy-start | bytes 18874372
  11.2 2.7 %copy-start = (bf16[128,24576]{1,0:T(8,128)(2,1)}, bf16[128,24576]{1,0:T(8,128)(2,1)S(1)}, u32[]{:S(2)}) copy-start(bf16[128,24576]{1,0:T(8,128)(2,1)S(1)} %broadcast_select_fusion) | copy-start | bytes 18874372
  13.9 6.5 %collective-permute-start = (bf16[192,256]{1,0:T(8,128)(2,1)S(1)}, bf16[192,256]{1,0:T(8,128)(2,1)S(1)}, u32[]{:S(2)}, u32[]{:S(2)}) collective-permute-start(bf16[192,256]{1,0:T(8,128)(2,1)S(1)} %get-tuple-element.21), channel_id=1, source_target_pairs={{0,1},{1,2},{2,3},{4,5},{5,6},{6,7},{8,9},{9,10},{10,11},{12,13},{... | collective-permute-start | bytes 294920 | tf_op jit(solution)/shard_map/ppermute | solution.py:27
  17.4 6.5 %collective-permute-start.1 = (bf16[192,256]{1,0:T(8,128)(2,1)S(1)}, bf16[192,256]{1,0:T(8,128)(2,1)S(1)}, u32[]{:S(2)}, u32[]{:S(2)}) collective-permute-start(bf16[192,256]{1,0:T(8,128)(2,1)S(1)} %get-tuple-element.22), channel_id=1, source_target_pairs={{1,0},{2,1},{3,2},{5,4},{6,5},{7,6},{9,8},{10,9},{11,10},{13,12},{... | collective-permute-start | bytes 294920 | tf_op jit(solution)/shard_map/ppermute | solution.py:28
  25.2 59.1 %collective-permute-start.3 = (bf16[32,25088]{1,0:T(8,128)(2,1)}, bf16[32,25088]{1,0:T(8,128)(2,1)S(1)}, u32[]{:S(2)}, u32[]{:S(2)}) collective-permute-start(bf16[32,25088]{1,0:T(8,128)(2,1)} %pad_maximum_fusion.2), channel_id=1, source_target_pairs={{4,0},{8,4},{12,8},{16,12},{20,16},{24,20},{28,24},{5,1},{9,5},{13... | collective-permute-start | bytes 4816904 | tf_op jit(solution)/shard_map/ppermute | solution.py:19
  27.1 57.2 %collective-permute-start.5 = (bf16[32,25088]{1,0:T(8,128)(2,1)}, bf16[32,25088]{1,0:T(8,128)(2,1)}, u32[]{:S(2)}, u32[]{:S(2)}) collective-permute-start(bf16[32,25088]{1,0:T(8,128)(2,1)} %pad_maximum_fusion.2), channel_id=1, source_target_pairs={{12,4},{20,12},{28,20},{13,5},{21,13},{29,21},{14,6},{22,14},{30,2... | collective-permute-start | bytes 4816904 | tf_op jit(solution)/shard_map/ppermute | solution.py:203
  30.2 68.9 %collective-permute-start.2 = (bf16[32,25088]{1,0:T(8,128)(2,1)}, bf16[32,25088]{1,0:T(8,128)(2,1)S(1)}, u32[]{:S(2)}, u32[]{:S(2)}) collective-permute-start(bf16[32,25088]{1,0:T(8,128)(2,1)} %pad_maximum_fusion.1), channel_id=1, source_target_pairs={{0,4},{4,8},{8,12},{12,16},{16,20},{20,24},{24,28},{1,5},{5,9},{9,... | collective-permute-start | bytes 4816904 | tf_op jit(solution)/shard_map/ppermute | solution.py:19
  33.8 65.2 %collective-permute-start.4 = (bf16[32,25088]{1,0:T(8,128)(2,1)}, bf16[32,25088]{1,0:T(8,128)(2,1)}, u32[]{:S(2)}, u32[]{:S(2)}) collective-permute-start(bf16[32,25088]{1,0:T(8,128)(2,1)} %pad_maximum_fusion.1), channel_id=1, source_target_pairs={{0,8},{8,16},{16,24},{1,9},{9,17},{17,25},{2,10},{10,18},{18,26},{... | collective-permute-start | bytes 4816904 | tf_op jit(solution)/shard_map/ppermute | solution.py:202
  60.9 40.6 %copy-start.7 = (s32[256,3]{0,1:T(4,128)S(1)}, s32[256,3]{0,1:T(4,128)}, u32[]{:S(2)}) copy-start(s32[256,3]{0,1:T(4,128)} %param.11) | copy-start | bytes 9220
  99.1 4.9 %collective-permute-start.6 = (bf16[32,25088]{1,0:T(8,128)(2,1)S(1)}, bf16[32,25088]{1,0:T(8,128)(2,1)}, u32[]{:S(2)}, u32[]{:S(2)}) collective-permute-start(bf16[32,25088]{1,0:T(8,128)(2,1)S(1)} %collective-permute-done.2), channel_id=1, source_target_pairs={{0,4},{8,12},{16,20},{24,28},{1,5},{9,13},{17,21},{25,29},{2,6},{1... | collective-permute-start | bytes 4816904 | tf_op jit(solution)/shard_map/ppermute | solution.py:208
  102.5 5.3 %collective-permute-start.7 = (bf16[32,25088]{1,0:T(8,128)(2,1)S(1)}, bf16[32,25088]{1,0:T(8,128)(2,1)S(1)}, u32[]{:S(2)}, u32[]{:S(2)}) collective-permute-start(bf16[32,25088]{1,0:T(8,128)(2,1)S(1)} %collective-permute-done.3), channel_id=1, source_target_pairs={{4,0},{12,8},{20,16},{28,24},{5,1},{13,9},{21,17},{29,25},{6,2},{1... | collective-permute-start | bytes 4816904 | tf_op jit(solution)/shard_map/ppermute | solution.py:210
  109.3 4.6 %copy-start.1 = (bf16[128,25088]{1,0:T(8,128)(2,1)}, bf16[128,25088]{1,0:T(8,128)(2,1)S(1)}, u32[]{:S(2)}) copy-start(bf16[128,25088]{1,0:T(8,128)(2,1)S(1)} %pad_maximum_fusion) | copy-start | bytes 19267588
  113.9 35.0 %slice-start = ((s8[6291456]{0:T(1024)(128)(4,1)}), s8[4194304]{0:T(1024)(128)(4,1)S(1)}, s32[]{:S(2)}) async-start(s8[6291456]{0:T(1024)(128)(4,1)} %bitcast.25), calls=%async_computation | async-start | bytes 8388608
  113.9 35.1 %slice-start.1 = ((s8[6291456]{0:T(1024)(128)(4,1)}), s8[2097152]{0:T(1024)(128)(4,1)S(1)}, s32[]{:S(2)}) async-start(s8[6291456]{0:T(1024)(128)(4,1)} %bitcast.25), calls=%async_computation.1 | async-start | bytes 4194304
  138.0 4.7 %collective-permute-start.8 = (f32[128,128]{1,0:T(8,128)}, f32[128,128]{1,0:T(8,128)S(1)}, u32[]{:S(2)}, u32[]{:S(2)}) collective-permute-start(f32[128,128]{1,0:T(8,128)} %bitcast.30), channel_id=1, source_target_pairs={{0,1},{1,0},{2,3},{3,2},{4,5},{5,4},{6,7},{7,6},{8,9},{9,8},{10,11... | collective-permute-start | bytes 196616 | tf_op jit(solution)/shard_map/ppermute | solution.py:168
  143.6 5.4 %collective-permute-start.9 = (f32[128,128]{1,0:T(8,128)S(1)}, f32[128,128]{1,0:T(8,128)S(1)}, u32[]{:S(2)}, u32[]{:S(2)}) collective-permute-start(f32[128,128]{1,0:T(8,128)S(1)} %bitcast_add_fusion), channel_id=1, source_target_pairs={{0,2},{1,3},{2,0},{3,1},{4,6},{5,7},{6,4},{7,5},{8,10},{9,11},{10,... | collective-permute-start | bytes 196616 | tf_op jit(solution)/shard_map/ppermute | solution.py:168
  149.0 7.4 %copy-start.6 = (bf16[128,256]{1,0:T(8,128)(2,1)S(1)}, bf16[128,256]{1,0:T(8,128)(2,1)}, u32[]{:S(2)}) copy-start(bf16[128,256]{1,0:T(8,128)(2,1)} %get-tuple-element.23.hi_ref) | copy-start | bytes 196612
  149.0 8.2 %copy-start.5 = (bf16[128,256]{1,0:T(8,128)(2,1)S(1)}, bf16[128,256]{1,0:T(8,128)(2,1)}, u32[]{:S(2)}) copy-start(bf16[128,256]{1,0:T(8,128)(2,1)} %get-tuple-element.24.lo_ref) | copy-start | bytes 196612
  190.5 5.2 %collective-permute-start.10 = (f32[2,128,128]{2,1,0:T(8,128)}, f32[2,128,128]{2,1,0:T(8,128)S(1)}, u32[]{:S(2)}, u32[]{:S(2)}) collective-permute-start(f32[2,128,128]{2,1,0:T(8,128)} %get-tuple-element.19), channel_id=1, source_target_pairs={{0,1},{1,0},{2,3},{3,2},{4,5},{5,4},{6,7},{7,6},{8,9},{9,8},{10,11... | collective-permute-start | bytes 393224 | tf_op jit(solution)/shard_map/ppermute | solution.py:168
  196.6 6.4 %collective-permute-start.11 = (f32[2,128,128]{2,1,0:T(8,128)S(1)}, f32[2,128,128]{2,1,0:T(8,128)S(1)}, u32[]{:S(2)}, u32[]{:S(2)}) collective-permute-start(f32[2,128,128]{2,1,0:T(8,128)S(1)} %add.71), channel_id=1, source_target_pairs={{0,2},{1,3},{2,0},{3,1},{4,6},{5,7},{6,4},{7,5},{8,10},{9,11},{10,... | collective-permute-start | bytes 393224 | tf_op jit(solution)/shard_map/ppermute | solution.py:168
  203.1 12.0 %copy-start.3 = (f32[1,128,128]{2,1,0:T(8,128)}, f32[1,128,128]{2,1,0:T(8,128)S(1)}, u32[]{:S(2)}) copy-start(f32[1,128,128]{2,1,0:T(8,128)S(1)} %get-tuple-element.27) | copy-start | bytes 196612
  203.1 12.0 %copy-start.4 = (f32[1,128,128]{2,1,0:T(8,128)}, f32[1,128,128]{2,1,0:T(8,128)S(1)}, u32[]{:S(2)}) copy-start(f32[1,128,128]{2,1,0:T(8,128)S(1)} %get-tuple-element.28) | copy-start | bytes 196612

commit v7 on v6

--- a/solution.py
+++ b/solution.py
@@ -57,19 +57,28 @@
 
     @pl.when(g == 0)
     def _():
-        copy = pltpu.make_async_copy(x_hbm, xbuf, sem.at[0])
-        copy.start()
+        pieces = sem.shape[0]
+        piece = entries // pieces
+        copies = [
+            pltpu.make_async_copy(
+                x_hbm.at[:, pl.ds(p * piece, piece)], xbuf.at[:, pl.ds(p * piece, piece)], sem.at[p]
+            )
+            for p in range(pieces)
+        ]
+        for copy in copies:
+            copy.start()
         xpad[pl.ds(0, halo), :] = flip(lo_ref[...])[rim - halo :]
         xpad[pl.ds(halo + entries, halo), :] = flip(hi_ref[...])[:halo]
         dots_ref[...] = jnp.zeros(dots_ref.shape, dots_ref.dtype)
-        copy.wait()
 
         def turn(c, carry):
             col = pl.multiple_of(c * chunk, chunk)
             xpad[pl.ds(halo + col, chunk), :] = flip(xbuf[:, pl.ds(col, chunk)])
             return carry
 
-        lax.fori_loop(0, entries // chunk, turn, 0)
+        for p in range(pieces):
+            copies[p].wait()
+            lax.fori_loop(p * piece // chunk, (p + 1) * piece // chunk, turn, 0)
 
     def body(j, carry):
         row = g * group + j
@@ -137,7 +146,7 @@
         + [
             pltpu.VMEM((slots, entries), cells.dtype),
             pltpu.VMEM((entries + 2 * HALO * blk, slots), cells.dtype),
-            pltpu.SemaphoreType.DMA((1,)),
+            pltpu.SemaphoreType.DMA((4 if entries % (4 * chunk) == 0 else 1,)),
         ],
     )
     return pl.pallas_call(
@@ -152,22 +161,17 @@
 
 def row_sum(part):
     count = lax.axis_size("row")
-    if count & (count - 1):
-        here = lax.axis_index("row")
-        got = [part] + [
-            lax.ppermute(part, "row", [(i, (i + step) % count) for i in range(count)])
-            for step in range(1, count)
-        ]
-        by_source = jnp.take(jnp.stack(got), (here - jnp.arange(count, dtype=jnp.int32)) % count, axis=0)
-        total = by_source[0]
-        for r in range(1, count):
-            total = total + by_source[r]
-        return total
-    step = 1
-    while step < count:
-        part = part + lax.ppermute(part, "row", [(i, i ^ step) for i in range(count)])
-        step *= 2
-    return part
+    here = lax.axis_index("row")
+    got = [part] + [
+        lax.ppermute(part, "row", [(i, (i + step) % count) for i in range(count)])
+        for step in range(1, count)
+    ]
+    stacked = jnp.stack(got)
+    total = None
+    for source in range(count):
+        term = lax.dynamic_index_in_dim(stacked, (here - source) % count, 0, keepdims=False)
+        total = term if total is None else total + term
+    return total
 
 
 def shards(vectors, counts, offsets, margin_blocks, energy_blocks, block_columns):
@@ -247,8 +251,9 @@
     pencils = row_sum(pencil_dots) / nmat_total
     margin_pencil = pencils[0]
     energy_pencil = pencils[1]
-    margin_diag = jnp.diagonal(margin_pencil)
-    energy_diag = jnp.diagonal(energy_pencil)
+    eye = jnp.arange(vector_count)[:, None] == jnp.arange(vector_count)[None, :]
+    margin_diag = jnp.sum(jnp.where(eye, margin_pencil, 0.0), axis=1)
+    energy_diag = jnp.sum(jnp.where(eye, energy_pencil, 0.0), axis=1)
     theta = jnp.where(
         valid_mask,
         energy_diag / jnp.where(valid_mask, margin_diag, jnp.float32(1.0)),

time: 219 us -> 216 us (0.986); the launches traced: 215 us -> 214 us
  Pallas kernels: 56.5 us -> 52.7 us
  waiting for transfers between devices: 37.2 us -> 39.4 us
    pallas_call x2, Pallas kernels: 56.5 us -> 52.7 us  [block_apply(): pl.pallas_call(kernel, grid_spec=grid_spec, out_shape=out_shape, compiler...]
    gather x2 -> x0, local copies, waits for them, and re-layouts: 2.49 us -> none  [the longest x1 1.25 us: shards(): energy_diag = jnp.diagonal(energy_pencil)]
    ppermute x4 -> x6, waiting for transfers between devices: 16 us -> 18.1 us  [row_sum(): lax.ppermute(part, 'row', [(i, (i + step) % count) for i in range(count)])]
    ppermute x4 -> x6, starting transfers between devices: 5.8 us -> 6.67 us  [row_sum(): lax.ppermute(part, 'row', [(i, (i + step) % count) for i in range(count)])]
    unnamed x22 -> x14, local copies, waits for them, and re-layouts: 49.3 us -> 49.3 us
  transfers between devices with their start and end apart: 12 -> 14, of which waited for: 8 -> 10; matrix products, arithmetic and copies ran while one was open for 24% -> 24% of each run, Pallas kernels for 0% -> 0%
where the time goes in v7:
time: 216 us; the launch traced here: 214 us
  local copies, waits for them, and re-layouts  56 us (26%)
  Pallas kernels  52.7 us (24%)
  waiting for transfers between devices  39.4 us (18%)
  starting transfers between devices  27.3 us (13%)
  other arithmetic  22.8 us (11%)
  matrix products  10.8 us (5%)
  between operations  5.4 us (2%)
    pallas_call x2, Pallas kernels, block_apply(): pl.pallas_call(kernel, grid_spec=grid_spec, out_shape=out_shape, compiler...  52.7 us
    unnamed x14, local copies, waits for them, and re-layouts  49.3 us
    ppermute x6, waiting for transfers between devices, row_sum(): lax.ppermute(part, 'row', [(i, (i + step) % count) for i in range(count)])  18.1 us
    ppermute x2, waiting for transfers between devices, from_behind(): return lax.ppermute(block, axis, route)  14.7 us
    dot_general x3, matrix products, clean(): lax.dot_general(margin_b, wins, (((0,), (0,)), ((), ())), preferred_eleme...  10.8 us
    broadcast_in_dim x1, other arithmetic, shards(): return (residual[None], margin_pencil[None], energy_pencil[None])  9.47 us
    ppermute x6, starting transfers between devices, row_sum(): lax.ppermute(part, 'row', [(i, (i + step) % count) for i in range(count)])  6.67 us
    ppermute x2, starting transfers between devices, from_behind(): return lax.ppermute(block, axis, route)  5.55 us
  transfers between devices with their start and end apart: 14, of which 10 were waited for; matrix products, arithmetic and copies ran while one was open for 24% of the time, Pallas kernels for 0%

profile of v7, /device:TPU:12, one launch (start us, length us, event | category | flops | bytes accessed | tf_op | source)
XLA Modules:
  0.0 214.5 jit_solution(3674700216608492801)
XLA Ops:
  0.6 1.3 fusion.8
  5.2 1.3 add_compare_fusion
  7.8 3.4 %broadcast_select_fusion = bf16[128,24576]{1,0:T(8,128)(2,1)S(1)} fusion(pred[128]{0:T(512)(128)(4,1)S(1)} %iota_compare_fusion.1, bf16[1,128,24576]{2,1,0:T(8,128)(2,1)} %param.6), kind=kLoop, calls=%fused_computation.5 | loop fusion | flops 3145728 | bytes 12583040 | tf_op jit(solution)/shard_map/jit(_where)/select_n | solution.py:217
  11.2 1.6 copy-done.2
  13.9 3.5 %collective-permute-start = (bf16[192,256]{1,0:T(8,128)(2,1)S(1)}, bf16[192,256]{1,0:T(8,128)(2,1)S(1)}, u32[]{:S(2)}, u32[]{:S(2)}) collective-permute-start(bf16[192,256]{1,0:T(8,128)(2,1)S(1)} %get-tuple-element.23), channel_id=1, source_target_pairs={{0,1},{1,2},{2,3},{4,5},{5,6},{6,7},{8,9},{9,10},{10,11},{12,13},{... | collective-permute-start | bytes 294920 | tf_op jit(solution)/shard_map/ppermute | solution.py:27
  17.4 2.4 %collective-permute-start.1 = (bf16[192,256]{1,0:T(8,128)(2,1)S(1)}, bf16[192,256]{1,0:T(8,128)(2,1)S(1)}, u32[]{:S(2)}, u32[]{:S(2)}) collective-permute-start(bf16[192,256]{1,0:T(8,128)(2,1)S(1)} %get-tuple-element.24), channel_id=1, source_target_pairs={{1,0},{2,1},{3,2},{5,4},{6,5},{7,6},{9,8},{10,9},{11,10},{13,12},{... | collective-permute-start | bytes 294920 | tf_op jit(solution)/shard_map/ppermute | solution.py:28
  20.4 3.5 %collective-permute-done.1 = bf16[192,256]{1,0:T(8,128)(2,1)S(1)} collective-permute-done((bf16[192,256]{1,0:T(8,128)(2,1)S(1)}, bf16[192,256]{1,0:T(8,128)(2,1)S(1)}, u32[]{:S(2)}, u32[]{:S(2)}) %collective-permute-start.1) | collective-permute-done | bytes 98336 | tf_op jit(solution)/shard_map/ppermute | solution.py:28
  25.2 1.9 collective-permute-start.3
  27.1 1.8 collective-permute-start.5
  28.9 1.3 pad_maximum_fusion.1
  30.2 3.6 %collective-permute-start.2 = (bf16[32,25088]{1,0:T(8,128)(2,1)}, bf16[32,25088]{1,0:T(8,128)(2,1)S(1)}, u32[]{:S(2)}, u32[]{:S(2)}) collective-permute-start(bf16[32,25088]{1,0:T(8,128)(2,1)} %pad_maximum_fusion.1), channel_id=1, source_target_pairs={{0,4},{4,8},{8,12},{12,16},{16,20},{20,24},{24,28},{1,5},{5,9},{9,... | collective-permute-start | bytes 4816904 | tf_op jit(solution)/shard_map/ppermute | solution.py:19
  33.9 3.7 %collective-permute-start.4 = (bf16[32,25088]{1,0:T(8,128)(2,1)}, bf16[32,25088]{1,0:T(8,128)(2,1)}, u32[]{:S(2)}, u32[]{:S(2)}) collective-permute-start(bf16[32,25088]{1,0:T(8,128)(2,1)} %pad_maximum_fusion.1), channel_id=1, source_target_pairs={{0,8},{8,16},{16,24},{1,9},{9,17},{17,25},{2,10},{10,18},{18,26},{... | collective-permute-start | bytes 4816904 | tf_op jit(solution)/shard_map/ppermute | solution.py:206
  37.5 23.5 %copy.12.refs_0_ = bf16[256,96,288]{2,1,0:T(8,128)(2,1)} copy(bf16[256,96,288]{0,2,1:T(8,128)(2,1)} %param.9) | data formatting | bytes 28311552 | tf_op args[3]
  61.0 23.4 %copy.13.refs_1_ = bf16[256,96,288]{2,1,0:T(8,128)(2,1)} copy(bf16[256,96,288]{0,2,1:T(8,128)(2,1)} %param.10) | data formatting | bytes 28311552 | tf_op args[4]
  84.3 14.7 %collective-permute-done.2 = bf16[32,25088]{1,0:T(8,128)(2,1)S(1)} collective-permute-done((bf16[32,25088]{1,0:T(8,128)(2,1)}, bf16[32,25088]{1,0:T(8,128)(2,1)S(1)}, u32[]{:S(2)}, u32[]{:S(2)}) %collective-permute-start.2) | collective-permute-done | bytes 1605664 | tf_op jit(solution)/shard_map/ppermute | solution.py:19
  99.1 2.5 %collective-permute-start.6 = (bf16[32,25088]{1,0:T(8,128)(2,1)S(1)}, bf16[32,25088]{1,0:T(8,128)(2,1)}, u32[]{:S(2)}, u32[]{:S(2)}) collective-permute-start(bf16[32,25088]{1,0:T(8,128)(2,1)S(1)} %collective-permute-done.2), channel_id=1, source_target_pairs={{0,4},{8,12},{16,20},{24,28},{1,5},{9,13},{17,21},{25,29},{2,6},{1... | collective-permute-start | bytes 4816904 | tf_op jit(solution)/shard_map/ppermute | solution.py:212
  102.5 1.3 collective-permute-start.7
  103.8 1.6 broadcast_select_fusion.2
  105.4 2.4 %collective-permute-done.7 = bf16[32,25088]{1,0:T(8,128)(2,1)S(1)} collective-permute-done((bf16[32,25088]{1,0:T(8,128)(2,1)S(1)}, bf16[32,25088]{1,0:T(8,128)(2,1)S(1)}, u32[]{:S(2)}, u32[]{:S(2)}) %collective-permute-start.7) | collective-permute-done | bytes 1605664 | tf_op jit(solution)/shard_map/ppermute | solution.py:214
  109.4 3.7 %slice.74.x_hbm = bf16[128,24576]{1,0:T(8,128)(2,1)} slice(bf16[128,25088]{1,0:T(8,128)(2,1)S(1)} %pad_maximum_fusion), slice={[0:128], [0:24576]} | slice | bytes 12582912 | tf_op jit(solution)/shard_map/slice | solution.py:228
  114.0 21.5 %shard_map.85 = f32[1,128,128]{2,1,0:T(8,128)} custom-call(s32[768]{0:T(1024)} %reshape.57.shift_ref, s32[1]{0:T(128)} %copy.14.count_ref, bf16[128,24576]{1,0:T(8,128)(2,1)} %slice.74.x_hbm, bf16[128,256]{1,0:T(8,128)(2,1)} %get-tuple-element.26.lo_ref, bf16[128,256]{1,0:T(8,128)(2,1)} %get-tuple-element.25.hi_ref, bf16[256,96,288]{2,1,0:T(8,128)(2,1)} %copy.12.refs_0_, ...), custom_call_target="tpu_custom_call" | custom-call | tf_op jit(solution)/shard_map/pallas_call | solution.py:152
  135.5 1.6 collective-permute-start.8
  138.7 1.5 collective-permute-done.8
  140.2 2.7 %collective-permute-done.9 = f32[128,128]{1,0:T(8,128)S(1)} collective-permute-done((f32[128,128]{1,0:T(8,128)}, f32[128,128]{1,0:T(8,128)S(1)}, u32[]{:S(2)}, u32[]{:S(2)}) %collective-permute-start.9) | collective-permute-done | bytes 65568 | tf_op jit(solution)/shard_map/ppermute | solution.py:166
  143.0 2.8 %collective-permute-done.10 = f32[128,128]{1,0:T(8,128)S(1)} collective-permute-done((f32[128,128]{1,0:T(8,128)}, f32[128,128]{1,0:T(8,128)S(1)}, u32[]{:S(2)}, u32[]{:S(2)}) %collective-permute-start.10) | collective-permute-done | bytes 65568 | tf_op jit(solution)/shard_map/ppermute | solution.py:166
  146.7 9.2 %fusion.x_hbm = bf16[128,24576]{1,0:T(8,128)(2,1)} fusion(bf16[128,128]{1,0:T(8,128)(2,1)S(1)} %fusion.4, bf16[128,24576]{1,0:T(8,128)(2,1)} %copy-done, bf16[128,25088]{1,0:T(8,128)(2,1)} %copy-done.1), kind=kOutput, calls=%fused_computation.1 | convolution fusion | flops 814743552 | bytes 18907136 | tf_op jit(solution)/shard_map/dot_general | solution.py:239
  157.5 31.1 %shard_map.86 = (bf16[128,24576]{1,0:T(8,128)(2,1)}, bf16[128,24576]{1,0:T(8,128)(2,1)}, f32[2,128,128]{2,1,0:T(8,128)}) custom-call(s32[768]{0:T(1024)} %reshape.57.shift_ref, s32[1]{0:T(128)} %copy.14.count_ref, bf16[128,24576]{1,0:T(8,128)(2,1)} %fusion.x_hbm, bf16[128,256]{1,0:T(8,128)(2,1)} %subtract_convert_fusion.2.lo_ref, ...), custom_call_target="tpu_custom_call" | custom-call | tf_op jit(solution)/shard_map/pallas_call | solution.py:152
  188.7 2.4 %collective-permute-start.12 = (f32[2,128,128]{2,1,0:T(8,128)}, f32[2,128,128]{2,1,0:T(8,128)S(1)}, u32[]{:S(2)}, u32[]{:S(2)}) collective-permute-start(f32[2,128,128]{2,1,0:T(8,128)} %get-tuple-element.19), channel_id=1, source_target_pairs={{0,2},{1,3},{2,0},{3,1},{4,6},{5,7},{6,4},{7,5},{8,10},{9,11},{10,... | collective-permute-start | bytes 393224 | tf_op jit(solution)/shard_map/ppermute | solution.py:166
  192.1 3.1 %collective-permute-done.11 = f32[2,128,128]{2,1,0:T(8,128)S(1)} collective-permute-done((f32[2,128,128]{2,1,0:T(8,128)}, f32[2,128,128]{2,1,0:T(8,128)S(1)}, u32[]{:S(2)}, u32[]{:S(2)}) %collective-permute-start.11) | collective-permute-done | bytes 131104 | tf_op jit(solution)/shard_map/ppermute | solution.py:166
  195.2 5.5 %collective-permute-done.12 = f32[2,128,128]{2,1,0:T(8,128)S(1)} collective-permute-done((f32[2,128,128]{2,1,0:T(8,128)}, f32[2,128,128]{2,1,0:T(8,128)S(1)}, u32[]{:S(2)}, u32[]{:S(2)}) %collective-permute-start.12) | collective-permute-done | bytes 131104 | tf_op jit(solution)/shard_map/ppermute | solution.py:166
  200.7 2.5 %collective-permute-done.13 = f32[2,128,128]{2,1,0:T(8,128)S(1)} collective-permute-done((f32[2,128,128]{2,1,0:T(8,128)}, f32[2,128,128]{2,1,0:T(8,128)S(1)}, u32[]{:S(2)}, u32[]{:S(2)}) %collective-permute-start.13) | collective-permute-done | bytes 131104 | tf_op jit(solution)/shard_map/ppermute | solution.py:166
  205.0 9.5 %fusion.1 = bf16[1,128,24576]{2,1,0:T(8,128)(2,1)} fusion(bf16[128,24576]{1,0:T(8,128)(2,1)} %get-tuple-element.20, bf16[128,24576]{1,0:T(8,128)(2,1)} %get-tuple-element.18, f32[128]{0:T(128)S(1)} %divide_select_fusion), kind=kLoop, calls=%fused_computation.4 | loop fusion | flops 15728640 | bytes 18874880 | tf_op jit(solution)/shard_map/broadcast_in_dim | solution.py:265
  (42 shorter events, 13.2 us)
Async XLA Ops:
  7.8 5.1 %copy-start.2 = (bf16[1,128,24576]{2,1,0:T(8,128)(2,1)S(1)}, bf16[1,128,24576]{2,1,0:T(8,128)(2,1)}, u32[]{:S(2)}) copy-start(bf16[1,128,24576]{2,1,0:T(8,128)(2,1)} %param.6) | copy-start | bytes 18874372
  11.2 2.7 %copy-start = (bf16[128,24576]{1,0:T(8,128)(2,1)}, bf16[128,24576]{1,0:T(8,128)(2,1)S(1)}, u32[]{:S(2)}) copy-start(bf16[128,24576]{1,0:T(8,128)(2,1)S(1)} %broadcast_select_fusion) | copy-start | bytes 18874372
  13.9 6.5 %collective-permute-start = (bf16[192,256]{1,0:T(8,128)(2,1)S(1)}, bf16[192,256]{1,0:T(8,128)(2,1)S(1)}, u32[]{:S(2)}, u32[]{:S(2)}) collective-permute-start(bf16[192,256]{1,0:T(8,128)(2,1)S(1)} %get-tuple-element.23), channel_id=1, source_target_pairs={{0,1},{1,2},{2,3},{4,5},{5,6},{6,7},{8,9},{9,10},{10,11},{12,13},{... | collective-permute-start | bytes 294920 | tf_op jit(solution)/shard_map/ppermute | solution.py:27
  17.4 6.5 %collective-permute-start.1 = (bf16[192,256]{1,0:T(8,128)(2,1)S(1)}, bf16[192,256]{1,0:T(8,128)(2,1)S(1)}, u32[]{:S(2)}, u32[]{:S(2)}) collective-permute-start(bf16[192,256]{1,0:T(8,128)(2,1)S(1)} %get-tuple-element.24), channel_id=1, source_target_pairs={{1,0},{2,1},{3,2},{5,4},{6,5},{7,6},{9,8},{10,9},{11,10},{13,12},{... | collective-permute-start | bytes 294920 | tf_op jit(solution)/shard_map/ppermute | solution.py:28
  25.2 59.2 %collective-permute-start.3 = (bf16[32,25088]{1,0:T(8,128)(2,1)}, bf16[32,25088]{1,0:T(8,128)(2,1)S(1)}, u32[]{:S(2)}, u32[]{:S(2)}) collective-permute-start(bf16[32,25088]{1,0:T(8,128)(2,1)} %pad_maximum_fusion.2), channel_id=1, source_target_pairs={{4,0},{8,4},{12,8},{16,12},{20,16},{24,20},{28,24},{5,1},{9,5},{13... | collective-permute-start | bytes 4816904 | tf_op jit(solution)/shard_map/ppermute | solution.py:19
  27.1 57.3 %collective-permute-start.5 = (bf16[32,25088]{1,0:T(8,128)(2,1)}, bf16[32,25088]{1,0:T(8,128)(2,1)}, u32[]{:S(2)}, u32[]{:S(2)}) collective-permute-start(bf16[32,25088]{1,0:T(8,128)(2,1)} %pad_maximum_fusion.2), channel_id=1, source_target_pairs={{12,4},{20,12},{28,20},{13,5},{21,13},{29,21},{14,6},{22,14},{30,2... | collective-permute-start | bytes 4816904 | tf_op jit(solution)/shard_map/ppermute | solution.py:207
  30.2 68.8 %collective-permute-start.2 = (bf16[32,25088]{1,0:T(8,128)(2,1)}, bf16[32,25088]{1,0:T(8,128)(2,1)S(1)}, u32[]{:S(2)}, u32[]{:S(2)}) collective-permute-start(bf16[32,25088]{1,0:T(8,128)(2,1)} %pad_maximum_fusion.1), channel_id=1, source_target_pairs={{0,4},{4,8},{8,12},{12,16},{16,20},{20,24},{24,28},{1,5},{5,9},{9,... | collective-permute-start | bytes 4816904 | tf_op jit(solution)/shard_map/ppermute | solution.py:19
  33.9 65.2 %collective-permute-start.4 = (bf16[32,25088]{1,0:T(8,128)(2,1)}, bf16[32,25088]{1,0:T(8,128)(2,1)}, u32[]{:S(2)}, u32[]{:S(2)}) collective-permute-start(bf16[32,25088]{1,0:T(8,128)(2,1)} %pad_maximum_fusion.1), channel_id=1, source_target_pairs={{0,8},{8,16},{16,24},{1,9},{9,17},{17,25},{2,10},{10,18},{18,26},{... | collective-permute-start | bytes 4816904 | tf_op jit(solution)/shard_map/ppermute | solution.py:206
  61.0 40.6 %copy-start.5 = (s32[256,3]{0,1:T(4,128)S(1)}, s32[256,3]{0,1:T(4,128)}, u32[]{:S(2)}) copy-start(s32[256,3]{0,1:T(4,128)} %param.11) | copy-start | bytes 9220
  99.1 4.7 %collective-permute-start.6 = (bf16[32,25088]{1,0:T(8,128)(2,1)S(1)}, bf16[32,25088]{1,0:T(8,128)(2,1)}, u32[]{:S(2)}, u32[]{:S(2)}) collective-permute-start(bf16[32,25088]{1,0:T(8,128)(2,1)S(1)} %collective-permute-done.2), channel_id=1, source_target_pairs={{0,4},{8,12},{16,20},{24,28},{1,5},{9,13},{17,21},{25,29},{2,6},{1... | collective-permute-start | bytes 4816904 | tf_op jit(solution)/shard_map/ppermute | solution.py:212
  102.5 5.3 %collective-permute-start.7 = (bf16[32,25088]{1,0:T(8,128)(2,1)S(1)}, bf16[32,25088]{1,0:T(8,128)(2,1)S(1)}, u32[]{:S(2)}, u32[]{:S(2)}) collective-permute-start(bf16[32,25088]{1,0:T(8,128)(2,1)S(1)} %collective-permute-done.3), channel_id=1, source_target_pairs={{4,0},{12,8},{20,16},{28,24},{5,1},{13,9},{21,17},{29,25},{6,2},{1... | collective-permute-start | bytes 4816904 | tf_op jit(solution)/shard_map/ppermute | solution.py:214
  109.4 4.6 %copy-start.1 = (bf16[128,25088]{1,0:T(8,128)(2,1)}, bf16[128,25088]{1,0:T(8,128)(2,1)S(1)}, u32[]{:S(2)}) copy-start(bf16[128,25088]{1,0:T(8,128)(2,1)S(1)} %pad_maximum_fusion) | copy-start | bytes 19267588
  135.5 4.7 %collective-permute-start.8 = (f32[128,128]{1,0:T(8,128)}, f32[128,128]{1,0:T(8,128)S(1)}, u32[]{:S(2)}, u32[]{:S(2)}) collective-permute-start(f32[128,128]{1,0:T(8,128)} %bitcast.42), channel_id=1, source_target_pairs={{0,1},{1,2},{2,3},{3,0},{4,5},{5,6},{6,7},{7,4},{8,9},{9,10},{10,1... | collective-permute-start | bytes 196616 | tf_op jit(solution)/shard_map/ppermute | solution.py:166
  137.2 5.8 %collective-permute-start.9 = (f32[128,128]{1,0:T(8,128)}, f32[128,128]{1,0:T(8,128)S(1)}, u32[]{:S(2)}, u32[]{:S(2)}) collective-permute-start(f32[128,128]{1,0:T(8,128)} %bitcast.43), channel_id=1, source_target_pairs={{0,2},{1,3},{2,0},{3,1},{4,6},{5,7},{6,4},{7,5},{8,10},{9,11},{10,... | collective-permute-start | bytes 196616 | tf_op jit(solution)/shard_map/ppermute | solution.py:166
  138.4 7.3 %collective-permute-start.10 = (f32[128,128]{1,0:T(8,128)}, f32[128,128]{1,0:T(8,128)S(1)}, u32[]{:S(2)}, u32[]{:S(2)}) collective-permute-start(f32[128,128]{1,0:T(8,128)} %bitcast.44), channel_id=1, source_target_pairs={{0,3},{1,0},{2,1},{3,2},{4,7},{5,4},{6,5},{7,6},{8,11},{9,8},{10,9... | collective-permute-start | bytes 196616 | tf_op jit(solution)/shard_map/ppermute | solution.py:166
  146.6 9.2 %copy-start.4 = (bf16[128,256]{1,0:T(8,128)(2,1)S(1)}, bf16[128,256]{1,0:T(8,128)(2,1)}, u32[]{:S(2)}) copy-start(bf16[128,256]{1,0:T(8,128)(2,1)} %get-tuple-element.25.hi_ref) | copy-start | bytes 196612
  146.7 10.0 %copy-start.3 = (bf16[128,256]{1,0:T(8,128)(2,1)S(1)}, bf16[128,256]{1,0:T(8,128)(2,1)}, u32[]{:S(2)}) copy-start(bf16[128,256]{1,0:T(8,128)(2,1)} %get-tuple-element.26.lo_ref) | copy-start | bytes 196612
  188.6 6.6 %collective-permute-start.11 = (f32[2,128,128]{2,1,0:T(8,128)}, f32[2,128,128]{2,1,0:T(8,128)S(1)}, u32[]{:S(2)}, u32[]{:S(2)}) collective-permute-start(f32[2,128,128]{2,1,0:T(8,128)} %get-tuple-element.19), channel_id=1, source_target_pairs={{0,1},{1,2},{2,3},{3,0},{4,5},{5,6},{6,7},{7,4},{8,9},{9,10},{10,1... | collective-permute-start | bytes 393224 | tf_op jit(solution)/shard_map/ppermute | solution.py:166
  188.7 12.0 %collective-permute-start.12 = (f32[2,128,128]{2,1,0:T(8,128)}, f32[2,128,128]{2,1,0:T(8,128)S(1)}, u32[]{:S(2)}, u32[]{:S(2)}) collective-permute-start(f32[2,128,128]{2,1,0:T(8,128)} %get-tuple-element.19), channel_id=1, source_target_pairs={{0,2},{1,3},{2,0},{3,1},{4,6},{5,7},{6,4},{7,5},{8,10},{9,11},{10,... | collective-permute-start | bytes 393224 | tf_op jit(solution)/shard_map/ppermute | solution.py:166
  191.1 12.1 %collective-permute-start.13 = (f32[2,128,128]{2,1,0:T(8,128)}, f32[2,128,128]{2,1,0:T(8,128)S(1)}, u32[]{:S(2)}, u32[]{:S(2)}) collective-permute-start(f32[2,128,128]{2,1,0:T(8,128)} %get-tuple-element.19), channel_id=1, source_target_pairs={{0,3},{1,0},{2,1},{3,2},{4,7},{5,4},{6,5},{7,6},{8,11},{9,8},{10,9... | collective-permute-start | bytes 393224 | tf_op jit(solution)/shard_map/ppermute | solution.py:166

commit v8 on v7

--- a/solution.py
+++ b/solution.py
@@ -215,7 +215,20 @@
         return [upper_2, upper_1, lower_1, lower_2]
 
     masked = jnp.where(valid_mask[:, None], own_vectors, jnp.zeros((), own_vectors.dtype))
-    below, above = row_halos(jnp.concatenate([upper_window, lower_window, masked], axis=0), rim)
+
+    def edge_rows(start, cols):
+        rows = lax.dynamic_slice_in_dim(own_vectors[:, cols], start, WIN, 0)
+        return jnp.where(window_rows + start < counts[0], rows, jnp.zeros((), rows.dtype))
+
+    def edges_of(cols):
+        return jnp.concatenate(
+            [edge_rows(offsets[0, 1], cols), edge_rows(offsets[0, 0], cols), masked[:, cols]], axis=0
+        )
+
+    below = lax.ppermute(
+        edges_of(slice(entries - rim, entries)), "row", [(i, i + 1) for i in range(lax.axis_size("row") - 1)]
+    )
+    above = lax.ppermute(edges_of(slice(0, rim)), "row", [(i + 1, i) for i in range(lax.axis_size("row") - 1)])
     masked_lower, masked_upper = below[2 * WIN :], above[2 * WIN :]
     upper_ext = jnp.concatenate([upper_window, below[:WIN], above[:WIN]], axis=1)
     lower_ext = jnp.concatenate([lower_window, below[WIN : 2 * WIN], above[WIN : 2 * WIN]], axis=1)
@@ -248,12 +261,13 @@
         clean(masked_lower, windows_lower),
         clean(masked_upper, windows_upper),
     )
+    eye = jnp.arange(vector_count)[:, None] == jnp.arange(vector_count)[None, :]
+    diagonals = row_sum(jnp.sum(jnp.where(eye[None], pencil_dots, 0.0), axis=2)) / nmat_total
+    margin_diag = diagonals[0]
+    energy_diag = diagonals[1]
     pencils = row_sum(pencil_dots) / nmat_total
     margin_pencil = pencils[0]
     energy_pencil = pencils[1]
-    eye = jnp.arange(vector_count)[:, None] == jnp.arange(vector_count)[None, :]
-    margin_diag = jnp.sum(jnp.where(eye, margin_pencil, 0.0), axis=1)
-    energy_diag = jnp.sum(jnp.where(eye, energy_pencil, 0.0), axis=1)
     theta = jnp.where(
         valid_mask,
         energy_diag / jnp.where(valid_mask, margin_diag, jnp.float32(1.0)),

time: 216 us -> 208 us (0.963)
  waiting for transfers between devices: 39.4 us -> 26.1 us
  other arithmetic: 22.8 us -> 26.9 us
  starting transfers between devices: 27.3 us -> 31.4 us
  matrix products: 10.8 us -> 7.3 us
    ppermute x6 -> x9, waiting for transfers between devices: 18.1 us -> 7.94 us  [row_sum(): lax.ppermute(part, 'row', [(i, (i + step) % count) for i in range(count)])]
    ppermute x6 -> x9, starting transfers between devices: 6.67 us -> 10.8 us  [row_sum(): lax.ppermute(part, 'row', [(i, (i + step) % count) for i in range(count)])]
    dot_general x3, matrix products: 10.8 us -> 7.3 us  [clean(): lax.dot_general(margin_b, wins, (((0,), (0,)), ((), ())), preferred_eleme...]
    ppermute x2, waiting for transfers between devices: 4.14 us -> 0.99 us  [the longest x1 0.98 us: shards(): lax.ppermute(edges_of(slice(0, rim)), 'row', [(i + 1, i) for i in range(l...]
    select_n x1 -> x2, other arithmetic: 0.98 us -> 3.22 us  [the longest x1 3.13 us: shards(): jnp.where(window_rows + offsets[0, 0] < counts[0], lax.dynamic_slice_in_d...]
    unnamed x14 -> x18, local copies, waits for them, and re-layouts: 49.3 us -> 49.4 us
  transfers between devices with their start and end apart: 14 -> 17, of which waited for: 10 -> 7; matrix products, arithmetic and copies ran while one was open for 24% -> 31% of each run, Pallas kernels for 0% -> 0%
where the time goes in v8:
time: 208 us; the launch traced here: 206 us
  local copies, waits for them, and re-layouts  56.6 us (27%)
  Pallas kernels  52.6 us (25%)
  starting transfers between devices  31.4 us (15%)
  other arithmetic  26.9 us (13%)
  waiting for transfers between devices  26.1 us (13%)
  matrix products  7.3 us (4%)
  between operations  5.46 us (3%)
    pallas_call x2, Pallas kernels, block_apply(): pl.pallas_call(kernel, grid_spec=grid_spec, out_shape=out_shape, compiler...  52.6 us
    unnamed x18, local copies, waits for them, and re-layouts  49.4 us
    ppermute x2, waiting for transfers between devices, from_behind(): return lax.ppermute(block, axis, route)  14.8 us
    ppermute x9, starting transfers between devices, row_sum(): lax.ppermute(part, 'row', [(i, (i + step) % count) for i in range(count)])  10.8 us
    broadcast_in_dim x1, other arithmetic, shards(): return (residual[None], margin_pencil[None], energy_pencil[None])  9.49 us
    ppermute x9, waiting for transfers between devices, row_sum(): lax.ppermute(part, 'row', [(i, (i + step) % count) for i in range(count)])  7.94 us
    dot_general x3, matrix products, clean(): lax.dot_general(margin_b, wins, (((0,), (0,)), ((), ())), preferred_eleme...  7.3 us
    ppermute x2, starting transfers between devices, from_behind(): return lax.ppermute(block, axis, route)  5.56 us
  transfers between devices with their start and end apart: 17, of which 7 were waited for; matrix products, arithmetic and copies ran while one was open for 31% of the time, Pallas kernels for 0%

profile of v8, /device:TPU:12, one launch (start us, length us, event | category | flops | bytes accessed | tf_op | source)
XLA Modules:
  0.0 206.2 jit_solution(9965200295267027022)
XLA Ops:
  0.6 1.3 fusion.14
  5.2 1.3 add_compare_fusion
  7.4 3.3 %broadcast_select_fusion = bf16[128,24576]{1,0:T(8,128)(2,1)S(1)} fusion(pred[128]{0:T(512)(128)(4,1)S(1)} %iota_compare_fusion.1, bf16[1,128,24576]{2,1,0:T(8,128)(2,1)} %param.6), kind=kLoop, calls=%fused_computation.5 | loop fusion | flops 3145728 | bytes 12583040 | tf_op jit(solution)/shard_map/jit(_where)/select_n | solution.py:217
  10.7 2.6 %copy-done = bf16[128,24576]{1,0:T(8,128)(2,1)} copy-done((bf16[128,24576]{1,0:T(8,128)(2,1)}, bf16[128,24576]{1,0:T(8,128)(2,1)S(1)}, u32[]{:S(2)}) %copy-start) | copy-done | bytes 6291480
  14.7 3.5 %collective-permute-start = (bf16[192,256]{1,0:T(8,128)(2,1)S(1)}, bf16[192,256]{1,0:T(8,128)(2,1)S(1)}, u32[]{:S(2)}, u32[]{:S(2)}) collective-permute-start(bf16[192,256]{1,0:T(8,128)(2,1)S(1)} %pad_maximum_fusion.5), channel_id=1, source_target_pairs={{0,1},{1,2},{2,3},{4,5},{5,6},{6,7},{8,9},{9,10},{10,11},{12,13},{... | collective-permute-start | bytes 294920 | tf_op jit(solution)/shard_map/ppermute | solution.py:228
  18.2 2.4 %collective-permute-start.1 = (bf16[192,256]{1,0:T(8,128)(2,1)S(1)}, bf16[192,256]{1,0:T(8,128)(2,1)S(1)}, u32[]{:S(2)}, u32[]{:S(2)}) collective-permute-start(bf16[192,256]{1,0:T(8,128)(2,1)S(1)} %pad_maximum_fusion.6), channel_id=1, source_target_pairs={{1,0},{2,1},{3,2},{5,4},{6,5},{7,6},{9,8},{10,9},{11,10},{13,12},{... | collective-permute-start | bytes 294920 | tf_op jit(solution)/shard_map/ppermute | solution.py:231
  20.6 3.1 %bitcast_select_fusion = (bf16[32,24576]{1,0:T(8,128)(2,1)S(1)}, bf16[32,24576]{1,0:T(8,128)(2,1)S(1)}) fusion(bf16[1,128,24576]{2,1,0:T(8,128)(2,1)} %param.6, s32[]{:T(128)S(6)} %select_n.133, pred[32]{0:T(512)(128)(4,1)S(1)} %get-tuple-element.43, s32[]{:T(128)S(6)} %select_n.130, pred[32]{0:T(512)(128)(4,1)S(1)} %get-tuple-element.44), kind=kLoop, calls=%fused_computation.10 | loop fusion | flops 1572864 | bytes 6291528 | tf_op jit(solution)/shard_map/jit(_where)/select_n | solution.py:184
  24.7 1.3 pad_maximum_fusion.2
  26.0 1.9 collective-permute-start.3
  27.9 1.8 collective-permute-start.5
  29.7 1.3 pad_maximum_fusion.1
  31.0 3.7 %collective-permute-start.2 = (bf16[32,25088]{1,0:T(8,128)(2,1)}, bf16[32,25088]{1,0:T(8,128)(2,1)S(1)}, u32[]{:S(2)}, u32[]{:S(2)}) collective-permute-start(bf16[32,25088]{1,0:T(8,128)(2,1)} %pad_maximum_fusion.1), channel_id=1, source_target_pairs={{0,4},{4,8},{8,12},{12,16},{16,20},{20,24},{24,28},{1,5},{5,9},{9,... | collective-permute-start | bytes 4816904 | tf_op jit(solution)/shard_map/ppermute | solution.py:19
  34.6 3.6 %collective-permute-start.4 = (bf16[32,25088]{1,0:T(8,128)(2,1)}, bf16[32,25088]{1,0:T(8,128)(2,1)}, u32[]{:S(2)}, u32[]{:S(2)}) collective-permute-start(bf16[32,25088]{1,0:T(8,128)(2,1)} %pad_maximum_fusion.1), channel_id=1, source_target_pairs={{0,8},{8,16},{16,24},{1,9},{9,17},{17,25},{2,10},{10,18},{18,26},{... | collective-permute-start | bytes 4816904 | tf_op jit(solution)/shard_map/ppermute | solution.py:206
  38.3 23.5 %copy.12.refs_0_ = bf16[256,96,288]{2,1,0:T(8,128)(2,1)} copy(bf16[256,96,288]{0,2,1:T(8,128)(2,1)} %param.9) | data formatting | bytes 28311552 | tf_op args[3]
  61.8 23.3 %copy.13.refs_1_ = bf16[256,96,288]{2,1,0:T(8,128)(2,1)} copy(bf16[256,96,288]{0,2,1:T(8,128)(2,1)} %param.10) | data formatting | bytes 28311552 | tf_op args[4]
  85.1 14.8 %collective-permute-done.2 = bf16[32,25088]{1,0:T(8,128)(2,1)S(1)} collective-permute-done((bf16[32,25088]{1,0:T(8,128)(2,1)}, bf16[32,25088]{1,0:T(8,128)(2,1)S(1)}, u32[]{:S(2)}, u32[]{:S(2)}) %collective-permute-start.2) | collective-permute-done | bytes 1605664 | tf_op jit(solution)/shard_map/ppermute | solution.py:19
  99.9 2.5 %collective-permute-start.6 = (bf16[32,25088]{1,0:T(8,128)(2,1)S(1)}, bf16[32,25088]{1,0:T(8,128)(2,1)}, u32[]{:S(2)}, u32[]{:S(2)}) collective-permute-start(bf16[32,25088]{1,0:T(8,128)(2,1)S(1)} %collective-permute-done.2), channel_id=1, source_target_pairs={{0,4},{8,12},{16,20},{24,28},{1,5},{9,13},{17,21},{25,29},{2,6},{1... | collective-permute-start | bytes 4816904 | tf_op jit(solution)/shard_map/ppermute | solution.py:212
  103.3 1.3 collective-permute-start.7
  104.6 1.6 broadcast_select_fusion.2
  106.2 2.4 %collective-permute-done.7 = bf16[32,25088]{1,0:T(8,128)(2,1)S(1)} collective-permute-done((bf16[32,25088]{1,0:T(8,128)(2,1)S(1)}, bf16[32,25088]{1,0:T(8,128)(2,1)S(1)}, u32[]{:S(2)}, u32[]{:S(2)}) %collective-permute-start.7) | collective-permute-done | bytes 1605664 | tf_op jit(solution)/shard_map/ppermute | solution.py:214
  109.5 2.5 %pad_maximum_fusion = bf16[128,25088]{1,0:T(8,128)(2,1)S(1)} fusion(bf16[32,25088]{1,0:T(8,128)(2,1)S(1)} %broadcast_select_fusion.1, bf16[32,25088]{1,0:T(8,128)(2,1)S(1)} %collective-permute-done.3, bf16[32,25088]{1,0:T(8,128)(2,1)} %copy-done.1, bf16[32,25088]{1,0:T(8,128)(2,1)S(1)} %broadcast_select_fusion.2), kind=kLoop, calls=%fused_computation.3 | loop fusion | flops 25690112 | bytes 12845056 | tf_op jit(solution)/shard_map/concatenate | solution.py:240
  112.1 3.3 %slice.102.x_hbm = bf16[128,24576]{1,0:T(8,128)(2,1)} slice(bf16[128,25088]{1,0:T(8,128)(2,1)S(1)} %pad_maximum_fusion), slice={[0:128], [0:24576]} | slice | bytes 12582912 | tf_op jit(solution)/shard_map/slice | solution.py:241
  115.4 21.5 %shard_map.85 = f32[1,128,128]{2,1,0:T(8,128)} custom-call(s32[768]{0:T(1024)} %reshape.80.shift_ref, s32[1]{0:T(128)} %copy.14.count_ref, bf16[128,24576]{1,0:T(8,128)(2,1)} %slice.102.x_hbm, bf16[128,256]{1,0:T(8,128)(2,1)} %get-tuple-element.22.lo_ref, bf16[128,256]{1,0:T(8,128)(2,1)} %get-tuple-element.21.hi_ref, bf16[256,96,288]{2,1,0:T(8,128)(2,1)} %copy.12.refs_0_, ...), custom_call_target="tpu_custom_call" | custom-call | tf_op jit(solution)/shard_map/pallas_call | solution.py:152
  136.9 1.6 collective-permute-start.8
  141.6 2.7 %collective-permute-done.9 = f32[128,128]{1,0:T(8,128)S(1)} collective-permute-done((f32[128,128]{1,0:T(8,128)}, f32[128,128]{1,0:T(8,128)S(1)}, u32[]{:S(2)}, u32[]{:S(2)}) %collective-permute-start.9) | collective-permute-done | bytes 65568 | tf_op jit(solution)/shard_map/ppermute | solution.py:166
  144.4 2.8 %collective-permute-done.10 = f32[128,128]{1,0:T(8,128)S(1)} collective-permute-done((f32[128,128]{1,0:T(8,128)}, f32[128,128]{1,0:T(8,128)S(1)}, u32[]{:S(2)}, u32[]{:S(2)}) %collective-permute-start.10) | collective-permute-done | bytes 65568 | tf_op jit(solution)/shard_map/ppermute | solution.py:166
  148.1 5.7 %fusion.x_hbm = bf16[128,24576]{1,0:T(8,128)(2,1)} fusion(bf16[128,128]{1,0:T(8,128)(2,1)S(1)} %fusion.2, bf16[128,24576]{1,0:T(8,128)(2,1)} %copy-done, bf16[128,25088]{1,0:T(8,128)(2,1)S(1)} %pad_maximum_fusion), kind=kOutput, calls=%fused_computation.1 | convolution fusion | flops 814743552 | bytes 18907136 | tf_op jit(solution)/shard_map/dot_general | solution.py:252
  155.4 31.0 %shard_map.86 = (bf16[128,24576]{1,0:T(8,128)(2,1)}, bf16[128,24576]{1,0:T(8,128)(2,1)}, f32[2,128,128]{2,1,0:T(8,128)}) custom-call(s32[768]{0:T(1024)} %reshape.80.shift_ref, s32[1]{0:T(128)} %copy.14.count_ref, bf16[128,24576]{1,0:T(8,128)(2,1)} %fusion.x_hbm, bf16[128,256]{1,0:T(8,128)(2,1)} %subtract_convert_fusion.2.lo_ref, ...), custom_call_target="tpu_custom_call" | custom-call | tf_op jit(solution)/shard_map/pallas_call | solution.py:152
  187.5 2.4 %collective-permute-start.12 = (f32[2,128]{1,0:T(2,128)S(1)}, f32[2,128]{1,0:T(2,128)S(1)}, u32[]{:S(2)}, u32[]{:S(2)}) collective-permute-start(f32[2,128]{1,0:T(2,128)S(1)} %select_reduce_fusion), channel_id=1, source_target_pairs={{0,2},{1,3},{2,0},{3,1},{4,6},{5,7},{6,4},{7,5},{8,10},{9,11},{10,... | collective-permute-start | bytes 3080 | tf_op jit(solution)/shard_map/ppermute | solution.py:166
  191.9 2.4 %collective-permute-start.15 = (f32[2,128,128]{2,1,0:T(8,128)}, f32[2,128,128]{2,1,0:T(8,128)S(1)}, u32[]{:S(2)}, u32[]{:S(2)}) collective-permute-start(f32[2,128,128]{2,1,0:T(8,128)} %get-tuple-element.19), channel_id=1, source_target_pairs={{0,2},{1,3},{2,0},{3,1},{4,6},{5,7},{6,4},{7,5},{8,10},{9,11},{10,... | collective-permute-start | bytes 393224 | tf_op jit(solution)/shard_map/ppermute | solution.py:166
  194.5 9.5 %fusion.1 = bf16[1,128,24576]{2,1,0:T(8,128)(2,1)} fusion(bf16[128,24576]{1,0:T(8,128)(2,1)} %get-tuple-element.20, bf16[128,24576]{1,0:T(8,128)(2,1)} %get-tuple-element.18, f32[128]{0:T(128)S(1)} %fusion.8), kind=kLoop, calls=%fused_computation.4 | loop fusion | flops 15728640 | bytes 18874880 | tf_op jit(solution)/shard_map/broadcast_in_dim | solution.py:279
  204.0 1.5 collective-permute-done.16
  (59 shorter events, 13.5 us)
Async XLA Ops:
  10.7 2.6 %copy-start = (bf16[128,24576]{1,0:T(8,128)(2,1)}, bf16[128,24576]{1,0:T(8,128)(2,1)S(1)}, u32[]{:S(2)}) copy-start(bf16[128,24576]{1,0:T(8,128)(2,1)S(1)} %broadcast_select_fusion) | copy-start | bytes 18874372
  14.7 9.0 %collective-permute-start = (bf16[192,256]{1,0:T(8,128)(2,1)S(1)}, bf16[192,256]{1,0:T(8,128)(2,1)S(1)}, u32[]{:S(2)}, u32[]{:S(2)}) collective-permute-start(bf16[192,256]{1,0:T(8,128)(2,1)S(1)} %pad_maximum_fusion.5), channel_id=1, source_target_pairs={{0,1},{1,2},{2,3},{4,5},{5,6},{6,7},{8,9},{9,10},{10,11},{12,13},{... | collective-permute-start | bytes 294920 | tf_op jit(solution)/shard_map/ppermute | solution.py:228
  18.2 6.5 %collective-permute-start.1 = (bf16[192,256]{1,0:T(8,128)(2,1)S(1)}, bf16[192,256]{1,0:T(8,128)(2,1)S(1)}, u32[]{:S(2)}, u32[]{:S(2)}) collective-permute-start(bf16[192,256]{1,0:T(8,128)(2,1)S(1)} %pad_maximum_fusion.6), channel_id=1, source_target_pairs={{1,0},{2,1},{3,2},{5,4},{6,5},{7,6},{9,8},{10,9},{11,10},{13,12},{... | collective-permute-start | bytes 294920 | tf_op jit(solution)/shard_map/ppermute | solution.py:231
  24.7 6.3 %copy-start.5 = (bf16[192,256]{1,0:T(8,128)(2,1)}, bf16[192,256]{1,0:T(8,128)(2,1)S(1)}, u32[]{:S(2)}) copy-start(bf16[192,256]{1,0:T(8,128)(2,1)S(1)} %collective-permute-done.1) | copy-start | bytes 294916
  26.0 59.1 %collective-permute-start.3 = (bf16[32,25088]{1,0:T(8,128)(2,1)}, bf16[32,25088]{1,0:T(8,128)(2,1)S(1)}, u32[]{:S(2)}, u32[]{:S(2)}) collective-permute-start(bf16[32,25088]{1,0:T(8,128)(2,1)} %pad_maximum_fusion.2), channel_id=1, source_target_pairs={{4,0},{8,4},{12,8},{16,12},{20,16},{24,20},{28,24},{5,1},{9,5},{13... | collective-permute-start | bytes 4816904 | tf_op jit(solution)/shard_map/ppermute | solution.py:19
  27.9 57.2 %collective-permute-start.5 = (bf16[32,25088]{1,0:T(8,128)(2,1)}, bf16[32,25088]{1,0:T(8,128)(2,1)}, u32[]{:S(2)}, u32[]{:S(2)}) collective-permute-start(bf16[32,25088]{1,0:T(8,128)(2,1)} %pad_maximum_fusion.2), channel_id=1, source_target_pairs={{12,4},{20,12},{28,20},{13,5},{21,13},{29,21},{14,6},{22,14},{30,2... | collective-permute-start | bytes 4816904 | tf_op jit(solution)/shard_map/ppermute | solution.py:207
  31.0 68.9 %collective-permute-start.2 = (bf16[32,25088]{1,0:T(8,128)(2,1)}, bf16[32,25088]{1,0:T(8,128)(2,1)S(1)}, u32[]{:S(2)}, u32[]{:S(2)}) collective-permute-start(bf16[32,25088]{1,0:T(8,128)(2,1)} %pad_maximum_fusion.1), channel_id=1, source_target_pairs={{0,4},{4,8},{8,12},{12,16},{16,20},{20,24},{24,28},{1,5},{5,9},{9,... | collective-permute-start | bytes 4816904 | tf_op jit(solution)/shard_map/ppermute | solution.py:19
  34.6 65.2 %collective-permute-start.4 = (bf16[32,25088]{1,0:T(8,128)(2,1)}, bf16[32,25088]{1,0:T(8,128)(2,1)}, u32[]{:S(2)}, u32[]{:S(2)}) collective-permute-start(bf16[32,25088]{1,0:T(8,128)(2,1)} %pad_maximum_fusion.1), channel_id=1, source_target_pairs={{0,8},{8,16},{16,24},{1,9},{9,17},{17,25},{2,10},{10,18},{18,26},{... | collective-permute-start | bytes 4816904 | tf_op jit(solution)/shard_map/ppermute | solution.py:206
  61.8 40.6 %copy-start.7 = (s32[256,3]{0,1:T(4,128)S(1)}, s32[256,3]{0,1:T(4,128)}, u32[]{:S(2)}) copy-start(s32[256,3]{0,1:T(4,128)} %param.11) | copy-start | bytes 9220
  99.9 9.0 %copy-start.1 = (bf16[32,25088]{1,0:T(8,128)(2,1)}, bf16[32,25088]{1,0:T(8,128)(2,1)S(1)}, u32[]{:S(2)}) copy-start(bf16[32,25088]{1,0:T(8,128)(2,1)S(1)} %collective-permute-done.2) | copy-start | bytes 4816900
  99.9 4.7 %collective-permute-start.6 = (bf16[32,25088]{1,0:T(8,128)(2,1)S(1)}, bf16[32,25088]{1,0:T(8,128)(2,1)}, u32[]{:S(2)}, u32[]{:S(2)}) collective-permute-start(bf16[32,25088]{1,0:T(8,128)(2,1)S(1)} %collective-permute-done.2), channel_id=1, source_target_pairs={{0,4},{8,12},{16,20},{24,28},{1,5},{9,13},{17,21},{25,29},{2,6},{1... | collective-permute-start | bytes 4816904 | tf_op jit(solution)/shard_map/ppermute | solution.py:212
  103.3 5.3 %collective-permute-start.7 = (bf16[32,25088]{1,0:T(8,128)(2,1)S(1)}, bf16[32,25088]{1,0:T(8,128)(2,1)S(1)}, u32[]{:S(2)}, u32[]{:S(2)}) collective-permute-start(bf16[32,25088]{1,0:T(8,128)(2,1)S(1)} %collective-permute-done.3), channel_id=1, source_target_pairs={{4,0},{12,8},{20,16},{28,24},{5,1},{13,9},{21,17},{29,25},{6,2},{1... | collective-permute-start | bytes 4816904 | tf_op jit(solution)/shard_map/ppermute | solution.py:214
  136.9 4.7 %collective-permute-start.8 = (f32[128,128]{1,0:T(8,128)}, f32[128,128]{1,0:T(8,128)S(1)}, u32[]{:S(2)}, u32[]{:S(2)}) collective-permute-start(f32[128,128]{1,0:T(8,128)} %bitcast.48), channel_id=1, source_target_pairs={{0,1},{1,2},{2,3},{3,0},{4,5},{5,6},{6,7},{7,4},{8,9},{9,10},{10,1... | collective-permute-start | bytes 196616 | tf_op jit(solution)/shard_map/ppermute | solution.py:166
  138.6 5.8 %collective-permute-start.9 = (f32[128,128]{1,0:T(8,128)}, f32[128,128]{1,0:T(8,128)S(1)}, u32[]{:S(2)}, u32[]{:S(2)}) collective-permute-start(f32[128,128]{1,0:T(8,128)} %bitcast.49), channel_id=1, source_target_pairs={{0,2},{1,3},{2,0},{3,1},{4,6},{5,7},{6,4},{7,5},{8,10},{9,11},{10,... | collective-permute-start | bytes 196616 | tf_op jit(solution)/shard_map/ppermute | solution.py:166
  139.8 7.3 %collective-permute-start.10 = (f32[128,128]{1,0:T(8,128)}, f32[128,128]{1,0:T(8,128)S(1)}, u32[]{:S(2)}, u32[]{:S(2)}) collective-permute-start(f32[128,128]{1,0:T(8,128)} %bitcast.50), channel_id=1, source_target_pairs={{0,3},{1,0},{2,1},{3,2},{4,7},{5,4},{6,5},{7,6},{8,11},{9,8},{10,9... | collective-permute-start | bytes 196616 | tf_op jit(solution)/shard_map/ppermute | solution.py:166
  148.0 5.7 %copy-start.3 = (bf16[128,256]{1,0:T(8,128)(2,1)S(1)}, bf16[128,256]{1,0:T(8,128)(2,1)}, u32[]{:S(2)}) copy-start(bf16[128,256]{1,0:T(8,128)(2,1)} %get-tuple-element.21.hi_ref) | copy-start | bytes 196612
  148.0 5.7 %copy-start.6 = (bf16[192,256]{1,0:T(8,128)(2,1)S(1)}, bf16[192,256]{1,0:T(8,128)(2,1)}, u32[]{:S(2)}) copy-start(bf16[192,256]{1,0:T(8,128)(2,1)} %copy-done.5) | copy-start | bytes 294916
  148.0 6.5 %copy-start.2 = (bf16[128,256]{1,0:T(8,128)(2,1)S(1)}, bf16[128,256]{1,0:T(8,128)(2,1)}, u32[]{:S(2)}) copy-start(bf16[128,256]{1,0:T(8,128)(2,1)} %get-tuple-element.22.lo_ref) | copy-start | bytes 196612
  187.4 6.9 %collective-permute-start.11 = (f32[2,128]{1,0:T(2,128)S(1)}, f32[2,128]{1,0:T(2,128)S(1)}, u32[]{:S(2)}, u32[]{:S(2)}) collective-permute-start(f32[2,128]{1,0:T(2,128)S(1)} %select_reduce_fusion), channel_id=1, source_target_pairs={{0,1},{1,2},{2,3},{3,0},{4,5},{5,6},{6,7},{7,4},{8,9},{9,10},{10,1... | collective-permute-start | bytes 3080 | tf_op jit(solution)/shard_map/ppermute | solution.py:166
  187.5 7.0 %collective-permute-start.12 = (f32[2,128]{1,0:T(2,128)S(1)}, f32[2,128]{1,0:T(2,128)S(1)}, u32[]{:S(2)}, u32[]{:S(2)}) collective-permute-start(f32[2,128]{1,0:T(2,128)S(1)} %select_reduce_fusion), channel_id=1, source_target_pairs={{0,2},{1,3},{2,0},{3,1},{4,6},{5,7},{6,4},{7,5},{8,10},{9,11},{10,... | collective-permute-start | bytes 3080 | tf_op jit(solution)/shard_map/ppermute | solution.py:166
  189.9 4.6 %collective-permute-start.13 = (f32[2,128]{1,0:T(2,128)S(1)}, f32[2,128]{1,0:T(2,128)S(1)}, u32[]{:S(2)}, u32[]{:S(2)}) collective-permute-start(f32[2,128]{1,0:T(2,128)S(1)} %select_reduce_fusion), channel_id=1, source_target_pairs={{0,3},{1,0},{2,1},{3,2},{4,7},{5,4},{6,5},{7,6},{8,11},{9,8},{10,9... | collective-permute-start | bytes 3080 | tf_op jit(solution)/shard_map/ppermute | solution.py:166
  191.0 13.0 %collective-permute-start.14 = (f32[2,128,128]{2,1,0:T(8,128)}, f32[2,128,128]{2,1,0:T(8,128)S(1)}, u32[]{:S(2)}, u32[]{:S(2)}) collective-permute-start(f32[2,128,128]{2,1,0:T(8,128)} %get-tuple-element.19), channel_id=1, source_target_pairs={{0,1},{1,2},{2,3},{3,0},{4,5},{5,6},{6,7},{7,4},{8,9},{9,10},{10,1... | collective-permute-start | bytes 393224 | tf_op jit(solution)/shard_map/ppermute | solution.py:166
  191.9 12.1 %collective-permute-start.15 = (f32[2,128,128]{2,1,0:T(8,128)}, f32[2,128,128]{2,1,0:T(8,128)S(1)}, u32[]{:S(2)}, u32[]{:S(2)}) collective-permute-start(f32[2,128,128]{2,1,0:T(8,128)} %get-tuple-element.19), channel_id=1, source_target_pairs={{0,2},{1,3},{2,0},{3,1},{4,6},{5,7},{6,4},{7,5},{8,10},{9,11},{10,... | collective-permute-start | bytes 393224 | tf_op jit(solution)/shard_map/ppermute | solution.py:166
  194.3 11.2 %collective-permute-start.16 = (f32[2,128,128]{2,1,0:T(8,128)}, f32[2,128,128]{2,1,0:T(8,128)S(1)}, u32[]{:S(2)}, u32[]{:S(2)}) collective-permute-start(f32[2,128,128]{2,1,0:T(8,128)} %get-tuple-element.19), channel_id=1, source_target_pairs={{0,3},{1,0},{2,1},{3,2},{4,7},{5,4},{6,5},{7,6},{8,11},{9,8},{10,9... | collective-permute-start | bytes 393224 | tf_op jit(solution)/shard_map/ppermute | solution.py:166
  194.5 11.0 %copy-start.4 = (f32[2,128,128]{2,1,0:T(8,128)S(1)}, f32[2,128,128]{2,1,0:T(8,128)}, u32[]{:S(2)}) copy-start(f32[2,128,128]{2,1,0:T(8,128)} %get-tuple-element.19) | copy-start | bytes 393220

commit v9 on v8

--- a/solution.py
+++ b/solution.py
@@ -225,22 +225,24 @@
             [edge_rows(offsets[0, 1], cols), edge_rows(offsets[0, 0], cols), masked[:, cols]], axis=0
         )
 
-    below = lax.ppermute(
-        edges_of(slice(entries - rim, entries)), "row", [(i, i + 1) for i in range(lax.axis_size("row") - 1)]
-    )
-    above = lax.ppermute(edges_of(slice(0, rim)), "row", [(i + 1, i) for i in range(lax.axis_size("row") - 1)])
-    masked_lower, masked_upper = below[2 * WIN :], above[2 * WIN :]
-    upper_ext = jnp.concatenate([upper_window, below[:WIN], above[:WIN]], axis=1)
-    lower_ext = jnp.concatenate([lower_window, below[WIN : 2 * WIN], above[WIN : 2 * WIN]], axis=1)
-    big = exchange(upper_ext, lower_ext)
+    big = exchange(upper_window, lower_window)
     row_major = Layout(major_to_minor=(0, 1, 2))
     margin_blocks = with_layout_constraint(margin_blocks, row_major)
     energy_blocks = with_layout_constraint(energy_blocks, row_major)
-    big, margin_blocks, energy_blocks = lax.optimization_barrier((big, margin_blocks, energy_blocks))
-    received = jnp.concatenate(finish(*big), axis=0)
-    windows = received[:, :entries]
-    windows_lower = received[:, entries : entries + rim]
-    windows_upper = received[:, entries + rim :]
+    below = lax.ppermute(
+        edges_of(slice(entries - rim, entries)), "row", [(i, i + 1) for i in range(lax.axis_size("row") - 1)]
+    )
+    above = lax.ppermute(edges_of(slice(0, rim)), "row", [(i + 1, i) for i in range(lax.axis_size("row") - 1)])
+    below, above, margin_blocks = lax.optimization_barrier((below, above, margin_blocks))
+    masked_lower, masked_upper = below[2 * WIN :], above[2 * WIN :]
+    upper_edges = jnp.concatenate([below[:WIN], above[:WIN]], axis=1)
+    lower_edges = jnp.concatenate([below[WIN : 2 * WIN], above[WIN : 2 * WIN]], axis=1)
+    small = exchange(upper_edges, lower_edges)
+    big, small, energy_blocks = lax.optimization_barrier((big, small, energy_blocks))
+    windows = jnp.concatenate(finish(*big), axis=0)
+    edges = jnp.concatenate(finish(*small), axis=0)
+    windows_lower = edges[:, :rim]
+    windows_upper = edges[:, rim:]
     count = counts[:1]
     (margin_dots,) = block_apply(
         (margin_blocks,), shifts_flat, count, windows, windows_lower, windows_upper, pair=own_vectors

time: 208 us -> 231 us (1.11)
  starting transfers between devices: 31.4 us -> 45.4 us
  waiting for transfers between devices: 26.1 us -> 37.6 us
  local copies, waits for them, and re-layouts: 56.6 us -> 52.9 us
    ppermute x2 -> x4, waiting for transfers between devices: 14.8 us -> 25.2 us  [from_behind(): return lax.ppermute(block, axis, route)]
    ppermute x9, waiting for transfers between devices: 7.94 us -> 2.54 us  [row_sum(): lax.ppermute(part, 'row', [(i, (i + step) % count) for i in range(count)])]
    ppermute x1 -> x2, waiting for transfers between devices: 0.01 us -> 4.43 us  [exchange(): lax.ppermute(upper, 'cuts', [(i, i + 2) for i in evens if i + 2 < cuts_co...]
    ppermute x9, starting transfers between devices: 10.8 us -> 14.8 us  [row_sum(): lax.ppermute(part, 'row', [(i, (i + step) % count) for i in range(count)])]
    ppermute x1, waiting for transfers between devices: 0.01 us -> 3.77 us  [shards(): lax.ppermute(edges_of(slice(entries - rim, entries)), 'row', [(i, i + 1)...]
    ppermute x2 -> x4, starting transfers between devices: 5.56 us -> 8.7 us  [from_behind(): return lax.ppermute(block, axis, route)]
    ppermute x1 -> x2, starting transfers between devices: 2.47 us -> 5.59 us  [finish(): lax.ppermute(upper_1, 'cuts', [(i, i + 1) for i in evens if i + 1 < cuts_...]
    select_n x1, other arithmetic: 3.26 us -> 0.47 us  [shards(): jnp.where(valid_mask[:, None], own_vectors, jnp.zeros((), own_vectors.dty...]
  transfers between devices with their start and end apart: 17 -> 23, of which waited for: 7 -> 7; matrix products, arithmetic and copies ran while one was open for 31% -> 26% of each run, Pallas kernels for 0% -> 0%
where the time goes in v9:
time: 231 us; the launch traced here: 229 us
  local copies, waits for them, and re-layouts  52.9 us (23%)
  Pallas kernels  52.7 us (23%)
  starting transfers between devices  45.4 us (20%)
  waiting for transfers between devices  37.6 us (16%)
  other arithmetic  27.5 us (12%)
  matrix products  7.01 us (3%)
  between operations  5.69 us (2%)
    pallas_call x2, Pallas kernels, block_apply(): pl.pallas_call(kernel, grid_spec=grid_spec, out_shape=out_shape, compiler...  52.7 us
    unnamed x18, local copies, waits for them, and re-layouts  49.3 us
    ppermute x4, waiting for transfers between devices, from_behind(): return lax.ppermute(block, axis, route)  25.2 us
    ppermute x9, starting transfers between devices, row_sum(): lax.ppermute(part, 'row', [(i, (i + step) % count) for i in range(count)])  14.8 us
    broadcast_in_dim x1, other arithmetic, shards(): return (residual[None], margin_pencil[None], energy_pencil[None])  9.49 us
    ppermute x4, starting transfers between devices, from_behind(): return lax.ppermute(block, axis, route)  8.7 us
    dot_general x3, matrix products, clean(): lax.dot_general(margin_b, wins, (((0,), (0,)), ((), ())), preferred_eleme...  7.01 us
    concatenate x1, other arithmetic, shards(): windows = jnp.concatenate(finish(*big), axis=0)  5.91 us
  transfers between devices with their start and end apart: 23, of which 7 were waited for; matrix products, arithmetic and copies ran while one was open for 26% of the time, Pallas kernels for 0%

profile of v9, /device:TPU:12, one launch (start us, length us, event | category | flops | bytes accessed | tf_op | source)
XLA Modules:
  0.0 228.9 jit_solution(4505953499440839868)
XLA Ops:
  7.8 5.0 %bitcast_select_fusion = (bf16[32,24576]{1,0:T(8,128)(2,1)}, bf16[32,24576]{1,0:T(8,128)(2,1)}) fusion(bf16[1,128,24576]{2,1,0:T(8,128)(2,1)} %param.6, s32[]{:T(128)S(6)} %select_n.144, pred[32]{0:T(512)(128)(4,1)S(1)} %get-tuple-element.55, s32[]{:T(128)S(6)} %select_n.142, pred[32]{0:T(512)(128)(4,1)S(1)} %get-tuple-element.56), kind=kLoop, calls=%fused_computation.6 | loop fusion | flops 1572864 | bytes 6291528 | tf_op jit(solution)/shard_map/jit(_where)/select_n | solution.py:184
  12.8 1.9 collective-permute-start
  14.7 3.4 %collective-permute-start.2 = (bf16[32,24576]{1,0:T(8,128)(2,1)}, bf16[32,24576]{1,0:T(8,128)(2,1)}, u32[]{:S(2)}, u32[]{:S(2)}) collective-permute-start(bf16[32,24576]{1,0:T(8,128)(2,1)} %get-tuple-element.38), channel_id=1, source_target_pairs={{0,8},{8,16},{16,24},{1,9},{9,17},{17,25},{2,10},{10,18},{18,26},{... | collective-permute-start | bytes 4718600 | tf_op jit(solution)/shard_map/ppermute | solution.py:206
  18.1 3.0 %collective-permute-start.1 = (bf16[32,24576]{1,0:T(8,128)(2,1)}, bf16[32,24576]{1,0:T(8,128)(2,1)}, u32[]{:S(2)}, u32[]{:S(2)}) collective-permute-start(bf16[32,24576]{1,0:T(8,128)(2,1)} %get-tuple-element.37), channel_id=1, source_target_pairs={{4,0},{8,4},{12,8},{16,12},{20,16},{24,20},{28,24},{5,1},{9,5},{13... | collective-permute-start | bytes 4718600 | tf_op jit(solution)/shard_map/ppermute | solution.py:19
  21.1 1.9 collective-permute-start.3
  23.6 2.5 %copy-done.1 = bf16[128,24576]{1,0:T(8,128)(2,1)} copy-done((bf16[128,24576]{1,0:T(8,128)(2,1)}, bf16[128,24576]{1,0:T(8,128)(2,1)S(1)}, u32[]{:S(2)}) %copy-start.1) | copy-done | bytes 6291480
  26.1 3.5 %collective-permute-start.4 = (bf16[192,256]{1,0:T(8,128)(2,1)S(1)}, bf16[192,256]{1,0:T(8,128)(2,1)S(1)}, u32[]{:S(2)}, u32[]{:S(2)}) collective-permute-start(bf16[192,256]{1,0:T(8,128)(2,1)S(1)} %pad_maximum_fusion.4), channel_id=1, source_target_pairs={{0,1},{1,2},{2,3},{4,5},{5,6},{6,7},{8,9},{9,10},{10,11},{12,13},{... | collective-permute-start | bytes 294920 | tf_op jit(solution)/shard_map/ppermute | solution.py:232
  29.6 3.8 %collective-permute-done.4 = bf16[192,256]{1,0:T(8,128)(2,1)S(1)} collective-permute-done((bf16[192,256]{1,0:T(8,128)(2,1)S(1)}, bf16[192,256]{1,0:T(8,128)(2,1)S(1)}, u32[]{:S(2)}, u32[]{:S(2)}) %collective-permute-start.4) | collective-permute-done | bytes 98336 | tf_op jit(solution)/shard_map/ppermute | solution.py:232
  33.4 1.9 collective-permute-start.5
  35.3 23.4 %copy.12.refs_0_ = bf16[256,96,288]{2,1,0:T(8,128)(2,1)} copy(bf16[256,96,288]{0,2,1:T(8,128)(2,1)} %param.9) | data formatting | bytes 28311552 | tf_op args[3]
  58.8 1.9 collective-permute-start.6
  60.7 23.6 %collective-permute-done.6 = bf16[32,512]{1,0:T(8,128)(2,1)S(1)} collective-permute-done((bf16[32,512]{1,0:T(8,128)(2,1)S(1)}, bf16[32,512]{1,0:T(8,128)(2,1)S(1)}, u32[]{:S(2)}, u32[]{:S(2)}) %collective-permute-start.6) | collective-permute-done | bytes 32800 | tf_op jit(solution)/shard_map/ppermute | solution.py:19
  84.3 1.9 collective-permute-start.7
  86.2 1.6 collective-permute-done.7
  87.8 2.5 %collective-permute-start.8 = (bf16[32,512]{1,0:T(8,128)(2,1)S(1)}, bf16[32,512]{1,0:T(8,128)(2,1)S(1)}, u32[]{:S(2)}, u32[]{:S(2)}) collective-permute-start(bf16[32,512]{1,0:T(8,128)(2,1)S(1)} %pad_maximum_fusion.6), channel_id=1, source_target_pairs={{0,8},{8,16},{16,24},{1,9},{9,17},{17,25},{2,10},{10,18},{18,26},{... | collective-permute-start | bytes 98312 | tf_op jit(solution)/shard_map/ppermute | solution.py:206
  90.3 4.4 %collective-permute-done.8 = bf16[32,512]{1,0:T(8,128)(2,1)S(1)} collective-permute-done((bf16[32,512]{1,0:T(8,128)(2,1)S(1)}, bf16[32,512]{1,0:T(8,128)(2,1)S(1)}, u32[]{:S(2)}, u32[]{:S(2)}) %collective-permute-start.8) | collective-permute-done | bytes 32800 | tf_op jit(solution)/shard_map/ppermute | solution.py:206
  95.4 23.4 %copy.13.refs_1_ = bf16[256,96,288]{2,1,0:T(8,128)(2,1)} copy(bf16[256,96,288]{0,2,1:T(8,128)(2,1)} %param.10) | data formatting | bytes 28311552 | tf_op args[4]
  122.5 4.3 %collective-permute-start.10 = (bf16[32,24576]{1,0:T(8,128)(2,1)S(1)}, bf16[32,24576]{1,0:T(8,128)(2,1)S(1)}, u32[]{:S(2)}, u32[]{:S(2)}) collective-permute-start(bf16[32,24576]{1,0:T(8,128)(2,1)S(1)} %collective-permute-done), channel_id=1, source_target_pairs={{0,4},{8,12},{16,20},{24,28},{1,5},{9,13},{17,21},{25,29},{2,6},{1... | collective-permute-start | bytes 4718600 | tf_op jit(solution)/shard_map/ppermute | solution.py:212
  128.1 1.6 collective-permute-done.12
  130.4 1.6 broadcast_select_fusion.1
  132.0 1.6 broadcast_select_fusion.2
  133.6 5.9 %pad_maximum_fusion.x_hbm = bf16[128,24576]{1,0:T(8,128)(2,1)} fusion(bf16[32,24576]{1,0:T(8,128)(2,1)S(1)} %broadcast_select_fusion.1, bf16[32,24576]{1,0:T(8,128)(2,1)} %collective-permute-done.1, bf16[32,24576]{1,0:T(8,128)(2,1)S(1)} %collective-permute-done, bf16[32,24576]{1,0:T(8,128)(2,1)S(1)} %broadcast_select_fusion.2), kind=kLoop, calls=%fused_computation.4 | loop fusion | flops 25165824 | bytes 12582912 | tf_op jit(solution)/shard_map/concatenate | solution.py:242
  139.5 21.7 %shard_map.85 = f32[1,128,128]{2,1,0:T(8,128)} custom-call(s32[768]{0:T(1024)} %reshape.80.shift_ref, s32[1]{0:T(128)} %copy.14.count_ref, bf16[128,24576]{1,0:T(8,128)(2,1)} %pad_maximum_fusion.x_hbm, bf16[128,256]{1,0:T(8,128)(2,1)} %get-tuple-element.42.lo_ref, bf16[128,256]{1,0:T(8,128)(2,1)} %get-tuple-element.41.hi_ref, ...), custom_call_target="tpu_custom_call" | custom-call | tf_op jit(solution)/shard_map/pallas_call | solution.py:152
  161.7 2.6 %collective-permute-start.15 = (f32[128,128]{1,0:T(8,128)}, f32[128,128]{1,0:T(8,128)S(1)}, u32[]{:S(2)}, u32[]{:S(2)}) collective-permute-start(f32[128,128]{1,0:T(8,128)} %bitcast.49), channel_id=1, source_target_pairs={{0,2},{1,3},{2,0},{3,1},{4,6},{5,7},{6,4},{7,5},{8,10},{9,11},{10,... | collective-permute-start | bytes 196616 | tf_op jit(solution)/shard_map/ppermute | solution.py:166
  164.3 2.5 %collective-permute-start.14 = (f32[128,128]{1,0:T(8,128)}, f32[128,128]{1,0:T(8,128)S(1)}, u32[]{:S(2)}, u32[]{:S(2)}) collective-permute-start(f32[128,128]{1,0:T(8,128)} %bitcast.50), channel_id=1, source_target_pairs={{0,1},{1,2},{2,3},{3,0},{4,5},{5,6},{6,7},{7,4},{8,9},{9,10},{10,1... | collective-permute-start | bytes 196616 | tf_op jit(solution)/shard_map/ppermute | solution.py:166
  166.8 1.6 collective-permute-done.15
  170.3 5.3 %fusion.x_hbm = bf16[128,24576]{1,0:T(8,128)(2,1)} fusion(bf16[128,128]{1,0:T(8,128)(2,1)S(1)} %fusion.2, bf16[128,24576]{1,0:T(8,128)(2,1)S(1)} %bitcast.46, bf16[32,24576]{1,0:T(8,128)(2,1)S(1)} %broadcast_select_fusion.1, bf16[32,24576]{1,0:T(8,128)(2,1)} %collective-permute-done.1, bf16[32,24576]{1,0:T(8,128)(2,1)} %copy-done.3, ...), kind=kOutput, calls=%fused_computation.1 | convolution fusion | flops 839909376 | bytes 18907136 | tf_op jit(solution)/shard_map/dot_general | solution.py:254
  177.3 31.1 %shard_map.86 = (bf16[128,24576]{1,0:T(8,128)(2,1)}, bf16[128,24576]{1,0:T(8,128)(2,1)}, f32[2,128,128]{2,1,0:T(8,128)}) custom-call(s32[768]{0:T(1024)} %reshape.80.shift_ref, s32[1]{0:T(128)} %copy.14.count_ref, bf16[128,24576]{1,0:T(8,128)(2,1)} %fusion.x_hbm, bf16[128,256]{1,0:T(8,128)(2,1)} %subtract_convert_fusion.2.lo_ref, ...), custom_call_target="tpu_custom_call" | custom-call | tf_op jit(solution)/shard_map/pallas_call | solution.py:152
  209.4 2.3 %collective-permute-start.19 = (f32[2,128]{1,0:T(2,128)S(1)}, f32[2,128]{1,0:T(2,128)S(1)}, u32[]{:S(2)}, u32[]{:S(2)}) collective-permute-start(f32[2,128]{1,0:T(2,128)S(1)} %select_reduce_fusion), channel_id=1, source_target_pairs={{0,3},{1,0},{2,1},{3,2},{4,7},{5,4},{6,5},{7,6},{8,11},{9,8},{10,9... | collective-permute-start | bytes 3080 | tf_op jit(solution)/shard_map/ppermute | solution.py:166
  213.1 1.7 collective-permute-start.17
  216.6 1.9 collective-permute-start.20
  218.6 9.5 %fusion.1 = bf16[1,128,24576]{2,1,0:T(8,128)(2,1)} fusion(bf16[128,24576]{1,0:T(8,128)(2,1)} %get-tuple-element.32, bf16[128,24576]{1,0:T(8,128)(2,1)} %get-tuple-element.30, f32[128]{0:T(128)S(1)} %fusion.8), kind=kLoop, calls=%fused_computation.3 | loop fusion | flops 15728640 | bytes 18874880 | tf_op jit(solution)/shard_map/broadcast_in_dim | solution.py:281
  (74 shorter events, 18.5 us)
Async XLA Ops:
  7.8 15.2 %copy-start = (bf16[1,128,24576]{2,1,0:T(8,128)(2,1)S(1)}, bf16[1,128,24576]{2,1,0:T(8,128)(2,1)}, u32[]{:S(2)}) copy-start(bf16[1,128,24576]{2,1,0:T(8,128)(2,1)} %param.6) | copy-start | bytes 18874372
  12.8 106.0 %collective-permute-start = (bf16[32,24576]{1,0:T(8,128)(2,1)}, bf16[32,24576]{1,0:T(8,128)(2,1)S(1)}, u32[]{:S(2)}, u32[]{:S(2)}) collective-permute-start(bf16[32,24576]{1,0:T(8,128)(2,1)} %get-tuple-element.38), channel_id=1, source_target_pairs={{0,4},{4,8},{8,12},{12,16},{16,20},{20,24},{24,28},{1,5},{5,9},{9,... | collective-permute-start | bytes 4718600 | tf_op jit(solution)/shard_map/ppermute | solution.py:19
  14.7 104.1 %collective-permute-start.2 = (bf16[32,24576]{1,0:T(8,128)(2,1)}, bf16[32,24576]{1,0:T(8,128)(2,1)}, u32[]{:S(2)}, u32[]{:S(2)}) collective-permute-start(bf16[32,24576]{1,0:T(8,128)(2,1)} %get-tuple-element.38), channel_id=1, source_target_pairs={{0,8},{8,16},{16,24},{1,9},{9,17},{17,25},{2,10},{10,18},{18,26},{... | collective-permute-start | bytes 4718600 | tf_op jit(solution)/shard_map/ppermute | solution.py:206
  18.1 100.6 %collective-permute-start.1 = (bf16[32,24576]{1,0:T(8,128)(2,1)}, bf16[32,24576]{1,0:T(8,128)(2,1)}, u32[]{:S(2)}, u32[]{:S(2)}) collective-permute-start(bf16[32,24576]{1,0:T(8,128)(2,1)} %get-tuple-element.37), channel_id=1, source_target_pairs={{4,0},{8,4},{12,8},{16,12},{20,16},{24,20},{28,24},{5,1},{9,5},{13... | collective-permute-start | bytes 4718600 | tf_op jit(solution)/shard_map/ppermute | solution.py:19
  21.1 97.7 %collective-permute-start.3 = (bf16[32,24576]{1,0:T(8,128)(2,1)}, bf16[32,24576]{1,0:T(8,128)(2,1)}, u32[]{:S(2)}, u32[]{:S(2)}) collective-permute-start(bf16[32,24576]{1,0:T(8,128)(2,1)} %get-tuple-element.37), channel_id=1, source_target_pairs={{12,4},{20,12},{28,20},{13,5},{21,13},{29,21},{14,6},{22,14},{30,2... | collective-permute-start | bytes 4718600 | tf_op jit(solution)/shard_map/ppermute | solution.py:207
  23.4 2.6 %copy-start.1 = (bf16[128,24576]{1,0:T(8,128)(2,1)}, bf16[128,24576]{1,0:T(8,128)(2,1)S(1)}, u32[]{:S(2)}) copy-start(bf16[128,24576]{1,0:T(8,128)(2,1)S(1)} %broadcast_select_fusion) | copy-start | bytes 18874372
  26.1 7.3 %collective-permute-start.4 = (bf16[192,256]{1,0:T(8,128)(2,1)S(1)}, bf16[192,256]{1,0:T(8,128)(2,1)S(1)}, u32[]{:S(2)}, u32[]{:S(2)}) collective-permute-start(bf16[192,256]{1,0:T(8,128)(2,1)S(1)} %pad_maximum_fusion.4), channel_id=1, source_target_pairs={{0,1},{1,2},{2,3},{4,5},{5,6},{6,7},{8,9},{9,10},{10,11},{12,13},{... | collective-permute-start | bytes 294920 | tf_op jit(solution)/shard_map/ppermute | solution.py:232
  33.4 25.4 %collective-permute-start.5 = (bf16[192,256]{1,0:T(8,128)(2,1)S(1)}, bf16[192,256]{1,0:T(8,128)(2,1)S(1)}, u32[]{:S(2)}, u32[]{:S(2)}) collective-permute-start(bf16[192,256]{1,0:T(8,128)(2,1)S(1)} %pad_maximum_fusion.5), channel_id=1, source_target_pairs={{1,0},{2,1},{3,2},{5,4},{6,5},{7,6},{9,8},{10,9},{11,10},{13,12},{... | collective-permute-start | bytes 294920 | tf_op jit(solution)/shard_map/ppermute | solution.py:235
  58.8 25.6 %collective-permute-start.6 = (bf16[32,512]{1,0:T(8,128)(2,1)S(1)}, bf16[32,512]{1,0:T(8,128)(2,1)S(1)}, u32[]{:S(2)}, u32[]{:S(2)}) collective-permute-start(bf16[32,512]{1,0:T(8,128)(2,1)S(1)} %pad_maximum_fusion.6), channel_id=1, source_target_pairs={{0,4},{4,8},{8,12},{12,16},{16,20},{20,24},{24,28},{1,5},{5,9},{9,... | collective-permute-start | bytes 98312 | tf_op jit(solution)/shard_map/ppermute | solution.py:19
  60.7 60.7 %copy-start.5 = (s32[256,3]{0,1:T(4,128)S(1)}, s32[256,3]{0,1:T(4,128)}, u32[]{:S(2)}) copy-start(s32[256,3]{0,1:T(4,128)} %param.11) | copy-start | bytes 9220
  84.3 3.5 %collective-permute-start.7 = (bf16[32,512]{1,0:T(8,128)(2,1)S(1)}, bf16[32,512]{1,0:T(8,128)(2,1)S(1)}, u32[]{:S(2)}, u32[]{:S(2)}) collective-permute-start(bf16[32,512]{1,0:T(8,128)(2,1)S(1)} %pad_maximum_fusion.7), channel_id=1, source_target_pairs={{4,0},{8,4},{12,8},{16,12},{20,16},{24,20},{28,24},{5,1},{9,5},{13... | collective-permute-start | bytes 98312 | tf_op jit(solution)/shard_map/ppermute | solution.py:19
  87.8 6.9 %collective-permute-start.8 = (bf16[32,512]{1,0:T(8,128)(2,1)S(1)}, bf16[32,512]{1,0:T(8,128)(2,1)S(1)}, u32[]{:S(2)}, u32[]{:S(2)}) collective-permute-start(bf16[32,512]{1,0:T(8,128)(2,1)S(1)} %pad_maximum_fusion.6), channel_id=1, source_target_pairs={{0,8},{8,16},{16,24},{1,9},{9,17},{17,25},{2,10},{10,18},{18,26},{... | collective-permute-start | bytes 98312 | tf_op jit(solution)/shard_map/ppermute | solution.py:206
  94.7 24.0 %collective-permute-start.9 = (bf16[32,512]{1,0:T(8,128)(2,1)S(1)}, bf16[32,512]{1,0:T(8,128)(2,1)S(1)}, u32[]{:S(2)}, u32[]{:S(2)}) collective-permute-start(bf16[32,512]{1,0:T(8,128)(2,1)S(1)} %pad_maximum_fusion.7), channel_id=1, source_target_pairs={{12,4},{20,12},{28,20},{13,5},{21,13},{29,21},{14,6},{22,14},{30,2... | collective-permute-start | bytes 98312 | tf_op jit(solution)/shard_map/ppermute | solution.py:207
  118.8 20.8 %copy-start.3 = (bf16[32,24576]{1,0:T(8,128)(2,1)}, bf16[32,24576]{1,0:T(8,128)(2,1)S(1)}, u32[]{:S(2)}) copy-start(bf16[32,24576]{1,0:T(8,128)(2,1)S(1)} %collective-permute-done) | copy-start | bytes 4718596
  118.8 11.6 %collective-permute-start.11 = (bf16[32,24576]{1,0:T(8,128)(2,1)}, bf16[32,24576]{1,0:T(8,128)(2,1)}, u32[]{:S(2)}, u32[]{:S(2)}) collective-permute-start(bf16[32,24576]{1,0:T(8,128)(2,1)} %collective-permute-done.1), channel_id=1, source_target_pairs={{4,0},{12,8},{20,16},{28,24},{5,1},{13,9},{21,17},{29,25},{6,2},{1... | collective-permute-start | bytes 4718600 | tf_op jit(solution)/shard_map/ppermute | solution.py:214
  120.1 7.9 %collective-permute-start.13 = (bf16[32,512]{1,0:T(8,128)(2,1)S(1)}, bf16[32,512]{1,0:T(8,128)(2,1)S(1)}, u32[]{:S(2)}, u32[]{:S(2)}) collective-permute-start(bf16[32,512]{1,0:T(8,128)(2,1)S(1)} %collective-permute-done.7), channel_id=1, source_target_pairs={{4,0},{12,8},{20,16},{28,24},{5,1},{13,9},{21,17},{29,25},{6,2},{1... | collective-permute-start | bytes 98312 | tf_op jit(solution)/shard_map/ppermute | solution.py:214
  122.5 9.5 %collective-permute-start.10 = (bf16[32,24576]{1,0:T(8,128)(2,1)S(1)}, bf16[32,24576]{1,0:T(8,128)(2,1)S(1)}, u32[]{:S(2)}, u32[]{:S(2)}) collective-permute-start(bf16[32,24576]{1,0:T(8,128)(2,1)S(1)} %collective-permute-done), channel_id=1, source_target_pairs={{0,4},{8,12},{16,20},{24,28},{1,5},{9,13},{17,21},{25,29},{2,6},{1... | collective-permute-start | bytes 4718600 | tf_op jit(solution)/shard_map/ppermute | solution.py:212
  126.8 3.0 %collective-permute-start.12 = (bf16[32,512]{1,0:T(8,128)(2,1)S(1)}, bf16[32,512]{1,0:T(8,128)(2,1)S(1)}, u32[]{:S(2)}, u32[]{:S(2)}) collective-permute-start(bf16[32,512]{1,0:T(8,128)(2,1)S(1)} %collective-permute-done.6), channel_id=1, source_target_pairs={{0,4},{8,12},{16,20},{24,28},{1,5},{9,13},{17,21},{25,29},{2,6},{1... | collective-permute-start | bytes 98312 | tf_op jit(solution)/shard_map/ppermute | solution.py:212
  133.6 5.9 %copy-start.2 = (bf16[32,24576]{1,0:T(8,128)(2,1)}, bf16[32,24576]{1,0:T(8,128)(2,1)S(1)}, u32[]{:S(2)}) copy-start(bf16[32,24576]{1,0:T(8,128)(2,1)S(1)} %broadcast_select_fusion.2) | copy-start | bytes 4718596
  133.6 36.7 %slice-start = ((s8[6291456]{0:T(1024)(128)(4,1)}), s8[4194304]{0:T(1024)(128)(4,1)S(1)}, s32[]{:S(2)}) async-start(s8[6291456]{0:T(1024)(128)(4,1)} %bitcast.45), calls=%async_computation | async-start | bytes 8388608
  139.5 30.8 %slice-start.1 = ((s8[6291456]{0:T(1024)(128)(4,1)}), s8[2097152]{0:T(1024)(128)(4,1)S(1)}, s32[]{:S(2)}) async-start(s8[6291456]{0:T(1024)(128)(4,1)} %bitcast.45), calls=%async_computation.1 | async-start | bytes 4194304
  161.2 5.6 %collective-permute-start.16 = (f32[128,128]{1,0:T(8,128)}, f32[128,128]{1,0:T(8,128)S(1)}, u32[]{:S(2)}, u32[]{:S(2)}) collective-permute-start(f32[128,128]{1,0:T(8,128)} %bitcast.48), channel_id=1, source_target_pairs={{0,3},{1,0},{2,1},{3,2},{4,7},{5,4},{6,5},{7,6},{8,11},{9,8},{10,9... | collective-permute-start | bytes 196616 | tf_op jit(solution)/shard_map/ppermute | solution.py:166
  161.7 6.7 %collective-permute-start.15 = (f32[128,128]{1,0:T(8,128)}, f32[128,128]{1,0:T(8,128)S(1)}, u32[]{:S(2)}, u32[]{:S(2)}) collective-permute-start(f32[128,128]{1,0:T(8,128)} %bitcast.49), channel_id=1, source_target_pairs={{0,2},{1,3},{2,0},{3,1},{4,6},{5,7},{6,4},{7,5},{8,10},{9,11},{10,... | collective-permute-start | bytes 196616 | tf_op jit(solution)/shard_map/ppermute | solution.py:166
  164.3 5.1 %collective-permute-start.14 = (f32[128,128]{1,0:T(8,128)}, f32[128,128]{1,0:T(8,128)S(1)}, u32[]{:S(2)}, u32[]{:S(2)}) collective-permute-start(f32[128,128]{1,0:T(8,128)} %bitcast.50), channel_id=1, source_target_pairs={{0,1},{1,2},{2,3},{3,0},{4,5},{5,6},{6,7},{7,4},{8,9},{9,10},{10,1... | collective-permute-start | bytes 196616 | tf_op jit(solution)/shard_map/ppermute | solution.py:166
  209.4 7.3 %collective-permute-start.19 = (f32[2,128]{1,0:T(2,128)S(1)}, f32[2,128]{1,0:T(2,128)S(1)}, u32[]{:S(2)}, u32[]{:S(2)}) collective-permute-start(f32[2,128]{1,0:T(2,128)S(1)} %select_reduce_fusion), channel_id=1, source_target_pairs={{0,3},{1,0},{2,1},{3,2},{4,7},{5,4},{6,5},{7,6},{8,11},{9,8},{10,9... | collective-permute-start | bytes 3080 | tf_op jit(solution)/shard_map/ppermute | solution.py:166
  211.7 6.9 %collective-permute-start.18 = (f32[2,128]{1,0:T(2,128)S(1)}, f32[2,128]{1,0:T(2,128)S(1)}, u32[]{:S(2)}, u32[]{:S(2)}) collective-permute-start(f32[2,128]{1,0:T(2,128)S(1)} %select_reduce_fusion), channel_id=1, source_target_pairs={{0,2},{1,3},{2,0},{3,1},{4,6},{5,7},{6,4},{7,5},{8,10},{9,11},{10,... | collective-permute-start | bytes 3080 | tf_op jit(solution)/shard_map/ppermute | solution.py:166
  213.1 5.5 %collective-permute-start.17 = (f32[2,128]{1,0:T(2,128)S(1)}, f32[2,128]{1,0:T(2,128)S(1)}, u32[]{:S(2)}, u32[]{:S(2)}) collective-permute-start(f32[2,128]{1,0:T(2,128)S(1)} %select_reduce_fusion), channel_id=1, source_target_pairs={{0,1},{1,2},{2,3},{3,0},{4,5},{5,6},{6,7},{7,4},{8,9},{9,10},{10,1... | collective-permute-start | bytes 3080 | tf_op jit(solution)/shard_map/ppermute | solution.py:166
  214.7 13.4 %collective-permute-start.22 = (f32[2,128,128]{2,1,0:T(8,128)}, f32[2,128,128]{2,1,0:T(8,128)S(1)}, u32[]{:S(2)}, u32[]{:S(2)}) collective-permute-start(f32[2,128,128]{2,1,0:T(8,128)} %get-tuple-element.31), channel_id=1, source_target_pairs={{0,3},{1,0},{2,1},{3,2},{4,7},{5,4},{6,5},{7,6},{8,11},{9,8},{10,9... | collective-permute-start | bytes 393224 | tf_op jit(solution)/shard_map/ppermute | solution.py:166
  215.1 13.0 %collective-permute-start.21 = (f32[2,128,128]{2,1,0:T(8,128)}, f32[2,128,128]{2,1,0:T(8,128)S(1)}, u32[]{:S(2)}, u32[]{:S(2)}) collective-permute-start(f32[2,128,128]{2,1,0:T(8,128)} %get-tuple-element.31), channel_id=1, source_target_pairs={{0,2},{1,3},{2,0},{3,1},{4,6},{5,7},{6,4},{7,5},{8,10},{9,11},{10,... | collective-permute-start | bytes 393224 | tf_op jit(solution)/shard_map/ppermute | solution.py:166
  216.6 11.5 %collective-permute-start.20 = (f32[2,128,128]{2,1,0:T(8,128)}, f32[2,128,128]{2,1,0:T(8,128)S(1)}, u32[]{:S(2)}, u32[]{:S(2)}) collective-permute-start(f32[2,128,128]{2,1,0:T(8,128)} %get-tuple-element.31), channel_id=1, source_target_pairs={{0,1},{1,2},{2,3},{3,0},{4,5},{5,6},{6,7},{7,4},{8,9},{9,10},{10,1... | collective-permute-start | bytes 393224 | tf_op jit(solution)/shard_map/ppermute | solution.py:166
  218.6 9.5 %copy-start.4 = (f32[2,128,128]{2,1,0:T(8,128)S(1)}, f32[2,128,128]{2,1,0:T(8,128)}, u32[]{:S(2)}) copy-start(f32[2,128,128]{2,1,0:T(8,128)} %get-tuple-element.31) | copy-start | bytes 393220

commit v10 on v8

--- a/solution.py
+++ b/solution.py
@@ -50,7 +50,7 @@
     accs = refs[at + 1 : at + 1 + nmat]
     xbuf, xpad, sem = refs[at + 1 + nmat :]
     g = pl.program_id(0)
-    slots, entries = x_hbm.shape
+    slots, entries = xbuf.shape
     halo = HALO * blk
     rim = lo_ref.shape[1]
     span = group * blk
@@ -95,7 +95,7 @@
             accs[m][pl.ds(pl.multiple_of(j * blk, 16), blk), :] = part.astype(accs[m].dtype)
         return carry
 
-    lax.fori_loop(0, group, body, 0, unroll=16)
+    lax.fori_loop(0, group, body, 0, unroll=32)
     live = lax.broadcasted_iota(jnp.int32, (slots, chunk), 0) < count_ref[0]
     for c in range(span // chunk):
         if given:
@@ -112,8 +112,9 @@
                 dots_ref[m] += nt(other, native)
 
 
-def block_apply(matrices, shifts_flat, count, cells, lower, upper, pair=None):
-    slots, entries = cells.shape
+def block_apply(matrices, shifts_flat, count, cells, lower, upper, pair=None, entries=None):
+    slots = cells.shape[0]
+    entries = cells.shape[1] if entries is None else entries
     block_rows, blk, width = matrices[0].shape
     rim = lower.shape[1]
     group = 64 if block_rows % 64 == 0 else block_rows
@@ -243,7 +244,14 @@
     windows_upper = received[:, entries + rim :]
     count = counts[:1]
     (margin_dots,) = block_apply(
-        (margin_blocks,), shifts_flat, count, windows, windows_lower, windows_upper, pair=own_vectors
+        (margin_blocks,),
+        shifts_flat,
+        count,
+        received,
+        windows_lower,
+        windows_upper,
+        pair=own_vectors,
+        entries=entries,
     )
     margin = row_sum(margin_dots[0]) / nmat_total
     margin_b = margin.astype(jnp.bfloat16)

time: 208 us -> 210 us (level)
  matrix products: 7.3 us -> 12.5 us
    dot_general x3, matrix products: 7.3 us -> 12.5 us  [clean(): lax.dot_general(margin_b, wins, (((0,), (0,)), ((), ())), preferred_eleme...]
    slice x1, local copies, waits for them, and re-layouts: 3.31 us -> 0.7 us  [shards(): windows_upper = received[:, entries + rim:]]
    unnamed x18 -> x14, local copies, waits for them, and re-layouts: 49.4 us -> 51.4 us
  transfers between devices with their start and end apart: 17 -> 17, of which waited for: 7 -> 7; matrix products, arithmetic and copies ran while one was open for 31% -> 30% of each run, Pallas kernels for 0% -> 0%
where the time goes in v10:
time: 210 us; the launch traced here: 207 us
  local copies, waits for them, and re-layouts  55.9 us (27%)
  Pallas kernels  51.1 us (24%)
  starting transfers between devices  30.3 us (14%)
  other arithmetic  26.1 us (12%)
  waiting for transfers between devices  26 us (12%)
  matrix products  12.5 us (6%)
  between operations  5.45 us (3%)
    unnamed x14, local copies, waits for them, and re-layouts  51.4 us
    pallas_call x2, Pallas kernels, block_apply(): pl.pallas_call(kernel, grid_spec=grid_spec, out_shape=out_shape, compiler...  51.1 us
    ppermute x2, waiting for transfers between devices, from_behind(): return lax.ppermute(block, axis, route)  16 us
    dot_general x3, matrix products, clean(): lax.dot_general(margin_b, wins, (((0,), (0,)), ((), ())), preferred_eleme...  12.5 us
    ppermute x9, starting transfers between devices, row_sum(): lax.ppermute(part, 'row', [(i, (i + step) % count) for i in range(count)])  10.7 us
    broadcast_in_dim x1, other arithmetic, shards(): return (residual[None], margin_pencil[None], energy_pencil[None])  9.49 us
    ppermute x2, starting transfers between devices, from_behind(): return lax.ppermute(block, axis, route)  6.6 us
    ppermute x9, waiting for transfers between devices, row_sum(): lax.ppermute(part, 'row', [(i, (i + step) % count) for i in range(count)])  6.49 us
  transfers between devices with their start and end apart: 17, of which 7 were waited for; matrix products, arithmetic and copies ran while one was open for 30% of the time, Pallas kernels for 0%

profile of v10, /device:TPU:12, one launch (start us, length us, event | category | flops | bytes accessed | tf_op | source)
XLA Modules:
  0.0 207.4 jit_solution(16184142971416655208)
XLA Ops:
  0.6 1.3 fusion.23
  5.2 1.3 add_compare_fusion
  7.4 3.3 %broadcast_select_fusion = bf16[128,24576]{1,0:T(8,128)(2,1)S(1)} fusion(pred[128]{0:T(512)(128)(4,1)S(1)} %iota_compare_fusion.1, bf16[1,128,24576]{2,1,0:T(8,128)(2,1)} %param.6), kind=kLoop, calls=%fused_computation.6 | loop fusion | flops 3145728 | bytes 12583040 | tf_op jit(solution)/shard_map/jit(_where)/select_n | solution.py:218
  10.7 2.7 %copy-done.1 = bf16[128,24576]{1,0:T(8,128)(2,1)} copy-done((bf16[128,24576]{1,0:T(8,128)(2,1)}, bf16[128,24576]{1,0:T(8,128)(2,1)S(1)}, u32[]{:S(2)}) %copy-start.1) | copy-done | bytes 6291480
  14.8 3.5 %collective-permute-start = (bf16[192,256]{1,0:T(8,128)(2,1)S(1)}, bf16[192,256]{1,0:T(8,128)(2,1)S(1)}, u32[]{:S(2)}, u32[]{:S(2)}) collective-permute-start(bf16[192,256]{1,0:T(8,128)(2,1)S(1)} %pad_maximum_fusion.5), channel_id=1, source_target_pairs={{0,1},{1,2},{2,3},{4,5},{5,6},{6,7},{8,9},{9,10},{10,11},{12,13},{... | collective-permute-start | bytes 294920 | tf_op jit(solution)/shard_map/ppermute | solution.py:229
  18.3 2.4 %collective-permute-start.1 = (bf16[192,256]{1,0:T(8,128)(2,1)S(1)}, bf16[192,256]{1,0:T(8,128)(2,1)S(1)}, u32[]{:S(2)}, u32[]{:S(2)}) collective-permute-start(bf16[192,256]{1,0:T(8,128)(2,1)S(1)} %pad_maximum_fusion.6), channel_id=1, source_target_pairs={{1,0},{2,1},{3,2},{5,4},{6,5},{7,6},{9,8},{10,9},{11,10},{13,12},{... | collective-permute-start | bytes 294920 | tf_op jit(solution)/shard_map/ppermute | solution.py:232
  20.7 3.0 %bitcast_select_fusion = (bf16[32,24576]{1,0:T(8,128)(2,1)S(1)}, bf16[32,24576]{1,0:T(8,128)(2,1)S(1)}) fusion(bf16[1,128,24576]{2,1,0:T(8,128)(2,1)} %param.6, s32[]{:T(128)S(6)} %select_n.133, pred[32]{0:T(512)(128)(4,1)S(1)} %get-tuple-element.43, s32[]{:T(128)S(6)} %select_n.130, pred[32]{0:T(512)(128)(4,1)S(1)} %get-tuple-element.44), kind=kLoop, calls=%fused_computation.11 | loop fusion | flops 1572864 | bytes 6291528 | tf_op jit(solution)/shard_map/jit(_where)/select_n | solution.py:185
  26.1 1.9 collective-permute-start.3
  28.8 1.3 pad_maximum_fusion.1
  30.1 4.7 %collective-permute-start.2 = (bf16[32,25088]{1,0:T(8,128)(2,1)}, bf16[32,25088]{1,0:T(8,128)(2,1)}, u32[]{:S(2)}, u32[]{:S(2)}) collective-permute-start(bf16[32,25088]{1,0:T(8,128)(2,1)} %pad_maximum_fusion.1), channel_id=1, source_target_pairs={{0,4},{4,8},{8,12},{12,16},{16,20},{20,24},{24,28},{1,5},{5,9},{9,... | collective-permute-start | bytes 4816904 | tf_op jit(solution)/shard_map/ppermute | solution.py:19
  34.8 2.6 %collective-permute-start.4 = (bf16[32,25088]{1,0:T(8,128)(2,1)}, bf16[32,25088]{1,0:T(8,128)(2,1)}, u32[]{:S(2)}, u32[]{:S(2)}) collective-permute-start(bf16[32,25088]{1,0:T(8,128)(2,1)} %pad_maximum_fusion.1), channel_id=1, source_target_pairs={{0,8},{8,16},{16,24},{1,9},{9,17},{17,25},{2,10},{10,18},{18,26},{... | collective-permute-start | bytes 4816904 | tf_op jit(solution)/shard_map/ppermute | solution.py:207
  37.4 23.3 %copy.12.refs_0_ = bf16[256,96,288]{2,1,0:T(8,128)(2,1)} copy(bf16[256,96,288]{0,2,1:T(8,128)(2,1)} %param.9) | data formatting | bytes 28311552 | tf_op args[3]
  60.7 23.3 %copy.13.refs_1_ = bf16[256,96,288]{2,1,0:T(8,128)(2,1)} copy(bf16[256,96,288]{0,2,1:T(8,128)(2,1)} %param.10) | data formatting | bytes 28311552 | tf_op args[4]
  84.1 16.0 %collective-permute-done.2 = bf16[32,25088]{1,0:T(8,128)(2,1)} collective-permute-done((bf16[32,25088]{1,0:T(8,128)(2,1)}, bf16[32,25088]{1,0:T(8,128)(2,1)}, u32[]{:S(2)}, u32[]{:S(2)}) %collective-permute-start.2) | collective-permute-done | bytes 1605664 | tf_op jit(solution)/shard_map/ppermute | solution.py:19
  100.1 2.5 %collective-permute-start.6 = (bf16[32,25088]{1,0:T(8,128)(2,1)}, bf16[32,25088]{1,0:T(8,128)(2,1)}, u32[]{:S(2)}, u32[]{:S(2)}) collective-permute-start(bf16[32,25088]{1,0:T(8,128)(2,1)} %collective-permute-done.2), channel_id=1, source_target_pairs={{0,4},{8,12},{16,20},{24,28},{1,5},{9,13},{17,21},{25,29},{2,6},{1... | collective-permute-start | bytes 4816904 | tf_op jit(solution)/shard_map/ppermute | solution.py:213
  104.8 1.6 broadcast_select_fusion.2
  106.4 2.4 %collective-permute-done.7 = bf16[32,25088]{1,0:T(8,128)(2,1)S(1)} collective-permute-done((bf16[32,25088]{1,0:T(8,128)(2,1)S(1)}, bf16[32,25088]{1,0:T(8,128)(2,1)S(1)}, u32[]{:S(2)}, u32[]{:S(2)}) %collective-permute-start.7) | collective-permute-done | bytes 1605664 | tf_op jit(solution)/shard_map/ppermute | solution.py:215
  109.0 2.6 %pad_maximum_fusion.x_hbm = bf16[128,25088]{1,0:T(8,128)(2,1)S(1)} fusion(bf16[32,25088]{1,0:T(8,128)(2,1)S(1)} %broadcast_select_fusion.1, bf16[32,25088]{1,0:T(8,128)(2,1)S(1)} %collective-permute-done.3, bf16[32,25088]{1,0:T(8,128)(2,1)} %collective-permute-done.2, bf16[32,25088]{1,0:T(8,128)(2,1)S(1)} %broadcast_select_fusion.2), kind=kLoop, calls=%fused_computation.3 | loop fusion | flops 25690112 | bytes 12845056 | tf_op jit(solution)/shard_map/concatenate | solution.py:241
  112.3 2.0 copy-done
  114.3 20.8 %shard_map.85 = f32[1,128,128]{2,1,0:T(8,128)} custom-call(s32[768]{0:T(1024)} %reshape.80.shift_ref, s32[1]{0:T(128)} %copy.14.count_ref, bf16[128,25088]{1,0:T(8,128)(2,1)} %copy-done, bf16[128,256]{1,0:T(8,128)(2,1)} %get-tuple-element.22.lo_ref, bf16[128,256]{1,0:T(8,128)(2,1)} %get-tuple-element.21.hi_ref, bf16[256,96,288]{2,1,0:T(8,128)(2,1)} %copy.12.refs_0_, ...), custom_call_target="tpu_custom_call" | custom-call | tf_op jit(solution)/shard_map/pallas_call | solution.py:153
  135.1 1.6 collective-permute-start.8
  138.8 1.8 collective-permute-done.8
  140.6 2.4 %collective-permute-done.9 = f32[128,128]{1,0:T(8,128)S(1)} collective-permute-done((f32[128,128]{1,0:T(8,128)}, f32[128,128]{1,0:T(8,128)S(1)}, u32[]{:S(2)}, u32[]{:S(2)}) %collective-permute-start.9) | collective-permute-done | bytes 65568 | tf_op jit(solution)/shard_map/ppermute | solution.py:167
  143.0 1.4 collective-permute-done.10
  145.4 9.2 %fusion.x_hbm = bf16[128,24576]{1,0:T(8,128)(2,1)} fusion(bf16[128,128]{1,0:T(8,128)(2,1)S(1)} %fusion.3, bf16[128,24576]{1,0:T(8,128)(2,1)} %copy-done.1, bf16[128,25088]{1,0:T(8,128)(2,1)} %copy-done), kind=kOutput, calls=%fused_computation.1 | convolution fusion | flops 814743552 | bytes 18907136 | tf_op jit(solution)/shard_map/dot_general | solution.py:260
  154.5 1.7 subtract_convert_fusion.1.hi_ref
  156.2 1.7 subtract_convert_fusion.2.lo_ref
  157.9 30.3 %shard_map.86 = (bf16[128,24576]{1,0:T(8,128)(2,1)}, bf16[128,24576]{1,0:T(8,128)(2,1)}, f32[2,128,128]{2,1,0:T(8,128)}) custom-call(s32[768]{0:T(1024)} %reshape.80.shift_ref, s32[1]{0:T(128)} %copy.14.count_ref, bf16[128,24576]{1,0:T(8,128)(2,1)} %fusion.x_hbm, bf16[128,256]{1,0:T(8,128)(2,1)} %subtract_convert_fusion.2.lo_ref, ...), custom_call_target="tpu_custom_call" | custom-call | tf_op jit(solution)/shard_map/pallas_call | solution.py:153
  189.3 2.5 %collective-permute-start.12 = (f32[2,128]{1,0:T(2,128)S(1)}, f32[2,128]{1,0:T(2,128)S(1)}, u32[]{:S(2)}, u32[]{:S(2)}) collective-permute-start(f32[2,128]{1,0:T(2,128)S(1)} %select_reduce_fusion), channel_id=1, source_target_pairs={{0,2},{1,3},{2,0},{3,1},{4,6},{5,7},{6,4},{7,5},{8,10},{9,11},{10,... | collective-permute-start | bytes 3080 | tf_op jit(solution)/shard_map/ppermute | solution.py:167
  191.8 1.3 collective-permute-start.13
  193.8 2.3 %collective-permute-start.15 = (f32[2,128,128]{2,1,0:T(8,128)}, f32[2,128,128]{2,1,0:T(8,128)S(1)}, u32[]{:S(2)}, u32[]{:S(2)}) collective-permute-start(f32[2,128,128]{2,1,0:T(8,128)} %get-tuple-element.19), channel_id=1, source_target_pairs={{0,2},{1,3},{2,0},{3,1},{4,6},{5,7},{6,4},{7,5},{8,10},{9,11},{10,... | collective-permute-start | bytes 393224 | tf_op jit(solution)/shard_map/ppermute | solution.py:167
  196.3 9.5 %fusion.1 = bf16[1,128,24576]{2,1,0:T(8,128)(2,1)} fusion(bf16[128,24576]{1,0:T(8,128)(2,1)} %get-tuple-element.20, bf16[128,24576]{1,0:T(8,128)(2,1)} %get-tuple-element.18, f32[128]{0:T(128)S(1)} %fusion.9), kind=kLoop, calls=%fused_computation.4 | loop fusion | flops 15728640 | bytes 18874880 | tf_op jit(solution)/shard_map/broadcast_in_dim | solution.py:287
  (54 shorter events, 13.8 us)
Async XLA Ops:
  10.7 2.7 %copy-start.1 = (bf16[128,24576]{1,0:T(8,128)(2,1)}, bf16[128,24576]{1,0:T(8,128)(2,1)S(1)}, u32[]{:S(2)}) copy-start(bf16[128,24576]{1,0:T(8,128)(2,1)S(1)} %broadcast_select_fusion) | copy-start | bytes 18874372
  14.8 8.9 %collective-permute-start = (bf16[192,256]{1,0:T(8,128)(2,1)S(1)}, bf16[192,256]{1,0:T(8,128)(2,1)S(1)}, u32[]{:S(2)}, u32[]{:S(2)}) collective-permute-start(bf16[192,256]{1,0:T(8,128)(2,1)S(1)} %pad_maximum_fusion.5), channel_id=1, source_target_pairs={{0,1},{1,2},{2,3},{4,5},{5,6},{6,7},{8,9},{9,10},{10,11},{12,13},{... | collective-permute-start | bytes 294920 | tf_op jit(solution)/shard_map/ppermute | solution.py:229
  18.3 6.5 %collective-permute-start.1 = (bf16[192,256]{1,0:T(8,128)(2,1)S(1)}, bf16[192,256]{1,0:T(8,128)(2,1)S(1)}, u32[]{:S(2)}, u32[]{:S(2)}) collective-permute-start(bf16[192,256]{1,0:T(8,128)(2,1)S(1)} %pad_maximum_fusion.6), channel_id=1, source_target_pairs={{1,0},{2,1},{3,2},{5,4},{6,5},{7,6},{9,8},{10,9},{11,10},{13,12},{... | collective-permute-start | bytes 294920 | tf_op jit(solution)/shard_map/ppermute | solution.py:232
  24.8 5.3 %copy-start.3 = (bf16[192,256]{1,0:T(8,128)(2,1)}, bf16[192,256]{1,0:T(8,128)(2,1)S(1)}, u32[]{:S(2)}) copy-start(bf16[192,256]{1,0:T(8,128)(2,1)S(1)} %collective-permute-done.1) | copy-start | bytes 294916
  26.1 58.0 %collective-permute-start.3 = (bf16[32,25088]{1,0:T(8,128)(2,1)}, bf16[32,25088]{1,0:T(8,128)(2,1)S(1)}, u32[]{:S(2)}, u32[]{:S(2)}) collective-permute-start(bf16[32,25088]{1,0:T(8,128)(2,1)} %pad_maximum_fusion.2), channel_id=1, source_target_pairs={{4,0},{8,4},{12,8},{16,12},{20,16},{24,20},{28,24},{5,1},{9,5},{13... | collective-permute-start | bytes 4816904 | tf_op jit(solution)/shard_map/ppermute | solution.py:19
  28.0 56.1 %collective-permute-start.5 = (bf16[32,25088]{1,0:T(8,128)(2,1)}, bf16[32,25088]{1,0:T(8,128)(2,1)S(1)}, u32[]{:S(2)}, u32[]{:S(2)}) collective-permute-start(bf16[32,25088]{1,0:T(8,128)(2,1)} %pad_maximum_fusion.2), channel_id=1, source_target_pairs={{12,4},{20,12},{28,20},{13,5},{21,13},{29,21},{14,6},{22,14},{30,2... | collective-permute-start | bytes 4816904 | tf_op jit(solution)/shard_map/ppermute | solution.py:208
  30.1 70.0 %collective-permute-start.2 = (bf16[32,25088]{1,0:T(8,128)(2,1)}, bf16[32,25088]{1,0:T(8,128)(2,1)}, u32[]{:S(2)}, u32[]{:S(2)}) collective-permute-start(bf16[32,25088]{1,0:T(8,128)(2,1)} %pad_maximum_fusion.1), channel_id=1, source_target_pairs={{0,4},{4,8},{8,12},{12,16},{16,20},{20,24},{24,28},{1,5},{5,9},{9,... | collective-permute-start | bytes 4816904 | tf_op jit(solution)/shard_map/ppermute | solution.py:19
  34.8 65.3 %collective-permute-start.4 = (bf16[32,25088]{1,0:T(8,128)(2,1)}, bf16[32,25088]{1,0:T(8,128)(2,1)}, u32[]{:S(2)}, u32[]{:S(2)}) collective-permute-start(bf16[32,25088]{1,0:T(8,128)(2,1)} %pad_maximum_fusion.1), channel_id=1, source_target_pairs={{0,8},{8,16},{16,24},{1,9},{9,17},{17,25},{2,10},{10,18},{18,26},{... | collective-permute-start | bytes 4816904 | tf_op jit(solution)/shard_map/ppermute | solution.py:207
  60.7 41.8 %copy-start.5 = (s32[256,3]{0,1:T(4,128)S(1)}, s32[256,3]{0,1:T(4,128)}, u32[]{:S(2)}) copy-start(s32[256,3]{0,1:T(4,128)} %param.11) | copy-start | bytes 9220
  100.1 4.7 %collective-permute-start.6 = (bf16[32,25088]{1,0:T(8,128)(2,1)}, bf16[32,25088]{1,0:T(8,128)(2,1)}, u32[]{:S(2)}, u32[]{:S(2)}) collective-permute-start(bf16[32,25088]{1,0:T(8,128)(2,1)} %collective-permute-done.2), channel_id=1, source_target_pairs={{0,4},{8,12},{16,20},{24,28},{1,5},{9,13},{17,21},{25,29},{2,6},{1... | collective-permute-start | bytes 4816904 | tf_op jit(solution)/shard_map/ppermute | solution.py:213
  103.5 5.3 %collective-permute-start.7 = (bf16[32,25088]{1,0:T(8,128)(2,1)S(1)}, bf16[32,25088]{1,0:T(8,128)(2,1)S(1)}, u32[]{:S(2)}, u32[]{:S(2)}) collective-permute-start(bf16[32,25088]{1,0:T(8,128)(2,1)S(1)} %collective-permute-done.3), channel_id=1, source_target_pairs={{4,0},{12,8},{20,16},{28,24},{5,1},{13,9},{21,17},{29,25},{6,2},{1... | collective-permute-start | bytes 4816904 | tf_op jit(solution)/shard_map/ppermute | solution.py:215
  111.6 2.7 %copy-start = (bf16[128,25088]{1,0:T(8,128)(2,1)}, bf16[128,25088]{1,0:T(8,128)(2,1)S(1)}, u32[]{:S(2)}) copy-start(bf16[128,25088]{1,0:T(8,128)(2,1)S(1)} %pad_maximum_fusion.x_hbm) | copy-start | bytes 19267588
  135.1 5.6 %collective-permute-start.8 = (f32[128,128]{1,0:T(8,128)}, f32[128,128]{1,0:T(8,128)S(1)}, u32[]{:S(2)}, u32[]{:S(2)}) collective-permute-start(f32[128,128]{1,0:T(8,128)} %bitcast.46), channel_id=1, source_target_pairs={{0,1},{1,2},{2,3},{3,0},{4,5},{5,6},{6,7},{7,4},{8,9},{9,10},{10,1... | collective-permute-start | bytes 196616 | tf_op jit(solution)/shard_map/ppermute | solution.py:167
  136.7 6.3 %collective-permute-start.9 = (f32[128,128]{1,0:T(8,128)}, f32[128,128]{1,0:T(8,128)S(1)}, u32[]{:S(2)}, u32[]{:S(2)}) collective-permute-start(f32[128,128]{1,0:T(8,128)} %bitcast.47), channel_id=1, source_target_pairs={{0,2},{1,3},{2,0},{3,1},{4,6},{5,7},{6,4},{7,5},{8,10},{9,11},{10,... | collective-permute-start | bytes 196616 | tf_op jit(solution)/shard_map/ppermute | solution.py:167
  137.9 6.5 %collective-permute-start.10 = (f32[128,128]{1,0:T(8,128)}, f32[128,128]{1,0:T(8,128)S(1)}, u32[]{:S(2)}, u32[]{:S(2)}) collective-permute-start(f32[128,128]{1,0:T(8,128)} %bitcast.48), channel_id=1, source_target_pairs={{0,3},{1,0},{2,1},{3,2},{4,7},{5,4},{6,5},{7,6},{8,11},{9,8},{10,9... | collective-permute-start | bytes 196616 | tf_op jit(solution)/shard_map/ppermute | solution.py:167
  145.4 9.2 %copy-start.4 = (bf16[192,256]{1,0:T(8,128)(2,1)S(1)}, bf16[192,256]{1,0:T(8,128)(2,1)}, u32[]{:S(2)}) copy-start(bf16[192,256]{1,0:T(8,128)(2,1)} %copy-done.3) | copy-start | bytes 294916
  189.2 6.9 %collective-permute-start.11 = (f32[2,128]{1,0:T(2,128)S(1)}, f32[2,128]{1,0:T(2,128)S(1)}, u32[]{:S(2)}, u32[]{:S(2)}) collective-permute-start(f32[2,128]{1,0:T(2,128)S(1)} %select_reduce_fusion), channel_id=1, source_target_pairs={{0,1},{1,2},{2,3},{3,0},{4,5},{5,6},{6,7},{7,4},{8,9},{9,10},{10,1... | collective-permute-start | bytes 3080 | tf_op jit(solution)/shard_map/ppermute | solution.py:167
  189.3 7.0 %collective-permute-start.12 = (f32[2,128]{1,0:T(2,128)S(1)}, f32[2,128]{1,0:T(2,128)S(1)}, u32[]{:S(2)}, u32[]{:S(2)}) collective-permute-start(f32[2,128]{1,0:T(2,128)S(1)} %select_reduce_fusion), channel_id=1, source_target_pairs={{0,2},{1,3},{2,0},{3,1},{4,6},{5,7},{6,4},{7,5},{8,10},{9,11},{10,... | collective-permute-start | bytes 3080 | tf_op jit(solution)/shard_map/ppermute | solution.py:167
  191.8 4.4 %collective-permute-start.13 = (f32[2,128]{1,0:T(2,128)S(1)}, f32[2,128]{1,0:T(2,128)S(1)}, u32[]{:S(2)}, u32[]{:S(2)}) collective-permute-start(f32[2,128]{1,0:T(2,128)S(1)} %select_reduce_fusion), channel_id=1, source_target_pairs={{0,3},{1,0},{2,1},{3,2},{4,7},{5,4},{6,5},{7,6},{8,11},{9,8},{10,9... | collective-permute-start | bytes 3080 | tf_op jit(solution)/shard_map/ppermute | solution.py:167
  193.1 12.7 %collective-permute-start.14 = (f32[2,128,128]{2,1,0:T(8,128)}, f32[2,128,128]{2,1,0:T(8,128)S(1)}, u32[]{:S(2)}, u32[]{:S(2)}) collective-permute-start(f32[2,128,128]{2,1,0:T(8,128)} %get-tuple-element.19), channel_id=1, source_target_pairs={{0,1},{1,2},{2,3},{3,0},{4,5},{5,6},{6,7},{7,4},{8,9},{9,10},{10,1... | collective-permute-start | bytes 393224 | tf_op jit(solution)/shard_map/ppermute | solution.py:167
  193.8 12.0 %collective-permute-start.15 = (f32[2,128,128]{2,1,0:T(8,128)}, f32[2,128,128]{2,1,0:T(8,128)S(1)}, u32[]{:S(2)}, u32[]{:S(2)}) collective-permute-start(f32[2,128,128]{2,1,0:T(8,128)} %get-tuple-element.19), channel_id=1, source_target_pairs={{0,2},{1,3},{2,0},{3,1},{4,6},{5,7},{6,4},{7,5},{8,10},{9,11},{10,... | collective-permute-start | bytes 393224 | tf_op jit(solution)/shard_map/ppermute | solution.py:167
  196.1 10.5 %collective-permute-start.16 = (f32[2,128,128]{2,1,0:T(8,128)}, f32[2,128,128]{2,1,0:T(8,128)S(1)}, u32[]{:S(2)}, u32[]{:S(2)}) collective-permute-start(f32[2,128,128]{2,1,0:T(8,128)} %get-tuple-element.19), channel_id=1, source_target_pairs={{0,3},{1,0},{2,1},{3,2},{4,7},{5,4},{6,5},{7,6},{8,11},{9,8},{10,9... | collective-permute-start | bytes 393224 | tf_op jit(solution)/shard_map/ppermute | solution.py:167
  196.3 10.3 %copy-start.2 = (f32[2,128,128]{2,1,0:T(8,128)S(1)}, f32[2,128,128]{2,1,0:T(8,128)}, u32[]{:S(2)}) copy-start(f32[2,128,128]{2,1,0:T(8,128)} %get-tuple-element.19) | copy-start | bytes 393220

commit v11 on v8

--- a/solution.py
+++ b/solution.py
@@ -116,7 +116,7 @@
     slots, entries = cells.shape
     block_rows, blk, width = matrices[0].shape
     rim = lower.shape[1]
-    group = 64 if block_rows % 64 == 0 else block_rows
+    group = 32 if block_rows % 32 == 0 else block_rows
     chunk = 512
     nmat = len(matrices)
     given = pair is not None

time: 208 us -> 208 us (level)
  no operation moved by 1% of the time
where the time goes in v11:
time: 208 us; the launch traced here: 206 us
  local copies, waits for them, and re-layouts  56.6 us (27%)
  Pallas kernels  52.1 us (25%)
  starting transfers between devices  31.3 us (15%)
  other arithmetic  26.9 us (13%)
  waiting for transfers between devices  26.2 us (13%)
  matrix products  7.3 us (4%)
  between operations  5.46 us (3%)
    pallas_call x2, Pallas kernels, block_apply(): pl.pallas_call(kernel, grid_spec=grid_spec, out_shape=out_shape, compiler...  52.1 us
    unnamed x18, local copies, waits for them, and re-layouts  49.4 us
    ppermute x2, waiting for transfers between devices, from_behind(): return lax.ppermute(block, axis, route)  14.8 us
    ppermute x9, starting transfers between devices, row_sum(): lax.ppermute(part, 'row', [(i, (i + step) % count) for i in range(count)])  10.7 us
    broadcast_in_dim x1, other arithmetic, shards(): return (residual[None], margin_pencil[None], energy_pencil[None])  9.49 us
    ppermute x9, waiting for transfers between devices, row_sum(): lax.ppermute(part, 'row', [(i, (i + step) % count) for i in range(count)])  7.97 us
    dot_general x3, matrix products, clean(): lax.dot_general(margin_b, wins, (((0,), (0,)), ((), ())), preferred_eleme...  7.3 us
    ppermute x2, starting transfers between devices, from_behind(): return lax.ppermute(block, axis, route)  5.56 us
  transfers between devices with their start and end apart: 17, of which 7 were waited for; matrix products, arithmetic and copies ran while one was open for 31% of the time, Pallas kernels for 0%

profile of v11, /device:TPU:12, one launch (start us, length us, event | category | flops | bytes accessed | tf_op | source)
XLA Modules:
  0.0 205.8 jit_solution(9620568633776447069)
XLA Ops:
  0.6 1.3 fusion.14
  5.2 1.3 add_compare_fusion
  7.4 3.3 %broadcast_select_fusion = bf16[128,24576]{1,0:T(8,128)(2,1)S(1)} fusion(pred[128]{0:T(512)(128)(4,1)S(1)} %iota_compare_fusion.1, bf16[1,128,24576]{2,1,0:T(8,128)(2,1)} %param.6), kind=kLoop, calls=%fused_computation.5 | loop fusion | flops 3145728 | bytes 12583040 | tf_op jit(solution)/shard_map/jit(_where)/select_n | solution.py:217
  10.7 2.6 %copy-done = bf16[128,24576]{1,0:T(8,128)(2,1)} copy-done((bf16[128,24576]{1,0:T(8,128)(2,1)}, bf16[128,24576]{1,0:T(8,128)(2,1)S(1)}, u32[]{:S(2)}) %copy-start) | copy-done | bytes 6291480
  14.7 3.5 %collective-permute-start = (bf16[192,256]{1,0:T(8,128)(2,1)S(1)}, bf16[192,256]{1,0:T(8,128)(2,1)S(1)}, u32[]{:S(2)}, u32[]{:S(2)}) collective-permute-start(bf16[192,256]{1,0:T(8,128)(2,1)S(1)} %pad_maximum_fusion.5), channel_id=1, source_target_pairs={{0,1},{1,2},{2,3},{4,5},{5,6},{6,7},{8,9},{9,10},{10,11},{12,13},{... | collective-permute-start | bytes 294920 | tf_op jit(solution)/shard_map/ppermute | solution.py:228
  18.2 2.4 %collective-permute-start.1 = (bf16[192,256]{1,0:T(8,128)(2,1)S(1)}, bf16[192,256]{1,0:T(8,128)(2,1)S(1)}, u32[]{:S(2)}, u32[]{:S(2)}) collective-permute-start(bf16[192,256]{1,0:T(8,128)(2,1)S(1)} %pad_maximum_fusion.6), channel_id=1, source_target_pairs={{1,0},{2,1},{3,2},{5,4},{6,5},{7,6},{9,8},{10,9},{11,10},{13,12},{... | collective-permute-start | bytes 294920 | tf_op jit(solution)/shard_map/ppermute | solution.py:231
  20.6 3.1 %bitcast_select_fusion = (bf16[32,24576]{1,0:T(8,128)(2,1)S(1)}, bf16[32,24576]{1,0:T(8,128)(2,1)S(1)}) fusion(bf16[1,128,24576]{2,1,0:T(8,128)(2,1)} %param.6, s32[]{:T(128)S(6)} %select_n.133, pred[32]{0:T(512)(128)(4,1)S(1)} %get-tuple-element.43, s32[]{:T(128)S(6)} %select_n.130, pred[32]{0:T(512)(128)(4,1)S(1)} %get-tuple-element.44), kind=kLoop, calls=%fused_computation.10 | loop fusion | flops 1572864 | bytes 6291528 | tf_op jit(solution)/shard_map/jit(_where)/select_n | solution.py:184
  24.7 1.3 pad_maximum_fusion.2
  26.0 1.9 collective-permute-start.3
  27.9 1.8 collective-permute-start.5
  29.7 1.3 pad_maximum_fusion.1
  31.0 3.7 %collective-permute-start.2 = (bf16[32,25088]{1,0:T(8,128)(2,1)}, bf16[32,25088]{1,0:T(8,128)(2,1)S(1)}, u32[]{:S(2)}, u32[]{:S(2)}) collective-permute-start(bf16[32,25088]{1,0:T(8,128)(2,1)} %pad_maximum_fusion.1), channel_id=1, source_target_pairs={{0,4},{4,8},{8,12},{12,16},{16,20},{20,24},{24,28},{1,5},{5,9},{9,... | collective-permute-start | bytes 4816904 | tf_op jit(solution)/shard_map/ppermute | solution.py:19
  34.6 3.6 %collective-permute-start.4 = (bf16[32,25088]{1,0:T(8,128)(2,1)}, bf16[32,25088]{1,0:T(8,128)(2,1)}, u32[]{:S(2)}, u32[]{:S(2)}) collective-permute-start(bf16[32,25088]{1,0:T(8,128)(2,1)} %pad_maximum_fusion.1), channel_id=1, source_target_pairs={{0,8},{8,16},{16,24},{1,9},{9,17},{17,25},{2,10},{10,18},{18,26},{... | collective-permute-start | bytes 4816904 | tf_op jit(solution)/shard_map/ppermute | solution.py:206
  38.3 23.5 %copy.12.refs_0_ = bf16[256,96,288]{2,1,0:T(8,128)(2,1)} copy(bf16[256,96,288]{0,2,1:T(8,128)(2,1)} %param.9) | data formatting | bytes 28311552 | tf_op args[3]
  61.8 23.3 %copy.13.refs_1_ = bf16[256,96,288]{2,1,0:T(8,128)(2,1)} copy(bf16[256,96,288]{0,2,1:T(8,128)(2,1)} %param.10) | data formatting | bytes 28311552 | tf_op args[4]
  85.1 14.8 %collective-permute-done.2 = bf16[32,25088]{1,0:T(8,128)(2,1)S(1)} collective-permute-done((bf16[32,25088]{1,0:T(8,128)(2,1)}, bf16[32,25088]{1,0:T(8,128)(2,1)S(1)}, u32[]{:S(2)}, u32[]{:S(2)}) %collective-permute-start.2) | collective-permute-done | bytes 1605664 | tf_op jit(solution)/shard_map/ppermute | solution.py:19
  99.9 2.5 %collective-permute-start.6 = (bf16[32,25088]{1,0:T(8,128)(2,1)S(1)}, bf16[32,25088]{1,0:T(8,128)(2,1)}, u32[]{:S(2)}, u32[]{:S(2)}) collective-permute-start(bf16[32,25088]{1,0:T(8,128)(2,1)S(1)} %collective-permute-done.2), channel_id=1, source_target_pairs={{0,4},{8,12},{16,20},{24,28},{1,5},{9,13},{17,21},{25,29},{2,6},{1... | collective-permute-start | bytes 4816904 | tf_op jit(solution)/shard_map/ppermute | solution.py:212
  103.3 1.3 collective-permute-start.7
  104.6 1.6 broadcast_select_fusion.2
  106.2 2.4 %collective-permute-done.7 = bf16[32,25088]{1,0:T(8,128)(2,1)S(1)} collective-permute-done((bf16[32,25088]{1,0:T(8,128)(2,1)S(1)}, bf16[32,25088]{1,0:T(8,128)(2,1)S(1)}, u32[]{:S(2)}, u32[]{:S(2)}) %collective-permute-start.7) | collective-permute-done | bytes 1605664 | tf_op jit(solution)/shard_map/ppermute | solution.py:214
  109.5 2.5 %pad_maximum_fusion = bf16[128,25088]{1,0:T(8,128)(2,1)S(1)} fusion(bf16[32,25088]{1,0:T(8,128)(2,1)S(1)} %broadcast_select_fusion.1, bf16[32,25088]{1,0:T(8,128)(2,1)S(1)} %collective-permute-done.3, bf16[32,25088]{1,0:T(8,128)(2,1)} %copy-done.1, bf16[32,25088]{1,0:T(8,128)(2,1)S(1)} %broadcast_select_fusion.2), kind=kLoop, calls=%fused_computation.3 | loop fusion | flops 25690112 | bytes 12845056 | tf_op jit(solution)/shard_map/concatenate | solution.py:240
  112.1 3.3 %slice.102.x_hbm = bf16[128,24576]{1,0:T(8,128)(2,1)} slice(bf16[128,25088]{1,0:T(8,128)(2,1)S(1)} %pad_maximum_fusion), slice={[0:128], [0:24576]} | slice | bytes 12582912 | tf_op jit(solution)/shard_map/slice | solution.py:241
  115.4 21.9 %shard_map.85 = f32[1,128,128]{2,1,0:T(8,128)} custom-call(s32[768]{0:T(1024)} %reshape.80.shift_ref, s32[1]{0:T(128)} %copy.14.count_ref, bf16[128,24576]{1,0:T(8,128)(2,1)} %slice.102.x_hbm, bf16[128,256]{1,0:T(8,128)(2,1)} %get-tuple-element.22.lo_ref, bf16[128,256]{1,0:T(8,128)(2,1)} %get-tuple-element.21.hi_ref, bf16[256,96,288]{2,1,0:T(8,128)(2,1)} %copy.12.refs_0_, ...), custom_call_target="tpu_custom_call" | custom-call | tf_op jit(solution)/shard_map/pallas_call | solution.py:152
  137.3 1.6 collective-permute-start.8
  142.0 2.7 %collective-permute-done.9 = f32[128,128]{1,0:T(8,128)S(1)} collective-permute-done((f32[128,128]{1,0:T(8,128)}, f32[128,128]{1,0:T(8,128)S(1)}, u32[]{:S(2)}, u32[]{:S(2)}) %collective-permute-start.9) | collective-permute-done | bytes 65568 | tf_op jit(solution)/shard_map/ppermute | solution.py:166
  144.7 2.8 %collective-permute-done.10 = f32[128,128]{1,0:T(8,128)S(1)} collective-permute-done((f32[128,128]{1,0:T(8,128)}, f32[128,128]{1,0:T(8,128)S(1)}, u32[]{:S(2)}, u32[]{:S(2)}) %collective-permute-start.10) | collective-permute-done | bytes 65568 | tf_op jit(solution)/shard_map/ppermute | solution.py:166
  148.5 5.7 %fusion.x_hbm = bf16[128,24576]{1,0:T(8,128)(2,1)} fusion(bf16[128,128]{1,0:T(8,128)(2,1)S(1)} %fusion.2, bf16[128,24576]{1,0:T(8,128)(2,1)} %copy-done, bf16[128,25088]{1,0:T(8,128)(2,1)S(1)} %pad_maximum_fusion), kind=kOutput, calls=%fused_computation.1 | convolution fusion | flops 814743552 | bytes 18907136 | tf_op jit(solution)/shard_map/dot_general | solution.py:252
  155.8 30.2 %shard_map.86 = (bf16[128,24576]{1,0:T(8,128)(2,1)}, bf16[128,24576]{1,0:T(8,128)(2,1)}, f32[2,128,128]{2,1,0:T(8,128)}) custom-call(s32[768]{0:T(1024)} %reshape.80.shift_ref, s32[1]{0:T(128)} %copy.14.count_ref, bf16[128,24576]{1,0:T(8,128)(2,1)} %fusion.x_hbm, bf16[128,256]{1,0:T(8,128)(2,1)} %subtract_convert_fusion.2.lo_ref, ...), custom_call_target="tpu_custom_call" | custom-call | tf_op jit(solution)/shard_map/pallas_call | solution.py:152
  187.1 2.4 %collective-permute-start.12 = (f32[2,128]{1,0:T(2,128)S(1)}, f32[2,128]{1,0:T(2,128)S(1)}, u32[]{:S(2)}, u32[]{:S(2)}) collective-permute-start(f32[2,128]{1,0:T(2,128)S(1)} %select_reduce_fusion), channel_id=1, source_target_pairs={{0,2},{1,3},{2,0},{3,1},{4,6},{5,7},{6,4},{7,5},{8,10},{9,11},{10,... | collective-permute-start | bytes 3080 | tf_op jit(solution)/shard_map/ppermute | solution.py:166
  191.5 2.4 %collective-permute-start.15 = (f32[2,128,128]{2,1,0:T(8,128)}, f32[2,128,128]{2,1,0:T(8,128)S(1)}, u32[]{:S(2)}, u32[]{:S(2)}) collective-permute-start(f32[2,128,128]{2,1,0:T(8,128)} %get-tuple-element.19), channel_id=1, source_target_pairs={{0,2},{1,3},{2,0},{3,1},{4,6},{5,7},{6,4},{7,5},{8,10},{9,11},{10,... | collective-permute-start | bytes 393224 | tf_op jit(solution)/shard_map/ppermute | solution.py:166
  194.1 9.5 %fusion.1 = bf16[1,128,24576]{2,1,0:T(8,128)(2,1)} fusion(bf16[128,24576]{1,0:T(8,128)(2,1)} %get-tuple-element.20, bf16[128,24576]{1,0:T(8,128)(2,1)} %get-tuple-element.18, f32[128]{0:T(128)S(1)} %fusion.8), kind=kLoop, calls=%fused_computation.4 | loop fusion | flops 15728640 | bytes 18874880 | tf_op jit(solution)/shard_map/broadcast_in_dim | solution.py:279
  203.6 1.5 collective-permute-done.16
  (59 shorter events, 13.5 us)
Async XLA Ops:
  10.7 2.6 %copy-start = (bf16[128,24576]{1,0:T(8,128)(2,1)}, bf16[128,24576]{1,0:T(8,128)(2,1)S(1)}, u32[]{:S(2)}) copy-start(bf16[128,24576]{1,0:T(8,128)(2,1)S(1)} %broadcast_select_fusion) | copy-start | bytes 18874372
  14.7 9.0 %collective-permute-start = (bf16[192,256]{1,0:T(8,128)(2,1)S(1)}, bf16[192,256]{1,0:T(8,128)(2,1)S(1)}, u32[]{:S(2)}, u32[]{:S(2)}) collective-permute-start(bf16[192,256]{1,0:T(8,128)(2,1)S(1)} %pad_maximum_fusion.5), channel_id=1, source_target_pairs={{0,1},{1,2},{2,3},{4,5},{5,6},{6,7},{8,9},{9,10},{10,11},{12,13},{... | collective-permute-start | bytes 294920 | tf_op jit(solution)/shard_map/ppermute | solution.py:228
  18.2 6.5 %collective-permute-start.1 = (bf16[192,256]{1,0:T(8,128)(2,1)S(1)}, bf16[192,256]{1,0:T(8,128)(2,1)S(1)}, u32[]{:S(2)}, u32[]{:S(2)}) collective-permute-start(bf16[192,256]{1,0:T(8,128)(2,1)S(1)} %pad_maximum_fusion.6), channel_id=1, source_target_pairs={{1,0},{2,1},{3,2},{5,4},{6,5},{7,6},{9,8},{10,9},{11,10},{13,12},{... | collective-permute-start | bytes 294920 | tf_op jit(solution)/shard_map/ppermute | solution.py:231
  24.7 6.3 %copy-start.5 = (bf16[192,256]{1,0:T(8,128)(2,1)}, bf16[192,256]{1,0:T(8,128)(2,1)S(1)}, u32[]{:S(2)}) copy-start(bf16[192,256]{1,0:T(8,128)(2,1)S(1)} %collective-permute-done.1) | copy-start | bytes 294916
  26.0 59.1 %collective-permute-start.3 = (bf16[32,25088]{1,0:T(8,128)(2,1)}, bf16[32,25088]{1,0:T(8,128)(2,1)S(1)}, u32[]{:S(2)}, u32[]{:S(2)}) collective-permute-start(bf16[32,25088]{1,0:T(8,128)(2,1)} %pad_maximum_fusion.2), channel_id=1, source_target_pairs={{4,0},{8,4},{12,8},{16,12},{20,16},{24,20},{28,24},{5,1},{9,5},{13... | collective-permute-start | bytes 4816904 | tf_op jit(solution)/shard_map/ppermute | solution.py:19
  27.9 57.2 %collective-permute-start.5 = (bf16[32,25088]{1,0:T(8,128)(2,1)}, bf16[32,25088]{1,0:T(8,128)(2,1)}, u32[]{:S(2)}, u32[]{:S(2)}) collective-permute-start(bf16[32,25088]{1,0:T(8,128)(2,1)} %pad_maximum_fusion.2), channel_id=1, source_target_pairs={{12,4},{20,12},{28,20},{13,5},{21,13},{29,21},{14,6},{22,14},{30,2... | collective-permute-start | bytes 4816904 | tf_op jit(solution)/shard_map/ppermute | solution.py:207
  31.0 68.9 %collective-permute-start.2 = (bf16[32,25088]{1,0:T(8,128)(2,1)}, bf16[32,25088]{1,0:T(8,128)(2,1)S(1)}, u32[]{:S(2)}, u32[]{:S(2)}) collective-permute-start(bf16[32,25088]{1,0:T(8,128)(2,1)} %pad_maximum_fusion.1), channel_id=1, source_target_pairs={{0,4},{4,8},{8,12},{12,16},{16,20},{20,24},{24,28},{1,5},{5,9},{9,... | collective-permute-start | bytes 4816904 | tf_op jit(solution)/shard_map/ppermute | solution.py:19
  34.6 65.2 %collective-permute-start.4 = (bf16[32,25088]{1,0:T(8,128)(2,1)}, bf16[32,25088]{1,0:T(8,128)(2,1)}, u32[]{:S(2)}, u32[]{:S(2)}) collective-permute-start(bf16[32,25088]{1,0:T(8,128)(2,1)} %pad_maximum_fusion.1), channel_id=1, source_target_pairs={{0,8},{8,16},{16,24},{1,9},{9,17},{17,25},{2,10},{10,18},{18,26},{... | collective-permute-start | bytes 4816904 | tf_op jit(solution)/shard_map/ppermute | solution.py:206
  61.8 40.6 %copy-start.7 = (s32[256,3]{0,1:T(4,128)S(1)}, s32[256,3]{0,1:T(4,128)}, u32[]{:S(2)}) copy-start(s32[256,3]{0,1:T(4,128)} %param.11) | copy-start | bytes 9220
  99.9 9.0 %copy-start.1 = (bf16[32,25088]{1,0:T(8,128)(2,1)}, bf16[32,25088]{1,0:T(8,128)(2,1)S(1)}, u32[]{:S(2)}) copy-start(bf16[32,25088]{1,0:T(8,128)(2,1)S(1)} %collective-permute-done.2) | copy-start | bytes 4816900
  99.9 4.7 %collective-permute-start.6 = (bf16[32,25088]{1,0:T(8,128)(2,1)S(1)}, bf16[32,25088]{1,0:T(8,128)(2,1)}, u32[]{:S(2)}, u32[]{:S(2)}) collective-permute-start(bf16[32,25088]{1,0:T(8,128)(2,1)S(1)} %collective-permute-done.2), channel_id=1, source_target_pairs={{0,4},{8,12},{16,20},{24,28},{1,5},{9,13},{17,21},{25,29},{2,6},{1... | collective-permute-start | bytes 4816904 | tf_op jit(solution)/shard_map/ppermute | solution.py:212
  103.3 5.3 %collective-permute-start.7 = (bf16[32,25088]{1,0:T(8,128)(2,1)S(1)}, bf16[32,25088]{1,0:T(8,128)(2,1)S(1)}, u32[]{:S(2)}, u32[]{:S(2)}) collective-permute-start(bf16[32,25088]{1,0:T(8,128)(2,1)S(1)} %collective-permute-done.3), channel_id=1, source_target_pairs={{4,0},{12,8},{20,16},{28,24},{5,1},{13,9},{21,17},{29,25},{6,2},{1... | collective-permute-start | bytes 4816904 | tf_op jit(solution)/shard_map/ppermute | solution.py:214
  137.3 4.7 %collective-permute-start.8 = (f32[128,128]{1,0:T(8,128)}, f32[128,128]{1,0:T(8,128)S(1)}, u32[]{:S(2)}, u32[]{:S(2)}) collective-permute-start(f32[128,128]{1,0:T(8,128)} %bitcast.48), channel_id=1, source_target_pairs={{0,1},{1,2},{2,3},{3,0},{4,5},{5,6},{6,7},{7,4},{8,9},{9,10},{10,1... | collective-permute-start | bytes 196616 | tf_op jit(solution)/shard_map/ppermute | solution.py:166
  139.0 5.8 %collective-permute-start.9 = (f32[128,128]{1,0:T(8,128)}, f32[128,128]{1,0:T(8,128)S(1)}, u32[]{:S(2)}, u32[]{:S(2)}) collective-permute-start(f32[128,128]{1,0:T(8,128)} %bitcast.49), channel_id=1, source_target_pairs={{0,2},{1,3},{2,0},{3,1},{4,6},{5,7},{6,4},{7,5},{8,10},{9,11},{10,... | collective-permute-start | bytes 196616 | tf_op jit(solution)/shard_map/ppermute | solution.py:166
  140.2 7.3 %collective-permute-start.10 = (f32[128,128]{1,0:T(8,128)}, f32[128,128]{1,0:T(8,128)S(1)}, u32[]{:S(2)}, u32[]{:S(2)}) collective-permute-start(f32[128,128]{1,0:T(8,128)} %bitcast.50), channel_id=1, source_target_pairs={{0,3},{1,0},{2,1},{3,2},{4,7},{5,4},{6,5},{7,6},{8,11},{9,8},{10,9... | collective-permute-start | bytes 196616 | tf_op jit(solution)/shard_map/ppermute | solution.py:166
  148.4 5.7 %copy-start.3 = (bf16[128,256]{1,0:T(8,128)(2,1)S(1)}, bf16[128,256]{1,0:T(8,128)(2,1)}, u32[]{:S(2)}) copy-start(bf16[128,256]{1,0:T(8,128)(2,1)} %get-tuple-element.21.hi_ref) | copy-start | bytes 196612
  148.5 5.7 %copy-start.6 = (bf16[192,256]{1,0:T(8,128)(2,1)S(1)}, bf16[192,256]{1,0:T(8,128)(2,1)}, u32[]{:S(2)}) copy-start(bf16[192,256]{1,0:T(8,128)(2,1)} %copy-done.5) | copy-start | bytes 294916
  148.5 6.5 %copy-start.2 = (bf16[128,256]{1,0:T(8,128)(2,1)S(1)}, bf16[128,256]{1,0:T(8,128)(2,1)}, u32[]{:S(2)}) copy-start(bf16[128,256]{1,0:T(8,128)(2,1)} %get-tuple-element.22.lo_ref) | copy-start | bytes 196612
  187.0 6.9 %collective-permute-start.11 = (f32[2,128]{1,0:T(2,128)S(1)}, f32[2,128]{1,0:T(2,128)S(1)}, u32[]{:S(2)}, u32[]{:S(2)}) collective-permute-start(f32[2,128]{1,0:T(2,128)S(1)} %select_reduce_fusion), channel_id=1, source_target_pairs={{0,1},{1,2},{2,3},{3,0},{4,5},{5,6},{6,7},{7,4},{8,9},{9,10},{10,1... | collective-permute-start | bytes 3080 | tf_op jit(solution)/shard_map/ppermute | solution.py:166
  187.1 7.0 %collective-permute-start.12 = (f32[2,128]{1,0:T(2,128)S(1)}, f32[2,128]{1,0:T(2,128)S(1)}, u32[]{:S(2)}, u32[]{:S(2)}) collective-permute-start(f32[2,128]{1,0:T(2,128)S(1)} %select_reduce_fusion), channel_id=1, source_target_pairs={{0,2},{1,3},{2,0},{3,1},{4,6},{5,7},{6,4},{7,5},{8,10},{9,11},{10,... | collective-permute-start | bytes 3080 | tf_op jit(solution)/shard_map/ppermute | solution.py:166
  189.5 4.6 %collective-permute-start.13 = (f32[2,128]{1,0:T(2,128)S(1)}, f32[2,128]{1,0:T(2,128)S(1)}, u32[]{:S(2)}, u32[]{:S(2)}) collective-permute-start(f32[2,128]{1,0:T(2,128)S(1)} %select_reduce_fusion), channel_id=1, source_target_pairs={{0,3},{1,0},{2,1},{3,2},{4,7},{5,4},{6,5},{7,6},{8,11},{9,8},{10,9... | collective-permute-start | bytes 3080 | tf_op jit(solution)/shard_map/ppermute | solution.py:166
  190.6 13.0 %collective-permute-start.14 = (f32[2,128,128]{2,1,0:T(8,128)}, f32[2,128,128]{2,1,0:T(8,128)S(1)}, u32[]{:S(2)}, u32[]{:S(2)}) collective-permute-start(f32[2,128,128]{2,1,0:T(8,128)} %get-tuple-element.19), channel_id=1, source_target_pairs={{0,1},{1,2},{2,3},{3,0},{4,5},{5,6},{6,7},{7,4},{8,9},{9,10},{10,1... | collective-permute-start | bytes 393224 | tf_op jit(solution)/shard_map/ppermute | solution.py:166
  191.5 12.1 %collective-permute-start.15 = (f32[2,128,128]{2,1,0:T(8,128)}, f32[2,128,128]{2,1,0:T(8,128)S(1)}, u32[]{:S(2)}, u32[]{:S(2)}) collective-permute-start(f32[2,128,128]{2,1,0:T(8,128)} %get-tuple-element.19), channel_id=1, source_target_pairs={{0,2},{1,3},{2,0},{3,1},{4,6},{5,7},{6,4},{7,5},{8,10},{9,11},{10,... | collective-permute-start | bytes 393224 | tf_op jit(solution)/shard_map/ppermute | solution.py:166
  193.9 11.2 %collective-permute-start.16 = (f32[2,128,128]{2,1,0:T(8,128)}, f32[2,128,128]{2,1,0:T(8,128)S(1)}, u32[]{:S(2)}, u32[]{:S(2)}) collective-permute-start(f32[2,128,128]{2,1,0:T(8,128)} %get-tuple-element.19), channel_id=1, source_target_pairs={{0,3},{1,0},{2,1},{3,2},{4,7},{5,4},{6,5},{7,6},{8,11},{9,8},{10,9... | collective-permute-start | bytes 393224 | tf_op jit(solution)/shard_map/ppermute | solution.py:166
  194.1 11.0 %copy-start.4 = (f32[2,128,128]{2,1,0:T(8,128)S(1)}, f32[2,128,128]{2,1,0:T(8,128)}, u32[]{:S(2)}) copy-start(f32[2,128,128]{2,1,0:T(8,128)} %get-tuple-element.19) | copy-start | bytes 393220

commit v12 on v11

--- a/solution.py
+++ b/solution.py
@@ -95,7 +95,7 @@
             accs[m][pl.ds(pl.multiple_of(j * blk, 16), blk), :] = part.astype(accs[m].dtype)
         return carry
 
-    lax.fori_loop(0, group, body, 0, unroll=16)
+    lax.fori_loop(0, group, body, 0, unroll=32)
     live = lax.broadcasted_iota(jnp.int32, (slots, chunk), 0) < count_ref[0]
     for c in range(span // chunk):
         if given:

time: 208 us -> 206 us (level)
  no operation moved by 1% of the time
where the time goes in v12:
time: 206 us; the launch traced here: 204 us
  local copies, waits for them, and re-layouts  56.6 us (27%)
  Pallas kernels  50.3 us (24%)
  starting transfers between devices  31.3 us (15%)
  other arithmetic  26.9 us (13%)
  waiting for transfers between devices  26.2 us (13%)
  matrix products  7.3 us (4%)
  between operations  5.46 us (3%)
    pallas_call x2, Pallas kernels, block_apply(): pl.pallas_call(kernel, grid_spec=grid_spec, out_shape=out_shape, compiler...  50.3 us
    unnamed x18, local copies, waits for them, and re-layouts  49.4 us
    ppermute x2, waiting for transfers between devices, from_behind(): return lax.ppermute(block, axis, route)  14.8 us
    ppermute x9, starting transfers between devices, row_sum(): lax.ppermute(part, 'row', [(i, (i + step) % count) for i in range(count)])  10.7 us
    broadcast_in_dim x1, other arithmetic, shards(): return (residual[None], margin_pencil[None], energy_pencil[None])  9.49 us
    ppermute x9, waiting for transfers between devices, row_sum(): lax.ppermute(part, 'row', [(i, (i + step) % count) for i in range(count)])  7.97 us
    dot_general x3, matrix products, clean(): lax.dot_general(margin_b, wins, (((0,), (0,)), ((), ())), preferred_eleme...  7.3 us
    ppermute x2, starting transfers between devices, from_behind(): return lax.ppermute(block, axis, route)  5.56 us
  transfers between devices with their start and end apart: 17, of which 7 were waited for; matrix products, arithmetic and copies ran while one was open for 31% of the time, Pallas kernels for 0%

profile of v12, /device:TPU:12, one launch (start us, length us, event | category | flops | bytes accessed | tf_op | source)
XLA Modules:
  0.0 204.0 jit_solution(8990759542267266138)
XLA Ops:
  0.6 1.3 fusion.14
  5.2 1.3 add_compare_fusion
  7.4 3.3 %broadcast_select_fusion = bf16[128,24576]{1,0:T(8,128)(2,1)S(1)} fusion(pred[128]{0:T(512)(128)(4,1)S(1)} %iota_compare_fusion.1, bf16[1,128,24576]{2,1,0:T(8,128)(2,1)} %param.6), kind=kLoop, calls=%fused_computation.5 | loop fusion | flops 3145728 | bytes 12583040 | tf_op jit(solution)/shard_map/jit(_where)/select_n | solution.py:217
  10.7 2.6 %copy-done = bf16[128,24576]{1,0:T(8,128)(2,1)} copy-done((bf16[128,24576]{1,0:T(8,128)(2,1)}, bf16[128,24576]{1,0:T(8,128)(2,1)S(1)}, u32[]{:S(2)}) %copy-start) | copy-done | bytes 6291480
  14.7 3.5 %collective-permute-start = (bf16[192,256]{1,0:T(8,128)(2,1)S(1)}, bf16[192,256]{1,0:T(8,128)(2,1)S(1)}, u32[]{:S(2)}, u32[]{:S(2)}) collective-permute-start(bf16[192,256]{1,0:T(8,128)(2,1)S(1)} %pad_maximum_fusion.5), channel_id=1, source_target_pairs={{0,1},{1,2},{2,3},{4,5},{5,6},{6,7},{8,9},{9,10},{10,11},{12,13},{... | collective-permute-start | bytes 294920 | tf_op jit(solution)/shard_map/ppermute | solution.py:228
  18.2 2.4 %collective-permute-start.1 = (bf16[192,256]{1,0:T(8,128)(2,1)S(1)}, bf16[192,256]{1,0:T(8,128)(2,1)S(1)}, u32[]{:S(2)}, u32[]{:S(2)}) collective-permute-start(bf16[192,256]{1,0:T(8,128)(2,1)S(1)} %pad_maximum_fusion.6), channel_id=1, source_target_pairs={{1,0},{2,1},{3,2},{5,4},{6,5},{7,6},{9,8},{10,9},{11,10},{13,12},{... | collective-permute-start | bytes 294920 | tf_op jit(solution)/shard_map/ppermute | solution.py:231
  20.6 3.1 %bitcast_select_fusion = (bf16[32,24576]{1,0:T(8,128)(2,1)S(1)}, bf16[32,24576]{1,0:T(8,128)(2,1)S(1)}) fusion(bf16[1,128,24576]{2,1,0:T(8,128)(2,1)} %param.6, s32[]{:T(128)S(6)} %select_n.133, pred[32]{0:T(512)(128)(4,1)S(1)} %get-tuple-element.43, s32[]{:T(128)S(6)} %select_n.130, pred[32]{0:T(512)(128)(4,1)S(1)} %get-tuple-element.44), kind=kLoop, calls=%fused_computation.10 | loop fusion | flops 1572864 | bytes 6291528 | tf_op jit(solution)/shard_map/jit(_where)/select_n | solution.py:184
  24.7 1.3 pad_maximum_fusion.2
  26.0 1.9 collective-permute-start.3
  27.9 1.8 collective-permute-start.5
  29.7 1.3 pad_maximum_fusion.1
  31.0 3.7 %collective-permute-start.2 = (bf16[32,25088]{1,0:T(8,128)(2,1)}, bf16[32,25088]{1,0:T(8,128)(2,1)S(1)}, u32[]{:S(2)}, u32[]{:S(2)}) collective-permute-start(bf16[32,25088]{1,0:T(8,128)(2,1)} %pad_maximum_fusion.1), channel_id=1, source_target_pairs={{0,4},{4,8},{8,12},{12,16},{16,20},{20,24},{24,28},{1,5},{5,9},{9,... | collective-permute-start | bytes 4816904 | tf_op jit(solution)/shard_map/ppermute | solution.py:19
  34.6 3.6 %collective-permute-start.4 = (bf16[32,25088]{1,0:T(8,128)(2,1)}, bf16[32,25088]{1,0:T(8,128)(2,1)}, u32[]{:S(2)}, u32[]{:S(2)}) collective-permute-start(bf16[32,25088]{1,0:T(8,128)(2,1)} %pad_maximum_fusion.1), channel_id=1, source_target_pairs={{0,8},{8,16},{16,24},{1,9},{9,17},{17,25},{2,10},{10,18},{18,26},{... | collective-permute-start | bytes 4816904 | tf_op jit(solution)/shard_map/ppermute | solution.py:206
  38.3 23.5 %copy.12.refs_0_ = bf16[256,96,288]{2,1,0:T(8,128)(2,1)} copy(bf16[256,96,288]{0,2,1:T(8,128)(2,1)} %param.9) | data formatting | bytes 28311552 | tf_op args[3]
  61.8 23.3 %copy.13.refs_1_ = bf16[256,96,288]{2,1,0:T(8,128)(2,1)} copy(bf16[256,96,288]{0,2,1:T(8,128)(2,1)} %param.10) | data formatting | bytes 28311552 | tf_op args[4]
  85.1 14.8 %collective-permute-done.2 = bf16[32,25088]{1,0:T(8,128)(2,1)S(1)} collective-permute-done((bf16[32,25088]{1,0:T(8,128)(2,1)}, bf16[32,25088]{1,0:T(8,128)(2,1)S(1)}, u32[]{:S(2)}, u32[]{:S(2)}) %collective-permute-start.2) | collective-permute-done | bytes 1605664 | tf_op jit(solution)/shard_map/ppermute | solution.py:19
  99.9 2.5 %collective-permute-start.6 = (bf16[32,25088]{1,0:T(8,128)(2,1)S(1)}, bf16[32,25088]{1,0:T(8,128)(2,1)}, u32[]{:S(2)}, u32[]{:S(2)}) collective-permute-start(bf16[32,25088]{1,0:T(8,128)(2,1)S(1)} %collective-permute-done.2), channel_id=1, source_target_pairs={{0,4},{8,12},{16,20},{24,28},{1,5},{9,13},{17,21},{25,29},{2,6},{1... | collective-permute-start | bytes 4816904 | tf_op jit(solution)/shard_map/ppermute | solution.py:212
  103.3 1.3 collective-permute-start.7
  104.6 1.6 broadcast_select_fusion.2
  106.2 2.4 %collective-permute-done.7 = bf16[32,25088]{1,0:T(8,128)(2,1)S(1)} collective-permute-done((bf16[32,25088]{1,0:T(8,128)(2,1)S(1)}, bf16[32,25088]{1,0:T(8,128)(2,1)S(1)}, u32[]{:S(2)}, u32[]{:S(2)}) %collective-permute-start.7) | collective-permute-done | bytes 1605664 | tf_op jit(solution)/shard_map/ppermute | solution.py:214
  109.5 2.5 %pad_maximum_fusion = bf16[128,25088]{1,0:T(8,128)(2,1)S(1)} fusion(bf16[32,25088]{1,0:T(8,128)(2,1)S(1)} %broadcast_select_fusion.1, bf16[32,25088]{1,0:T(8,128)(2,1)S(1)} %collective-permute-done.3, bf16[32,25088]{1,0:T(8,128)(2,1)} %copy-done.1, bf16[32,25088]{1,0:T(8,128)(2,1)S(1)} %broadcast_select_fusion.2), kind=kLoop, calls=%fused_computation.3 | loop fusion | flops 25690112 | bytes 12845056 | tf_op jit(solution)/shard_map/concatenate | solution.py:240
  112.1 3.3 %slice.102.x_hbm = bf16[128,24576]{1,0:T(8,128)(2,1)} slice(bf16[128,25088]{1,0:T(8,128)(2,1)S(1)} %pad_maximum_fusion), slice={[0:128], [0:24576]} | slice | bytes 12582912 | tf_op jit(solution)/shard_map/slice | solution.py:241
  115.4 21.3 %shard_map.85 = f32[1,128,128]{2,1,0:T(8,128)} custom-call(s32[768]{0:T(1024)} %reshape.80.shift_ref, s32[1]{0:T(128)} %copy.14.count_ref, bf16[128,24576]{1,0:T(8,128)(2,1)} %slice.102.x_hbm, bf16[128,256]{1,0:T(8,128)(2,1)} %get-tuple-element.22.lo_ref, bf16[128,256]{1,0:T(8,128)(2,1)} %get-tuple-element.21.hi_ref, bf16[256,96,288]{2,1,0:T(8,128)(2,1)} %copy.12.refs_0_, ...), custom_call_target="tpu_custom_call" | custom-call | tf_op jit(solution)/shard_map/pallas_call | solution.py:152
  136.7 1.6 collective-permute-start.8
  141.4 2.7 %collective-permute-done.9 = f32[128,128]{1,0:T(8,128)S(1)} collective-permute-done((f32[128,128]{1,0:T(8,128)}, f32[128,128]{1,0:T(8,128)S(1)}, u32[]{:S(2)}, u32[]{:S(2)}) %collective-permute-start.9) | collective-permute-done | bytes 65568 | tf_op jit(solution)/shard_map/ppermute | solution.py:166
  144.1 2.8 %collective-permute-done.10 = f32[128,128]{1,0:T(8,128)S(1)} collective-permute-done((f32[128,128]{1,0:T(8,128)}, f32[128,128]{1,0:T(8,128)S(1)}, u32[]{:S(2)}, u32[]{:S(2)}) %collective-permute-start.10) | collective-permute-done | bytes 65568 | tf_op jit(solution)/shard_map/ppermute | solution.py:166
  147.8 5.7 %fusion.x_hbm = bf16[128,24576]{1,0:T(8,128)(2,1)} fusion(bf16[128,128]{1,0:T(8,128)(2,1)S(1)} %fusion.2, bf16[128,24576]{1,0:T(8,128)(2,1)} %copy-done, bf16[128,25088]{1,0:T(8,128)(2,1)S(1)} %pad_maximum_fusion), kind=kOutput, calls=%fused_computation.1 | convolution fusion | flops 814743552 | bytes 18907136 | tf_op jit(solution)/shard_map/dot_general | solution.py:252
  155.1 29.0 %shard_map.86 = (bf16[128,24576]{1,0:T(8,128)(2,1)}, bf16[128,24576]{1,0:T(8,128)(2,1)}, f32[2,128,128]{2,1,0:T(8,128)}) custom-call(s32[768]{0:T(1024)} %reshape.80.shift_ref, s32[1]{0:T(128)} %copy.14.count_ref, bf16[128,24576]{1,0:T(8,128)(2,1)} %fusion.x_hbm, bf16[128,256]{1,0:T(8,128)(2,1)} %subtract_convert_fusion.2.lo_ref, ...), custom_call_target="tpu_custom_call" | custom-call | tf_op jit(solution)/shard_map/pallas_call | solution.py:152
  185.2 2.4 %collective-permute-start.12 = (f32[2,128]{1,0:T(2,128)S(1)}, f32[2,128]{1,0:T(2,128)S(1)}, u32[]{:S(2)}, u32[]{:S(2)}) collective-permute-start(f32[2,128]{1,0:T(2,128)S(1)} %select_reduce_fusion), channel_id=1, source_target_pairs={{0,2},{1,3},{2,0},{3,1},{4,6},{5,7},{6,4},{7,5},{8,10},{9,11},{10,... | collective-permute-start | bytes 3080 | tf_op jit(solution)/shard_map/ppermute | solution.py:166
  189.7 2.4 %collective-permute-start.15 = (f32[2,128,128]{2,1,0:T(8,128)}, f32[2,128,128]{2,1,0:T(8,128)S(1)}, u32[]{:S(2)}, u32[]{:S(2)}) collective-permute-start(f32[2,128,128]{2,1,0:T(8,128)} %get-tuple-element.19), channel_id=1, source_target_pairs={{0,2},{1,3},{2,0},{3,1},{4,6},{5,7},{6,4},{7,5},{8,10},{9,11},{10,... | collective-permute-start | bytes 393224 | tf_op jit(solution)/shard_map/ppermute | solution.py:166
  192.3 9.5 %fusion.1 = bf16[1,128,24576]{2,1,0:T(8,128)(2,1)} fusion(bf16[128,24576]{1,0:T(8,128)(2,1)} %get-tuple-element.20, bf16[128,24576]{1,0:T(8,128)(2,1)} %get-tuple-element.18, f32[128]{0:T(128)S(1)} %fusion.8), kind=kLoop, calls=%fused_computation.4 | loop fusion | flops 15728640 | bytes 18874880 | tf_op jit(solution)/shard_map/broadcast_in_dim | solution.py:279
  201.8 1.5 collective-permute-done.16
  (59 shorter events, 13.5 us)
Async XLA Ops:
  10.7 2.6 %copy-start = (bf16[128,24576]{1,0:T(8,128)(2,1)}, bf16[128,24576]{1,0:T(8,128)(2,1)S(1)}, u32[]{:S(2)}) copy-start(bf16[128,24576]{1,0:T(8,128)(2,1)S(1)} %broadcast_select_fusion) | copy-start | bytes 18874372
  14.7 9.0 %collective-permute-start = (bf16[192,256]{1,0:T(8,128)(2,1)S(1)}, bf16[192,256]{1,0:T(8,128)(2,1)S(1)}, u32[]{:S(2)}, u32[]{:S(2)}) collective-permute-start(bf16[192,256]{1,0:T(8,128)(2,1)S(1)} %pad_maximum_fusion.5), channel_id=1, source_target_pairs={{0,1},{1,2},{2,3},{4,5},{5,6},{6,7},{8,9},{9,10},{10,11},{12,13},{... | collective-permute-start | bytes 294920 | tf_op jit(solution)/shard_map/ppermute | solution.py:228
  18.2 6.5 %collective-permute-start.1 = (bf16[192,256]{1,0:T(8,128)(2,1)S(1)}, bf16[192,256]{1,0:T(8,128)(2,1)S(1)}, u32[]{:S(2)}, u32[]{:S(2)}) collective-permute-start(bf16[192,256]{1,0:T(8,128)(2,1)S(1)} %pad_maximum_fusion.6), channel_id=1, source_target_pairs={{1,0},{2,1},{3,2},{5,4},{6,5},{7,6},{9,8},{10,9},{11,10},{13,12},{... | collective-permute-start | bytes 294920 | tf_op jit(solution)/shard_map/ppermute | solution.py:231
  24.7 6.3 %copy-start.5 = (bf16[192,256]{1,0:T(8,128)(2,1)}, bf16[192,256]{1,0:T(8,128)(2,1)S(1)}, u32[]{:S(2)}) copy-start(bf16[192,256]{1,0:T(8,128)(2,1)S(1)} %collective-permute-done.1) | copy-start | bytes 294916
  26.0 59.1 %collective-permute-start.3 = (bf16[32,25088]{1,0:T(8,128)(2,1)}, bf16[32,25088]{1,0:T(8,128)(2,1)S(1)}, u32[]{:S(2)}, u32[]{:S(2)}) collective-permute-start(bf16[32,25088]{1,0:T(8,128)(2,1)} %pad_maximum_fusion.2), channel_id=1, source_target_pairs={{4,0},{8,4},{12,8},{16,12},{20,16},{24,20},{28,24},{5,1},{9,5},{13... | collective-permute-start | bytes 4816904 | tf_op jit(solution)/shard_map/ppermute | solution.py:19
  27.9 57.2 %collective-permute-start.5 = (bf16[32,25088]{1,0:T(8,128)(2,1)}, bf16[32,25088]{1,0:T(8,128)(2,1)}, u32[]{:S(2)}, u32[]{:S(2)}) collective-permute-start(bf16[32,25088]{1,0:T(8,128)(2,1)} %pad_maximum_fusion.2), channel_id=1, source_target_pairs={{12,4},{20,12},{28,20},{13,5},{21,13},{29,21},{14,6},{22,14},{30,2... | collective-permute-start | bytes 4816904 | tf_op jit(solution)/shard_map/ppermute | solution.py:207
  31.0 68.9 %collective-permute-start.2 = (bf16[32,25088]{1,0:T(8,128)(2,1)}, bf16[32,25088]{1,0:T(8,128)(2,1)S(1)}, u32[]{:S(2)}, u32[]{:S(2)}) collective-permute-start(bf16[32,25088]{1,0:T(8,128)(2,1)} %pad_maximum_fusion.1), channel_id=1, source_target_pairs={{0,4},{4,8},{8,12},{12,16},{16,20},{20,24},{24,28},{1,5},{5,9},{9,... | collective-permute-start | bytes 4816904 | tf_op jit(solution)/shard_map/ppermute | solution.py:19
  34.6 65.2 %collective-permute-start.4 = (bf16[32,25088]{1,0:T(8,128)(2,1)}, bf16[32,25088]{1,0:T(8,128)(2,1)}, u32[]{:S(2)}, u32[]{:S(2)}) collective-permute-start(bf16[32,25088]{1,0:T(8,128)(2,1)} %pad_maximum_fusion.1), channel_id=1, source_target_pairs={{0,8},{8,16},{16,24},{1,9},{9,17},{17,25},{2,10},{10,18},{18,26},{... | collective-permute-start | bytes 4816904 | tf_op jit(solution)/shard_map/ppermute | solution.py:206
  61.8 40.6 %copy-start.7 = (s32[256,3]{0,1:T(4,128)S(1)}, s32[256,3]{0,1:T(4,128)}, u32[]{:S(2)}) copy-start(s32[256,3]{0,1:T(4,128)} %param.11) | copy-start | bytes 9220
  99.9 9.0 %copy-start.1 = (bf16[32,25088]{1,0:T(8,128)(2,1)}, bf16[32,25088]{1,0:T(8,128)(2,1)S(1)}, u32[]{:S(2)}) copy-start(bf16[32,25088]{1,0:T(8,128)(2,1)S(1)} %collective-permute-done.2) | copy-start | bytes 4816900
  99.9 4.7 %collective-permute-start.6 = (bf16[32,25088]{1,0:T(8,128)(2,1)S(1)}, bf16[32,25088]{1,0:T(8,128)(2,1)}, u32[]{:S(2)}, u32[]{:S(2)}) collective-permute-start(bf16[32,25088]{1,0:T(8,128)(2,1)S(1)} %collective-permute-done.2), channel_id=1, source_target_pairs={{0,4},{8,12},{16,20},{24,28},{1,5},{9,13},{17,21},{25,29},{2,6},{1... | collective-permute-start | bytes 4816904 | tf_op jit(solution)/shard_map/ppermute | solution.py:212
  103.3 5.3 %collective-permute-start.7 = (bf16[32,25088]{1,0:T(8,128)(2,1)S(1)}, bf16[32,25088]{1,0:T(8,128)(2,1)S(1)}, u32[]{:S(2)}, u32[]{:S(2)}) collective-permute-start(bf16[32,25088]{1,0:T(8,128)(2,1)S(1)} %collective-permute-done.3), channel_id=1, source_target_pairs={{4,0},{12,8},{20,16},{28,24},{5,1},{13,9},{21,17},{29,25},{6,2},{1... | collective-permute-start | bytes 4816904 | tf_op jit(solution)/shard_map/ppermute | solution.py:214
  136.7 4.7 %collective-permute-start.8 = (f32[128,128]{1,0:T(8,128)}, f32[128,128]{1,0:T(8,128)S(1)}, u32[]{:S(2)}, u32[]{:S(2)}) collective-permute-start(f32[128,128]{1,0:T(8,128)} %bitcast.48), channel_id=1, source_target_pairs={{0,1},{1,2},{2,3},{3,0},{4,5},{5,6},{6,7},{7,4},{8,9},{9,10},{10,1... | collective-permute-start | bytes 196616 | tf_op jit(solution)/shard_map/ppermute | solution.py:166
  138.3 5.8 %collective-permute-start.9 = (f32[128,128]{1,0:T(8,128)}, f32[128,128]{1,0:T(8,128)S(1)}, u32[]{:S(2)}, u32[]{:S(2)}) collective-permute-start(f32[128,128]{1,0:T(8,128)} %bitcast.49), channel_id=1, source_target_pairs={{0,2},{1,3},{2,0},{3,1},{4,6},{5,7},{6,4},{7,5},{8,10},{9,11},{10,... | collective-permute-start | bytes 196616 | tf_op jit(solution)/shard_map/ppermute | solution.py:166
  139.6 7.3 %collective-permute-start.10 = (f32[128,128]{1,0:T(8,128)}, f32[128,128]{1,0:T(8,128)S(1)}, u32[]{:S(2)}, u32[]{:S(2)}) collective-permute-start(f32[128,128]{1,0:T(8,128)} %bitcast.50), channel_id=1, source_target_pairs={{0,3},{1,0},{2,1},{3,2},{4,7},{5,4},{6,5},{7,6},{8,11},{9,8},{10,9... | collective-permute-start | bytes 196616 | tf_op jit(solution)/shard_map/ppermute | solution.py:166
  147.8 5.7 %copy-start.3 = (bf16[128,256]{1,0:T(8,128)(2,1)S(1)}, bf16[128,256]{1,0:T(8,128)(2,1)}, u32[]{:S(2)}) copy-start(bf16[128,256]{1,0:T(8,128)(2,1)} %get-tuple-element.21.hi_ref) | copy-start | bytes 196612
  147.8 5.7 %copy-start.6 = (bf16[192,256]{1,0:T(8,128)(2,1)S(1)}, bf16[192,256]{1,0:T(8,128)(2,1)}, u32[]{:S(2)}) copy-start(bf16[192,256]{1,0:T(8,128)(2,1)} %copy-done.5) | copy-start | bytes 294916
  147.8 6.5 %copy-start.2 = (bf16[128,256]{1,0:T(8,128)(2,1)S(1)}, bf16[128,256]{1,0:T(8,128)(2,1)}, u32[]{:S(2)}) copy-start(bf16[128,256]{1,0:T(8,128)(2,1)} %get-tuple-element.22.lo_ref) | copy-start | bytes 196612
  185.2 6.9 %collective-permute-start.11 = (f32[2,128]{1,0:T(2,128)S(1)}, f32[2,128]{1,0:T(2,128)S(1)}, u32[]{:S(2)}, u32[]{:S(2)}) collective-permute-start(f32[2,128]{1,0:T(2,128)S(1)} %select_reduce_fusion), channel_id=1, source_target_pairs={{0,1},{1,2},{2,3},{3,0},{4,5},{5,6},{6,7},{7,4},{8,9},{9,10},{10,1... | collective-permute-start | bytes 3080 | tf_op jit(solution)/shard_map/ppermute | solution.py:166
  185.2 7.0 %collective-permute-start.12 = (f32[2,128]{1,0:T(2,128)S(1)}, f32[2,128]{1,0:T(2,128)S(1)}, u32[]{:S(2)}, u32[]{:S(2)}) collective-permute-start(f32[2,128]{1,0:T(2,128)S(1)} %select_reduce_fusion), channel_id=1, source_target_pairs={{0,2},{1,3},{2,0},{3,1},{4,6},{5,7},{6,4},{7,5},{8,10},{9,11},{10,... | collective-permute-start | bytes 3080 | tf_op jit(solution)/shard_map/ppermute | solution.py:166
  187.6 4.6 %collective-permute-start.13 = (f32[2,128]{1,0:T(2,128)S(1)}, f32[2,128]{1,0:T(2,128)S(1)}, u32[]{:S(2)}, u32[]{:S(2)}) collective-permute-start(f32[2,128]{1,0:T(2,128)S(1)} %select_reduce_fusion), channel_id=1, source_target_pairs={{0,3},{1,0},{2,1},{3,2},{4,7},{5,4},{6,5},{7,6},{8,11},{9,8},{10,9... | collective-permute-start | bytes 3080 | tf_op jit(solution)/shard_map/ppermute | solution.py:166
  188.7 13.0 %collective-permute-start.14 = (f32[2,128,128]{2,1,0:T(8,128)}, f32[2,128,128]{2,1,0:T(8,128)S(1)}, u32[]{:S(2)}, u32[]{:S(2)}) collective-permute-start(f32[2,128,128]{2,1,0:T(8,128)} %get-tuple-element.19), channel_id=1, source_target_pairs={{0,1},{1,2},{2,3},{3,0},{4,5},{5,6},{6,7},{7,4},{8,9},{9,10},{10,1... | collective-permute-start | bytes 393224 | tf_op jit(solution)/shard_map/ppermute | solution.py:166
  189.7 12.1 %collective-permute-start.15 = (f32[2,128,128]{2,1,0:T(8,128)}, f32[2,128,128]{2,1,0:T(8,128)S(1)}, u32[]{:S(2)}, u32[]{:S(2)}) collective-permute-start(f32[2,128,128]{2,1,0:T(8,128)} %get-tuple-element.19), channel_id=1, source_target_pairs={{0,2},{1,3},{2,0},{3,1},{4,6},{5,7},{6,4},{7,5},{8,10},{9,11},{10,... | collective-permute-start | bytes 393224 | tf_op jit(solution)/shard_map/ppermute | solution.py:166
  192.1 11.2 %collective-permute-start.16 = (f32[2,128,128]{2,1,0:T(8,128)}, f32[2,128,128]{2,1,0:T(8,128)S(1)}, u32[]{:S(2)}, u32[]{:S(2)}) collective-permute-start(f32[2,128,128]{2,1,0:T(8,128)} %get-tuple-element.19), channel_id=1, source_target_pairs={{0,3},{1,0},{2,1},{3,2},{4,7},{5,4},{6,5},{7,6},{8,11},{9,8},{10,9... | collective-permute-start | bytes 393224 | tf_op jit(solution)/shard_map/ppermute | solution.py:166
  192.3 11.0 %copy-start.4 = (f32[2,128,128]{2,1,0:T(8,128)S(1)}, f32[2,128,128]{2,1,0:T(8,128)}, u32[]{:S(2)}) copy-start(f32[2,128,128]{2,1,0:T(8,128)} %get-tuple-element.19) | copy-start | bytes 393220

commit v13 on v11

--- a/solution.py
+++ b/solution.py
@@ -116,7 +116,7 @@
     slots, entries = cells.shape
     block_rows, blk, width = matrices[0].shape
     rim = lower.shape[1]
-    group = 32 if block_rows % 32 == 0 else block_rows
+    group = 16 if block_rows % 16 == 0 else block_rows
     chunk = 512
     nmat = len(matrices)
     given = pair is not None

time: 208 us -> 214 us (1.029)
  Pallas kernels: 52.1 us -> 58 us
    pallas_call x2, Pallas kernels: 52.1 us -> 58 us  [block_apply(): pl.pallas_call(kernel, grid_spec=grid_spec, out_shape=out_shape, compiler...]
  transfers between devices with their start and end apart: 17 -> 17, of which waited for: 7 -> 7; matrix products, arithmetic and copies ran while one was open for 31% -> 30% of each run, Pallas kernels for 0% -> 0%
where the time goes in v13:
time: 214 us; the launch traced here: 212 us
  Pallas kernels  58 us (27%)
  local copies, waits for them, and re-layouts  56.6 us (26%)
  starting transfers between devices  31.3 us (15%)
  other arithmetic  26.9 us (13%)
  waiting for transfers between devices  26.1 us (12%)
  matrix products  7.3 us (3%)
  between operations  5.46 us (3%)
    pallas_call x2, Pallas kernels, block_apply(): pl.pallas_call(kernel, grid_spec=grid_spec, out_shape=out_shape, compiler...  58 us
    unnamed x18, local copies, waits for them, and re-layouts  49.4 us
    ppermute x2, waiting for transfers between devices, from_behind(): return lax.ppermute(block, axis, route)  14.8 us
    ppermute x9, starting transfers between devices, row_sum(): lax.ppermute(part, 'row', [(i, (i + step) % count) for i in range(count)])  10.7 us
    broadcast_in_dim x1, other arithmetic, shards(): return (residual[None], margin_pencil[None], energy_pencil[None])  9.49 us
    ppermute x9, waiting for transfers between devices, row_sum(): lax.ppermute(part, 'row', [(i, (i + step) % count) for i in range(count)])  7.95 us
    dot_general x3, matrix products, clean(): lax.dot_general(margin_b, wins, (((0,), (0,)), ((), ())), preferred_eleme...  7.3 us
    ppermute x2, starting transfers between devices, from_behind(): return lax.ppermute(block, axis, route)  5.56 us
  transfers between devices with their start and end apart: 17, of which 7 were waited for; matrix products, arithmetic and copies ran while one was open for 30% of the time, Pallas kernels for 0%

profile of v13, /device:TPU:12, one launch (start us, length us, event | category | flops | bytes accessed | tf_op | source)
XLA Modules:
  0.0 211.7 jit_solution(13629172536536505097)
XLA Ops:
  0.6 1.3 fusion.14
  5.2 1.3 add_compare_fusion
  7.4 3.3 %broadcast_select_fusion = bf16[128,24576]{1,0:T(8,128)(2,1)S(1)} fusion(pred[128]{0:T(512)(128)(4,1)S(1)} %iota_compare_fusion.1, bf16[1,128,24576]{2,1,0:T(8,128)(2,1)} %param.6), kind=kLoop, calls=%fused_computation.5 | loop fusion | flops 3145728 | bytes 12583040 | tf_op jit(solution)/shard_map/jit(_where)/select_n | solution.py:217
  10.7 2.6 %copy-done = bf16[128,24576]{1,0:T(8,128)(2,1)} copy-done((bf16[128,24576]{1,0:T(8,128)(2,1)}, bf16[128,24576]{1,0:T(8,128)(2,1)S(1)}, u32[]{:S(2)}) %copy-start) | copy-done | bytes 6291480
  14.7 3.5 %collective-permute-start = (bf16[192,256]{1,0:T(8,128)(2,1)S(1)}, bf16[192,256]{1,0:T(8,128)(2,1)S(1)}, u32[]{:S(2)}, u32[]{:S(2)}) collective-permute-start(bf16[192,256]{1,0:T(8,128)(2,1)S(1)} %pad_maximum_fusion.5), channel_id=1, source_target_pairs={{0,1},{1,2},{2,3},{4,5},{5,6},{6,7},{8,9},{9,10},{10,11},{12,13},{... | collective-permute-start | bytes 294920 | tf_op jit(solution)/shard_map/ppermute | solution.py:228
  18.2 2.4 %collective-permute-start.1 = (bf16[192,256]{1,0:T(8,128)(2,1)S(1)}, bf16[192,256]{1,0:T(8,128)(2,1)S(1)}, u32[]{:S(2)}, u32[]{:S(2)}) collective-permute-start(bf16[192,256]{1,0:T(8,128)(2,1)S(1)} %pad_maximum_fusion.6), channel_id=1, source_target_pairs={{1,0},{2,1},{3,2},{5,4},{6,5},{7,6},{9,8},{10,9},{11,10},{13,12},{... | collective-permute-start | bytes 294920 | tf_op jit(solution)/shard_map/ppermute | solution.py:231
  20.6 3.1 %bitcast_select_fusion = (bf16[32,24576]{1,0:T(8,128)(2,1)S(1)}, bf16[32,24576]{1,0:T(8,128)(2,1)S(1)}) fusion(bf16[1,128,24576]{2,1,0:T(8,128)(2,1)} %param.6, s32[]{:T(128)S(6)} %select_n.133, pred[32]{0:T(512)(128)(4,1)S(1)} %get-tuple-element.43, s32[]{:T(128)S(6)} %select_n.130, pred[32]{0:T(512)(128)(4,1)S(1)} %get-tuple-element.44), kind=kLoop, calls=%fused_computation.10 | loop fusion | flops 1572864 | bytes 6291528 | tf_op jit(solution)/shard_map/jit(_where)/select_n | solution.py:184
  24.7 1.3 pad_maximum_fusion.2
  26.0 1.9 collective-permute-start.3
  27.9 1.8 collective-permute-start.5
  29.7 1.3 pad_maximum_fusion.1
  31.0 3.7 %collective-permute-start.2 = (bf16[32,25088]{1,0:T(8,128)(2,1)}, bf16[32,25088]{1,0:T(8,128)(2,1)S(1)}, u32[]{:S(2)}, u32[]{:S(2)}) collective-permute-start(bf16[32,25088]{1,0:T(8,128)(2,1)} %pad_maximum_fusion.1), channel_id=1, source_target_pairs={{0,4},{4,8},{8,12},{12,16},{16,20},{20,24},{24,28},{1,5},{5,9},{9,... | collective-permute-start | bytes 4816904 | tf_op jit(solution)/shard_map/ppermute | solution.py:19
  34.6 3.6 %collective-permute-start.4 = (bf16[32,25088]{1,0:T(8,128)(2,1)}, bf16[32,25088]{1,0:T(8,128)(2,1)}, u32[]{:S(2)}, u32[]{:S(2)}) collective-permute-start(bf16[32,25088]{1,0:T(8,128)(2,1)} %pad_maximum_fusion.1), channel_id=1, source_target_pairs={{0,8},{8,16},{16,24},{1,9},{9,17},{17,25},{2,10},{10,18},{18,26},{... | collective-permute-start | bytes 4816904 | tf_op jit(solution)/shard_map/ppermute | solution.py:206
  38.3 23.5 %copy.12.refs_0_ = bf16[256,96,288]{2,1,0:T(8,128)(2,1)} copy(bf16[256,96,288]{0,2,1:T(8,128)(2,1)} %param.9) | data formatting | bytes 28311552 | tf_op args[3]
  61.8 23.3 %copy.13.refs_1_ = bf16[256,96,288]{2,1,0:T(8,128)(2,1)} copy(bf16[256,96,288]{0,2,1:T(8,128)(2,1)} %param.10) | data formatting | bytes 28311552 | tf_op args[4]
  85.1 14.8 %collective-permute-done.2 = bf16[32,25088]{1,0:T(8,128)(2,1)S(1)} collective-permute-done((bf16[32,25088]{1,0:T(8,128)(2,1)}, bf16[32,25088]{1,0:T(8,128)(2,1)S(1)}, u32[]{:S(2)}, u32[]{:S(2)}) %collective-permute-start.2) | collective-permute-done | bytes 1605664 | tf_op jit(solution)/shard_map/ppermute | solution.py:19
  99.9 2.5 %collective-permute-start.6 = (bf16[32,25088]{1,0:T(8,128)(2,1)S(1)}, bf16[32,25088]{1,0:T(8,128)(2,1)}, u32[]{:S(2)}, u32[]{:S(2)}) collective-permute-start(bf16[32,25088]{1,0:T(8,128)(2,1)S(1)} %collective-permute-done.2), channel_id=1, source_target_pairs={{0,4},{8,12},{16,20},{24,28},{1,5},{9,13},{17,21},{25,29},{2,6},{1... | collective-permute-start | bytes 4816904 | tf_op jit(solution)/shard_map/ppermute | solution.py:212
  103.3 1.3 collective-permute-start.7
  104.6 1.6 broadcast_select_fusion.2
  106.2 2.4 %collective-permute-done.7 = bf16[32,25088]{1,0:T(8,128)(2,1)S(1)} collective-permute-done((bf16[32,25088]{1,0:T(8,128)(2,1)S(1)}, bf16[32,25088]{1,0:T(8,128)(2,1)S(1)}, u32[]{:S(2)}, u32[]{:S(2)}) %collective-permute-start.7) | collective-permute-done | bytes 1605664 | tf_op jit(solution)/shard_map/ppermute | solution.py:214
  109.5 2.5 %pad_maximum_fusion = bf16[128,25088]{1,0:T(8,128)(2,1)S(1)} fusion(bf16[32,25088]{1,0:T(8,128)(2,1)S(1)} %broadcast_select_fusion.1, bf16[32,25088]{1,0:T(8,128)(2,1)S(1)} %collective-permute-done.3, bf16[32,25088]{1,0:T(8,128)(2,1)} %copy-done.1, bf16[32,25088]{1,0:T(8,128)(2,1)S(1)} %broadcast_select_fusion.2), kind=kLoop, calls=%fused_computation.3 | loop fusion | flops 25690112 | bytes 12845056 | tf_op jit(solution)/shard_map/concatenate | solution.py:240
  112.1 3.3 %slice.102.x_hbm = bf16[128,24576]{1,0:T(8,128)(2,1)} slice(bf16[128,25088]{1,0:T(8,128)(2,1)S(1)} %pad_maximum_fusion), slice={[0:128], [0:24576]} | slice | bytes 12582912 | tf_op jit(solution)/shard_map/slice | solution.py:241
  115.4 26.2 %shard_map.85 = f32[1,128,128]{2,1,0:T(8,128)} custom-call(s32[768]{0:T(1024)} %reshape.80.shift_ref, s32[1]{0:T(128)} %copy.14.count_ref, bf16[128,24576]{1,0:T(8,128)(2,1)} %slice.102.x_hbm, bf16[128,256]{1,0:T(8,128)(2,1)} %get-tuple-element.22.lo_ref, bf16[128,256]{1,0:T(8,128)(2,1)} %get-tuple-element.21.hi_ref, bf16[256,96,288]{2,1,0:T(8,128)(2,1)} %copy.12.refs_0_, ...), custom_call_target="tpu_custom_call" | custom-call | tf_op jit(solution)/shard_map/pallas_call | solution.py:152
  141.6 1.6 collective-permute-start.8
  146.3 2.6 %collective-permute-done.9 = f32[128,128]{1,0:T(8,128)S(1)} collective-permute-done((f32[128,128]{1,0:T(8,128)}, f32[128,128]{1,0:T(8,128)S(1)}, u32[]{:S(2)}, u32[]{:S(2)}) %collective-permute-start.9) | collective-permute-done | bytes 65568 | tf_op jit(solution)/shard_map/ppermute | solution.py:166
  149.0 2.8 %collective-permute-done.10 = f32[128,128]{1,0:T(8,128)S(1)} collective-permute-done((f32[128,128]{1,0:T(8,128)}, f32[128,128]{1,0:T(8,128)S(1)}, u32[]{:S(2)}, u32[]{:S(2)}) %collective-permute-start.10) | collective-permute-done | bytes 65568 | tf_op jit(solution)/shard_map/ppermute | solution.py:166
  152.7 5.7 %fusion.x_hbm = bf16[128,24576]{1,0:T(8,128)(2,1)} fusion(bf16[128,128]{1,0:T(8,128)(2,1)S(1)} %fusion.2, bf16[128,24576]{1,0:T(8,128)(2,1)} %copy-done, bf16[128,25088]{1,0:T(8,128)(2,1)S(1)} %pad_maximum_fusion), kind=kOutput, calls=%fused_computation.1 | convolution fusion | flops 814743552 | bytes 18907136 | tf_op jit(solution)/shard_map/dot_general | solution.py:252
  160.0 31.8 %shard_map.86 = (bf16[128,24576]{1,0:T(8,128)(2,1)}, bf16[128,24576]{1,0:T(8,128)(2,1)}, f32[2,128,128]{2,1,0:T(8,128)}) custom-call(s32[768]{0:T(1024)} %reshape.80.shift_ref, s32[1]{0:T(128)} %copy.14.count_ref, bf16[128,24576]{1,0:T(8,128)(2,1)} %fusion.x_hbm, bf16[128,256]{1,0:T(8,128)(2,1)} %subtract_convert_fusion.2.lo_ref, ...), custom_call_target="tpu_custom_call" | custom-call | tf_op jit(solution)/shard_map/pallas_call | solution.py:152
  192.9 2.4 %collective-permute-start.12 = (f32[2,128]{1,0:T(2,128)S(1)}, f32[2,128]{1,0:T(2,128)S(1)}, u32[]{:S(2)}, u32[]{:S(2)}) collective-permute-start(f32[2,128]{1,0:T(2,128)S(1)} %select_reduce_fusion), channel_id=1, source_target_pairs={{0,2},{1,3},{2,0},{3,1},{4,6},{5,7},{6,4},{7,5},{8,10},{9,11},{10,... | collective-permute-start | bytes 3080 | tf_op jit(solution)/shard_map/ppermute | solution.py:166
  197.4 2.4 %collective-permute-start.15 = (f32[2,128,128]{2,1,0:T(8,128)}, f32[2,128,128]{2,1,0:T(8,128)S(1)}, u32[]{:S(2)}, u32[]{:S(2)}) collective-permute-start(f32[2,128,128]{2,1,0:T(8,128)} %get-tuple-element.19), channel_id=1, source_target_pairs={{0,2},{1,3},{2,0},{3,1},{4,6},{5,7},{6,4},{7,5},{8,10},{9,11},{10,... | collective-permute-start | bytes 393224 | tf_op jit(solution)/shard_map/ppermute | solution.py:166
  200.0 9.5 %fusion.1 = bf16[1,128,24576]{2,1,0:T(8,128)(2,1)} fusion(bf16[128,24576]{1,0:T(8,128)(2,1)} %get-tuple-element.20, bf16[128,24576]{1,0:T(8,128)(2,1)} %get-tuple-element.18, f32[128]{0:T(128)S(1)} %fusion.8), kind=kLoop, calls=%fused_computation.4 | loop fusion | flops 15728640 | bytes 18874880 | tf_op jit(solution)/shard_map/broadcast_in_dim | solution.py:279
  209.5 1.5 collective-permute-done.16
  (59 shorter events, 13.5 us)
Async XLA Ops:
  10.7 2.6 %copy-start = (bf16[128,24576]{1,0:T(8,128)(2,1)}, bf16[128,24576]{1,0:T(8,128)(2,1)S(1)}, u32[]{:S(2)}) copy-start(bf16[128,24576]{1,0:T(8,128)(2,1)S(1)} %broadcast_select_fusion) | copy-start | bytes 18874372
  14.7 9.0 %collective-permute-start = (bf16[192,256]{1,0:T(8,128)(2,1)S(1)}, bf16[192,256]{1,0:T(8,128)(2,1)S(1)}, u32[]{:S(2)}, u32[]{:S(2)}) collective-permute-start(bf16[192,256]{1,0:T(8,128)(2,1)S(1)} %pad_maximum_fusion.5), channel_id=1, source_target_pairs={{0,1},{1,2},{2,3},{4,5},{5,6},{6,7},{8,9},{9,10},{10,11},{12,13},{... | collective-permute-start | bytes 294920 | tf_op jit(solution)/shard_map/ppermute | solution.py:228
  18.2 6.5 %collective-permute-start.1 = (bf16[192,256]{1,0:T(8,128)(2,1)S(1)}, bf16[192,256]{1,0:T(8,128)(2,1)S(1)}, u32[]{:S(2)}, u32[]{:S(2)}) collective-permute-start(bf16[192,256]{1,0:T(8,128)(2,1)S(1)} %pad_maximum_fusion.6), channel_id=1, source_target_pairs={{1,0},{2,1},{3,2},{5,4},{6,5},{7,6},{9,8},{10,9},{11,10},{13,12},{... | collective-permute-start | bytes 294920 | tf_op jit(solution)/shard_map/ppermute | solution.py:231
  24.7 6.3 %copy-start.5 = (bf16[192,256]{1,0:T(8,128)(2,1)}, bf16[192,256]{1,0:T(8,128)(2,1)S(1)}, u32[]{:S(2)}) copy-start(bf16[192,256]{1,0:T(8,128)(2,1)S(1)} %collective-permute-done.1) | copy-start | bytes 294916
  26.0 59.1 %collective-permute-start.3 = (bf16[32,25088]{1,0:T(8,128)(2,1)}, bf16[32,25088]{1,0:T(8,128)(2,1)S(1)}, u32[]{:S(2)}, u32[]{:S(2)}) collective-permute-start(bf16[32,25088]{1,0:T(8,128)(2,1)} %pad_maximum_fusion.2), channel_id=1, source_target_pairs={{4,0},{8,4},{12,8},{16,12},{20,16},{24,20},{28,24},{5,1},{9,5},{13... | collective-permute-start | bytes 4816904 | tf_op jit(solution)/shard_map/ppermute | solution.py:19
  27.9 57.2 %collective-permute-start.5 = (bf16[32,25088]{1,0:T(8,128)(2,1)}, bf16[32,25088]{1,0:T(8,128)(2,1)}, u32[]{:S(2)}, u32[]{:S(2)}) collective-permute-start(bf16[32,25088]{1,0:T(8,128)(2,1)} %pad_maximum_fusion.2), channel_id=1, source_target_pairs={{12,4},{20,12},{28,20},{13,5},{21,13},{29,21},{14,6},{22,14},{30,2... | collective-permute-start | bytes 4816904 | tf_op jit(solution)/shard_map/ppermute | solution.py:207
  31.0 68.9 %collective-permute-start.2 = (bf16[32,25088]{1,0:T(8,128)(2,1)}, bf16[32,25088]{1,0:T(8,128)(2,1)S(1)}, u32[]{:S(2)}, u32[]{:S(2)}) collective-permute-start(bf16[32,25088]{1,0:T(8,128)(2,1)} %pad_maximum_fusion.1), channel_id=1, source_target_pairs={{0,4},{4,8},{8,12},{12,16},{16,20},{20,24},{24,28},{1,5},{5,9},{9,... | collective-permute-start | bytes 4816904 | tf_op jit(solution)/shard_map/ppermute | solution.py:19
  34.6 65.2 %collective-permute-start.4 = (bf16[32,25088]{1,0:T(8,128)(2,1)}, bf16[32,25088]{1,0:T(8,128)(2,1)}, u32[]{:S(2)}, u32[]{:S(2)}) collective-permute-start(bf16[32,25088]{1,0:T(8,128)(2,1)} %pad_maximum_fusion.1), channel_id=1, source_target_pairs={{0,8},{8,16},{16,24},{1,9},{9,17},{17,25},{2,10},{10,18},{18,26},{... | collective-permute-start | bytes 4816904 | tf_op jit(solution)/shard_map/ppermute | solution.py:206
  61.8 40.6 %copy-start.7 = (s32[256,3]{0,1:T(4,128)S(1)}, s32[256,3]{0,1:T(4,128)}, u32[]{:S(2)}) copy-start(s32[256,3]{0,1:T(4,128)} %param.11) | copy-start | bytes 9220
  99.9 9.0 %copy-start.1 = (bf16[32,25088]{1,0:T(8,128)(2,1)}, bf16[32,25088]{1,0:T(8,128)(2,1)S(1)}, u32[]{:S(2)}) copy-start(bf16[32,25088]{1,0:T(8,128)(2,1)S(1)} %collective-permute-done.2) | copy-start | bytes 4816900
  99.9 4.7 %collective-permute-start.6 = (bf16[32,25088]{1,0:T(8,128)(2,1)S(1)}, bf16[32,25088]{1,0:T(8,128)(2,1)}, u32[]{:S(2)}, u32[]{:S(2)}) collective-permute-start(bf16[32,25088]{1,0:T(8,128)(2,1)S(1)} %collective-permute-done.2), channel_id=1, source_target_pairs={{0,4},{8,12},{16,20},{24,28},{1,5},{9,13},{17,21},{25,29},{2,6},{1... | collective-permute-start | bytes 4816904 | tf_op jit(solution)/shard_map/ppermute | solution.py:212
  103.3 5.3 %collective-permute-start.7 = (bf16[32,25088]{1,0:T(8,128)(2,1)S(1)}, bf16[32,25088]{1,0:T(8,128)(2,1)S(1)}, u32[]{:S(2)}, u32[]{:S(2)}) collective-permute-start(bf16[32,25088]{1,0:T(8,128)(2,1)S(1)} %collective-permute-done.3), channel_id=1, source_target_pairs={{4,0},{12,8},{20,16},{28,24},{5,1},{13,9},{21,17},{29,25},{6,2},{1... | collective-permute-start | bytes 4816904 | tf_op jit(solution)/shard_map/ppermute | solution.py:214
  141.6 4.7 %collective-permute-start.8 = (f32[128,128]{1,0:T(8,128)}, f32[128,128]{1,0:T(8,128)S(1)}, u32[]{:S(2)}, u32[]{:S(2)}) collective-permute-start(f32[128,128]{1,0:T(8,128)} %bitcast.48), channel_id=1, source_target_pairs={{0,1},{1,2},{2,3},{3,0},{4,5},{5,6},{6,7},{7,4},{8,9},{9,10},{10,1... | collective-permute-start | bytes 196616 | tf_op jit(solution)/shard_map/ppermute | solution.py:166
  143.2 5.8 %collective-permute-start.9 = (f32[128,128]{1,0:T(8,128)}, f32[128,128]{1,0:T(8,128)S(1)}, u32[]{:S(2)}, u32[]{:S(2)}) collective-permute-start(f32[128,128]{1,0:T(8,128)} %bitcast.49), channel_id=1, source_target_pairs={{0,2},{1,3},{2,0},{3,1},{4,6},{5,7},{6,4},{7,5},{8,10},{9,11},{10,... | collective-permute-start | bytes 196616 | tf_op jit(solution)/shard_map/ppermute | solution.py:166
  144.4 7.3 %collective-permute-start.10 = (f32[128,128]{1,0:T(8,128)}, f32[128,128]{1,0:T(8,128)S(1)}, u32[]{:S(2)}, u32[]{:S(2)}) collective-permute-start(f32[128,128]{1,0:T(8,128)} %bitcast.50), channel_id=1, source_target_pairs={{0,3},{1,0},{2,1},{3,2},{4,7},{5,4},{6,5},{7,6},{8,11},{9,8},{10,9... | collective-permute-start | bytes 196616 | tf_op jit(solution)/shard_map/ppermute | solution.py:166
  152.7 5.7 %copy-start.3 = (bf16[128,256]{1,0:T(8,128)(2,1)S(1)}, bf16[128,256]{1,0:T(8,128)(2,1)}, u32[]{:S(2)}) copy-start(bf16[128,256]{1,0:T(8,128)(2,1)} %get-tuple-element.21.hi_ref) | copy-start | bytes 196612
  152.7 5.7 %copy-start.6 = (bf16[192,256]{1,0:T(8,128)(2,1)S(1)}, bf16[192,256]{1,0:T(8,128)(2,1)}, u32[]{:S(2)}) copy-start(bf16[192,256]{1,0:T(8,128)(2,1)} %copy-done.5) | copy-start | bytes 294916
  152.7 6.5 %copy-start.2 = (bf16[128,256]{1,0:T(8,128)(2,1)S(1)}, bf16[128,256]{1,0:T(8,128)(2,1)}, u32[]{:S(2)}) copy-start(bf16[128,256]{1,0:T(8,128)(2,1)} %get-tuple-element.22.lo_ref) | copy-start | bytes 196612
  192.9 6.9 %collective-permute-start.11 = (f32[2,128]{1,0:T(2,128)S(1)}, f32[2,128]{1,0:T(2,128)S(1)}, u32[]{:S(2)}, u32[]{:S(2)}) collective-permute-start(f32[2,128]{1,0:T(2,128)S(1)} %select_reduce_fusion), channel_id=1, source_target_pairs={{0,1},{1,2},{2,3},{3,0},{4,5},{5,6},{6,7},{7,4},{8,9},{9,10},{10,1... | collective-permute-start | bytes 3080 | tf_op jit(solution)/shard_map/ppermute | solution.py:166
  192.9 7.0 %collective-permute-start.12 = (f32[2,128]{1,0:T(2,128)S(1)}, f32[2,128]{1,0:T(2,128)S(1)}, u32[]{:S(2)}, u32[]{:S(2)}) collective-permute-start(f32[2,128]{1,0:T(2,128)S(1)} %select_reduce_fusion), channel_id=1, source_target_pairs={{0,2},{1,3},{2,0},{3,1},{4,6},{5,7},{6,4},{7,5},{8,10},{9,11},{10,... | collective-permute-start | bytes 3080 | tf_op jit(solution)/shard_map/ppermute | solution.py:166
  195.4 4.6 %collective-permute-start.13 = (f32[2,128]{1,0:T(2,128)S(1)}, f32[2,128]{1,0:T(2,128)S(1)}, u32[]{:S(2)}, u32[]{:S(2)}) collective-permute-start(f32[2,128]{1,0:T(2,128)S(1)} %select_reduce_fusion), channel_id=1, source_target_pairs={{0,3},{1,0},{2,1},{3,2},{4,7},{5,4},{6,5},{7,6},{8,11},{9,8},{10,9... | collective-permute-start | bytes 3080 | tf_op jit(solution)/shard_map/ppermute | solution.py:166
  196.5 13.0 %collective-permute-start.14 = (f32[2,128,128]{2,1,0:T(8,128)}, f32[2,128,128]{2,1,0:T(8,128)S(1)}, u32[]{:S(2)}, u32[]{:S(2)}) collective-permute-start(f32[2,128,128]{2,1,0:T(8,128)} %get-tuple-element.19), channel_id=1, source_target_pairs={{0,1},{1,2},{2,3},{3,0},{4,5},{5,6},{6,7},{7,4},{8,9},{9,10},{10,1... | collective-permute-start | bytes 393224 | tf_op jit(solution)/shard_map/ppermute | solution.py:166
  197.4 12.1 %collective-permute-start.15 = (f32[2,128,128]{2,1,0:T(8,128)}, f32[2,128,128]{2,1,0:T(8,128)S(1)}, u32[]{:S(2)}, u32[]{:S(2)}) collective-permute-start(f32[2,128,128]{2,1,0:T(8,128)} %get-tuple-element.19), channel_id=1, source_target_pairs={{0,2},{1,3},{2,0},{3,1},{4,6},{5,7},{6,4},{7,5},{8,10},{9,11},{10,... | collective-permute-start | bytes 393224 | tf_op jit(solution)/shard_map/ppermute | solution.py:166
  199.8 11.2 %collective-permute-start.16 = (f32[2,128,128]{2,1,0:T(8,128)}, f32[2,128,128]{2,1,0:T(8,128)S(1)}, u32[]{:S(2)}, u32[]{:S(2)}) collective-permute-start(f32[2,128,128]{2,1,0:T(8,128)} %get-tuple-element.19), channel_id=1, source_target_pairs={{0,3},{1,0},{2,1},{3,2},{4,7},{5,4},{6,5},{7,6},{8,11},{9,8},{10,9... | collective-permute-start | bytes 393224 | tf_op jit(solution)/shard_map/ppermute | solution.py:166
  200.0 11.0 %copy-start.4 = (f32[2,128,128]{2,1,0:T(8,128)S(1)}, f32[2,128,128]{2,1,0:T(8,128)}, u32[]{:S(2)}) copy-start(f32[2,128,128]{2,1,0:T(8,128)} %get-tuple-element.19) | copy-start | bytes 393220

commit v14 on v12

--- a/solution.py
+++ b/solution.py
@@ -117,7 +117,7 @@
     block_rows, blk, width = matrices[0].shape
     rim = lower.shape[1]
     group = 32 if block_rows % 32 == 0 else block_rows
-    chunk = 512
+    chunk = 1024
     nmat = len(matrices)
     given = pair is not None
     keep = not given

time: 206 us -> 203 us (0.985)
  Pallas kernels: 50.3 us -> 47.7 us
    pallas_call x2, Pallas kernels: 50.3 us -> 47.7 us  [block_apply(): pl.pallas_call(kernel, grid_spec=grid_spec, out_shape=out_shape, compiler...]
where the time goes in v14:
time: 203 us; the launch traced here: 201 us
  local copies, waits for them, and re-layouts  56.6 us (28%)
  Pallas kernels  47.7 us (23%)
  starting transfers between devices  31.3 us (15%)
  other arithmetic  26.7 us (13%)
  waiting for transfers between devices  26.3 us (13%)
  matrix products  7.3 us (4%)
  between operations  5.46 us (3%)
    unnamed x18, local copies, waits for them, and re-layouts  49.4 us
    pallas_call x2, Pallas kernels, block_apply(): pl.pallas_call(kernel, grid_spec=grid_spec, out_shape=out_shape, compiler...  47.7 us
    ppermute x2, waiting for transfers between devices, from_behind(): return lax.ppermute(block, axis, route)  14.8 us
    ppermute x9, starting transfers between devices, row_sum(): lax.ppermute(part, 'row', [(i, (i + step) % count) for i in range(count)])  10.7 us
    broadcast_in_dim x1, other arithmetic, shards(): return (residual[None], margin_pencil[None], energy_pencil[None])  9.49 us
    ppermute x9, waiting for transfers between devices, row_sum(): lax.ppermute(part, 'row', [(i, (i + step) % count) for i in range(count)])  7.94 us
    dot_general x3, matrix products, clean(): lax.dot_general(margin_b, wins, (((0,), (0,)), ((), ())), preferred_eleme...  7.3 us
    ppermute x2, starting transfers between devices, from_behind(): return lax.ppermute(block, axis, route)  5.56 us
  transfers between devices with their start and end apart: 17, of which 7 were waited for; matrix products, arithmetic and copies ran while one was open for 31% of the time, Pallas kernels for 0%

profile of v14, /device:TPU:12, one launch (start us, length us, event | category | flops | bytes accessed | tf_op | source)
XLA Modules:
  0.0 201.3 jit_solution(4505950577797297942)
XLA Ops:
  0.6 1.3 fusion.14
  5.2 1.3 add_compare_fusion
  7.4 3.3 %broadcast_select_fusion = bf16[128,24576]{1,0:T(8,128)(2,1)S(1)} fusion(pred[128]{0:T(512)(128)(4,1)S(1)} %iota_compare_fusion.1, bf16[1,128,24576]{2,1,0:T(8,128)(2,1)} %param.6), kind=kLoop, calls=%fused_computation.5 | loop fusion | flops 3145728 | bytes 12583040 | tf_op jit(solution)/shard_map/jit(_where)/select_n | solution.py:217
  10.7 2.6 %copy-done = bf16[128,24576]{1,0:T(8,128)(2,1)} copy-done((bf16[128,24576]{1,0:T(8,128)(2,1)}, bf16[128,24576]{1,0:T(8,128)(2,1)S(1)}, u32[]{:S(2)}) %copy-start) | copy-done | bytes 6291480
  14.7 3.5 %collective-permute-start = (bf16[192,256]{1,0:T(8,128)(2,1)S(1)}, bf16[192,256]{1,0:T(8,128)(2,1)S(1)}, u32[]{:S(2)}, u32[]{:S(2)}) collective-permute-start(bf16[192,256]{1,0:T(8,128)(2,1)S(1)} %pad_maximum_fusion.5), channel_id=1, source_target_pairs={{0,1},{1,2},{2,3},{4,5},{5,6},{6,7},{8,9},{9,10},{10,11},{12,13},{... | collective-permute-start | bytes 294920 | tf_op jit(solution)/shard_map/ppermute | solution.py:228
  18.2 2.4 %collective-permute-start.1 = (bf16[192,256]{1,0:T(8,128)(2,1)S(1)}, bf16[192,256]{1,0:T(8,128)(2,1)S(1)}, u32[]{:S(2)}, u32[]{:S(2)}) collective-permute-start(bf16[192,256]{1,0:T(8,128)(2,1)S(1)} %pad_maximum_fusion.6), channel_id=1, source_target_pairs={{1,0},{2,1},{3,2},{5,4},{6,5},{7,6},{9,8},{10,9},{11,10},{13,12},{... | collective-permute-start | bytes 294920 | tf_op jit(solution)/shard_map/ppermute | solution.py:231
  20.6 3.0 %bitcast_select_fusion = (bf16[32,24576]{1,0:T(8,128)(2,1)S(1)}, bf16[32,24576]{1,0:T(8,128)(2,1)S(1)}) fusion(bf16[1,128,24576]{2,1,0:T(8,128)(2,1)} %param.6, s32[]{:T(128)S(6)} %select_n.133, pred[32]{0:T(512)(128)(4,1)S(1)} %get-tuple-element.43, s32[]{:T(128)S(6)} %select_n.130, pred[32]{0:T(512)(128)(4,1)S(1)} %get-tuple-element.44), kind=kLoop, calls=%fused_computation.10 | loop fusion | flops 1572864 | bytes 6291528 | tf_op jit(solution)/shard_map/jit(_where)/select_n | solution.py:184
  24.7 1.3 pad_maximum_fusion.2
  26.0 1.9 collective-permute-start.3
  27.9 1.8 collective-permute-start.5
  29.7 1.3 pad_maximum_fusion.1
  31.0 3.7 %collective-permute-start.2 = (bf16[32,25088]{1,0:T(8,128)(2,1)}, bf16[32,25088]{1,0:T(8,128)(2,1)S(1)}, u32[]{:S(2)}, u32[]{:S(2)}) collective-permute-start(bf16[32,25088]{1,0:T(8,128)(2,1)} %pad_maximum_fusion.1), channel_id=1, source_target_pairs={{0,4},{4,8},{8,12},{12,16},{16,20},{20,24},{24,28},{1,5},{5,9},{9,... | collective-permute-start | bytes 4816904 | tf_op jit(solution)/shard_map/ppermute | solution.py:19
  34.6 3.6 %collective-permute-start.4 = (bf16[32,25088]{1,0:T(8,128)(2,1)}, bf16[32,25088]{1,0:T(8,128)(2,1)}, u32[]{:S(2)}, u32[]{:S(2)}) collective-permute-start(bf16[32,25088]{1,0:T(8,128)(2,1)} %pad_maximum_fusion.1), channel_id=1, source_target_pairs={{0,8},{8,16},{16,24},{1,9},{9,17},{17,25},{2,10},{10,18},{18,26},{... | collective-permute-start | bytes 4816904 | tf_op jit(solution)/shard_map/ppermute | solution.py:206
  38.3 23.5 %copy.12.refs_0_ = bf16[256,96,288]{2,1,0:T(8,128)(2,1)} copy(bf16[256,96,288]{0,2,1:T(8,128)(2,1)} %param.9) | data formatting | bytes 28311552 | tf_op args[3]
  61.8 23.3 %copy.13.refs_1_ = bf16[256,96,288]{2,1,0:T(8,128)(2,1)} copy(bf16[256,96,288]{0,2,1:T(8,128)(2,1)} %param.10) | data formatting | bytes 28311552 | tf_op args[4]
  85.1 14.8 %collective-permute-done.2 = bf16[32,25088]{1,0:T(8,128)(2,1)S(1)} collective-permute-done((bf16[32,25088]{1,0:T(8,128)(2,1)}, bf16[32,25088]{1,0:T(8,128)(2,1)S(1)}, u32[]{:S(2)}, u32[]{:S(2)}) %collective-permute-start.2) | collective-permute-done | bytes 1605664 | tf_op jit(solution)/shard_map/ppermute | solution.py:19
  99.9 2.5 %collective-permute-start.6 = (bf16[32,25088]{1,0:T(8,128)(2,1)S(1)}, bf16[32,25088]{1,0:T(8,128)(2,1)}, u32[]{:S(2)}, u32[]{:S(2)}) collective-permute-start(bf16[32,25088]{1,0:T(8,128)(2,1)S(1)} %collective-permute-done.2), channel_id=1, source_target_pairs={{0,4},{8,12},{16,20},{24,28},{1,5},{9,13},{17,21},{25,29},{2,6},{1... | collective-permute-start | bytes 4816904 | tf_op jit(solution)/shard_map/ppermute | solution.py:212
  103.3 1.3 collective-permute-start.7
  104.6 1.6 broadcast_select_fusion.2
  106.2 2.4 %collective-permute-done.7 = bf16[32,25088]{1,0:T(8,128)(2,1)S(1)} collective-permute-done((bf16[32,25088]{1,0:T(8,128)(2,1)S(1)}, bf16[32,25088]{1,0:T(8,128)(2,1)S(1)}, u32[]{:S(2)}, u32[]{:S(2)}) %collective-permute-start.7) | collective-permute-done | bytes 1605664 | tf_op jit(solution)/shard_map/ppermute | solution.py:214
  109.5 2.5 %pad_maximum_fusion = bf16[128,25088]{1,0:T(8,128)(2,1)S(1)} fusion(bf16[32,25088]{1,0:T(8,128)(2,1)S(1)} %broadcast_select_fusion.1, bf16[32,25088]{1,0:T(8,128)(2,1)S(1)} %collective-permute-done.3, bf16[32,25088]{1,0:T(8,128)(2,1)} %copy-done.1, bf16[32,25088]{1,0:T(8,128)(2,1)S(1)} %broadcast_select_fusion.2), kind=kLoop, calls=%fused_computation.3 | loop fusion | flops 25690112 | bytes 12845056 | tf_op jit(solution)/shard_map/concatenate | solution.py:240
  112.1 3.3 %slice.102.x_hbm = bf16[128,24576]{1,0:T(8,128)(2,1)} slice(bf16[128,25088]{1,0:T(8,128)(2,1)S(1)} %pad_maximum_fusion), slice={[0:128], [0:24576]} | slice | bytes 12582912 | tf_op jit(solution)/shard_map/slice | solution.py:241
  115.4 20.0 %shard_map.85 = f32[1,128,128]{2,1,0:T(8,128)} custom-call(s32[768]{0:T(1024)} %reshape.80.shift_ref, s32[1]{0:T(128)} %copy.14.count_ref, bf16[128,24576]{1,0:T(8,128)(2,1)} %slice.102.x_hbm, bf16[128,256]{1,0:T(8,128)(2,1)} %get-tuple-element.22.lo_ref, bf16[128,256]{1,0:T(8,128)(2,1)} %get-tuple-element.21.hi_ref, bf16[256,96,288]{2,1,0:T(8,128)(2,1)} %copy.12.refs_0_, ...), custom_call_target="tpu_custom_call" | custom-call | tf_op jit(solution)/shard_map/pallas_call | solution.py:152
  135.4 1.6 collective-permute-start.8
  140.1 2.7 %collective-permute-done.9 = f32[128,128]{1,0:T(8,128)S(1)} collective-permute-done((f32[128,128]{1,0:T(8,128)}, f32[128,128]{1,0:T(8,128)S(1)}, u32[]{:S(2)}, u32[]{:S(2)}) %collective-permute-start.9) | collective-permute-done | bytes 65568 | tf_op jit(solution)/shard_map/ppermute | solution.py:166
  142.8 2.8 %collective-permute-done.10 = f32[128,128]{1,0:T(8,128)S(1)} collective-permute-done((f32[128,128]{1,0:T(8,128)}, f32[128,128]{1,0:T(8,128)S(1)}, u32[]{:S(2)}, u32[]{:S(2)}) %collective-permute-start.10) | collective-permute-done | bytes 65568 | tf_op jit(solution)/shard_map/ppermute | solution.py:166
  146.5 5.7 %fusion.x_hbm = bf16[128,24576]{1,0:T(8,128)(2,1)} fusion(bf16[128,128]{1,0:T(8,128)(2,1)S(1)} %fusion.2, bf16[128,24576]{1,0:T(8,128)(2,1)} %copy-done, bf16[128,25088]{1,0:T(8,128)(2,1)S(1)} %pad_maximum_fusion), kind=kOutput, calls=%fused_computation.1 | convolution fusion | flops 814743552 | bytes 18907136 | tf_op jit(solution)/shard_map/dot_general | solution.py:252
  153.8 27.7 %shard_map.86 = (bf16[128,24576]{1,0:T(8,128)(2,1)}, bf16[128,24576]{1,0:T(8,128)(2,1)}, f32[2,128,128]{2,1,0:T(8,128)}) custom-call(s32[768]{0:T(1024)} %reshape.80.shift_ref, s32[1]{0:T(128)} %copy.14.count_ref, bf16[128,24576]{1,0:T(8,128)(2,1)} %fusion.x_hbm, bf16[128,256]{1,0:T(8,128)(2,1)} %subtract_convert_fusion.2.lo_ref, ...), custom_call_target="tpu_custom_call" | custom-call | tf_op jit(solution)/shard_map/pallas_call | solution.py:152
  182.6 2.4 %collective-permute-start.12 = (f32[2,128]{1,0:T(2,128)S(1)}, f32[2,128]{1,0:T(2,128)S(1)}, u32[]{:S(2)}, u32[]{:S(2)}) collective-permute-start(f32[2,128]{1,0:T(2,128)S(1)} %select_reduce_fusion), channel_id=1, source_target_pairs={{0,2},{1,3},{2,0},{3,1},{4,6},{5,7},{6,4},{7,5},{8,10},{9,11},{10,... | collective-permute-start | bytes 3080 | tf_op jit(solution)/shard_map/ppermute | solution.py:166
  187.0 2.4 %collective-permute-start.15 = (f32[2,128,128]{2,1,0:T(8,128)}, f32[2,128,128]{2,1,0:T(8,128)S(1)}, u32[]{:S(2)}, u32[]{:S(2)}) collective-permute-start(f32[2,128,128]{2,1,0:T(8,128)} %get-tuple-element.19), channel_id=1, source_target_pairs={{0,2},{1,3},{2,0},{3,1},{4,6},{5,7},{6,4},{7,5},{8,10},{9,11},{10,... | collective-permute-start | bytes 393224 | tf_op jit(solution)/shard_map/ppermute | solution.py:166
  189.6 9.5 %fusion.1 = bf16[1,128,24576]{2,1,0:T(8,128)(2,1)} fusion(bf16[128,24576]{1,0:T(8,128)(2,1)} %get-tuple-element.20, bf16[128,24576]{1,0:T(8,128)(2,1)} %get-tuple-element.18, f32[128]{0:T(128)S(1)} %fusion.8), kind=kLoop, calls=%fused_computation.4 | loop fusion | flops 15728640 | bytes 18874880 | tf_op jit(solution)/shard_map/broadcast_in_dim | solution.py:279
  199.1 1.5 collective-permute-done.16
  (59 shorter events, 13.6 us)
Async XLA Ops:
  10.7 2.6 %copy-start = (bf16[128,24576]{1,0:T(8,128)(2,1)}, bf16[128,24576]{1,0:T(8,128)(2,1)S(1)}, u32[]{:S(2)}) copy-start(bf16[128,24576]{1,0:T(8,128)(2,1)S(1)} %broadcast_select_fusion) | copy-start | bytes 18874372
  14.7 8.9 %collective-permute-start = (bf16[192,256]{1,0:T(8,128)(2,1)S(1)}, bf16[192,256]{1,0:T(8,128)(2,1)S(1)}, u32[]{:S(2)}, u32[]{:S(2)}) collective-permute-start(bf16[192,256]{1,0:T(8,128)(2,1)S(1)} %pad_maximum_fusion.5), channel_id=1, source_target_pairs={{0,1},{1,2},{2,3},{4,5},{5,6},{6,7},{8,9},{9,10},{10,11},{12,13},{... | collective-permute-start | bytes 294920 | tf_op jit(solution)/shard_map/ppermute | solution.py:228
  18.2 6.5 %collective-permute-start.1 = (bf16[192,256]{1,0:T(8,128)(2,1)S(1)}, bf16[192,256]{1,0:T(8,128)(2,1)S(1)}, u32[]{:S(2)}, u32[]{:S(2)}) collective-permute-start(bf16[192,256]{1,0:T(8,128)(2,1)S(1)} %pad_maximum_fusion.6), channel_id=1, source_target_pairs={{1,0},{2,1},{3,2},{5,4},{6,5},{7,6},{9,8},{10,9},{11,10},{13,12},{... | collective-permute-start | bytes 294920 | tf_op jit(solution)/shard_map/ppermute | solution.py:231
  24.7 6.3 %copy-start.5 = (bf16[192,256]{1,0:T(8,128)(2,1)}, bf16[192,256]{1,0:T(8,128)(2,1)S(1)}, u32[]{:S(2)}) copy-start(bf16[192,256]{1,0:T(8,128)(2,1)S(1)} %collective-permute-done.1) | copy-start | bytes 294916
  26.0 59.1 %collective-permute-start.3 = (bf16[32,25088]{1,0:T(8,128)(2,1)}, bf16[32,25088]{1,0:T(8,128)(2,1)S(1)}, u32[]{:S(2)}, u32[]{:S(2)}) collective-permute-start(bf16[32,25088]{1,0:T(8,128)(2,1)} %pad_maximum_fusion.2), channel_id=1, source_target_pairs={{4,0},{8,4},{12,8},{16,12},{20,16},{24,20},{28,24},{5,1},{9,5},{13... | collective-permute-start | bytes 4816904 | tf_op jit(solution)/shard_map/ppermute | solution.py:19
  27.9 57.2 %collective-permute-start.5 = (bf16[32,25088]{1,0:T(8,128)(2,1)}, bf16[32,25088]{1,0:T(8,128)(2,1)}, u32[]{:S(2)}, u32[]{:S(2)}) collective-permute-start(bf16[32,25088]{1,0:T(8,128)(2,1)} %pad_maximum_fusion.2), channel_id=1, source_target_pairs={{12,4},{20,12},{28,20},{13,5},{21,13},{29,21},{14,6},{22,14},{30,2... | collective-permute-start | bytes 4816904 | tf_op jit(solution)/shard_map/ppermute | solution.py:207
  31.0 68.9 %collective-permute-start.2 = (bf16[32,25088]{1,0:T(8,128)(2,1)}, bf16[32,25088]{1,0:T(8,128)(2,1)S(1)}, u32[]{:S(2)}, u32[]{:S(2)}) collective-permute-start(bf16[32,25088]{1,0:T(8,128)(2,1)} %pad_maximum_fusion.1), channel_id=1, source_target_pairs={{0,4},{4,8},{8,12},{12,16},{16,20},{20,24},{24,28},{1,5},{5,9},{9,... | collective-permute-start | bytes 4816904 | tf_op jit(solution)/shard_map/ppermute | solution.py:19
  34.6 65.2 %collective-permute-start.4 = (bf16[32,25088]{1,0:T(8,128)(2,1)}, bf16[32,25088]{1,0:T(8,128)(2,1)}, u32[]{:S(2)}, u32[]{:S(2)}) collective-permute-start(bf16[32,25088]{1,0:T(8,128)(2,1)} %pad_maximum_fusion.1), channel_id=1, source_target_pairs={{0,8},{8,16},{16,24},{1,9},{9,17},{17,25},{2,10},{10,18},{18,26},{... | collective-permute-start | bytes 4816904 | tf_op jit(solution)/shard_map/ppermute | solution.py:206
  61.8 40.6 %copy-start.7 = (s32[256,3]{0,1:T(4,128)S(1)}, s32[256,3]{0,1:T(4,128)}, u32[]{:S(2)}) copy-start(s32[256,3]{0,1:T(4,128)} %param.11) | copy-start | bytes 9220
  99.9 9.0 %copy-start.1 = (bf16[32,25088]{1,0:T(8,128)(2,1)}, bf16[32,25088]{1,0:T(8,128)(2,1)S(1)}, u32[]{:S(2)}) copy-start(bf16[32,25088]{1,0:T(8,128)(2,1)S(1)} %collective-permute-done.2) | copy-start | bytes 4816900
  99.9 4.7 %collective-permute-start.6 = (bf16[32,25088]{1,0:T(8,128)(2,1)S(1)}, bf16[32,25088]{1,0:T(8,128)(2,1)}, u32[]{:S(2)}, u32[]{:S(2)}) collective-permute-start(bf16[32,25088]{1,0:T(8,128)(2,1)S(1)} %collective-permute-done.2), channel_id=1, source_target_pairs={{0,4},{8,12},{16,20},{24,28},{1,5},{9,13},{17,21},{25,29},{2,6},{1... | collective-permute-start | bytes 4816904 | tf_op jit(solution)/shard_map/ppermute | solution.py:212
  103.3 5.3 %collective-permute-start.7 = (bf16[32,25088]{1,0:T(8,128)(2,1)S(1)}, bf16[32,25088]{1,0:T(8,128)(2,1)S(1)}, u32[]{:S(2)}, u32[]{:S(2)}) collective-permute-start(bf16[32,25088]{1,0:T(8,128)(2,1)S(1)} %collective-permute-done.3), channel_id=1, source_target_pairs={{4,0},{12,8},{20,16},{28,24},{5,1},{13,9},{21,17},{29,25},{6,2},{1... | collective-permute-start | bytes 4816904 | tf_op jit(solution)/shard_map/ppermute | solution.py:214
  135.4 4.7 %collective-permute-start.8 = (f32[128,128]{1,0:T(8,128)}, f32[128,128]{1,0:T(8,128)S(1)}, u32[]{:S(2)}, u32[]{:S(2)}) collective-permute-start(f32[128,128]{1,0:T(8,128)} %bitcast.48), channel_id=1, source_target_pairs={{0,1},{1,2},{2,3},{3,0},{4,5},{5,6},{6,7},{7,4},{8,9},{9,10},{10,1... | collective-permute-start | bytes 196616 | tf_op jit(solution)/shard_map/ppermute | solution.py:166
  137.0 5.8 %collective-permute-start.9 = (f32[128,128]{1,0:T(8,128)}, f32[128,128]{1,0:T(8,128)S(1)}, u32[]{:S(2)}, u32[]{:S(2)}) collective-permute-start(f32[128,128]{1,0:T(8,128)} %bitcast.49), channel_id=1, source_target_pairs={{0,2},{1,3},{2,0},{3,1},{4,6},{5,7},{6,4},{7,5},{8,10},{9,11},{10,... | collective-permute-start | bytes 196616 | tf_op jit(solution)/shard_map/ppermute | solution.py:166
  138.2 7.3 %collective-permute-start.10 = (f32[128,128]{1,0:T(8,128)}, f32[128,128]{1,0:T(8,128)S(1)}, u32[]{:S(2)}, u32[]{:S(2)}) collective-permute-start(f32[128,128]{1,0:T(8,128)} %bitcast.50), channel_id=1, source_target_pairs={{0,3},{1,0},{2,1},{3,2},{4,7},{5,4},{6,5},{7,6},{8,11},{9,8},{10,9... | collective-permute-start | bytes 196616 | tf_op jit(solution)/shard_map/ppermute | solution.py:166
  146.5 5.7 %copy-start.3 = (bf16[128,256]{1,0:T(8,128)(2,1)S(1)}, bf16[128,256]{1,0:T(8,128)(2,1)}, u32[]{:S(2)}) copy-start(bf16[128,256]{1,0:T(8,128)(2,1)} %get-tuple-element.21.hi_ref) | copy-start | bytes 196612
  146.5 5.7 %copy-start.6 = (bf16[192,256]{1,0:T(8,128)(2,1)S(1)}, bf16[192,256]{1,0:T(8,128)(2,1)}, u32[]{:S(2)}) copy-start(bf16[192,256]{1,0:T(8,128)(2,1)} %copy-done.5) | copy-start | bytes 294916
  146.5 6.5 %copy-start.2 = (bf16[128,256]{1,0:T(8,128)(2,1)S(1)}, bf16[128,256]{1,0:T(8,128)(2,1)}, u32[]{:S(2)}) copy-start(bf16[128,256]{1,0:T(8,128)(2,1)} %get-tuple-element.22.lo_ref) | copy-start | bytes 196612
  182.5 6.9 %collective-permute-start.11 = (f32[2,128]{1,0:T(2,128)S(1)}, f32[2,128]{1,0:T(2,128)S(1)}, u32[]{:S(2)}, u32[]{:S(2)}) collective-permute-start(f32[2,128]{1,0:T(2,128)S(1)} %select_reduce_fusion), channel_id=1, source_target_pairs={{0,1},{1,2},{2,3},{3,0},{4,5},{5,6},{6,7},{7,4},{8,9},{9,10},{10,1... | collective-permute-start | bytes 3080 | tf_op jit(solution)/shard_map/ppermute | solution.py:166
  182.6 7.0 %collective-permute-start.12 = (f32[2,128]{1,0:T(2,128)S(1)}, f32[2,128]{1,0:T(2,128)S(1)}, u32[]{:S(2)}, u32[]{:S(2)}) collective-permute-start(f32[2,128]{1,0:T(2,128)S(1)} %select_reduce_fusion), channel_id=1, source_target_pairs={{0,2},{1,3},{2,0},{3,1},{4,6},{5,7},{6,4},{7,5},{8,10},{9,11},{10,... | collective-permute-start | bytes 3080 | tf_op jit(solution)/shard_map/ppermute | solution.py:166
  185.0 4.6 %collective-permute-start.13 = (f32[2,128]{1,0:T(2,128)S(1)}, f32[2,128]{1,0:T(2,128)S(1)}, u32[]{:S(2)}, u32[]{:S(2)}) collective-permute-start(f32[2,128]{1,0:T(2,128)S(1)} %select_reduce_fusion), channel_id=1, source_target_pairs={{0,3},{1,0},{2,1},{3,2},{4,7},{5,4},{6,5},{7,6},{8,11},{9,8},{10,9... | collective-permute-start | bytes 3080 | tf_op jit(solution)/shard_map/ppermute | solution.py:166
  186.1 13.0 %collective-permute-start.14 = (f32[2,128,128]{2,1,0:T(8,128)}, f32[2,128,128]{2,1,0:T(8,128)S(1)}, u32[]{:S(2)}, u32[]{:S(2)}) collective-permute-start(f32[2,128,128]{2,1,0:T(8,128)} %get-tuple-element.19), channel_id=1, source_target_pairs={{0,1},{1,2},{2,3},{3,0},{4,5},{5,6},{6,7},{7,4},{8,9},{9,10},{10,1... | collective-permute-start | bytes 393224 | tf_op jit(solution)/shard_map/ppermute | solution.py:166
  187.0 12.1 %collective-permute-start.15 = (f32[2,128,128]{2,1,0:T(8,128)}, f32[2,128,128]{2,1,0:T(8,128)S(1)}, u32[]{:S(2)}, u32[]{:S(2)}) collective-permute-start(f32[2,128,128]{2,1,0:T(8,128)} %get-tuple-element.19), channel_id=1, source_target_pairs={{0,2},{1,3},{2,0},{3,1},{4,6},{5,7},{6,4},{7,5},{8,10},{9,11},{10,... | collective-permute-start | bytes 393224 | tf_op jit(solution)/shard_map/ppermute | solution.py:166
  189.4 11.2 %collective-permute-start.16 = (f32[2,128,128]{2,1,0:T(8,128)}, f32[2,128,128]{2,1,0:T(8,128)S(1)}, u32[]{:S(2)}, u32[]{:S(2)}) collective-permute-start(f32[2,128,128]{2,1,0:T(8,128)} %get-tuple-element.19), channel_id=1, source_target_pairs={{0,3},{1,0},{2,1},{3,2},{4,7},{5,4},{6,5},{7,6},{8,11},{9,8},{10,9... | collective-permute-start | bytes 393224 | tf_op jit(solution)/shard_map/ppermute | solution.py:166
  189.6 11.0 %copy-start.4 = (f32[2,128,128]{2,1,0:T(8,128)S(1)}, f32[2,128,128]{2,1,0:T(8,128)}, u32[]{:S(2)}) copy-start(f32[2,128,128]{2,1,0:T(8,128)} %get-tuple-element.19) | copy-start | bytes 393220
